TPU v7x, 32 devices: a whole 2x2x4 slice. The times are simulated.
32 devices in a mesh: slab: 2 (over y), blk: 4 (over z), bag: 2 (over x), sub: 2 (over core).
Axes of the slice: x: 2, y: 2, z: 4, core: 2. Of those that a mesh axis runs over, the one named last changes fastest.
Arguments:
- real_points: bfloat16 [64, 8192], P(None, ('slab', 'blk')), parts along dimension 1, may hold values from -4 to 4
- synth_points: bfloat16 [64, 8192], P(None, ('slab', 'blk')), parts along dimension 1, may hold values from -4 to 4
- real_cluster: int32 [8192], P(('slab', 'blk')), parts along dimension 0, may hold values from 0 to 3
- synth_cluster: int32 [8192], P(('slab', 'blk')), parts along dimension 0, may hold values from 0 to 3
- real_weight: int32 [32, 8192], P('bag', ('slab', 'blk')), parts along dimension 1, may hold values from 0 to 4
- synth_weight: int32 [32, 8192], P('bag', ('slab', 'blk')), parts along dimension 1, may hold values from 0 to 4
- pair_block: int32 [64, 2], P(('slab', 'blk', 'sub')), parts along dimension 0, may hold values from 0 to 7, as said below
- pair_row: int32 [64, 2], P(('slab', 'blk', 'sub')), parts along dimension 0, may hold values from 0 to 7
- pair_count: int32 [64], P(('slab', 'blk', 'sub')), parts along dimension 0, may hold values from 1 to 2, as said below
Outputs:
- real_potential: float32 [32, 8192], P('bag', ('slab', 'blk')), parts along dimension 1
- synth_potential: float32 [32, 8192], P('bag', ('slab', 'blk')), parts along dimension 1
There are 2 independent parts, one for each index of `slab`. A program takes and returns all parts, laid end to end along the dimension named above; each array names one. Nothing has to cross between parts.
Inputs may be any that keep to these rules, and one draw needn't show every extreme that they name: `pair_block`: row 4 * (2 * b + s) + p belongs to the device at blk index b and sub index s; all listed pairs of the whole list are distinct. `pair_count`: in every draw all devices of one sub index list 2 pairs with one blk index.
All inputs are finite; a program needn't handle non-finite values.
Results may differ from a plain program's by a relative error of at most 0.0015.
Values may be sent and summed in bfloat16 or wider, within the bound.
No kernel may reach another device: no remote copies, remote signals or barrier semaphores. Data moves between devices by JAX's collectives and lax.ppermute only.
A program may use at most 64 MiB of HBM per device.

v0:
```python
import math

import jax
import jax.numpy as jnp
from jax import lax
from jax.sharding import PartitionSpec as P

BLOCK = 128
ITERS = 2


SMOOTH = 0.1
PENALTY = 0.3
SENTINEL = -1e30


def joined(value, axis, join):
    pieces = jax.tree.map(lambda part: lax.all_gather(part, axis), value)
    head = jax.tree.map(lambda part: part[0], pieces)
    tail = jax.tree.map(lambda part: part[1:], pieces)
    subtotal, _ = lax.scan(lambda subtotal, share: (join(subtotal, share), None), head, tail)
    return subtotal


def join_parts(earlier, latter):
    larger = jnp.maximum(earlier[0], latter[0])
    return (
        larger,
        earlier[1] * jnp.exp(earlier[0] - larger) + latter[1] * jnp.exp(latter[0] - larger),
    )


def fold_blocks(highest, mass_sum, owners, blocks):
    matches = owners[:, None] == jnp.arange(blocks, dtype=jnp.int32)[None, :]
    match_mask = matches[None, :, :, None]
    block_top = jnp.max(jnp.where(match_mask, highest[:, :, None, :], SENTINEL), axis=1)
    slot_top = jnp.take(block_top, owners, axis=1)
    scaled = mass_sum * jnp.exp(highest - slot_top)
    summed = jnp.sum(jnp.where(match_mask, scaled[:, :, None, :], 0.0), axis=1)
    return (block_top, summed)


def finish(log_weight, block_top, summed):
    spread = jnp.where(summed > 0.5, block_top + jnp.log(jnp.maximum(summed, 0.5)), 0.0)
    return SMOOTH * log_weight - SMOOTH * spread


def slot_costs(slot_real, slot_real_tag, slot_synth, slot_synth_tag):
    inner_prod = jnp.einsum(
        "dgi,dgj->gij", slot_real, slot_synth, preferred_element_type=jnp.float32
    )
    real_sq = jnp.sum(jnp.square(slot_real.astype(jnp.float32)), axis=0)
    synth_sq = jnp.sum(jnp.square(slot_synth.astype(jnp.float32)), axis=0)
    differ = (slot_real_tag[:, :, None] != slot_synth_tag[:, None, :]).astype(jnp.float32)
    return 0.5 * real_sq[:, :, None] + 0.5 * synth_sq[:, None, :] - inner_prod + PENALTY * differ


def sweep(slot_x, slot_tags, far_y, far_tags, panel_rows, along_rows, group_size):
    marginals, slot_count, width_pts = panel_rows.shape
    group_total = slot_count // group_size

    def one_group(group_index):
        first_slot = group_index * group_size
        pair_cost = slot_costs(
            lax.dynamic_slice_in_dim(slot_x, first_slot, group_size, 1),
            lax.dynamic_slice_in_dim(slot_tags, first_slot, group_size, 0),
            lax.dynamic_slice_in_dim(far_y, first_slot, group_size, 1),
            lax.dynamic_slice_in_dim(far_tags, first_slot, group_size, 0),
        )
        panel_part = lax.dynamic_slice_in_dim(panel_rows, first_slot, group_size, 1)
        if along_rows:
            scores = (panel_part[:, :, None, :] - pair_cost[None]) / SMOOTH
            highest = jnp.max(scores, axis=3)
            mass_sum = jnp.sum(jnp.exp(scores - highest[:, :, :, None]), axis=3)
        else:
            scores = (panel_part[:, :, :, None] - pair_cost[None]) / SMOOTH
            highest = jnp.max(scores, axis=2)
            mass_sum = jnp.sum(jnp.exp(scores - highest[:, :, None, :]), axis=2)
        return (highest, mass_sum)

    highest, mass_sum = lax.map(one_group, jnp.arange(group_total, dtype=jnp.int32))
    highest = jnp.transpose(highest, (1, 0, 2, 3)).reshape(marginals, slot_count, width_pts)
    mass_sum = jnp.transpose(mass_sum, (1, 0, 2, 3)).reshape(marginals, slot_count, width_pts)
    return (highest, mass_sum)


def fetch_panel(synth_pot, requested, global_col):
    marginals, blocks, width_pts = synth_pot.shape
    replies = jnp.take(synth_pot, requested, axis=1)
    arrived = lax.all_to_all(replies, "blk", split_axis=1, concat_axis=1, tiled=True)
    return arrived.reshape(marginals, global_col.shape[0], width_pts)


def column_update(highest, mass_sum, requested, log_synth):
    marginals, blocks, width_pts = log_synth.shape
    peer_count, capacity = requested.shape
    back_top, back_sum = (
        lax.all_to_all(
            highest.reshape(marginals, peer_count, capacity, width_pts),
            "blk",
            split_axis=1,
            concat_axis=1,
            tiled=True,
        ),
        lax.all_to_all(
            mass_sum.reshape(marginals, peer_count, capacity, width_pts),
            "blk",
            split_axis=1,
            concat_axis=1,
            tiled=True,
        ),
    )
    block_top, summed = fold_blocks(
        back_top.reshape(marginals, peer_count * capacity, width_pts),
        back_sum.reshape(marginals, peer_count * capacity, width_pts),
        requested.reshape(peer_count * capacity),
        blocks,
    )
    block_top, summed = joined((block_top, summed), "sub", join_parts)
    return finish(log_synth, block_top, summed)


def shards(
    real_points,
    synth_points,
    real_cluster,
    synth_cluster,
    real_weight,
    synth_weight,
    pair_block,
    pair_row,
    pair_count,
):
    features, point_count = real_points.shape
    blocks = point_count // BLOCK
    marginals = real_weight.shape[0]
    peer_count, capacity = pair_block.shape
    slot_count = peer_count * capacity
    group_size = math.gcd(slot_count, 4)
    own_real = real_points.reshape(features, blocks, BLOCK)
    own_synth = synth_points.reshape(features, blocks, BLOCK)
    real_tags = real_cluster.reshape(blocks, BLOCK).astype(jnp.bfloat16)
    synth_tags = synth_cluster.reshape(1, blocks, BLOCK).astype(jnp.bfloat16)
    log_real = jnp.log(real_weight.astype(jnp.float32) + 0.5).reshape(marginals, blocks, BLOCK)
    log_synth = jnp.log(synth_weight.astype(jnp.float32) + 0.5).reshape(marginals, blocks, BLOCK)
    listed = lax.broadcasted_iota(jnp.int32, (peer_count, capacity), 1) < pair_count[:, None]
    wanted = jnp.where(listed, pair_block, 0)
    rows_used = jnp.where(listed, pair_row, 0).reshape(slot_count)
    usable = listed.reshape(slot_count)[None, :, None]
    global_col = (jnp.arange(peer_count, dtype=jnp.int32)[:, None] * blocks + wanted).reshape(
        slot_count
    )
    requested = lax.all_to_all(wanted, "blk", split_axis=0, concat_axis=0, tiled=True)
    far_y, far_tags = (
        lax.all_to_all(
            jnp.take(own_synth, requested, axis=1), "blk", split_axis=1, concat_axis=1, tiled=True
        ),
        lax.all_to_all(
            jnp.take(synth_tags, requested, axis=1), "blk", split_axis=1, concat_axis=1, tiled=True
        ),
    )
    far_y = far_y.reshape(features, slot_count, BLOCK)
    far_tags = far_tags.reshape(slot_count, BLOCK)
    slot_x = jnp.take(own_real, rows_used, axis=1)
    slot_tags = jnp.take(real_tags, rows_used, axis=0)
    synth_pot = jnp.zeros((marginals, blocks, BLOCK), jnp.float32)
    real_pot = jnp.zeros((marginals, blocks, BLOCK), jnp.float32)
    for sweep_index in range(ITERS):
        if sweep_index == 0:
            panel_rows = jnp.zeros((marginals, slot_count, BLOCK), jnp.float32)
        else:
            panel_rows = fetch_panel(synth_pot, requested, global_col)
        highest, mass_sum = sweep(slot_x, slot_tags, far_y, far_tags, panel_rows, True, group_size)
        highest = jnp.where(usable, highest, SENTINEL)
        mass_sum = jnp.where(usable, mass_sum, 0.0)
        block_top, summed = fold_blocks(highest, mass_sum, rows_used, blocks)
        block_top, summed = joined((block_top, summed), "sub", join_parts)
        real_pot = finish(log_real, block_top, summed)
        own_rows = jnp.take(real_pot, rows_used, axis=1)
        highest, mass_sum = sweep(slot_x, slot_tags, far_y, far_tags, own_rows, False, group_size)
        highest = jnp.where(usable, highest, SENTINEL)
        mass_sum = jnp.where(usable, mass_sum, 0.0)
        synth_pot = column_update(highest, mass_sum, requested, log_synth)
    return (real_pot.reshape(marginals, point_count), synth_pot.reshape(marginals, point_count))


def solution(mesh):
    placed = (
        P(None, ("slab", "blk")),
        P(None, ("slab", "blk")),
        P(("slab", "blk")),
        P(("slab", "blk")),
        P("bag", ("slab", "blk")),
        P("bag", ("slab", "blk")),
        P(("slab", "blk", "sub"), None),
        P(("slab", "blk", "sub"), None),
        P(("slab", "blk", "sub")),
    )
    return jax.shard_map(
        shards,
        mesh=mesh,
        in_specs=placed,
        out_specs=(P("bag", ("slab", "blk")), P("bag", ("slab", "blk"))),
        check_vma=False,
    )
```

profile of v0, /device:TPU:0, one launch (start us, length us, event | category | flops | bytes accessed | tf_op | source)
XLA Modules:
  0.0 132.3 jit_solution(11505282491066260187)
XLA Ops:
  0.7 0.8 select_bitcast_fusion.5
  1.4 0.7 copy.188
  2.1 6.3 %all-to-all-start = ((s32[4,1,2]{2,1,0:T(1,128)}), s32[4,1,2]{2,1,0:T(1,128)S(1)}, u32[]{:S(2)}, u32[]{:S(2)}) async-start(s32[4,1,2]{2,1,0:T(1,128)} %copy.188), calls=%async_computation | async-start | bytes 4096 | tf_op jit(solution)/shard_map/all_to_all | solution.py:153
  8.7 0.7 iota_compare_fusion.2
  9.5 0.6 gather_fusion
  10.1 0.6 gather_fusion.2
  11.5 2.3 %all-to-all-done = s32[4,1,2]{2,1,0:T(1,128)S(1)} async-done(((s32[4,1,2]{2,1,0:T(1,128)}), s32[4,1,2]{2,1,0:T(1,128)S(1)}, u32[]{:S(2)}, u32[]{:S(2)}) %all-to-all-start) | async-done | bytes 64 | tf_op jit(solution)/shard_map/all_to_all | solution.py:153
  14.3 0.6 gather_fusion.1
  14.8 0.6 gather_fusion.3
  15.4 0.7 select_bitcast_fusion
  16.1 0.7 broadcast_select_fusion.4
  16.8 3.2 %all-to-all-start.2 = ((bf16[1,4,2,128]{3,2,0,1:T(2,128)(2,1)}), bf16[1,4,2,128]{3,2,0,1:T(2,128)(2,1)S(1)}, u32[]{:S(2)}, u32[]{:S(2)}) async-start(bf16[1,4,2,128]{3,2,0,1:T(2,128)(2,1)} %broadcast_select_fusion.4), calls=%async_computation.2 | async-start | bytes 4096 | tf_op jit(solution)/shard_map/all_to_all | solution.py:158
  20.0 0.6 broadcast.508
  20.6 0.7 reduce.4
  21.5 4.0 %all-to-all-done.2 = bf16[1,4,2,128]{3,2,0,1:T(2,128)(2,1)S(1)} async-done(((bf16[1,4,2,128]{3,2,0,1:T(2,128)(2,1)}), bf16[1,4,2,128]{3,2,0,1:T(2,128)(2,1)S(1)}, u32[]{:S(2)}, u32[]{:S(2)}) %all-to-all-start.2) | async-done | bytes 2080 | tf_op jit(solution)/shard_map/all_to_all | solution.py:158
  25.5 3.3 %all-to-all-start.1 = ((bf16[64,4,2,128]{3,0,2,1:T(8,128)(2,1)}), bf16[64,4,2,128]{3,0,2,1:T(8,128)(2,1)S(1)}, u32[]{:S(2)}, u32[]{:S(2)}) async-start(bf16[64,4,2,128]{3,0,2,1:T(8,128)(2,1)} %select_bitcast_fusion), calls=%async_computation.1 | async-start | bytes 262144 | tf_op jit(solution)/shard_map/all_to_all | solution.py:155
  28.8 5.9 %all-to-all-done.1 = bf16[64,4,2,128]{3,0,2,1:T(8,128)(2,1)S(1)} async-done(((bf16[64,4,2,128]{3,0,2,1:T(8,128)(2,1)}), bf16[64,4,2,128]{3,0,2,1:T(8,128)(2,1)S(1)}, u32[]{:S(2)}, u32[]{:S(2)}) %all-to-all-start.1) | async-done | bytes 131104 | tf_op jit(solution)/shard_map/all_to_all | solution.py:155
  34.7 6.2 %while.8 = (s32[]{:T(128)}, f32[2,16,4,128]{3,1,2,0:T(8,128)S(1)}, f32[2,16,4,128]{3,1,2,0:T(8,128)S(1)}, s32[2]{0:T(128)S(1)}, bf16[64,8,128]{2,0,1:T(8,128)(2,...) while((s32[]{:T(128)}, f32[2,16,4,128]{3,1,2,0:T(8,128)S(1)}, ...), condition=%wide.region_5.6_spmd, body=%wide.region_0.5_spmd.sunk | while | flops 11197958 | bytes 1471679 | solution.py:81
  34.7 0.6 dynamic_slice.153
  36.5 1.3 exponential_reduce_fusion.8
  37.8 0.6 dynamic_slice.153
  39.6 1.3 exponential_reduce_fusion.8
  41.2 1.9 %all-gather.1 = f32[32,8,128]{2,0,1:T(8,128)S(1)} all-gather(f32[16,8,128]{2,0,1:T(8,128)S(1)} %copy.203), channel_id=3, replica_groups=mesh['slab'=2,'blk'=4,'bag'=2,'sub'=2] {'sub'}, dimensions={0}, use_global_device_ids=true | all-gather | bytes 196608 | tf_op jit(solution)/shard_map/all_gather | solution.py:18
  43.9 1.9 %all-gather = f32[32,8,128]{2,0,1:T(8,128)S(1)} all-gather(f32[16,8,128]{2,0,1:T(8,128)S(1)} %copy.205), channel_id=2, replica_groups=mesh['slab'=2,'blk'=4,'bag'=2,'sub'=2] {'sub'}, dimensions={0}, use_global_device_ids=true | all-gather | bytes 196608 | tf_op jit(solution)/shard_map/all_gather | solution.py:18
  46.6 8.7 %while.9 = (s32[]{:T(128)}, f32[2,16,4,128]{3,1,2,0:T(8,128)S(1)}, f32[2,16,4,128]{3,1,2,0:T(8,128)S(1)}, s32[2]{0:T(128)S(1)}, f32[16,8,128]{2,0,1:T(8,128)S(1)...) while((s32[]{:T(128)}, f32[2,16,4,128]{3,1,2,0:T(8,128)S(1)}, ...), condition=%wide.region_13.15_spmd, body=%wide.region_8.14_spmd.sunk | while | flops 16236550 | bytes 1498315 | solution.py:81
  46.6 0.6 dynamic_slice.159
  48.2 1.3 fusion.75
  49.5 1.3 %exponential_reduce_fusion.9 = f32[16,4,128]{2,1,0:T(4,128)S(1)} fusion(f32[16,4,128]{2,1,0:T(4,128)S(1)} %fusion.75, f32[4,128,128]{2,1,0:T(8,128)S(1)} %fusion.74, f32[16,4,128]{2,1,0:T(4,128)S(1)} %copy.313), kind=kLoop, calls=%fused_computation.27.clone.1 | loop fusion | flops 4186112 | bytes 360448 | tf_op jit(solution)/shard_map/while/body/eval_jaxpr/reduce_sum | solution.py:78
  50.9 0.6 dynamic_slice.159
  52.6 1.3 fusion.75
  53.9 1.3 %exponential_reduce_fusion.9 = f32[16,4,128]{2,1,0:T(4,128)S(1)} fusion(f32[16,4,128]{2,1,0:T(4,128)S(1)} %fusion.75, f32[4,128,128]{2,1,0:T(8,128)S(1)} %fusion.74, f32[16,4,128]{2,1,0:T(4,128)S(1)} %copy.313), kind=kLoop, calls=%fused_computation.27.clone.1 | loop fusion | flops 4186112 | bytes 360448 | tf_op jit(solution)/shard_map/while/body/eval_jaxpr/reduce_sum | solution.py:78
  55.3 0.7 broadcast_select_fusion.1
  56.0 3.3 %all-to-all-start.4 = ((f32[16,4,2,128]{3,0,2,1:T(8,128)}), f32[16,4,2,128]{3,0,2,1:T(8,128)S(1)}, u32[]{:S(2)}, u32[]{:S(2)}) async-start(f32[16,4,2,128]{3,0,2,1:T(8,128)} %get-tuple-element.447), calls=%async_computation.4 | async-start | bytes 131072 | tf_op jit(solution)/shard_map/all_to_all | solution.py:98
  59.3 5.7 %all-to-all-done.4 = f32[16,4,2,128]{3,0,2,1:T(8,128)S(1)} async-done(((f32[16,4,2,128]{3,0,2,1:T(8,128)}), f32[16,4,2,128]{3,0,2,1:T(8,128)S(1)}, u32[]{:S(2)}, u32[]{:S(2)}) %all-to-all-start.4) | async-done | bytes 65568 | tf_op jit(solution)/shard_map/all_to_all | solution.py:98
  65.0 3.3 %all-to-all-start.3 = ((f32[16,4,2,128]{3,0,2,1:T(8,128)}), f32[16,4,2,128]{3,0,2,1:T(8,128)S(1)}, u32[]{:S(2)}, u32[]{:S(2)}) async-start(f32[16,4,2,128]{3,0,2,1:T(8,128)} %get-tuple-element.448), calls=%async_computation.3 | async-start | bytes 131072 | tf_op jit(solution)/shard_map/all_to_all | solution.py:105
  69.0 1.9 %all-gather.3 = f32[32,8,128]{2,0,1:T(8,128)S(1)} all-gather(f32[16,8,128]{2,0,1:T(8,128)S(1)} %copy.212), channel_id=5, replica_groups=mesh['slab'=2,'blk'=4,'bag'=2,'sub'=2] {'sub'}, dimensions={0}, use_global_device_ids=true | all-gather | bytes 196608 | tf_op jit(solution)/shard_map/all_gather | solution.py:18
  70.9 3.1 %all-to-all-done.3 = f32[16,4,2,128]{3,0,2,1:T(8,128)S(1)} async-done(((f32[16,4,2,128]{3,0,2,1:T(8,128)}), f32[16,4,2,128]{3,0,2,1:T(8,128)S(1)}, u32[]{:S(2)}, u32[]{:S(2)}) %all-to-all-start.3) | async-done | bytes 65568 | tf_op jit(solution)/shard_map/all_to_all | solution.py:105
  74.3 1.9 %all-gather.2 = f32[32,8,128]{2,0,1:T(8,128)S(1)} all-gather(f32[16,8,128]{2,0,1:T(8,128)S(1)} %copy.214), channel_id=4, replica_groups=mesh['slab'=2,'blk'=4,'bag'=2,'sub'=2] {'sub'}, dimensions={0}, use_global_device_ids=true | all-gather | bytes 196608 | tf_op jit(solution)/shard_map/all_gather | solution.py:18
  76.8 0.7 select_bitcast_fusion.4
  77.5 3.3 %all-to-all-start.5 = ((f32[16,4,2,128]{3,0,2,1:T(8,128)}), f32[16,4,2,128]{3,0,2,1:T(8,128)S(1)}, u32[]{:S(2)}, u32[]{:S(2)}) async-start(f32[16,4,2,128]{3,0,2,1:T(8,128)} %select_bitcast_fusion.4), calls=%async_computation.5 | async-start | bytes 131072 | tf_op jit(solution)/shard_map/all_to_all | solution.py:90
  80.8 5.7 %all-to-all-done.5 = f32[16,4,2,128]{3,0,2,1:T(8,128)S(1)} async-done(((f32[16,4,2,128]{3,0,2,1:T(8,128)}), f32[16,4,2,128]{3,0,2,1:T(8,128)S(1)}, u32[]{:S(2)}, u32[]{:S(2)}) %all-to-all-start.5) | async-done | bytes 65568 | tf_op jit(solution)/shard_map/all_to_all | solution.py:90
  86.6 10.6 %while.10 = (s32[]{:T(128)}, f32[2,16,4,128]{3,1,2,0:T(8,128)S(1)}, f32[2,16,4,128]{3,1,2,0:T(8,128)S(1)}, s32[2]{0:T(128)S(1)}, f32[16,8,128]{2,1,0:T(8,128)S(1...) while((s32[]{:T(128)}, f32[2,16,4,128]{3,1,2,0:T(8,128)S(1)}, ...), condition=%wide.region_21.23_spmd, body=%wide.region_16.22_spmd.sunk | while | flops 16236550 | bytes 1432779 | solution.py:81
  86.6 0.6 dynamic_slice.165
  88.3 1.2 fusion.79
  89.4 2.4 %exponential_reduce_fusion.10 = f32[16,4,128]{2,1,0:T(4,128)S(1)} fusion(f32[16,4,128]{2,1,0:T(4,128)S(1)} %fusion.79, f32[4,128,128]{2,1,0:T(8,128)S(1)} %fusion.78, f32[16,4,128]{2,1,0:T(4,128)S(1)} %constant_dynamic-slice_fusion.22), kind=kLoop, calls=%fused_computation.44.clone.1 | loop fusion | flops 4186112 | bytes 360448 | tf_op jit(solution)/shard_map/while/body/eval_jaxpr/reduce_sum | solution.py:74
  91.9 0.6 dynamic_slice.165
  93.6 1.2 fusion.79
  94.8 2.4 %exponential_reduce_fusion.10 = f32[16,4,128]{2,1,0:T(4,128)S(1)} fusion(f32[16,4,128]{2,1,0:T(4,128)S(1)} %fusion.79, f32[4,128,128]{2,1,0:T(8,128)S(1)} %fusion.78, f32[16,4,128]{2,1,0:T(4,128)S(1)} %constant_dynamic-slice_fusion.22), kind=kLoop, calls=%fused_computation.44.clone.1 | loop fusion | flops 4186112 | bytes 360448 | tf_op jit(solution)/shard_map/while/body/eval_jaxpr/reduce_sum | solution.py:74
  98.0 1.9 %all-gather.5 = f32[32,8,128]{2,0,1:T(8,128)S(1)} all-gather(f32[16,8,128]{2,0,1:T(8,128)S(1)} %copy.221), channel_id=7, replica_groups=mesh['slab'=2,'blk'=4,'bag'=2,'sub'=2] {'sub'}, dimensions={0}, use_global_device_ids=true | all-gather | bytes 196608 | tf_op jit(solution)/shard_map/all_gather | solution.py:18
  100.2 1.9 %all-gather.4 = f32[32,8,128]{2,0,1:T(8,128)S(1)} all-gather(f32[16,8,128]{2,0,1:T(8,128)S(1)} %copy.223), channel_id=6, replica_groups=mesh['slab'=2,'blk'=4,'bag'=2,'sub'=2] {'sub'}, dimensions={0}, use_global_device_ids=true | all-gather | bytes 196608 | tf_op jit(solution)/shard_map/all_gather | solution.py:18
  102.9 8.7 %while.11 = (s32[]{:T(128)}, f32[2,16,4,128]{3,1,2,0:T(8,128)S(1)}, f32[2,16,4,128]{3,1,2,0:T(8,128)S(1)}, s32[2]{0:T(128)S(1)}, f32[16,8,128]{2,0,1:T(8,128)S(1...) while((s32[]{:T(128)}, f32[2,16,4,128]{3,1,2,0:T(8,128)S(1)}, ...), condition=%wide.region_29.31_spmd, body=%wide.region_24.30_spmd.sunk | while | flops 16236550 | bytes 1498315 | solution.py:81
  102.9 0.6 dynamic_slice.171
  104.5 1.3 fusion.83
  105.8 1.3 %exponential_reduce_fusion.11 = f32[16,4,128]{2,1,0:T(4,128)S(1)} fusion(f32[16,4,128]{2,1,0:T(4,128)S(1)} %fusion.83, f32[4,128,128]{2,1,0:T(8,128)S(1)} %fusion.82, f32[16,4,128]{2,1,0:T(4,128)S(1)} %copy.318), kind=kLoop, calls=%fused_computation.61.clone.1 | loop fusion | flops 4186112 | bytes 360448 | tf_op jit(solution)/shard_map/while/body/eval_jaxpr/reduce_sum | solution.py:78
  107.2 0.6 dynamic_slice.171
  108.9 1.3 fusion.83
  110.2 1.3 %exponential_reduce_fusion.11 = f32[16,4,128]{2,1,0:T(4,128)S(1)} fusion(f32[16,4,128]{2,1,0:T(4,128)S(1)} %fusion.83, f32[4,128,128]{2,1,0:T(8,128)S(1)} %fusion.82, f32[16,4,128]{2,1,0:T(4,128)S(1)} %copy.318), kind=kLoop, calls=%fused_computation.61.clone.1 | loop fusion | flops 4186112 | bytes 360448 | tf_op jit(solution)/shard_map/while/body/eval_jaxpr/reduce_sum | solution.py:78
  111.5 0.7 broadcast_select_fusion
  112.3 8.1 %all_to_all.50 = f32[16,4,2,128]{3,0,2,1:T(8,128)S(1)} all-to-all(f32[16,4,2,128]{3,0,2,1:T(8,128)S(1)} %get-tuple-element.445), channel_id=1, replica_groups=mesh['slab'=2,'blk'=4,'bag'=2,'sub'=2] {'blk'}, dimensions={1} | all-to-all | bytes 131072 | tf_op jit(solution)/shard_map/all_to_all | solution.py:98
  120.4 3.3 %all-to-all-start.6 = ((f32[16,4,2,128]{3,0,2,1:T(8,128)}), f32[16,4,2,128]{3,0,2,1:T(8,128)S(1)}, u32[]{:S(2)}, u32[]{:S(2)}) async-start(f32[16,4,2,128]{3,0,2,1:T(8,128)} %get-tuple-element.446), calls=%async_computation.6 | async-start | bytes 131072 | tf_op jit(solution)/shard_map/all_to_all | solution.py:105
  124.4 1.9 %all-gather.7 = f32[32,8,128]{2,1,0:T(8,128)S(1)} all-gather(f32[16,8,128]{2,1,0:T(8,128)S(1)} %select_reduce_fusion.1), channel_id=9, replica_groups=mesh['slab'=2,'blk'=4,'bag'=2,'sub'=2] {'sub'}, dimensions={0}, use_global_device_ids=true | all-gather | bytes 196608 | tf_op jit(solution)/shard_map/all_gather | solution.py:18
  126.3 3.1 %all-to-all-done.6 = f32[16,4,2,128]{3,0,2,1:T(8,128)S(1)} async-done(((f32[16,4,2,128]{3,0,2,1:T(8,128)}), f32[16,4,2,128]{3,0,2,1:T(8,128)S(1)}, u32[]{:S(2)}, u32[]{:S(2)}) %all-to-all-start.6) | async-done | bytes 65568 | tf_op jit(solution)/shard_map/all_to_all | solution.py:105
  129.6 1.9 %all-gather.6 = f32[32,8,128]{2,1,0:T(8,128)S(1)} all-gather(f32[16,8,128]{2,1,0:T(8,128)S(1)} %select_reduce_fusion), channel_id=8, replica_groups=mesh['slab'=2,'blk'=4,'bag'=2,'sub'=2] {'sub'}, dimensions={0}, use_global_device_ids=true | all-gather | bytes 196608 | tf_op jit(solution)/shard_map/all_gather | solution.py:18
  131.5 0.8 fusion.28
  (165 shorter events, 11.3 us)
Async XLA Ops:
  0.6 8.8 %copy-start = (bf16[64,1024]{1,0:T(8,128)(2,1)S(1)}, bf16[64,1024]{1,0:T(8,128)(2,1)}, u32[]{:S(2)}) copy-start(bf16[64,1024]{1,0:T(8,128)(2,1)} %param.19) | copy-start | bytes 393220
  0.6 8.8 %copy-start.4 = (s32[1024]{0:T(1024)S(1)}, s32[1024]{0:T(1024)}, u32[]{:S(2)}) copy-start(s32[1024]{0:T(1024)} %param.21) | copy-start | bytes 12292
  2.1 11.8 %all-to-all-start = ((s32[4,1,2]{2,1,0:T(1,128)}), s32[4,1,2]{2,1,0:T(1,128)S(1)}, u32[]{:S(2)}, u32[]{:S(2)}) async-start(s32[4,1,2]{2,1,0:T(1,128)} %copy.188), calls=%async_computation | async-start | bytes 4096 | tf_op jit(solution)/shard_map/all_to_all | solution.py:153
  9.5 1.3 %copy-start.3 = (bf16[64,1024]{1,0:T(8,128)(2,1)S(1)}, bf16[64,1024]{1,0:T(8,128)(2,1)}, u32[]{:S(2)}) copy-start(bf16[64,1024]{1,0:T(8,128)(2,1)} %param.20) | copy-start | bytes 393220
  10.6 0.7 copy-start.5
  16.8 8.7 %all-to-all-start.2 = ((bf16[1,4,2,128]{3,2,0,1:T(2,128)(2,1)}), bf16[1,4,2,128]{3,2,0,1:T(2,128)(2,1)S(1)}, u32[]{:S(2)}, u32[]{:S(2)}) async-start(bf16[1,4,2,128]{3,2,0,1:T(2,128)(2,1)} %broadcast_select_fusion.4), calls=%async_computation.2 | async-start | bytes 4096 | tf_op jit(solution)/shard_map/all_to_all | solution.py:158
  25.5 9.2 %all-to-all-start.1 = ((bf16[64,4,2,128]{3,0,2,1:T(8,128)(2,1)}), bf16[64,4,2,128]{3,0,2,1:T(8,128)(2,1)S(1)}, u32[]{:S(2)}, u32[]{:S(2)}) async-start(bf16[64,4,2,128]{3,0,2,1:T(8,128)(2,1)} %select_bitcast_fusion), calls=%async_computation.1 | async-start | bytes 262144 | tf_op jit(solution)/shard_map/all_to_all | solution.py:155
  43.8 2.0 %copy-start.1 = (s32[16,1024]{1,0:T(8,128)S(1)}, s32[16,1024]{1,0:T(8,128)}, u32[]{:S(2)}) copy-start(s32[16,1024]{1,0:T(8,128)} %param.23) | copy-start | bytes 196612
  56.0 9.0 %all-to-all-start.4 = ((f32[16,4,2,128]{3,0,2,1:T(8,128)}), f32[16,4,2,128]{3,0,2,1:T(8,128)S(1)}, u32[]{:S(2)}, u32[]{:S(2)}) async-start(f32[16,4,2,128]{3,0,2,1:T(8,128)} %get-tuple-element.447), calls=%async_computation.4 | async-start | bytes 131072 | tf_op jit(solution)/shard_map/all_to_all | solution.py:98
  65.0 9.0 %all-to-all-start.3 = ((f32[16,4,2,128]{3,0,2,1:T(8,128)}), f32[16,4,2,128]{3,0,2,1:T(8,128)S(1)}, u32[]{:S(2)}, u32[]{:S(2)}) async-start(f32[16,4,2,128]{3,0,2,1:T(8,128)} %get-tuple-element.448), calls=%async_computation.3 | async-start | bytes 131072 | tf_op jit(solution)/shard_map/all_to_all | solution.py:105
  74.1 2.0 %copy-start.2 = (s32[16,1024]{1,0:T(8,128)S(1)}, s32[16,1024]{1,0:T(8,128)}, u32[]{:S(2)}) copy-start(s32[16,1024]{1,0:T(8,128)} %param.24) | copy-start | bytes 196612
  77.5 9.0 %all-to-all-start.5 = ((f32[16,4,2,128]{3,0,2,1:T(8,128)}), f32[16,4,2,128]{3,0,2,1:T(8,128)S(1)}, u32[]{:S(2)}, u32[]{:S(2)}) async-start(f32[16,4,2,128]{3,0,2,1:T(8,128)} %select_bitcast_fusion.4), calls=%async_computation.5 | async-start | bytes 131072 | tf_op jit(solution)/shard_map/all_to_all | solution.py:90
  120.4 9.0 %all-to-all-start.6 = ((f32[16,4,2,128]{3,0,2,1:T(8,128)}), f32[16,4,2,128]{3,0,2,1:T(8,128)S(1)}, u32[]{:S(2)}, u32[]{:S(2)}) async-start(f32[16,4,2,128]{3,0,2,1:T(8,128)} %get-tuple-element.446), calls=%async_computation.6 | async-start | bytes 131072 | tf_op jit(solution)/shard_map/all_to_all | solution.py:105
where the time goes:
time: 133 us; the launch traced here: 132 us
  waiting for transfers between devices  29.7 us (22%)
  other arithmetic  29.2 us (22%)
  starting transfers between devices  26 us (20%)
  blocking collectives  23.3 us (18%)
  local copies, waits for them, and re-layouts  14.6 us (11%)
  loops' own time  5.91 us (4%)
  matrix products  2.3 us (2%)
    all_gather x8, blocking collectives, joined(): pieces = jax.tree.map(lambda part: lax.all_gather(part, axis), value)  15.2 us
    all_to_all x1, blocking collectives, column_update(): lax.all_to_all(highest.reshape(marginals, peer_count, capacity, width_pts...  8.1 us
    reduce_sum x4, other arithmetic, one_group(): mass_sum = jnp.sum(jnp.exp(scores - highest[:, :, :, None]), axis=3)  7.43 us
    all_to_all x2, starting transfers between devices, column_update(): lax.all_to_all(mass_sum.reshape(marginals, peer_count, capacity, width_pt...  6.57 us
    all_to_all x1, starting transfers between devices, shards(): lax.all_to_all(wanted, 'blk', split_axis=0, concat_axis=0, tiled=True)  6.32 us
    all_to_all x2, waiting for transfers between devices, column_update(): lax.all_to_all(mass_sum.reshape(marginals, peer_count, capacity, width_pt...  6.15 us
    another operation x4, loops' own time, sweep(): lax.map(one_group, jnp.arange(group_total, dtype=jnp.int32))  5.91 us
    all_to_all x1, waiting for transfers between devices, shards(): lax.all_to_all(jnp.take(own_synth, requested, axis=1), 'blk', split_axis=...  5.87 us
  transfers between devices with their start and end apart: 7, of which 7 were waited for; matrix products, arithmetic and copies ran while one was open for 4% of the time, Pallas kernels for 0%

commit v1 on v0

v1 whole, which is shorter than its diff:
```python
import jax
import jax.numpy as jnp
from jax import lax
from jax.sharding import PartitionSpec as P

BLOCK = 128
ITERS = 2


SMOOTH = 0.1
PENALTY = 0.3
SENTINEL = -1e30


def join_parts(earlier, latter):
    larger = jnp.maximum(earlier[0], latter[0])
    return (
        larger,
        earlier[1] * jnp.exp(earlier[0] - larger) + latter[1] * jnp.exp(latter[0] - larger),
    )


def fold_blocks(highest, mass_sum, owners, blocks):
    matches = owners[:, None] == jnp.arange(blocks, dtype=jnp.int32)[None, :]
    match_mask = matches[None, :, :, None]
    block_top = jnp.max(jnp.where(match_mask, highest[:, :, None, :], SENTINEL), axis=1)
    slot_top = jnp.take(block_top, owners, axis=1)
    scaled = mass_sum * jnp.exp(highest - slot_top)
    summed = jnp.sum(jnp.where(match_mask, scaled[:, :, None, :], 0.0), axis=1)
    return (block_top, summed)


def finish(log_weight, block_top, summed):
    spread = jnp.where(summed > 0.5, block_top + jnp.log(jnp.maximum(summed, 0.5)), 0.0)
    return SMOOTH * log_weight - SMOOTH * spread


def slot_costs(slot_real, slot_real_tag, slot_synth, slot_synth_tag):
    inner_prod = jnp.einsum(
        "dgi,dgj->gij", slot_real, slot_synth, preferred_element_type=jnp.float32
    )
    real_sq = jnp.sum(jnp.square(slot_real.astype(jnp.float32)), axis=0)
    synth_sq = jnp.sum(jnp.square(slot_synth.astype(jnp.float32)), axis=0)
    differ = (slot_real_tag[:, :, None] != slot_synth_tag[:, None, :]).astype(jnp.float32)
    return 0.5 * real_sq[:, :, None] + 0.5 * synth_sq[:, None, :] - inner_prod + PENALTY * differ


def lse_parts(scores, axis):
    highest = jnp.max(scores, axis=axis)
    mass_sum = jnp.sum(jnp.exp(scores - jnp.expand_dims(highest, axis)), axis=axis)
    return (highest, mass_sum)


def make_shards(n_sub):
    group = ("blk", "sub")

    def sub_join(parts):
        if n_sub == 2:
            other = lax.ppermute(jnp.stack(parts), "sub", [(0, 1), (1, 0)])
            return join_parts(parts, (other[0], other[1]))
        pieces = lax.all_gather(jnp.stack(parts), "sub")
        subtotal = (pieces[0, 0], pieces[0, 1])
        for index in range(1, n_sub):
            subtotal = join_parts(subtotal, (pieces[index, 0], pieces[index, 1]))
        return subtotal

    def shards(
        real_points,
        synth_points,
        real_cluster,
        synth_cluster,
        real_weight,
        synth_weight,
        pair_block,
        pair_row,
        pair_count,
    ):
        features, point_count = real_points.shape
        blocks = point_count // BLOCK
        marginals = real_weight.shape[0]
        peer_count, capacity = pair_block.shape
        slot_count = peer_count * capacity
        my_sub = lax.axis_index("sub")
        own_real = real_points.reshape(features, blocks, BLOCK)
        real_tags = real_cluster.reshape(blocks, BLOCK)
        own_synth = jnp.concatenate(
            [synth_points, synth_cluster.astype(jnp.bfloat16)[None, :]], axis=0
        ).reshape(features + 1, blocks, BLOCK)
        log_real = jnp.log(real_weight.astype(jnp.float32) + 0.5).reshape(marginals, blocks, BLOCK)
        log_synth = jnp.log(synth_weight.astype(jnp.float32) + 0.5).reshape(marginals, blocks, BLOCK)
        listed = lax.broadcasted_iota(jnp.int32, (peer_count, capacity), 1) < pair_count[:, None]
        wanted = jnp.where(listed, pair_block, 0)
        rows_used = jnp.where(listed, pair_row, 0).reshape(slot_count)
        usable = listed.reshape(slot_count)[None, :, None]

        asked = jnp.broadcast_to(wanted[:, None, :], (peer_count, n_sub, capacity))
        requested = lax.all_to_all(
            asked.reshape(peer_count * n_sub, capacity), group, split_axis=0, concat_axis=0, tiled=True
        )
        requested_all = requested.reshape(peer_count * n_sub * capacity)
        requested_same = lax.dynamic_index_in_dim(
            requested.reshape(peer_count, n_sub, capacity), my_sub, axis=1, keepdims=False
        ).reshape(slot_count)

        far = lax.all_to_all(
            jnp.take(own_synth, requested_same, axis=1).reshape(features + 1, peer_count, capacity, BLOCK),
            "blk",
            split_axis=1,
            concat_axis=1,
            tiled=True,
        ).reshape(features + 1, slot_count, BLOCK)
        far_y = far[:features]
        far_tags = far[features]
        slot_x = jnp.take(own_real, rows_used, axis=1)
        slot_tags = jnp.take(real_tags, rows_used, axis=0).astype(jnp.bfloat16)
        cost = slot_costs(slot_x, slot_tags, far_y, far_tags)

        synth_pot = jnp.zeros((marginals, blocks, BLOCK), jnp.float32)
        real_pot = jnp.zeros((marginals, blocks, BLOCK), jnp.float32)
        for sweep_index in range(ITERS):
            if sweep_index == 0:
                panel = jnp.zeros((marginals, slot_count, BLOCK), jnp.float32)
            else:
                panel = lax.all_to_all(
                    jnp.take(synth_pot, requested_same, axis=1).reshape(
                        marginals, peer_count, capacity, BLOCK
                    ),
                    "blk",
                    split_axis=1,
                    concat_axis=1,
                    tiled=True,
                ).reshape(marginals, slot_count, BLOCK)
            scores = (panel[:, :, None, :] - cost[None]) / SMOOTH
            highest, mass_sum = lse_parts(scores, 3)
            highest = jnp.where(usable, highest, SENTINEL)
            mass_sum = jnp.where(usable, mass_sum, 0.0)
            block_top, summed = fold_blocks(highest, mass_sum, rows_used, blocks)
            block_top, summed = sub_join((block_top, summed))
            real_pot = finish(log_real, block_top, summed)

            own_rows = jnp.take(real_pot, rows_used, axis=1)
            scores = (own_rows[:, :, :, None] - cost[None]) / SMOOTH
            highest, mass_sum = lse_parts(scores, 2)
            highest = jnp.where(usable, highest, SENTINEL)
            mass_sum = jnp.where(usable, mass_sum, 0.0)
            outgoing = jnp.stack([highest, mass_sum]).reshape(2, marginals, peer_count, 1, capacity, BLOCK)
            outgoing = jnp.broadcast_to(
                outgoing, (2, marginals, peer_count, n_sub, capacity, BLOCK)
            ).reshape(2, marginals, peer_count * n_sub * capacity, BLOCK)
            back = lax.all_to_all(outgoing, group, split_axis=2, concat_axis=2, tiled=True)
            block_top, summed = fold_blocks(back[0], back[1], requested_all, blocks)
            synth_pot = finish(log_synth, block_top, summed)
        return (real_pot.reshape(marginals, point_count), synth_pot.reshape(marginals, point_count))

    return shards


def solution(mesh):
    placed = (
        P(None, ("slab", "blk")),
        P(None, ("slab", "blk")),
        P(("slab", "blk")),
        P(("slab", "blk")),
        P("bag", ("slab", "blk")),
        P("bag", ("slab", "blk")),
        P(("slab", "blk", "sub"), None),
        P(("slab", "blk", "sub"), None),
        P(("slab", "blk", "sub")),
    )
    return jax.shard_map(
        make_shards(mesh.shape["sub"]),
        mesh=mesh,
        in_specs=placed,
        out_specs=(P("bag", ("slab", "blk")), P("bag", ("slab", "blk"))),
        check_vma=False,
    )
```

time: 133 us -> 94.5 us (0.71)
  blocking collectives: 23.3 us -> 8.1 us
  starting transfers between devices: 26 us -> 17.2 us
  loops' own time: 5.91 us -> 0 us
  local copies, waits for them, and re-layouts: 14.6 us -> 11.8 us
  other arithmetic: 29.2 us -> 27.1 us
  waiting for transfers between devices: 29.7 us -> 27.8 us
  matrix products: 2.3 us -> 0.69 us
    all_gather x8 -> x0, blocking collectives: 15.2 us -> none  [joined(): pieces = jax.tree.map(lambda part: lax.all_gather(part, axis), value)]
    all_to_all x7 -> x4, starting transfers between devices: 26 us -> 17 us  [the longest x2 6.82 us: shards(): lax.all_to_all(outgoing, group, split_axis=2, concat_axis=2, tiled=True)]
    another operation x4 -> x0, loops' own time: 5.91 us -> none  [sweep(): lax.map(one_group, jnp.arange(group_total, dtype=jnp.int32))]
    dynamic_slice x26 -> x1, local copies, waits for them, and re-layouts: 4.92 us -> 0.01 us  [shards(): lax.dynamic_index_in_dim(requested.reshape(peer_count, n_sub, capacity),...]
    all_to_all x7 -> x4, waiting for transfers between devices: 29.7 us -> 25.3 us  [the longest x2 19.1 us: shards(): lax.all_to_all(outgoing, group, split_axis=2, concat_axis=2, tiled=True)]
    ppermute x0 -> x2, waiting for transfers between devices: none -> 2.43 us  [sub_join(): other = lax.ppermute(jnp.stack(parts), 'sub', [(0, 1), (1, 0)])]
    broadcast_in_dim x0 -> x5, local copies, waits for them, and re-layouts: none -> 2.09 us  [the longest x4 1.49 us: shards(): jnp.broadcast_to(outgoing, (2, marginals, peer_count, n_sub, capacity, BL...]
    dot_general x8 -> x1, matrix products: 2.3 us -> 0.69 us  [slot_costs(): jnp.einsum('dgi,dgj->gij', slot_real, slot_synth, preferred_element_type=...]
  transfers between devices with their start and end apart: 7 -> 6, of which waited for: 7 -> 6; matrix products, arithmetic and copies ran while one was open for 4% -> 6% of each run, Pallas kernels for 0% -> 0%
where the time goes in v1:
time: 94.5 us; the launch traced here: 93.9 us
  waiting for transfers between devices  27.8 us (29%)
  other arithmetic  27.1 us (29%)
  starting transfers between devices  17.2 us (18%)
  local copies, waits for them, and re-layouts  11.8 us (12%)
  blocking collectives  8.1 us (9%)
  between operations  1.25 us (1%)
    all_to_all x2, waiting for transfers between devices, shards(): lax.all_to_all(outgoing, group, split_axis=2, concat_axis=2, tiled=True)  19.1 us
    reduce_sum x4, other arithmetic, lse_parts(): jnp.sum(jnp.exp(scores - jnp.expand_dims(highest, axis)), axis=axis)  12.5 us
    all_to_all x1, blocking collectives, shards(): lax.all_to_all(jnp.take(synth_pot, requested_same, axis=1).reshape(margin...  8.1 us
    reduce_max x3, other arithmetic, lse_parts(): highest = jnp.max(scores, axis=axis)  7.27 us
    all_to_all x2, starting transfers between devices, shards(): lax.all_to_all(outgoing, group, split_axis=2, concat_axis=2, tiled=True)  6.82 us
    all_to_all x1, starting transfers between devices, shards(): lax.all_to_all(asked.reshape(peer_count * n_sub, capacity), group, split_...  6.33 us
    all_to_all x1, waiting for transfers between devices, shards(): lax.all_to_all(jnp.take(own_synth, requested_same, axis=1).reshape(featur...  4.98 us
    all_to_all x1, starting transfers between devices, shards(): lax.all_to_all(jnp.take(own_synth, requested_same, axis=1).reshape(featur...  3.88 us
  transfers between devices with their start and end apart: 6, of which 6 were waited for; matrix products, arithmetic and copies ran while one was open for 6% of the time, Pallas kernels for 0%

profile of v1, /device:TPU:0, one launch (start us, length us, event | category | flops | bytes accessed | tf_op | source)
XLA Modules:
  0.0 93.9 jit_solution(12721157853608474020)
XLA Ops:
  0.7 0.8 broadcast_select_fusion.10
  1.4 0.1 copy.196
  1.5 0.6 broadcast_in_dim.258.clone
  2.1 6.3 %all-to-all-start = ((s32[8,1,2]{2,1,0:T(1,128)}), s32[8,1,2]{2,1,0:T(1,128)S(1)}, u32[]{:S(2)}, u32[]{:S(2)}) async-start(s32[8,1,2]{2,1,0:T(1,128)} %bitcast), calls=%async_computation | async-start | bytes 8192 | tf_op jit(solution)/shard_map/all_to_all | solution.py:97
  8.4 0.1 copy.127
  8.7 0.7 iota_compare_fusion.2
  9.5 0.7 convert_bitcast_fusion
  10.2 0.9 copy_bitcast_fusion.1
  11.1 0.6 gather_fusion
  11.7 0.1 multiply_reduce_fusion.1
  11.8 0.6 gather_fusion.2
  12.5 0.1 copy.128
  12.7 1.2 %all-to-all-done = s32[8,1,2]{2,1,0:T(1,128)S(1)} async-done(((s32[8,1,2]{2,1,0:T(1,128)}), s32[8,1,2]{2,1,0:T(1,128)S(1)}, u32[]{:S(2)}, u32[]{:S(2)}) %all-to-all-start) | async-done | bytes 96 | tf_op jit(solution)/shard_map/all_to_all | solution.py:97
  14.1 0.1 copy.198
  14.2 0.1 copy.135
  14.3 0.6 gather_fusion.1
  14.9 0.8 broadcast_select_fusion
  15.7 3.9 %all-to-all-start.1 = ((bf16[65,4,2,128]{3,2,0,1:T(2,128)(2,1)}), bf16[65,4,2,128]{3,2,0,1:T(2,128)(2,1)S(1)}, u32[]{:S(2)}, u32[]{:S(2)}) async-start(bf16[65,4,2,128]{3,2,0,1:T(2,128)(2,1)} %broadcast_select_fusion), calls=%async_computation.1 | async-start | bytes 266240 | tf_op jit(solution)/shard_map/all_to_all | solution.py:105
  19.6 0.5 broadcast.500
  20.1 0.7 reduce.6
  20.9 5.0 %all-to-all-done.1 = bf16[65,4,2,128]{3,2,0,1:T(2,128)(2,1)S(1)} async-done(((bf16[65,4,2,128]{3,2,0,1:T(2,128)(2,1)}), bf16[65,4,2,128]{3,2,0,1:T(2,128)(2,1)S(1)}, u32[]{:S(2)}, u32[]{:S(2)}) %all-to-all-start.1) | async-done | bytes 133152 | tf_op jit(solution)/shard_map/all_to_all | solution.py:105
  26.0 0.1 multiply_reduce_fusion
  26.1 0.7 subtract_multiply_fusion.3
  26.8 0.2 copy.141
  27.0 2.4 %exponential_reduce_fusion.3 = f32[16,8,128]{2,1,0:T(8,128)S(1)} fusion(f32[8,128]{1,0:T(8,128)S(1)} %get-tuple-element.5, f32[8,128,128]{2,1,0:T(8,128)S(1)} %copy.141), kind=kLoop, calls=%fused_computation.19 | loop fusion | flops 4177920 | bytes 593920 | tf_op jit(solution)/shard_map/reduce_sum | solution.py:50
  29.6 0.1 select_reduce_fusion.7
  29.7 0.6 gather_fusion.3
  30.3 0.1 fusion.24
  30.4 0.1 select_reduce_fusion.6
  30.7 0.2 copy.153
  30.9 1.1 %collective-permute-done = f32[2,16,8,128]{3,1,2,0:T(8,128)S(1)} collective-permute-done((f32[2,16,8,128]{3,1,2,0:T(8,128)S(1)}, f32[2,16,8,128]{3,1,2,0:T(8,128)S(1)}, u32[]{:S(2)}, u32[]{:S(2)}) %collective-permute-start) | collective-permute-done | bytes 131104 | tf_op jit(solution)/shard_map/ppermute | solution.py:59
  32.1 0.6 gather_fusion.4
  32.7 2.5 %fusion.2 = f32[16,8,128]{2,1,0:T(8,128)S(1)} fusion(f32[8,128,128]{2,1,0:T(8,128)S(1)} %copy.153, f32[16,8,128]{2,1,0:T(8,128)S(1)} %copy.152), kind=kLoop, calls=%fused_computation.18 | loop fusion | flops 6275072 | bytes 655360 | tf_op jit(solution)/shard_map/reduce_max | solution.py:49
  35.3 2.7 %exponential_reduce_fusion.2 = f32[16,8,128]{2,1,0:T(8,128)S(1)} fusion(f32[16,8,128]{2,1,0:T(8,128)S(1)} %fusion.2, f32[8,128,128]{2,1,0:T(8,128)S(1)} %copy.153, f32[16,8,128]{2,1,0:T(8,128)S(1)} %copy.152), kind=kLoop, calls=%fused_computation.16 | loop fusion | flops 8372224 | bytes 720896 | tf_op jit(solution)/shard_map/reduce_sum | solution.py:50
  37.9 0.1 broadcast_select_fusion.5
  38.2 0.7 broadcast_in_dim.276
  38.9 3.4 %all-to-all-start.2 = ((f32[2,16,16,128]{3,1,0,2:T(8,128)}), f32[2,16,16,128]{3,1,0,2:T(8,128)S(1)}, u32[]{:S(2)}, u32[]{:S(2)}) async-start(f32[2,16,16,128]{3,1,0,2:T(8,128)} %bitcast.21), calls=%async_computation.2 | async-start | bytes 524288 | tf_op jit(solution)/shard_map/all_to_all | solution.py:150
  42.4 9.6 %all-to-all-done.2 = f32[2,16,16,128]{3,1,0,2:T(8,128)S(1)} async-done(((f32[2,16,16,128]{3,1,0,2:T(8,128)}), f32[2,16,16,128]{3,1,0,2:T(8,128)S(1)}, u32[]{:S(2)}, u32[]{:S(2)}) %all-to-all-start.2) | async-done | bytes 262176 | tf_op jit(solution)/shard_map/all_to_all | solution.py:150
  52.0 0.2 select_reduce_fusion.3
  52.2 0.6 gather_fusion.5
  52.8 0.1 fusion.5
  53.0 0.1 select_reduce_fusion.2
  53.1 0.5 copy-done.3
  53.7 0.6 gather_fusion.6
  54.3 8.1 %all_to_all.29 = f32[16,4,2,128]{3,0,2,1:T(8,128)S(1)} all-to-all(f32[16,4,2,128]{3,0,2,1:T(8,128)S(1)} %bitcast.230), channel_id=1, replica_groups=mesh['slab'=2,'blk'=4,'bag'=2,'sub'=2] {'blk'}, dimensions={1} | all-to-all | bytes 131072 | tf_op jit(solution)/shard_map/all_to_all | solution.py:124
  62.4 2.2 %fusion.1 = f32[16,8,128]{2,1,0:T(8,128)S(1)} fusion(f32[16,8,128]{2,1,0:T(8,128)S(1)} %copy.164, f32[8,128,128]{2,1,0:T(8,128)S(1)} %copy.153), kind=kLoop, calls=%fused_computation.15 | loop fusion | flops 6275072 | bytes 655360 | tf_op jit(solution)/shard_map/reduce_max | solution.py:49
  64.8 4.8 %exponential_reduce_fusion.1 = f32[16,8,128]{2,1,0:T(8,128)S(1)} fusion(f32[16,8,128]{2,1,0:T(8,128)S(1)} %fusion.1, f32[16,8,128]{2,1,0:T(8,128)S(1)} %copy.164, f32[8,128,128]{2,1,0:T(8,128)S(1)} %copy.153), kind=kLoop, calls=%fused_computation.13 | loop fusion | flops 8372224 | bytes 720896 | tf_op jit(solution)/shard_map/reduce_sum | solution.py:50
  69.6 0.1 select_reduce_fusion.5
  69.7 0.6 gather_fusion.7
  70.3 0.1 fusion.22
  70.4 0.1 select_reduce_fusion.4
  70.7 1.3 %collective-permute-done.1 = f32[2,16,8,128]{3,1,2,0:T(8,128)S(1)} collective-permute-done((f32[2,16,8,128]{3,1,2,0:T(8,128)S(1)}, f32[2,16,8,128]{3,1,2,0:T(8,128)S(1)}, u32[]{:S(2)}, u32[]{:S(2)}) %collective-permute-start.1) | collective-permute-done | bytes 131104 | tf_op jit(solution)/shard_map/ppermute | solution.py:59
  72.1 0.6 gather_fusion.8
  72.7 2.5 %fusion = f32[16,8,128]{2,1,0:T(8,128)S(1)} fusion(f32[16,8,128]{2,1,0:T(8,128)S(1)} %copy.178, f32[8,128,128]{2,1,0:T(8,128)S(1)} %copy.153), kind=kLoop, calls=%fused_computation.12 | loop fusion | flops 6275072 | bytes 655360 | tf_op jit(solution)/shard_map/reduce_max | solution.py:49
  75.3 2.7 %exponential_reduce_fusion = f32[16,8,128]{2,1,0:T(8,128)S(1)} fusion(f32[16,8,128]{2,1,0:T(8,128)S(1)} %fusion, f32[16,8,128]{2,1,0:T(8,128)S(1)} %copy.178, f32[8,128,128]{2,1,0:T(8,128)S(1)} %copy.153), kind=kLoop, calls=%fused_computation.10 | loop fusion | flops 8372224 | bytes 720896 | tf_op jit(solution)/shard_map/reduce_sum | solution.py:50
  77.9 0.1 broadcast_select_fusion.3
  78.2 0.7 broadcast_in_dim.285
  78.9 3.4 %all-to-all-start.4 = ((f32[2,16,16,128]{3,1,0,2:T(8,128)}), f32[2,16,16,128]{3,1,0,2:T(8,128)S(1)}, u32[]{:S(2)}, u32[]{:S(2)}) async-start(f32[2,16,16,128]{3,1,0,2:T(8,128)} %bitcast.37), calls=%async_computation.4 | async-start | bytes 524288 | tf_op jit(solution)/shard_map/all_to_all | solution.py:150
  82.4 9.6 %all-to-all-done.4 = f32[2,16,16,128]{3,1,0,2:T(8,128)S(1)} async-done(((f32[2,16,16,128]{3,1,0,2:T(8,128)}), f32[2,16,16,128]{3,1,0,2:T(8,128)S(1)}, u32[]{:S(2)}, u32[]{:S(2)}) %all-to-all-start.4) | async-done | bytes 262176 | tf_op jit(solution)/shard_map/all_to_all | solution.py:150
  92.0 0.2 select_reduce_fusion.1
  92.2 0.6 gather_fusion.9
  92.8 0.1 fusion.4
  93.0 0.1 select_reduce_fusion
  93.1 0.8 fusion.16
  (77 shorter events, 2.4 us)
Async XLA Ops:
  0.6 8.8 %copy-start = (bf16[64,1024]{1,0:T(8,128)(2,1)S(1)}, bf16[64,1024]{1,0:T(8,128)(2,1)}, u32[]{:S(2)}) copy-start(bf16[64,1024]{1,0:T(8,128)(2,1)} %param.14) | copy-start | bytes 393220
  0.6 11.2 %copy-start.2 = (s32[1024]{0:T(1024)S(1)}, s32[1024]{0:T(1024)}, u32[]{:S(2)}) copy-start(s32[1024]{0:T(1024)} %param.15) | copy-start | bytes 12292
  2.1 11.8 %all-to-all-start = ((s32[8,1,2]{2,1,0:T(1,128)}), s32[8,1,2]{2,1,0:T(1,128)S(1)}, u32[]{:S(2)}, u32[]{:S(2)}) async-start(s32[8,1,2]{2,1,0:T(1,128)} %bitcast), calls=%async_computation | async-start | bytes 8192 | tf_op jit(solution)/shard_map/all_to_all | solution.py:97
  15.7 10.1 %all-to-all-start.1 = ((bf16[65,4,2,128]{3,2,0,1:T(2,128)(2,1)}), bf16[65,4,2,128]{3,2,0,1:T(2,128)(2,1)S(1)}, u32[]{:S(2)}, u32[]{:S(2)}) async-start(bf16[65,4,2,128]{3,2,0,1:T(2,128)(2,1)} %broadcast_select_fusion), calls=%async_computation.1 | async-start | bytes 266240 | tf_op jit(solution)/shard_map/all_to_all | solution.py:105
  30.6 1.4 %collective-permute-start = (f32[2,16,8,128]{3,1,2,0:T(8,128)S(1)}, f32[2,16,8,128]{3,1,2,0:T(8,128)S(1)}, u32[]{:S(2)}, u32[]{:S(2)}) collective-permute-start(f32[2,16,8,128]{3,1,2,0:T(8,128)S(1)} %pad_maximum_fusion.1), channel_id=1, source_target_pairs={{0,1},{1,0},{2,3},{3,2},{4,5},{5,4},{6,7},{7,6},{8,9},{9,8},{10,11... | collective-permute-start | bytes 393224 | tf_op jit(solution)/shard_map/ppermute | solution.py:59
  30.7 1.3 %copy-start.1 = (s32[16,1024]{1,0:T(8,128)S(1)}, s32[16,1024]{1,0:T(8,128)}, u32[]{:S(2)}) copy-start(s32[16,1024]{1,0:T(8,128)} %param.17) | copy-start | bytes 196612
  38.9 13.1 %all-to-all-start.2 = ((f32[2,16,16,128]{3,1,0,2:T(8,128)}), f32[2,16,16,128]{3,1,0,2:T(8,128)S(1)}, u32[]{:S(2)}, u32[]{:S(2)}) async-start(f32[2,16,16,128]{3,1,0,2:T(8,128)} %bitcast.21), calls=%async_computation.2 | async-start | bytes 524288 | tf_op jit(solution)/shard_map/all_to_all | solution.py:150
  52.8 0.8 copy-start.3
  70.6 1.4 %collective-permute-start.1 = (f32[2,16,8,128]{3,1,2,0:T(8,128)S(1)}, f32[2,16,8,128]{3,1,2,0:T(8,128)S(1)}, u32[]{:S(2)}, u32[]{:S(2)}) collective-permute-start(f32[2,16,8,128]{3,1,2,0:T(8,128)S(1)} %pad_maximum_fusion.2), channel_id=1, source_target_pairs={{0,1},{1,0},{2,3},{3,2},{4,5},{5,4},{6,7},{7,6},{8,9},{9,8},{10,11... | collective-permute-start | bytes 393224 | tf_op jit(solution)/shard_map/ppermute | solution.py:59
  78.9 13.1 %all-to-all-start.4 = ((f32[2,16,16,128]{3,1,0,2:T(8,128)}), f32[2,16,16,128]{3,1,0,2:T(8,128)S(1)}, u32[]{:S(2)}, u32[]{:S(2)}) async-start(f32[2,16,16,128]{3,1,0,2:T(8,128)} %bitcast.37), calls=%async_computation.4 | async-start | bytes 524288 | tf_op jit(solution)/shard_map/all_to_all | solution.py:150

commit v2 on v1

--- a/solution.py
+++ b/solution.py
@@ -20,12 +20,28 @@
     )
 
 
+def pick(values, ids, blocks):
+    hits = ids[:, None] == jnp.arange(blocks, dtype=jnp.int32)[None, :]
+    chosen = jnp.where(hits[None, :, :, None], values[:, None, :, :], jnp.zeros((), values.dtype))
+    return jnp.sum(chosen, axis=2, dtype=values.dtype)
+
+
 def fold_blocks(highest, mass_sum, owners, blocks):
     matches = owners[:, None] == jnp.arange(blocks, dtype=jnp.int32)[None, :]
     match_mask = matches[None, :, :, None]
     block_top = jnp.max(jnp.where(match_mask, highest[:, :, None, :], SENTINEL), axis=1)
-    slot_top = jnp.take(block_top, owners, axis=1)
+    slot_top = pick(block_top, owners, blocks)
     scaled = mass_sum * jnp.exp(highest - slot_top)
+    summed = jnp.sum(jnp.where(match_mask, scaled[:, :, None, :], 0.0), axis=1)
+    return (block_top, summed)
+
+
+def fold_lse(lse, owners, blocks):
+    matches = owners[:, None] == jnp.arange(blocks, dtype=jnp.int32)[None, :]
+    match_mask = matches[None, :, :, None]
+    block_top = jnp.max(jnp.where(match_mask, lse[:, :, None, :], SENTINEL), axis=1)
+    slot_top = pick(block_top, owners, blocks)
+    scaled = jnp.where(lse > 0.5 * SENTINEL, jnp.exp(lse - slot_top), 0.0)
     summed = jnp.sum(jnp.where(match_mask, scaled[:, :, None, :], 0.0), axis=1)
     return (block_top, summed)
 
@@ -103,7 +119,7 @@
         ).reshape(slot_count)
 
         far = lax.all_to_all(
-            jnp.take(own_synth, requested_same, axis=1).reshape(features + 1, peer_count, capacity, BLOCK),
+            pick(own_synth, requested_same, blocks).reshape(features + 1, peer_count, capacity, BLOCK),
             "blk",
             split_axis=1,
             concat_axis=1,
@@ -111,9 +127,11 @@
         ).reshape(features + 1, slot_count, BLOCK)
         far_y = far[:features]
         far_tags = far[features]
-        slot_x = jnp.take(own_real, rows_used, axis=1)
-        slot_tags = jnp.take(real_tags, rows_used, axis=0).astype(jnp.bfloat16)
+        slot_x = pick(own_real, rows_used, blocks)
+        slot_tags = pick(real_tags[None], rows_used, blocks)[0].astype(jnp.bfloat16)
         cost = slot_costs(slot_x, slot_tags, far_y, far_tags)
+        cost_cols = cost / SMOOTH
+        cost_rows = jnp.transpose(cost_cols, (0, 2, 1))
 
         synth_pot = jnp.zeros((marginals, blocks, BLOCK), jnp.float32)
         real_pot = jnp.zeros((marginals, blocks, BLOCK), jnp.float32)
@@ -122,7 +140,7 @@
                 panel = jnp.zeros((marginals, slot_count, BLOCK), jnp.float32)
             else:
                 panel = lax.all_to_all(
-                    jnp.take(synth_pot, requested_same, axis=1).reshape(
+                    pick(synth_pot, requested_same, blocks).reshape(
                         marginals, peer_count, capacity, BLOCK
                     ),
                     "blk",
@@ -130,25 +148,24 @@
                     concat_axis=1,
                     tiled=True,
                 ).reshape(marginals, slot_count, BLOCK)
-            scores = (panel[:, :, None, :] - cost[None]) / SMOOTH
-            highest, mass_sum = lse_parts(scores, 3)
+            scores = (panel / SMOOTH)[:, :, :, None] - cost_rows[None]
+            highest, mass_sum = lse_parts(scores, 2)
             highest = jnp.where(usable, highest, SENTINEL)
             mass_sum = jnp.where(usable, mass_sum, 0.0)
             block_top, summed = fold_blocks(highest, mass_sum, rows_used, blocks)
             block_top, summed = sub_join((block_top, summed))
             real_pot = finish(log_real, block_top, summed)
 
-            own_rows = jnp.take(real_pot, rows_used, axis=1)
-            scores = (own_rows[:, :, :, None] - cost[None]) / SMOOTH
+            own_rows = pick(real_pot, rows_used, blocks)
+            scores = (own_rows / SMOOTH)[:, :, :, None] - cost_cols[None]
             highest, mass_sum = lse_parts(scores, 2)
-            highest = jnp.where(usable, highest, SENTINEL)
-            mass_sum = jnp.where(usable, mass_sum, 0.0)
-            outgoing = jnp.stack([highest, mass_sum]).reshape(2, marginals, peer_count, 1, capacity, BLOCK)
+            lse = jnp.where(usable, highest + jnp.log(mass_sum), SENTINEL)
+            outgoing = lse.reshape(marginals, peer_count, 1, capacity, BLOCK)
             outgoing = jnp.broadcast_to(
-                outgoing, (2, marginals, peer_count, n_sub, capacity, BLOCK)
-            ).reshape(2, marginals, peer_count * n_sub * capacity, BLOCK)
-            back = lax.all_to_all(outgoing, group, split_axis=2, concat_axis=2, tiled=True)
-            block_top, summed = fold_blocks(back[0], back[1], requested_all, blocks)
+                outgoing, (marginals, peer_count, n_sub, capacity, BLOCK)
+            ).reshape(marginals, peer_count * n_sub * capacity, BLOCK)
+            back = lax.all_to_all(outgoing, group, split_axis=1, concat_axis=1, tiled=True)
+            block_top, summed = fold_lse(back, requested_all, blocks)
             synth_pot = finish(log_synth, block_top, summed)
         return (real_pot.reshape(marginals, point_count), synth_pot.reshape(marginals, point_count))
 

time: 94.5 us -> 83 us (0.88)
  blocking collectives: 8.1 us -> 0 us
  local copies, waits for them, and re-layouts: 11.8 us -> 7.52 us
  starting transfers between devices: 17.2 us -> 20.8 us
  other arithmetic: 27.1 us -> 25.7 us
    all_to_all x1 -> x0, blocking collectives: 8.1 us -> none  [shards(): lax.all_to_all(jnp.take(synth_pot, requested_same, axis=1).reshape(margin...]
    gather x10 -> x0, local copies, waits for them, and re-layouts: 5.61 us -> none  [the longest x4 2.24 us: fold_blocks(): slot_top = jnp.take(block_top, owners, axis=1)]
    reduce_sum x4, other arithmetic: 12.5 us -> 7.83 us  [lse_parts(): jnp.sum(jnp.exp(scores - jnp.expand_dims(highest, axis)), axis=axis)]
    reduce_sum x0 -> x12, other arithmetic: none -> 3.74 us  [the longest x10 3.46 us: pick(): return jnp.sum(chosen, axis=2, dtype=values.dtype)]
    all_to_all x3 -> x4, starting transfers between devices: 10.7 us -> 14.3 us  [the longest x2 6.74 us: shards(): lax.all_to_all(outgoing, group, split_axis=1, concat_axis=1, tiled=True)]
    unnamed x10 -> x11, local copies, waits for them, and re-layouts: 0.74 us -> 2.11 us
    reduce_max x3 -> x4, other arithmetic: 7.27 us -> 7.71 us  [lse_parts(): highest = jnp.max(scores, axis=axis)]
    all_to_all x3 -> x4, waiting for transfers between devices: 24.1 us -> 23.8 us  [the longest x2 12 us: shards(): lax.all_to_all(outgoing, group, split_axis=1, concat_axis=1, tiled=True)]
  transfers between devices with their start and end apart: 6 -> 7, of which waited for: 6 -> 7; matrix products, arithmetic and copies ran while one was open for 6% -> 8% of each run, Pallas kernels for 0% -> 0%
where the time goes in v2:
time: 83 us; the launch traced here: 82.3 us
  waiting for transfers between devices  26.9 us (32%)
  other arithmetic  25.7 us (31%)
  starting transfers between devices  20.8 us (25%)
  local copies, waits for them, and re-layouts  7.52 us (9%)
  between operations  1.14 us (1%)
    all_to_all x2, waiting for transfers between devices, shards(): lax.all_to_all(outgoing, group, split_axis=1, concat_axis=1, tiled=True)  12 us
    reduce_sum x4, other arithmetic, lse_parts(): jnp.sum(jnp.exp(scores - jnp.expand_dims(highest, axis)), axis=axis)  7.83 us
    reduce_max x4, other arithmetic, lse_parts(): highest = jnp.max(scores, axis=axis)  7.71 us
    all_to_all x2, starting transfers between devices, shards(): lax.all_to_all(outgoing, group, split_axis=1, concat_axis=1, tiled=True)  6.74 us
    all_to_all x1, starting transfers between devices, shards(): lax.all_to_all(asked.reshape(peer_count * n_sub, capacity), group, split_...  6.33 us
    all_to_all x1, waiting for transfers between devices, shards(): lax.all_to_all(pick(own_synth, requested_same, blocks).reshape(features +...  6.25 us
    all_to_all x1, waiting for transfers between devices, shards(): lax.all_to_all(pick(synth_pot, requested_same, blocks).reshape(marginals,...  5.51 us
    all_to_all x1, starting transfers between devices, shards(): lax.all_to_all(pick(own_synth, requested_same, blocks).reshape(features +...  4.27 us
  transfers between devices with their start and end apart: 7, of which 7 were waited for; matrix products, arithmetic and copies ran while one was open for 8% of the time, Pallas kernels for 0%

profile of v2, /device:TPU:0, one launch (start us, length us, event | category | flops | bytes accessed | tf_op | source)
XLA Modules:
  0.0 82.3 jit_solution(17851043395543052254)
XLA Ops:
  0.6 0.7 broadcast_select_fusion.5
  1.4 0.1 copy.98
  1.5 0.6 broadcast_in_dim.376.clone
  2.1 6.3 %all-to-all-start = ((s32[8,1,2]{2,1,0:T(1,128)}), s32[8,1,2]{2,1,0:T(1,128)S(1)}, u32[]{:S(2)}, u32[]{:S(2)}) async-start(s32[8,1,2]{2,1,0:T(1,128)} %bitcast), calls=%async_computation | async-start | bytes 8192 | tf_op jit(solution)/shard_map/all_to_all | solution.py:113
  8.4 0.7 iota_compare_fusion.3
  9.0 0.9 %copy.103 = bf16[8,8,8,128]{3,2,1,0:T(8,128)(2,1)S(1)} copy(bf16[8,8,8,128]{3,1,2,0:T(8,128)(2,1)} %bitcast.151) | data formatting | bytes 262144
  10.0 0.7 convert_bitcast_fusion
  10.7 0.1 copy.68
  10.9 0.9 %copy.102 = bf16[8,8,8,128]{3,2,1,0:T(8,128)(2,1)S(1)} copy(bf16[8,8,8,128]{3,1,2,0:T(8,128)(2,1)} %bitcast.152) | data formatting | bytes 262144
  11.8 0.8 select_reduce_fusion.7
  12.8 0.1 copy.69
  13.0 0.8 %all-to-all-done = s32[8,1,2]{2,1,0:T(1,128)S(1)} async-done(((s32[8,1,2]{2,1,0:T(1,128)}), s32[8,1,2]{2,1,0:T(1,128)S(1)}, u32[]{:S(2)}, u32[]{:S(2)}) %all-to-all-start) | async-done | bytes 96 | tf_op jit(solution)/shard_map/all_to_all | solution.py:113
  14.0 0.8 select_reduce_fusion
  14.9 0.7 copy.74
  15.6 4.3 %all-to-all-start.1 = ((bf16[65,4,2,128]{3,2,0,1:T(2,128)(2,1)}), bf16[65,4,2,128]{3,2,0,1:T(2,128)(2,1)S(1)}, u32[]{:S(2)}, u32[]{:S(2)}) async-start(bf16[65,4,2,128]{3,2,0,1:T(2,128)(2,1)} %copy.74), calls=%async_computation.1 | async-start | bytes 266240 | tf_op jit(solution)/shard_map/all_to_all | solution.py:121
  19.9 6.2 %all-to-all-done.1 = bf16[65,4,2,128]{3,2,0,1:T(2,128)(2,1)S(1)} async-done(((bf16[65,4,2,128]{3,2,0,1:T(2,128)(2,1)}), bf16[65,4,2,128]{3,2,0,1:T(2,128)(2,1)S(1)}, u32[]{:S(2)}, u32[]{:S(2)}) %all-to-all-start.1) | async-done | bytes 133152 | tf_op jit(solution)/shard_map/all_to_all | solution.py:121
  26.1 0.1 slice.29
  26.3 0.3 fusion.8
  26.5 0.2 copy.77
  26.7 0.1 multiply_reduce_fusion
  26.9 0.8 broadcast_subtract_fusion
  27.7 0.2 fusion.24
  27.9 0.2 copy.78
  28.1 0.1 exponential_reduce_fusion
  28.3 0.1 select_reduce_fusion.16
  28.4 0.2 select_reduce_fusion.15
  28.7 0.1 select_reduce_fusion.14
  28.9 0.1 copy-done
  29.1 0.2 copy.79
  29.3 1.0 %collective-permute-done = f32[2,16,8,128]{3,2,1,0:T(8,128)S(1)} collective-permute-done((f32[2,16,8,128]{3,2,1,0:T(8,128)S(1)}, f32[2,16,8,128]{3,2,1,0:T(8,128)S(1)}, u32[]{:S(2)}, u32[]{:S(2)}) %collective-permute-start) | collective-permute-done | bytes 131104 | tf_op jit(solution)/shard_map/ppermute | solution.py:75
  30.3 0.2 select_reduce_fusion.13
  30.6 2.5 %subtract_reduce_fusion.2 = f32[16,8,128]{2,1,0:T(8,128)S(1)} fusion(f32[8,128,128]{2,1,0:T(8,128)S(1)} %copy.79, f32[16,8,128]{2,1,0:T(8,128)S(1)} %broadcast_multiply_fusion.1), kind=kLoop, calls=%fused_computation.5 | loop fusion | flops 4177920 | bytes 655360 | tf_op jit(solution)/shard_map/reduce_max | solution.py:65
  33.1 2.6 %fusion.1 = f32[16,8,128]{2,1,0:T(8,128)S(1)} fusion(f32[16,8,128]{2,1,0:T(8,128)S(1)} %subtract_reduce_fusion.2, f32[8,128,128]{2,1,0:T(8,128)S(1)} %copy.79, f32[16,8,128]{2,1,0:T(8,128)S(1)} %broadcast_multiply_fusion.1), kind=kLoop, calls=%fused_computation.7 | loop fusion | flops 6275072 | bytes 720896 | tf_op jit(solution)/shard_map/reduce_sum | solution.py:66
  35.7 0.1 broadcast_select_fusion.1
  35.8 0.6 broadcast_in_dim.401
  36.5 3.4 %all-to-all-start.2 = ((f32[16,16,128]{2,0,1:T(8,128)}), f32[16,16,128]{2,0,1:T(8,128)S(1)}, u32[]{:S(2)}, u32[]{:S(2)}) async-start(f32[16,16,128]{2,0,1:T(8,128)} %bitcast.15), calls=%async_computation.2 | async-start | bytes 262144 | tf_op jit(solution)/shard_map/all_to_all | solution.py:167
  39.9 0.5 broadcast.324
  40.4 0.7 reduce.9
  41.2 5.3 %all-to-all-done.2 = f32[16,16,128]{2,0,1:T(8,128)S(1)} async-done(((f32[16,16,128]{2,0,1:T(8,128)}), f32[16,16,128]{2,0,1:T(8,128)S(1)}, u32[]{:S(2)}, u32[]{:S(2)}) %all-to-all-start.2) | async-done | bytes 131104 | tf_op jit(solution)/shard_map/all_to_all | solution.py:167
  46.6 0.2 select_reduce_fusion.6
  46.8 0.4 select_reduce_fusion.5
  47.2 0.1 select_reduce_fusion.4
  47.4 0.2 select_reduce_fusion.12
  47.6 0.7 copy.85
  48.3 3.3 %all-to-all-start.3 = ((f32[16,4,2,128]{3,2,0,1:T(2,128)}), f32[16,4,2,128]{3,2,0,1:T(2,128)S(1)}, u32[]{:S(2)}, u32[]{:S(2)}) async-start(f32[16,4,2,128]{3,2,0,1:T(2,128)} %copy.85), calls=%async_computation.3 | async-start | bytes 131072 | tf_op jit(solution)/shard_map/all_to_all | solution.py:142
  51.5 0.2 copy.88
  51.7 5.5 %all-to-all-done.3 = f32[16,4,2,128]{3,2,0,1:T(2,128)S(1)} async-done(((f32[16,4,2,128]{3,2,0,1:T(2,128)}), f32[16,4,2,128]{3,2,0,1:T(2,128)S(1)}, u32[]{:S(2)}, u32[]{:S(2)}) %all-to-all-start.3) | async-done | bytes 65568 | tf_op jit(solution)/shard_map/all_to_all | solution.py:142
  57.3 2.5 %subtract_reduce_fusion.1 = f32[16,8,128]{2,1,0:T(8,128)S(1)} fusion(f32[8,128,128]{2,1,0:T(8,128)S(1)} %copy.88, f32[16,8,128]{2,1,0:T(8,128)S(1)} %copy.87), kind=kLoop, calls=%fused_computation.3 | loop fusion | flops 4177920 | bytes 655360 | tf_op jit(solution)/shard_map/reduce_max | solution.py:65
  59.8 2.6 %fusion.3 = f32[16,8,128]{2,1,0:T(8,128)S(1)} fusion(f32[16,8,128]{2,1,0:T(8,128)S(1)} %subtract_reduce_fusion.1, f32[8,128,128]{2,1,0:T(8,128)S(1)} %copy.88, f32[16,8,128]{2,1,0:T(8,128)S(1)} %copy.87), kind=kLoop, calls=%fused_computation.9 | loop fusion | flops 6275072 | bytes 720896 | tf_op jit(solution)/shard_map/reduce_sum | solution.py:66
  62.5 0.1 select_reduce_fusion.11
  62.6 0.2 select_reduce_fusion.10
  62.9 0.1 select_reduce_fusion.9
  63.1 1.3 %collective-permute-done.1 = f32[2,16,8,128]{3,2,1,0:T(8,128)S(1)} collective-permute-done((f32[2,16,8,128]{3,2,1,0:T(8,128)S(1)}, f32[2,16,8,128]{3,2,1,0:T(8,128)S(1)}, u32[]{:S(2)}, u32[]{:S(2)}) %collective-permute-start.1) | collective-permute-done | bytes 131104 | tf_op jit(solution)/shard_map/ppermute | solution.py:75
  64.5 0.2 select_reduce_fusion.8
  64.7 2.5 %subtract_reduce_fusion = f32[16,8,128]{2,1,0:T(8,128)S(1)} fusion(f32[16,8,128]{2,1,0:T(8,128)S(1)} %broadcast_multiply_fusion, f32[8,128,128]{2,1,0:T(8,128)S(1)} %copy.79), kind=kLoop, calls=%fused_computation.1 | loop fusion | flops 4177920 | bytes 655360 | tf_op jit(solution)/shard_map/reduce_max | solution.py:65
  67.2 2.6 %fusion.5 = f32[16,8,128]{2,1,0:T(8,128)S(1)} fusion(f32[16,8,128]{2,1,0:T(8,128)S(1)} %subtract_reduce_fusion, f32[16,8,128]{2,1,0:T(8,128)S(1)} %broadcast_multiply_fusion, f32[8,128,128]{2,1,0:T(8,128)S(1)} %copy.79), kind=kLoop, calls=%fused_computation.11 | loop fusion | flops 6275072 | bytes 720896 | tf_op jit(solution)/shard_map/reduce_sum | solution.py:66
  69.8 0.1 broadcast_select_fusion
  70.0 0.6 broadcast_in_dim.414
  70.6 3.4 %all-to-all-start.4 = ((f32[16,16,128]{2,0,1:T(8,128)}), f32[16,16,128]{2,0,1:T(8,128)S(1)}, u32[]{:S(2)}, u32[]{:S(2)}) async-start(f32[16,16,128]{2,0,1:T(8,128)} %bitcast.23), calls=%async_computation.4 | async-start | bytes 262144 | tf_op jit(solution)/shard_map/all_to_all | solution.py:167
  74.0 6.7 %all-to-all-done.4 = f32[16,16,128]{2,0,1:T(8,128)S(1)} async-done(((f32[16,16,128]{2,0,1:T(8,128)}), f32[16,16,128]{2,0,1:T(8,128)S(1)}, u32[]{:S(2)}, u32[]{:S(2)}) %all-to-all-start.4) | async-done | bytes 131104 | tf_op jit(solution)/shard_map/all_to_all | solution.py:167
  80.7 0.2 select_reduce_fusion.3
  80.9 0.4 select_reduce_fusion.2
  81.3 0.1 select_reduce_fusion.1
  81.5 0.7 bitcast_subtract_fusion.1
  (50 shorter events, 1.9 us)
Async XLA Ops:
  0.6 12.1 %copy-start.2 = (s32[1024]{0:T(1024)S(1)}, s32[1024]{0:T(1024)}, u32[]{:S(2)}) copy-start(s32[1024]{0:T(1024)} %param.11) | copy-start | bytes 12292
  2.1 11.8 %all-to-all-start = ((s32[8,1,2]{2,1,0:T(1,128)}), s32[8,1,2]{2,1,0:T(1,128)S(1)}, u32[]{:S(2)}, u32[]{:S(2)}) async-start(s32[8,1,2]{2,1,0:T(1,128)} %bitcast), calls=%async_computation | async-start | bytes 8192 | tf_op jit(solution)/shard_map/all_to_all | solution.py:113
  15.6 10.5 %all-to-all-start.1 = ((bf16[65,4,2,128]{3,2,0,1:T(2,128)(2,1)}), bf16[65,4,2,128]{3,2,0,1:T(2,128)(2,1)S(1)}, u32[]{:S(2)}, u32[]{:S(2)}) async-start(bf16[65,4,2,128]{3,2,0,1:T(2,128)(2,1)} %copy.74), calls=%async_computation.1 | async-start | bytes 266240 | tf_op jit(solution)/shard_map/all_to_all | solution.py:121
  28.2 0.8 %copy-start = (s32[16,1024]{1,0:T(8,128)S(1)}, s32[16,1024]{1,0:T(8,128)}, u32[]{:S(2)}) copy-start(s32[16,1024]{1,0:T(8,128)} %param.13) | copy-start | bytes 196612
  28.9 1.4 %collective-permute-start = (f32[2,16,8,128]{3,2,1,0:T(8,128)S(1)}, f32[2,16,8,128]{3,2,1,0:T(8,128)S(1)}, u32[]{:S(2)}, u32[]{:S(2)}) collective-permute-start(f32[2,16,8,128]{3,2,1,0:T(8,128)S(1)} %pad_maximum_fusion), channel_id=1, source_target_pairs={{0,1},{1,0},{2,3},{3,2},{4,5},{5,4},{6,7},{7,6},{8,9},{9,8},{10,11... | collective-permute-start | bytes 393224 | tf_op jit(solution)/shard_map/ppermute | solution.py:75
  35.7 4.2 %copy-start.1 = (s32[16,1024]{1,0:T(8,128)S(1)}, s32[16,1024]{1,0:T(8,128)}, u32[]{:S(2)}) copy-start(s32[16,1024]{1,0:T(8,128)} %param.14) | copy-start | bytes 196612
  36.5 10.1 %all-to-all-start.2 = ((f32[16,16,128]{2,0,1:T(8,128)}), f32[16,16,128]{2,0,1:T(8,128)S(1)}, u32[]{:S(2)}, u32[]{:S(2)}) async-start(f32[16,16,128]{2,0,1:T(8,128)} %bitcast.15), calls=%async_computation.2 | async-start | bytes 262144 | tf_op jit(solution)/shard_map/all_to_all | solution.py:167
  48.3 9.0 %all-to-all-start.3 = ((f32[16,4,2,128]{3,2,0,1:T(2,128)}), f32[16,4,2,128]{3,2,0,1:T(2,128)S(1)}, u32[]{:S(2)}, u32[]{:S(2)}) async-start(f32[16,4,2,128]{3,2,0,1:T(2,128)} %copy.85), calls=%async_computation.3 | async-start | bytes 131072 | tf_op jit(solution)/shard_map/all_to_all | solution.py:142
  63.0 1.4 %collective-permute-start.1 = (f32[2,16,8,128]{3,2,1,0:T(8,128)S(1)}, f32[2,16,8,128]{3,2,1,0:T(8,128)S(1)}, u32[]{:S(2)}, u32[]{:S(2)}) collective-permute-start(f32[2,16,8,128]{3,2,1,0:T(8,128)S(1)} %pad_maximum_fusion.1), channel_id=1, source_target_pairs={{0,1},{1,0},{2,3},{3,2},{4,5},{5,4},{6,7},{7,6},{8,9},{9,8},{10,11... | collective-permute-start | bytes 393224 | tf_op jit(solution)/shard_map/ppermute | solution.py:75
  70.6 10.1 %all-to-all-start.4 = ((f32[16,16,128]{2,0,1:T(8,128)}), f32[16,16,128]{2,0,1:T(8,128)S(1)}, u32[]{:S(2)}, u32[]{:S(2)}) async-start(f32[16,16,128]{2,0,1:T(8,128)} %bitcast.23), calls=%async_computation.4 | async-start | bytes 262144 | tf_op jit(solution)/shard_map/all_to_all | solution.py:167

commit v3 on v2

v3 whole, which is shorter than its diff:
```python
import jax
import jax.numpy as jnp
from jax import lax
from jax.sharding import PartitionSpec as P

BLOCK = 128
ITERS = 2


SMOOTH = 0.1
PENALTY = 0.3
SENTINEL = -1e30


def join_parts(earlier, latter):
    larger = jnp.maximum(earlier[0], latter[0])
    return (
        larger,
        earlier[1] * jnp.exp(earlier[0] - larger) + latter[1] * jnp.exp(latter[0] - larger),
    )


def pick_rows(values, ids, blocks):
    hits = ids[:, None] == jnp.arange(blocks, dtype=jnp.int32)[None, :]
    chosen = jnp.where(hits[:, None, :, None], values[None], jnp.zeros((), values.dtype))
    return jnp.sum(chosen, axis=2, dtype=values.dtype)


def pick_lead(values, ids):
    hits = ids[:, None] == jnp.arange(values.shape[0], dtype=jnp.int32)[None, :]
    hits = hits.reshape(hits.shape + (1,) * (values.ndim - 1))
    return jnp.sum(jnp.where(hits, values[None], jnp.zeros((), values.dtype)), axis=1, dtype=values.dtype)


def fold_blocks(highest, mass_sum, owners, blocks):
    matches = owners[:, None] == jnp.arange(blocks, dtype=jnp.int32)[None, :]
    match_mask = matches[:, None, :, None]
    block_top = jnp.max(jnp.where(match_mask, highest[:, :, None, :], SENTINEL), axis=0)
    slot_top = pick_rows(block_top, owners, blocks)
    scaled = mass_sum * jnp.exp(highest - slot_top)
    summed = jnp.sum(jnp.where(match_mask, scaled[:, :, None, :], 0.0), axis=0)
    return (block_top, summed)


def fold_lse(lse, owners, blocks):
    matches = owners[:, None] == jnp.arange(blocks, dtype=jnp.int32)[None, :]
    match_mask = matches[:, None, :, None]
    block_top = jnp.max(jnp.where(match_mask, lse[:, :, None, :], SENTINEL), axis=0)
    slot_top = pick_rows(block_top, owners, blocks)
    scaled = jnp.where(lse > 0.5 * SENTINEL, jnp.exp(lse - slot_top), 0.0)
    summed = jnp.sum(jnp.where(match_mask, scaled[:, :, None, :], 0.0), axis=0)
    return (block_top, summed)


def finish(log_weight, block_top, summed):
    spread = jnp.where(summed > 0.5, block_top + jnp.log(jnp.maximum(summed, 0.5)), 0.0)
    return SMOOTH * log_weight - SMOOTH * spread


def slot_costs(slot_real, slot_real_tag, slot_synth, slot_synth_tag):
    inner_prod = jnp.einsum(
        "gdi,gdj->gij", slot_real, slot_synth, preferred_element_type=jnp.float32
    )
    real_sq = jnp.sum(jnp.square(slot_real.astype(jnp.float32)), axis=1)
    synth_sq = jnp.sum(jnp.square(slot_synth.astype(jnp.float32)), axis=1)
    differ = (slot_real_tag[:, :, None] != slot_synth_tag[:, None, :]).astype(jnp.float32)
    return 0.5 * real_sq[:, :, None] + 0.5 * synth_sq[:, None, :] - inner_prod + PENALTY * differ


def lse_parts(scores, axis):
    highest = jnp.max(scores, axis=axis)
    mass_sum = jnp.sum(jnp.exp(scores - jnp.expand_dims(highest, axis)), axis=axis)
    return (highest, mass_sum)


def make_shards(n_blk, n_sub):
    def sub_join(parts):
        if n_sub == 2:
            other = lax.ppermute(jnp.stack(parts), "sub", [(0, 1), (1, 0)])
            return join_parts(parts, (other[0], other[1]))
        pieces = lax.all_gather(jnp.stack(parts), "sub")
        subtotal = (pieces[0, 0], pieces[0, 1])
        for index in range(1, n_sub):
            subtotal = join_parts(subtotal, (pieces[index, 0], pieces[index, 1]))
        return subtotal

    def send_up(chunks):
        moved = [chunks[0]]
        for offset in range(1, n_blk):
            perm = [(index, (index + offset) % n_blk) for index in range(n_blk)]
            moved.append(lax.ppermute(chunks[offset], "blk", perm))
        return moved

    def send_down(chunks):
        moved = [chunks[0]]
        for offset in range(1, n_blk):
            perm = [(index, (index - offset) % n_blk) for index in range(n_blk)]
            moved.append(lax.ppermute(chunks[offset], "blk", perm))
        return moved

    def shards(
        real_points,
        synth_points,
        real_cluster,
        synth_cluster,
        real_weight,
        synth_weight,
        pair_block,
        pair_row,
        pair_count,
    ):
        features, point_count = real_points.shape
        blocks = point_count // BLOCK
        marginals = real_weight.shape[0]
        peer_count, capacity = pair_block.shape
        slot_count = peer_count * capacity
        my_blk = lax.axis_index("blk")
        own_real = real_points.reshape(features, blocks, BLOCK)
        real_tags = real_cluster.reshape(1, blocks, BLOCK).astype(jnp.bfloat16)
        own_synth = jnp.concatenate(
            [synth_points, synth_cluster.astype(jnp.bfloat16)[None, :]], axis=0
        ).reshape(features + 1, blocks, BLOCK)
        log_real = jnp.log(real_weight.astype(jnp.float32) + 0.5).reshape(marginals, blocks, BLOCK)
        log_synth = jnp.log(synth_weight.astype(jnp.float32) + 0.5).reshape(marginals, blocks, BLOCK)

        peers = (my_blk + jnp.arange(peer_count, dtype=jnp.int32)) % peer_count
        listed = lax.broadcasted_iota(jnp.int32, (peer_count, capacity), 1) < pair_count[:, None]
        wanted = pick_lead(jnp.where(listed, pair_block, 0), peers)
        rows_used = pick_lead(jnp.where(listed, pair_row, 0), peers).reshape(slot_count)
        usable = pick_lead(listed.astype(jnp.int32), peers).reshape(slot_count)[:, None, None] > 0

        requested = jnp.stack(send_up([wanted[offset] for offset in range(peer_count)]))
        far = jnp.concatenate(
            send_down([pick_rows(own_synth, requested[offset], blocks) for offset in range(peer_count)]),
            axis=0,
        )
        requested = requested.reshape(slot_count)
        far_y = far[:, :features]
        far_tags = far[:, features]
        slot_x = pick_rows(own_real, rows_used, blocks)
        slot_tags = pick_rows(real_tags, rows_used, blocks)[:, 0]
        cost = slot_costs(slot_x, slot_tags, far_y, far_tags)
        cost_cols = cost / SMOOTH
        cost_rows = jnp.transpose(cost_cols, (0, 2, 1))

        synth_pot = jnp.zeros((marginals, blocks, BLOCK), jnp.float32)
        real_pot = jnp.zeros((marginals, blocks, BLOCK), jnp.float32)
        for sweep_index in range(ITERS):
            if sweep_index == 0:
                panel = jnp.zeros((slot_count, marginals, BLOCK), jnp.float32)
            else:
                panel = jnp.concatenate(
                    send_down(
                        [
                            pick_rows(synth_pot, requested[offset * capacity : (offset + 1) * capacity], blocks)
                            for offset in range(peer_count)
                        ]
                    ),
                    axis=0,
                )
            scores = (panel / SMOOTH)[:, :, :, None] - cost_rows[:, None]
            highest, mass_sum = lse_parts(scores, 2)
            highest = jnp.where(usable, highest, SENTINEL)
            mass_sum = jnp.where(usable, mass_sum, 0.0)
            block_top, summed = fold_blocks(highest, mass_sum, rows_used, blocks)
            block_top, summed = sub_join((block_top, summed))
            real_pot = finish(log_real, block_top, summed)

            own_rows = pick_rows(real_pot, rows_used, blocks)
            scores = (own_rows / SMOOTH)[:, :, :, None] - cost_cols[:, None]
            highest, mass_sum = lse_parts(scores, 2)
            lse = jnp.where(usable, highest + jnp.log(mass_sum), SENTINEL)
            back = jnp.concatenate(
                send_up([lse[offset * capacity : (offset + 1) * capacity] for offset in range(peer_count)]),
                axis=0,
            )
            block_top, summed = fold_lse(back, requested, blocks)
            block_top, summed = sub_join((block_top, summed))
            synth_pot = finish(log_synth, block_top, summed)
        return (real_pot.reshape(marginals, point_count), synth_pot.reshape(marginals, point_count))

    return shards


def solution(mesh):
    placed = (
        P(None, ("slab", "blk")),
        P(None, ("slab", "blk")),
        P(("slab", "blk")),
        P(("slab", "blk")),
        P("bag", ("slab", "blk")),
        P("bag", ("slab", "blk")),
        P(("slab", "blk", "sub"), None),
        P(("slab", "blk", "sub"), None),
        P(("slab", "blk", "sub")),
    )
    return jax.shard_map(
        make_shards(mesh.shape["blk"], mesh.shape["sub"]),
        mesh=mesh,
        in_specs=placed,
        out_specs=(P("bag", ("slab", "blk")), P("bag", ("slab", "blk"))),
        check_vma=False,
    )
```

time: 83 us -> 71.8 us (0.87)
  waiting for transfers between devices: 26.9 us -> 19.7 us
  local copies, waits for them, and re-layouts: 7.52 us -> 3.87 us
  starting transfers between devices: 20.8 us -> 21.7 us
    all_to_all x5 -> x0, waiting for transfers between devices: 24.6 us -> none  [the longest x2 12 us: shards(): lax.all_to_all(outgoing, group, split_axis=1, concat_axis=1, tiled=True)]
    ppermute x0 -> x15, starting transfers between devices: none -> 21.4 us  [the longest x9 13.9 us: send_up(): moved.append(lax.ppermute(chunks[offset], 'blk', perm))]
    all_to_all x5 -> x0, starting transfers between devices: 20.6 us -> none  [the longest x2 6.74 us: shards(): lax.all_to_all(outgoing, group, split_axis=1, concat_axis=1, tiled=True)]
    ppermute x0 -> x15, waiting for transfers between devices: none -> 15.3 us  [the longest x6 10.4 us: send_down(): moved.append(lax.ppermute(chunks[offset], 'blk', perm))]
    ppermute x2 -> x4, waiting for transfers between devices: 2.3 us -> 4.38 us  [sub_join(): other = lax.ppermute(jnp.stack(parts), 'sub', [(0, 1), (1, 0)])]
    broadcast_in_dim x3 -> x0, local copies, waits for them, and re-layouts: 1.89 us -> none  [the longest x2 1.29 us: shards(): jnp.broadcast_to(outgoing, (marginals, peer_count, n_sub, capacity, BLOCK))]
    reshape x2 -> x0, local copies, waits for them, and re-layouts: 1.39 us -> none  [the longest x1 0.74 us: shards(): pick(own_synth, requested_same, blocks)]
    reduce_sum x16 -> x17, other arithmetic: 4.17 us -> 3.77 us  [the longest x10 3.1 us: pick_rows(): return jnp.sum(chosen, axis=2, dtype=values.dtype)]
  transfers between devices with their start and end apart: 7 -> 19, of which waited for: 7 -> 15; matrix products, arithmetic and copies ran while one was open for 8% -> 7% of each run, Pallas kernels for 0% -> 0%
where the time goes in v3:
time: 71.8 us; the launch traced here: 71.6 us
  other arithmetic  24.9 us (35%)
  starting transfers between devices  21.7 us (30%)
  waiting for transfers between devices  19.7 us (27%)
  local copies, waits for them, and re-layouts  3.87 us (5%)
  between operations  1.14 us (2%)
    ppermute x9, starting transfers between devices, send_up(): moved.append(lax.ppermute(chunks[offset], 'blk', perm))  13.9 us
    ppermute x6, waiting for transfers between devices, send_down(): moved.append(lax.ppermute(chunks[offset], 'blk', perm))  10.4 us
    reduce_sum x4, other arithmetic, lse_parts(): jnp.sum(jnp.exp(scores - jnp.expand_dims(highest, axis)), axis=axis)  7.88 us
    reduce_max x4, other arithmetic, lse_parts(): highest = jnp.max(scores, axis=axis)  7.72 us
    ppermute x6, starting transfers between devices, send_down(): moved.append(lax.ppermute(chunks[offset], 'blk', perm))  7.53 us
    ppermute x9, waiting for transfers between devices, send_up(): moved.append(lax.ppermute(chunks[offset], 'blk', perm))  4.91 us
    ppermute x4, waiting for transfers between devices, sub_join(): other = lax.ppermute(jnp.stack(parts), 'sub', [(0, 1), (1, 0)])  4.38 us
    reduce_sum x10, other arithmetic, pick_rows(): return jnp.sum(chosen, axis=2, dtype=values.dtype)  3.1 us
  transfers between devices with their start and end apart: 19, of which 15 were waited for; matrix products, arithmetic and copies ran while one was open for 7% of the time, Pallas kernels for 0%

profile of v3, /device:TPU:0, one launch (start us, length us, event | category | flops | bytes accessed | tf_op | source)
XLA Modules:
  0.0 71.6 jit_solution(15047875129305181234)
XLA Ops:
  0.7 0.7 fusion.34
  1.4 0.7 fusion.35
  2.1 0.2 select_reduce_fusion.25
  2.3 0.2 slice_reduce_fusion.3
  2.5 5.1 %collective-permute-start.2 = (s32[2]{0:T(128)S(1)}, s32[2]{0:T(128)S(1)}, u32[]{:S(2)}, u32[]{:S(2)}) collective-permute-start(s32[2]{0:T(128)S(1)} %get-tuple-element.11), channel_id=1, source_target_pairs={{0,12},{4,0},{8,4},{12,8},{1,13},{5,1},{9,5},{13,9},{2,14},{6,2},{... | collective-permute-start | bytes 32 | tf_op jit(solution)/shard_map/ppermute | solution.py:91
  7.6 1.0 %collective-permute-start = (s32[2]{0:T(128)S(1)}, s32[2]{0:T(128)S(1)}, u32[]{:S(2)}, u32[]{:S(2)}) collective-permute-start(s32[2]{0:T(128)S(1)} %get-tuple-element.13), channel_id=1, source_target_pairs={{0,4},{4,8},{8,12},{12,0},{1,5},{5,9},{9,13},{13,1},{2,6},{6,10},{... | collective-permute-start | bytes 32 | tf_op jit(solution)/shard_map/ppermute | solution.py:91
  8.7 0.9 %copy.51 = bf16[8,8,8,128]{3,2,1,0:T(8,128)(2,1)S(1)} copy(bf16[8,8,8,128]{3,1,2,0:T(8,128)(2,1)} %bitcast.198) | data formatting | bytes 262144
  9.6 0.7 convert_bitcast_fusion.1
  10.6 0.9 %copy.50 = bf16[8,8,8,128]{3,2,1,0:T(8,128)(2,1)S(1)} copy(bf16[8,8,8,128]{3,1,2,0:T(8,128)(2,1)} %bitcast.199) | data formatting | bytes 262144
  11.5 0.8 %select_reduce_fusion = bf16[8,64,128]{2,1,0:T(8,128)(2,1)S(1)} fusion(pred[8,8]{1,0:T(8,128)(4,1)S(1)} %iota_compare_fusion.1, bf16[64,8,128]{2,1,0:T(8,128)(2,1)S(1)} %bitcast.192), kind=kLoop, calls=%fused_computation.13 | loop fusion | flops 983040 | bytes 262208 | tf_op jit(solution)/shard_map/reduce_sum | solution.py:26
  12.5 0.4 collective-permute-done
  13.0 0.8 %select_reduce_fusion.18 = (bf16[2,65,128]{2,1,0:T(8,128)(2,1)S(1)}, bf16[2,65,128]{2,1,0:T(8,128)(2,1)S(1)}, bf16[2,65,128]{2,1,0:T(8,128)(2,1)S(1)}, bf16[2,65,128]{2,1,0:T(8,128)(2,1)S(1)}) fusion(pred[2,8]{1,0:T(4,128)(4,1)S(1)} %iota_compare_fusion.6, bf16[65,8,128]{2,1,0:T(8,128)(2,1)S(1)} %maximum_bitcast_fusion, ...), kind=kLoop, calls=%fused_computation.35 | loop fusion | flops 998400 | bytes 266304 | tf_op jit(solution)/shard_map/reduce_sum | solution.py:26
  13.8 2.4 %collective-permute-start.3 = (bf16[2,65,128]{2,1,0:T(8,128)(2,1)S(1)}, bf16[2,65,128]{2,1,0:T(8,128)(2,1)S(1)}, u32[]{:S(2)}, u32[]{:S(2)}) collective-permute-start(bf16[2,65,128]{2,1,0:T(8,128)(2,1)S(1)} %get-tuple-element.3), channel_id=1, source_target_pairs={{0,12},{4,0},{8,4},{12,8},{1,13},{5,1},{9,5},{13,9},{2,14},{6,2},{... | collective-permute-start | bytes 99848 | tf_op jit(solution)/shard_map/ppermute | solution.py:98
  16.2 1.1 %collective-permute-start.4 = (bf16[2,65,128]{2,1,0:T(8,128)(2,1)S(1)}, bf16[2,65,128]{2,1,0:T(8,128)(2,1)S(1)}, u32[]{:S(2)}, u32[]{:S(2)}) collective-permute-start(bf16[2,65,128]{2,1,0:T(8,128)(2,1)S(1)} %get-tuple-element.4), channel_id=1, source_target_pairs={{0,8},{4,12},{8,0},{12,4},{1,9},{5,13},{9,1},{13,5},{2,10},{6,14},... | collective-permute-start | bytes 99848 | tf_op jit(solution)/shard_map/ppermute | solution.py:98
  17.5 0.1 copy.38
  17.7 0.2 collective-permute-done.3
  17.9 3.2 %collective-permute-done.4 = bf16[2,65,128]{2,1,0:T(8,128)(2,1)S(1)} collective-permute-done((bf16[2,65,128]{2,1,0:T(8,128)(2,1)S(1)}, bf16[2,65,128]{2,1,0:T(8,128)(2,1)S(1)}, u32[]{:S(2)}, u32[]{:S(2)}) %collective-permute-start.4) | collective-permute-done | bytes 33312 | tf_op jit(solution)/shard_map/ppermute | solution.py:98
  21.1 2.0 %collective-permute-done.5 = bf16[2,65,128]{2,1,0:T(8,128)(2,1)S(1)} collective-permute-done((bf16[2,65,128]{2,1,0:T(8,128)(2,1)S(1)}, bf16[2,65,128]{2,1,0:T(8,128)(2,1)S(1)}, u32[]{:S(2)}, u32[]{:S(2)}) %collective-permute-start.5) | collective-permute-done | bytes 33312 | tf_op jit(solution)/shard_map/ppermute | solution.py:98
  23.1 0.3 fusion.8
  23.5 0.2 copy.43
  23.7 0.8 %broadcast_subtract_fusion = (f32[8,128,128]{1,2,0:T(8,128)S(1)}, f32[8,128,128]{1,2,0:T(8,128)S(1)}, f32[8,128,128]{1,2,0:T(8,128)S(1)}) fusion(bf16[8,128]{1,0:T(8,128)(2,1)S(1)} %bitcast.200, bf16[8,128]{1,0:T(8,128)(2,1)S(1)} %select_reduce_fusion.23, f32[8,128,128]{2,1,0:T(8,128)S(1)} %copy.43, f32[8,128]{1,0:T(8,128)S(1)} %broadcast_multiply_fusion.2, ...), kind=kLoop, calls=%fused_computation.38 | loop fusion | flops 1703936 | bytes 2633728 | tf_op jit(solution)/shard_map/sub | solution.py:161
  24.5 0.2 copy.44
  24.7 0.2 fusion.37
  24.9 0.1 exponential_reduce_fusion
  25.1 0.1 select_reduce_fusion.14
  25.3 0.2 select_reduce_fusion.13
  25.6 0.1 select_reduce_fusion.12
  25.8 0.1 copy-done
  26.5 0.2 copy.45
  26.7 0.4 collective-permute-done.6
  27.2 0.2 select_reduce_fusion.11
  27.4 2.5 %subtract_reduce_fusion.2 = f32[8,16,128]{2,1,0:T(8,128)S(1)} fusion(f32[8,128,128]{2,1,0:T(8,128)S(1)} %copy.45, f32[8,16,128]{2,1,0:T(8,128)S(1)} %broadcast_multiply_fusion.1), kind=kLoop, calls=%fused_computation.5 | loop fusion | flops 4177920 | bytes 655360 | tf_op jit(solution)/shard_map/reduce_max | solution.py:71
  29.9 2.6 %fusion.1 = f32[8,16,128]{2,1,0:T(8,128)S(1)} fusion(f32[8,16,128]{2,1,0:T(8,128)S(1)} %subtract_reduce_fusion.2, f32[8,128,128]{2,1,0:T(8,128)S(1)} %copy.45, f32[8,16,128]{2,1,0:T(8,128)S(1)} %broadcast_multiply_fusion.1), kind=kLoop, calls=%fused_computation.7 | loop fusion | flops 6275072 | bytes 720896 | tf_op jit(solution)/shard_map/reduce_sum | solution.py:72
  32.7 0.3 collective-permute-start.8
  32.9 3.6 %collective-permute-start.9 = (f32[2,16,128]{2,1,0:T(8,128)S(1)}, f32[2,16,128]{2,1,0:T(8,128)S(1)}, u32[]{:S(2)}, u32[]{:S(2)}) collective-permute-start(f32[2,16,128]{2,1,0:T(8,128)S(1)} %get-tuple-element.29), channel_id=1, source_target_pairs={{0,12},{4,0},{8,4},{12,8},{1,13},{5,1},{9,5},{13,9},{2,14},{6,2},{... | collective-permute-start | bytes 49160 | tf_op jit(solution)/shard_map/ppermute | solution.py:91
  36.6 1.6 %collective-permute-done.7 = f32[2,16,128]{2,1,0:T(8,128)S(1)} collective-permute-done((f32[2,16,128]{2,1,0:T(8,128)S(1)}, f32[2,16,128]{2,1,0:T(8,128)S(1)}, u32[]{:S(2)}, u32[]{:S(2)}) %collective-permute-start.7) | collective-permute-done | bytes 16416 | tf_op jit(solution)/shard_map/ppermute | solution.py:91
  38.2 0.6 collective-permute-done.9
  38.8 0.1 select_reduce_fusion.10
  38.9 0.2 select_reduce_fusion.9
  39.4 1.3 %collective-permute-done.10 = f32[2,16,8,128]{3,2,1,0:T(8,128)S(1)} collective-permute-done((f32[2,16,8,128]{3,2,1,0:T(8,128)S(1)}, f32[2,16,8,128]{3,2,1,0:T(8,128)S(1)}, u32[]{:S(2)}, u32[]{:S(2)}) %collective-permute-start.10) | collective-permute-done | bytes 131104 | tf_op jit(solution)/shard_map/ppermute | solution.py:79
  40.7 0.2 select_reduce_fusion.22
  41.0 3.3 %collective-permute-start.11 = (f32[2,16,128]{2,1,0:T(8,128)S(1)}, f32[2,16,128]{2,1,0:T(8,128)S(1)}, u32[]{:S(2)}, u32[]{:S(2)}) collective-permute-start(f32[2,16,128]{2,1,0:T(8,128)S(1)} %get-tuple-element.7), channel_id=1, source_target_pairs={{0,12},{4,0},{8,4},{12,8},{1,13},{5,1},{9,5},{13,9},{2,14},{6,2},{... | collective-permute-start | bytes 49160 | tf_op jit(solution)/shard_map/ppermute | solution.py:98
  44.3 0.2 collective-permute-start.12
  44.5 0.4 collective-permute-start.13
  44.9 0.2 copy.46
  45.1 0.6 collective-permute-done.11
  45.7 3.2 %collective-permute-done.12 = f32[2,16,128]{2,1,0:T(8,128)S(1)} collective-permute-done((f32[2,16,128]{2,1,0:T(8,128)S(1)}, f32[2,16,128]{2,1,0:T(8,128)S(1)}, u32[]{:S(2)}, u32[]{:S(2)}) %collective-permute-start.12) | collective-permute-done | bytes 16416 | tf_op jit(solution)/shard_map/ppermute | solution.py:98
  48.9 1.1 %collective-permute-done.13 = f32[2,16,128]{2,1,0:T(8,128)S(1)} collective-permute-done((f32[2,16,128]{2,1,0:T(8,128)S(1)}, f32[2,16,128]{2,1,0:T(8,128)S(1)}, u32[]{:S(2)}, u32[]{:S(2)}) %collective-permute-start.13) | collective-permute-done | bytes 16416 | tf_op jit(solution)/shard_map/ppermute | solution.py:98
  50.0 2.5 %subtract_reduce_fusion.1 = f32[8,16,128]{2,1,0:T(8,128)S(1)} fusion(f32[8,128,128]{2,1,0:T(8,128)S(1)} %copy.46, f32[8,16,128]{2,1,0:T(8,128)S(1)} %maximum_multiply_fusion), kind=kLoop, calls=%fused_computation.3 | loop fusion | flops 4177920 | bytes 655360 | tf_op jit(solution)/shard_map/reduce_max | solution.py:71
  52.5 2.6 %fusion.3 = f32[8,16,128]{2,1,0:T(8,128)S(1)} fusion(f32[8,16,128]{2,1,0:T(8,128)S(1)} %subtract_reduce_fusion.1, f32[8,128,128]{2,1,0:T(8,128)S(1)} %copy.46, f32[8,16,128]{2,1,0:T(8,128)S(1)} %maximum_multiply_fusion), kind=kLoop, calls=%fused_computation.9 | loop fusion | flops 6275072 | bytes 720896 | tf_op jit(solution)/shard_map/reduce_sum | solution.py:72
  55.2 0.1 select_reduce_fusion.7
  55.3 0.2 select_reduce_fusion.6
  55.9 1.3 %collective-permute-done.14 = f32[2,16,8,128]{3,2,1,0:T(8,128)S(1)} collective-permute-done((f32[2,16,8,128]{3,2,1,0:T(8,128)S(1)}, f32[2,16,8,128]{3,2,1,0:T(8,128)S(1)}, u32[]{:S(2)}, u32[]{:S(2)}) %collective-permute-start.14) | collective-permute-done | bytes 131104 | tf_op jit(solution)/shard_map/ppermute | solution.py:79
  57.3 0.2 select_reduce_fusion.4
  57.5 2.5 %subtract_reduce_fusion = f32[8,16,128]{2,1,0:T(8,128)S(1)} fusion(f32[8,16,128]{2,1,0:T(8,128)S(1)} %broadcast_multiply_fusion, f32[8,128,128]{2,1,0:T(8,128)S(1)} %copy.45), kind=kLoop, calls=%fused_computation.1 | loop fusion | flops 4177920 | bytes 655360 | tf_op jit(solution)/shard_map/reduce_max | solution.py:71
  60.0 2.6 %fusion.5 = f32[8,16,128]{2,1,0:T(8,128)S(1)} fusion(f32[8,16,128]{2,1,0:T(8,128)S(1)} %subtract_reduce_fusion, f32[8,16,128]{2,1,0:T(8,128)S(1)} %broadcast_multiply_fusion, f32[8,128,128]{2,1,0:T(8,128)S(1)} %copy.45), kind=kLoop, calls=%fused_computation.11 | loop fusion | flops 6275072 | bytes 720896 | tf_op jit(solution)/shard_map/reduce_sum | solution.py:72
  62.8 1.0 %collective-permute-start.16 = (f32[2,16,128]{2,1,0:T(8,128)S(1)}, f32[2,16,128]{2,1,0:T(8,128)S(1)}, u32[]{:S(2)}, u32[]{:S(2)}) collective-permute-start(f32[2,16,128]{2,1,0:T(8,128)S(1)} %get-tuple-element.26), channel_id=1, source_target_pairs={{0,8},{4,12},{8,0},{12,4},{1,9},{5,13},{9,1},{13,5},{2,10},{6,14},... | collective-permute-start | bytes 49160 | tf_op jit(solution)/shard_map/ppermute | solution.py:91
  63.7 2.8 %collective-permute-start.17 = (f32[2,16,128]{2,1,0:T(8,128)S(1)}, f32[2,16,128]{2,1,0:T(8,128)S(1)}, u32[]{:S(2)}, u32[]{:S(2)}) collective-permute-start(f32[2,16,128]{2,1,0:T(8,128)S(1)} %get-tuple-element.25), channel_id=1, source_target_pairs={{0,12},{4,0},{8,4},{12,8},{1,13},{5,1},{9,5},{13,9},{2,14},{6,2},{... | collective-permute-start | bytes 49160 | tf_op jit(solution)/shard_map/ppermute | solution.py:91
  66.6 1.7 %collective-permute-done.15 = f32[2,16,128]{2,1,0:T(8,128)S(1)} collective-permute-done((f32[2,16,128]{2,1,0:T(8,128)S(1)}, f32[2,16,128]{2,1,0:T(8,128)S(1)}, u32[]{:S(2)}, u32[]{:S(2)}) %collective-permute-start.15) | collective-permute-done | bytes 16416 | tf_op jit(solution)/shard_map/ppermute | solution.py:91
  68.3 0.6 collective-permute-done.17
  68.8 0.1 select_reduce_fusion.3
  69.0 0.2 select_reduce_fusion.2
  69.4 1.3 %collective-permute-done.18 = f32[2,16,8,128]{3,2,1,0:T(8,128)S(1)} collective-permute-done((f32[2,16,8,128]{3,2,1,0:T(8,128)S(1)}, f32[2,16,8,128]{3,2,1,0:T(8,128)S(1)}, u32[]{:S(2)}, u32[]{:S(2)}) %collective-permute-start.18) | collective-permute-done | bytes 131104 | tf_op jit(solution)/shard_map/ppermute | solution.py:79
  70.8 0.8 %fusion.17 = (f32[16,1024]{1,0:T(8,128)}, f32[16,1024]{1,0:T(8,128)}) fusion(f32[2,8,8,128]{3,2,1,0:T(8,128)S(1)} %bitcast.194, f32[2,8,8,128]{3,2,1,0:T(8,128)S(1)} %bitcast.186, f32[2,8,8,128]{3,2,1,0:T(8,128)S(1)} %bitcast.193, f32[2,8,8,128]{3,2,1,0:T(8,128)S(1)} %bitcast.180, s32[16,1024]{1,0:T(8,128)S(1)} %copy-done.1, ...), kind=kLoop, calls=%fused_computation.62 | loop fusion | flops 491520 | bytes 786432 | tf_op jit(solution)/shard_map/sub | solution.py:57
  (75 shorter events, 3.2 us)
Async XLA Ops:
  0.6 11.7 %copy-start.2 = (s32[1024]{0:T(1024)S(1)}, s32[1024]{0:T(1024)}, u32[]{:S(2)}) copy-start(s32[1024]{0:T(1024)} %param.11) | copy-start | bytes 12292
  2.5 9.9 %collective-permute-start.2 = (s32[2]{0:T(128)S(1)}, s32[2]{0:T(128)S(1)}, u32[]{:S(2)}, u32[]{:S(2)}) collective-permute-start(s32[2]{0:T(128)S(1)} %get-tuple-element.11), channel_id=1, source_target_pairs={{0,12},{4,0},{8,4},{12,8},{1,13},{5,1},{9,5},{13,9},{2,14},{6,2},{... | collective-permute-start | bytes 32 | tf_op jit(solution)/shard_map/ppermute | solution.py:91
  7.6 4.8 %collective-permute-start.1 = (s32[2]{0:T(128)S(1)}, s32[2]{0:T(128)S(1)}, u32[]{:S(2)}, u32[]{:S(2)}) collective-permute-start(s32[2]{0:T(128)S(1)} %get-tuple-element.12), channel_id=1, source_target_pairs={{0,8},{4,12},{8,0},{12,4},{1,9},{5,13},{9,1},{13,5},{2,10},{6,14},... | collective-permute-start | bytes 32 | tf_op jit(solution)/shard_map/ppermute | solution.py:91
  7.6 5.3 %collective-permute-start = (s32[2]{0:T(128)S(1)}, s32[2]{0:T(128)S(1)}, u32[]{:S(2)}, u32[]{:S(2)}) collective-permute-start(s32[2]{0:T(128)S(1)} %get-tuple-element.13), channel_id=1, source_target_pairs={{0,4},{4,8},{8,12},{12,0},{1,5},{5,9},{9,13},{13,1},{2,6},{6,10},{... | collective-permute-start | bytes 32 | tf_op jit(solution)/shard_map/ppermute | solution.py:91
  13.8 4.1 %collective-permute-start.3 = (bf16[2,65,128]{2,1,0:T(8,128)(2,1)S(1)}, bf16[2,65,128]{2,1,0:T(8,128)(2,1)S(1)}, u32[]{:S(2)}, u32[]{:S(2)}) collective-permute-start(bf16[2,65,128]{2,1,0:T(8,128)(2,1)S(1)} %get-tuple-element.3), channel_id=1, source_target_pairs={{0,12},{4,0},{8,4},{12,8},{1,13},{5,1},{9,5},{13,9},{2,14},{6,2},{... | collective-permute-start | bytes 99848 | tf_op jit(solution)/shard_map/ppermute | solution.py:98
  16.2 4.9 %collective-permute-start.4 = (bf16[2,65,128]{2,1,0:T(8,128)(2,1)S(1)}, bf16[2,65,128]{2,1,0:T(8,128)(2,1)S(1)}, u32[]{:S(2)}, u32[]{:S(2)}) collective-permute-start(bf16[2,65,128]{2,1,0:T(8,128)(2,1)S(1)} %get-tuple-element.4), channel_id=1, source_target_pairs={{0,8},{4,12},{8,0},{12,4},{1,9},{5,13},{9,1},{13,5},{2,10},{6,14},... | collective-permute-start | bytes 99848 | tf_op jit(solution)/shard_map/ppermute | solution.py:98
  17.4 5.8 %collective-permute-start.5 = (bf16[2,65,128]{2,1,0:T(8,128)(2,1)S(1)}, bf16[2,65,128]{2,1,0:T(8,128)(2,1)S(1)}, u32[]{:S(2)}, u32[]{:S(2)}) collective-permute-start(bf16[2,65,128]{2,1,0:T(8,128)(2,1)S(1)} %get-tuple-element.5), channel_id=1, source_target_pairs={{0,4},{4,8},{8,12},{12,0},{1,5},{5,9},{9,13},{13,1},{2,6},{6,10},{... | collective-permute-start | bytes 99848 | tf_op jit(solution)/shard_map/ppermute | solution.py:98
  25.0 0.8 %copy-start = (s32[16,1024]{1,0:T(8,128)S(1)}, s32[16,1024]{1,0:T(8,128)}, u32[]{:S(2)}) copy-start(s32[16,1024]{1,0:T(8,128)} %param.13) | copy-start | bytes 196612
  25.7 1.4 %collective-permute-start.6 = (f32[2,16,8,128]{3,2,1,0:T(8,128)S(1)}, f32[2,16,8,128]{3,2,1,0:T(8,128)S(1)}, u32[]{:S(2)}, u32[]{:S(2)}) collective-permute-start(f32[2,16,8,128]{3,2,1,0:T(8,128)S(1)} %pad_maximum_fusion.1), channel_id=1, source_target_pairs={{0,1},{1,0},{2,3},{3,2},{4,5},{5,4},{6,7},{7,6},{8,9},{9,8},{10,11... | collective-permute-start | bytes 393224 | tf_op jit(solution)/shard_map/ppermute | solution.py:79
  32.6 6.7 %copy-start.1 = (s32[16,1024]{1,0:T(8,128)S(1)}, s32[16,1024]{1,0:T(8,128)}, u32[]{:S(2)}) copy-start(s32[16,1024]{1,0:T(8,128)} %param.14) | copy-start | bytes 196612
  32.6 5.6 %collective-permute-start.7 = (f32[2,16,128]{2,1,0:T(8,128)S(1)}, f32[2,16,128]{2,1,0:T(8,128)S(1)}, u32[]{:S(2)}, u32[]{:S(2)}) collective-permute-start(f32[2,16,128]{2,1,0:T(8,128)S(1)} %get-tuple-element.31), channel_id=1, source_target_pairs={{0,4},{4,8},{8,12},{12,0},{1,5},{5,9},{9,13},{13,1},{2,6},{6,10},{... | collective-permute-start | bytes 49160 | tf_op jit(solution)/shard_map/ppermute | solution.py:91
  32.7 5.5 %collective-permute-start.8 = (f32[2,16,128]{2,1,0:T(8,128)S(1)}, f32[2,16,128]{2,1,0:T(8,128)S(1)}, u32[]{:S(2)}, u32[]{:S(2)}) collective-permute-start(f32[2,16,128]{2,1,0:T(8,128)S(1)} %get-tuple-element.30), channel_id=1, source_target_pairs={{0,8},{4,12},{8,0},{12,4},{1,9},{5,13},{9,1},{13,5},{2,10},{6,14},... | collective-permute-start | bytes 49160 | tf_op jit(solution)/shard_map/ppermute | solution.py:91
  32.9 5.8 %collective-permute-start.9 = (f32[2,16,128]{2,1,0:T(8,128)S(1)}, f32[2,16,128]{2,1,0:T(8,128)S(1)}, u32[]{:S(2)}, u32[]{:S(2)}) collective-permute-start(f32[2,16,128]{2,1,0:T(8,128)S(1)} %get-tuple-element.29), channel_id=1, source_target_pairs={{0,12},{4,0},{8,4},{12,8},{1,13},{5,1},{9,5},{13,9},{2,14},{6,2},{... | collective-permute-start | bytes 49160 | tf_op jit(solution)/shard_map/ppermute | solution.py:91
  39.3 1.4 %collective-permute-start.10 = (f32[2,16,8,128]{3,2,1,0:T(8,128)S(1)}, f32[2,16,8,128]{3,2,1,0:T(8,128)S(1)}, u32[]{:S(2)}, u32[]{:S(2)}) collective-permute-start(f32[2,16,8,128]{3,2,1,0:T(8,128)S(1)} %pad_maximum_fusion.2), channel_id=1, source_target_pairs={{0,1},{1,0},{2,3},{3,2},{4,5},{5,4},{6,7},{7,6},{8,9},{9,8},{10,11... | collective-permute-start | bytes 393224 | tf_op jit(solution)/shard_map/ppermute | solution.py:79
  41.0 4.8 %collective-permute-start.11 = (f32[2,16,128]{2,1,0:T(8,128)S(1)}, f32[2,16,128]{2,1,0:T(8,128)S(1)}, u32[]{:S(2)}, u32[]{:S(2)}) collective-permute-start(f32[2,16,128]{2,1,0:T(8,128)S(1)} %get-tuple-element.7), channel_id=1, source_target_pairs={{0,12},{4,0},{8,4},{12,8},{1,13},{5,1},{9,5},{13,9},{2,14},{6,2},{... | collective-permute-start | bytes 49160 | tf_op jit(solution)/shard_map/ppermute | solution.py:98
  44.3 4.6 %collective-permute-start.12 = (f32[2,16,128]{2,1,0:T(8,128)S(1)}, f32[2,16,128]{2,1,0:T(8,128)S(1)}, u32[]{:S(2)}, u32[]{:S(2)}) collective-permute-start(f32[2,16,128]{2,1,0:T(8,128)S(1)} %get-tuple-element.8), channel_id=1, source_target_pairs={{0,8},{4,12},{8,0},{12,4},{1,9},{5,13},{9,1},{13,5},{2,10},{6,14},... | collective-permute-start | bytes 49160 | tf_op jit(solution)/shard_map/ppermute | solution.py:98
  44.5 5.5 %collective-permute-start.13 = (f32[2,16,128]{2,1,0:T(8,128)S(1)}, f32[2,16,128]{2,1,0:T(8,128)S(1)}, u32[]{:S(2)}, u32[]{:S(2)}) collective-permute-start(f32[2,16,128]{2,1,0:T(8,128)S(1)} %get-tuple-element.9), channel_id=1, source_target_pairs={{0,4},{4,8},{8,12},{12,0},{1,5},{5,9},{9,13},{13,1},{2,6},{6,10},{... | collective-permute-start | bytes 49160 | tf_op jit(solution)/shard_map/ppermute | solution.py:98
  55.8 1.4 %collective-permute-start.14 = (f32[2,16,8,128]{3,2,1,0:T(8,128)S(1)}, f32[2,16,8,128]{3,2,1,0:T(8,128)S(1)}, u32[]{:S(2)}, u32[]{:S(2)}) collective-permute-start(f32[2,16,8,128]{3,2,1,0:T(8,128)S(1)} %pad_maximum_fusion.3), channel_id=1, source_target_pairs={{0,1},{1,0},{2,3},{3,2},{4,5},{5,4},{6,7},{7,6},{8,9},{9,8},{10,11... | collective-permute-start | bytes 393224 | tf_op jit(solution)/shard_map/ppermute | solution.py:79
  62.7 5.6 %collective-permute-start.15 = (f32[2,16,128]{2,1,0:T(8,128)S(1)}, f32[2,16,128]{2,1,0:T(8,128)S(1)}, u32[]{:S(2)}, u32[]{:S(2)}) collective-permute-start(f32[2,16,128]{2,1,0:T(8,128)S(1)} %get-tuple-element.27), channel_id=1, source_target_pairs={{0,4},{4,8},{8,12},{12,0},{1,5},{5,9},{9,13},{13,1},{2,6},{6,10},{... | collective-permute-start | bytes 49160 | tf_op jit(solution)/shard_map/ppermute | solution.py:91
  62.8 5.5 %collective-permute-start.16 = (f32[2,16,128]{2,1,0:T(8,128)S(1)}, f32[2,16,128]{2,1,0:T(8,128)S(1)}, u32[]{:S(2)}, u32[]{:S(2)}) collective-permute-start(f32[2,16,128]{2,1,0:T(8,128)S(1)} %get-tuple-element.26), channel_id=1, source_target_pairs={{0,8},{4,12},{8,0},{12,4},{1,9},{5,13},{9,1},{13,5},{2,10},{6,14},... | collective-permute-start | bytes 49160 | tf_op jit(solution)/shard_map/ppermute | solution.py:91
  63.7 5.1 %collective-permute-start.17 = (f32[2,16,128]{2,1,0:T(8,128)S(1)}, f32[2,16,128]{2,1,0:T(8,128)S(1)}, u32[]{:S(2)}, u32[]{:S(2)}) collective-permute-start(f32[2,16,128]{2,1,0:T(8,128)S(1)} %get-tuple-element.25), channel_id=1, source_target_pairs={{0,12},{4,0},{8,4},{12,8},{1,13},{5,1},{9,5},{13,9},{2,14},{6,2},{... | collective-permute-start | bytes 49160 | tf_op jit(solution)/shard_map/ppermute | solution.py:91
  69.3 1.4 %collective-permute-start.18 = (f32[2,16,8,128]{3,2,1,0:T(8,128)S(1)}, f32[2,16,8,128]{3,2,1,0:T(8,128)S(1)}, u32[]{:S(2)}, u32[]{:S(2)}) collective-permute-start(f32[2,16,8,128]{3,2,1,0:T(8,128)S(1)} %pad_maximum_fusion.4), channel_id=1, source_target_pairs={{0,1},{1,0},{2,3},{3,2},{4,5},{5,4},{6,7},{7,6},{8,9},{9,8},{10,11... | collective-permute-start | bytes 393224 | tf_op jit(solution)/shard_map/ppermute | solution.py:79

commit v4 on v3

--- a/solution.py
+++ b/solution.py
@@ -1,6 +1,8 @@
 import jax
 import jax.numpy as jnp
 from jax import lax
+from jax.experimental import pallas as pl
+from jax.experimental.pallas import tpu as pltpu
 from jax.sharding import PartitionSpec as P
 
 BLOCK = 128
@@ -67,10 +69,36 @@
     return 0.5 * real_sq[:, :, None] + 0.5 * synth_sq[:, None, :] - inner_prod + PENALTY * differ
 
 
-def lse_parts(scores, axis):
-    highest = jnp.max(scores, axis=axis)
-    mass_sum = jnp.sum(jnp.exp(scores - jnp.expand_dims(highest, axis)), axis=axis)
-    return (highest, mass_sum)
+def lse_kernel(cost_ref, pot_ref, out_ref):
+    slots, _, marginals = pot_ref.shape
+
+    def one_slot(slot, carry):
+        tile = cost_ref[slot]
+        pots = pot_ref[slot]
+        for marginal in range(marginals):
+            scores = pots[:, marginal : marginal + 1] - tile
+            highest = jnp.max(scores, axis=0, keepdims=True)
+            mass_sum = jnp.sum(jnp.exp(scores - highest), axis=0, keepdims=True)
+            out_ref[slot, pl.ds(marginal, 1), :] = highest + jnp.log(mass_sum)
+        return carry
+
+    lax.fori_loop(0, slots, one_slot, 0)
+
+
+def slot_lse(cost, pots):
+    slots, width, _ = cost.shape
+    marginals = pots.shape[1]
+    return pl.pallas_call(
+        lse_kernel,
+        out_shape=jax.ShapeDtypeStruct((slots, marginals, width), jnp.float32),
+        in_specs=[pl.BlockSpec(memory_space=pltpu.VMEM)] * 2,
+        out_specs=pl.BlockSpec(memory_space=pltpu.VMEM),
+        cost_estimate=pl.CostEstimate(
+            flops=6 * slots * marginals * width * width,
+            transcendentals=slots * marginals * width * width,
+            bytes_accessed=4 * (slots * width * width + 2 * slots * marginals * width),
+        ),
+    )(cost, jnp.transpose(pots, (0, 2, 1)))
 
 
 def make_shards(n_blk, n_sub):
@@ -158,18 +186,13 @@
                     ),
                     axis=0,
                 )
-            scores = (panel / SMOOTH)[:, :, :, None] - cost_rows[:, None]
-            highest, mass_sum = lse_parts(scores, 2)
-            highest = jnp.where(usable, highest, SENTINEL)
-            mass_sum = jnp.where(usable, mass_sum, 0.0)
-            block_top, summed = fold_blocks(highest, mass_sum, rows_used, blocks)
+            lse = jnp.where(usable, slot_lse(cost_rows, panel / SMOOTH), SENTINEL)
+            block_top, summed = fold_lse(lse, rows_used, blocks)
             block_top, summed = sub_join((block_top, summed))
             real_pot = finish(log_real, block_top, summed)
 
             own_rows = pick_rows(real_pot, rows_used, blocks)
-            scores = (own_rows / SMOOTH)[:, :, :, None] - cost_cols[:, None]
-            highest, mass_sum = lse_parts(scores, 2)
-            lse = jnp.where(usable, highest + jnp.log(mass_sum), SENTINEL)
+            lse = jnp.where(usable, slot_lse(cost_cols, own_rows / SMOOTH), SENTINEL)
             back = jnp.concatenate(
                 send_up([lse[offset * capacity : (offset + 1) * capacity] for offset in range(peer_count)]),
                 axis=0,

time: 71.8 us -> 86.1 us (1.20)
  Pallas kernels: 0 us -> 21 us
  other arithmetic: 24.9 us -> 11.4 us
  local copies, waits for them, and re-layouts: 3.87 us -> 10.8 us
  waiting for transfers between devices: 19.7 us -> 18.4 us
    pallas_call x0 -> x4, Pallas kernels: none -> 21 us  [slot_lse(): pl.pallas_call(lse_kernel, out_shape=jax.ShapeDtypeStruct((slots, margina...]
    reduce_sum x6 -> x0, other arithmetic: 8.09 us -> none  [the longest x4 7.88 us: lse_parts(): jnp.sum(jnp.exp(scores - jnp.expand_dims(highest, axis)), axis=axis)]
    reduce_max x6 -> x0, other arithmetic: 7.95 us -> none  [the longest x4 7.72 us: lse_parts(): highest = jnp.max(scores, axis=axis)]
    ppermute x6, waiting for transfers between devices: 10.4 us -> 4.99 us  [send_down(): moved.append(lax.ppermute(chunks[offset], 'blk', perm))]
    ppermute x9, waiting for transfers between devices: 4.91 us -> 10.2 us  [send_up(): moved.append(lax.ppermute(chunks[offset], 'blk', perm))]
    unnamed x11 -> x25, local copies, waits for them, and re-layouts: 2.01 us -> 5.64 us
    select_n x4, other arithmetic: 0.31 us -> 3.65 us  [the longest x2 1.83 us: shards(): lse = jnp.where(usable, slot_lse(cost_rows, panel / SMOOTH), SENTINEL)]
    div x2 -> x3, local copies, waits for them, and re-layouts: 0.39 us -> 3.07 us  [the longest x2 2.04 us: shards(): lse = jnp.where(usable, slot_lse(cost_cols, own_rows / SMOOTH), SENTINEL)]
  transfers between devices with their start and end apart: 19 -> 19, of which waited for: 15 -> 14; matrix products, arithmetic and copies ran while one was open for 7% -> 4% of each run, Pallas kernels for 0% -> 0%
where the time goes in v4:
time: 86.1 us; the launch traced here: 85.4 us
  starting transfers between devices  22.4 us (26%)
  Pallas kernels  21 us (24%)
  waiting for transfers between devices  18.4 us (21%)
  other arithmetic  11.4 us (13%)
  local copies, waits for them, and re-layouts  10.8 us (13%)
  between operations  1.06 us (1%)
    pallas_call x4, Pallas kernels, slot_lse(): pl.pallas_call(lse_kernel, out_shape=jax.ShapeDtypeStruct((slots, margina...  21 us
    ppermute x9, starting transfers between devices, send_up(): moved.append(lax.ppermute(chunks[offset], 'blk', perm))  14.4 us
    ppermute x9, waiting for transfers between devices, send_up(): moved.append(lax.ppermute(chunks[offset], 'blk', perm))  10.2 us
    ppermute x6, starting transfers between devices, send_down(): moved.append(lax.ppermute(chunks[offset], 'blk', perm))  7.75 us
    unnamed x25, local copies, waits for them, and re-layouts  5.64 us
    ppermute x6, waiting for transfers between devices, send_down(): moved.append(lax.ppermute(chunks[offset], 'blk', perm))  4.99 us
    ppermute x4, waiting for transfers between devices, sub_join(): other = lax.ppermute(jnp.stack(parts), 'sub', [(0, 1), (1, 0)])  3.24 us
    reduce_sum x10, other arithmetic, pick_rows(): return jnp.sum(chosen, axis=2, dtype=values.dtype)  3.1 us
  transfers between devices with their start and end apart: 19, of which 14 were waited for; matrix products, arithmetic and copies ran while one was open for 4% of the time, Pallas kernels for 0%

profile of v4, /device:TPU:0, one launch (start us, length us, event | category | flops | bytes accessed | tf_op | source)
XLA Modules:
  0.0 85.4 jit_solution(16424478802530938241)
XLA Ops:
  0.6 0.6 copy-done.9
  1.4 0.6 copy-done.8
  2.0 0.2 select_reduce_fusion.25
  2.2 0.2 slice_reduce_fusion.3
  2.4 3.1 %collective-permute-start = (s32[2]{0:T(128)S(1)}, s32[2]{0:T(128)S(1)}, u32[]{:S(2)}, u32[]{:S(2)}) collective-permute-start(s32[2]{0:T(128)S(1)} %get-tuple-element.13), channel_id=1, source_target_pairs={{0,4},{4,8},{8,12},{12,0},{1,5},{5,9},{9,13},{13,1},{2,6},{6,10},{... | collective-permute-start | bytes 32 | tf_op jit(solution)/shard_map/ppermute | solution.py:119
  5.5 2.6 %collective-permute-start.2 = (s32[2]{0:T(128)S(1)}, s32[2]{0:T(128)S(1)}, u32[]{:S(2)}, u32[]{:S(2)}) collective-permute-start(s32[2]{0:T(128)S(1)} %get-tuple-element.12), channel_id=1, source_target_pairs={{0,8},{4,12},{8,0},{12,4},{1,9},{5,13},{9,1},{13,5},{2,10},{6,14},... | collective-permute-start | bytes 32 | tf_op jit(solution)/shard_map/ppermute | solution.py:119
  8.1 1.3 %collective-permute-start.4 = (s32[2]{0:T(128)S(1)}, s32[2]{0:T(128)S(1)}, u32[]{:S(2)}, u32[]{:S(2)}) collective-permute-start(s32[2]{0:T(128)S(1)} %get-tuple-element.11), channel_id=1, source_target_pairs={{0,12},{4,0},{8,4},{12,8},{1,13},{5,1},{9,5},{13,9},{2,14},{6,2},{... | collective-permute-start | bytes 32 | tf_op jit(solution)/shard_map/ppermute | solution.py:119
  9.7 1.0 %copy.65 = bf16[8,8,8,128]{3,2,1,0:T(8,128)(2,1)S(1)} copy(bf16[8,8,8,128]{3,1,2,0:T(8,128)(2,1)} %bitcast.203) | data formatting | bytes 262144
  10.7 0.8 select_reduce_fusion
  11.6 0.7 copy-done.6
  12.5 0.8 select_reduce_fusion.18
  13.3 0.7 collective-permute-start.5
  14.0 2.2 %collective-permute-start.3 = (bf16[2,65,128]{2,1,0:T(8,128)(2,1)S(1)}, bf16[2,65,128]{2,1,0:T(8,128)(2,1)S(1)}, u32[]{:S(2)}, u32[]{:S(2)}) collective-permute-start(bf16[2,65,128]{2,1,0:T(8,128)(2,1)S(1)} %get-tuple-element.4), channel_id=1, source_target_pairs={{0,8},{4,12},{8,0},{12,4},{1,9},{5,13},{9,1},{13,5},{2,10},{6,14},... | collective-permute-start | bytes 99848 | tf_op jit(solution)/shard_map/ppermute | solution.py:126
  16.2 0.9 %collective-permute-start.1 = (bf16[2,65,128]{2,1,0:T(8,128)(2,1)S(1)}, bf16[2,65,128]{2,1,0:T(8,128)(2,1)S(1)}, u32[]{:S(2)}, u32[]{:S(2)}) collective-permute-start(bf16[2,65,128]{2,1,0:T(8,128)(2,1)S(1)} %get-tuple-element.3), channel_id=1, source_target_pairs={{0,12},{4,0},{8,4},{12,8},{1,13},{5,1},{9,5},{13,9},{2,14},{6,2},{... | collective-permute-start | bytes 99848 | tf_op jit(solution)/shard_map/ppermute | solution.py:126
  17.4 1.7 %collective-permute-done.5 = bf16[2,65,128]{2,1,0:T(8,128)(2,1)S(1)} collective-permute-done((bf16[2,65,128]{2,1,0:T(8,128)(2,1)S(1)}, bf16[2,65,128]{2,1,0:T(8,128)(2,1)S(1)}, u32[]{:S(2)}, u32[]{:S(2)}) %collective-permute-start.5) | collective-permute-done | bytes 33312 | tf_op jit(solution)/shard_map/ppermute | solution.py:126
  19.2 0.6 collective-permute-done.3
  19.8 0.4 collective-permute-done.1
  20.2 0.3 fusion.2
  20.6 0.2 copy.56
  20.8 1.5 %add_multiply_fusion = (f32[8,128,128]{2,1,0:T(8,128)}, f32[8,128,128]{2,1,0:T(8,128)}) fusion(f32[8,128,128]{2,1,0:T(8,128)S(1)} %fusion.2, f32[8,128]{1,0:T(8,128)S(1)} %broadcast_multiply_fusion.2, f32[8,128]{1,0:T(8,128)S(1)} %broadcast_multiply_fusion.3, bf16[8,128]{1,0:T(8,128)(2,1)S(1)} %bitcast.205, bf16[8,128]{1,0:T(8,128)(2,1)S(1)} %select_reduce_fusion.23, ...), kind=kLoop, calls=%fused_computation.18 | loop fusion | flops 1572864 | bytes 2109440 | tf_op jit(solution)/shard_map/div | solution.py:171
  22.3 0.9 %transpose.71.pot_ref = f32[8,128,16]{2,1,0:T(8,128)} broadcast(f32[]{:T(128)} %constant.44.clone.1), dimensions={} | broadcast | bytes 65540 | tf_op jit(solution)/shard_map/transpose | solution.py:101
  23.1 5.3 %shard_map.104 = f32[8,16,128]{2,1,0:T(8,128)} custom-call(f32[8,128,128]{2,1,0:T(8,128)} %get-tuple-element.31.cost_ref, f32[8,128,16]{2,1,0:T(8,128)} %transpose.71.pot_ref), custom_call_target="tpu_custom_call" | custom-call | flops 12582912 | bytes 655360 | tf_op jit(solution)/shard_map/pallas_call | solution.py:91
  28.4 0.9 %broadcast_select_fusion.3 = f32[8,16,128]{2,1,0:T(8,128)S(1)} fusion(f32[8,16,128]{2,1,0:T(8,128)} %shard_map.104, pred[8]{0:T(512)(128)(4,1)S(1)} %gt.51), kind=kLoop, calls=%fused_computation.88 | loop fusion | flops 16384 | bytes 131080 | tf_op jit(solution)/shard_map/jit(_where)/select_n | solution.py:189
  29.3 0.1 select_reduce_fusion.14
  29.4 0.2 select_reduce_fusion.13
  29.7 0.6 copy-done.3
  30.6 0.7 copy-done
  32.0 0.2 select_reduce_fusion.11
  32.2 1.0 %copy.61 = f32[8,16,128]{1,2,0:T(8,128)} copy(f32[8,16,128]{2,1,0:T(8,128)S(1)} %broadcast_multiply_fusion.1) | data formatting | bytes 131072 | tf_op jit(solution)/shard_map/div | solution.py:195
  33.2 5.3 %shard_map.105 = f32[8,16,128]{2,1,0:T(8,128)} custom-call(f32[8,128,128]{2,1,0:T(8,128)} %get-tuple-element.30.cost_ref, f32[8,128,16]{2,1,0:T(8,128)} %bitcast.193), custom_call_target="tpu_custom_call" | custom-call | flops 12582912 | bytes 655360 | tf_op jit(solution)/shard_map/pallas_call | solution.py:91
  38.5 0.9 %broadcast_select_fusion.2 = f32[8,16,128]{2,1,0:T(8,128)S(1)} fusion(f32[8,16,128]{2,1,0:T(8,128)} %shard_map.105, pred[8]{0:T(512)(128)(4,1)S(1)} %gt.51), kind=kLoop, calls=%fused_computation.87 | loop fusion | flops 16384 | bytes 131080 | tf_op jit(solution)/shard_map/jit(_where)/select_n | solution.py:195
  39.4 2.8 %collective-permute-start.9 = (f32[2,16,128]{2,1,0:T(8,128)S(1)}, f32[2,16,128]{2,1,0:T(8,128)S(1)}, u32[]{:S(2)}, u32[]{:S(2)}) collective-permute-start(f32[2,16,128]{2,1,0:T(8,128)S(1)} %get-tuple-element.27), channel_id=1, source_target_pairs={{0,12},{4,0},{8,4},{12,8},{1,13},{5,1},{9,5},{13,9},{2,14},{6,2},{... | collective-permute-start | bytes 49160 | tf_op jit(solution)/shard_map/ppermute | solution.py:119
  42.2 0.2 collective-permute-start.8
  42.4 0.4 collective-permute-start.7
  42.9 0.7 collective-permute-done.9
  43.7 3.2 %collective-permute-done.8 = f32[2,16,128]{2,1,0:T(8,128)S(1)} collective-permute-done((f32[2,16,128]{2,1,0:T(8,128)S(1)}, f32[2,16,128]{2,1,0:T(8,128)S(1)}, u32[]{:S(2)}, u32[]{:S(2)}) %collective-permute-start.8) | collective-permute-done | bytes 16416 | tf_op jit(solution)/shard_map/ppermute | solution.py:119
  46.9 1.1 %collective-permute-done.7 = f32[2,16,128]{2,1,0:T(8,128)S(1)} collective-permute-done((f32[2,16,128]{2,1,0:T(8,128)S(1)}, f32[2,16,128]{2,1,0:T(8,128)S(1)}, u32[]{:S(2)}, u32[]{:S(2)}) %collective-permute-start.7) | collective-permute-done | bytes 16416 | tf_op jit(solution)/shard_map/ppermute | solution.py:119
  48.1 0.2 select_reduce_fusion.9
  48.6 0.7 copy-done.1
  49.3 0.6 collective-permute-done.10
  50.0 0.2 select_reduce_fusion.22
  50.2 1.0 %collective-permute-start.12 = (f32[2,16,128]{2,1,0:T(8,128)S(1)}, f32[2,16,128]{2,1,0:T(8,128)S(1)}, u32[]{:S(2)}, u32[]{:S(2)}) collective-permute-start(f32[2,16,128]{2,1,0:T(8,128)S(1)} %get-tuple-element.8), channel_id=1, source_target_pairs={{0,8},{4,12},{8,0},{12,4},{1,9},{5,13},{9,1},{13,5},{2,10},{6,14},... | collective-permute-start | bytes 49160 | tf_op jit(solution)/shard_map/ppermute | solution.py:126
  51.2 2.8 %collective-permute-start.11 = (f32[2,16,128]{2,1,0:T(8,128)S(1)}, f32[2,16,128]{2,1,0:T(8,128)S(1)}, u32[]{:S(2)}, u32[]{:S(2)}) collective-permute-start(f32[2,16,128]{2,1,0:T(8,128)S(1)} %get-tuple-element.7), channel_id=1, source_target_pairs={{0,12},{4,0},{8,4},{12,8},{1,13},{5,1},{9,5},{13,9},{2,14},{6,2},{... | collective-permute-start | bytes 49160 | tf_op jit(solution)/shard_map/ppermute | solution.py:126
  54.1 1.7 %collective-permute-done.13 = f32[2,16,128]{2,1,0:T(8,128)S(1)} collective-permute-done((f32[2,16,128]{2,1,0:T(8,128)S(1)}, f32[2,16,128]{2,1,0:T(8,128)S(1)}, u32[]{:S(2)}, u32[]{:S(2)}) %collective-permute-start.13) | collective-permute-done | bytes 16416 | tf_op jit(solution)/shard_map/ppermute | solution.py:126
  55.8 0.6 collective-permute-done.11
  56.3 1.0 %copy.62 = f32[8,16,128]{1,2,0:T(8,128)} copy(f32[8,16,128]{2,1,0:T(8,128)S(1)} %maximum_multiply_fusion) | data formatting | bytes 131072 | tf_op jit(solution)/shard_map/div | solution.py:189
  57.4 5.3 %shard_map.106 = f32[8,16,128]{2,1,0:T(8,128)} custom-call(f32[8,128,128]{2,1,0:T(8,128)} %get-tuple-element.31.cost_ref, f32[8,128,16]{2,1,0:T(8,128)} %bitcast.194), custom_call_target="tpu_custom_call" | custom-call | flops 12582912 | bytes 655360 | tf_op jit(solution)/shard_map/pallas_call | solution.py:91
  62.6 0.9 %broadcast_select_fusion.1 = f32[8,16,128]{2,1,0:T(8,128)S(1)} fusion(f32[8,16,128]{2,1,0:T(8,128)} %shard_map.106, pred[8]{0:T(512)(128)(4,1)S(1)} %gt.51), kind=kLoop, calls=%fused_computation.86 | loop fusion | flops 16384 | bytes 131080 | tf_op jit(solution)/shard_map/jit(_where)/select_n | solution.py:189
  63.7 0.2 select_reduce_fusion.6
  63.9 0.6 copy-done.2
  64.8 1.3 %collective-permute-done.14 = f32[2,16,8,128]{3,2,1,0:T(8,128)S(1)} collective-permute-done((f32[2,16,8,128]{3,2,1,0:T(8,128)S(1)}, f32[2,16,8,128]{3,2,1,0:T(8,128)S(1)}, u32[]{:S(2)}, u32[]{:S(2)}) %collective-permute-start.14) | collective-permute-done | bytes 131104 | tf_op jit(solution)/shard_map/ppermute | solution.py:107
  66.2 0.2 select_reduce_fusion.4
  66.4 1.0 %copy.63 = f32[8,16,128]{1,2,0:T(8,128)} copy(f32[8,16,128]{2,1,0:T(8,128)S(1)} %broadcast_multiply_fusion) | data formatting | bytes 131072 | tf_op jit(solution)/shard_map/div | solution.py:195
  67.4 5.3 %shard_map.107 = f32[8,16,128]{2,1,0:T(8,128)} custom-call(f32[8,128,128]{2,1,0:T(8,128)} %get-tuple-element.30.cost_ref, f32[8,128,16]{2,1,0:T(8,128)} %bitcast.195), custom_call_target="tpu_custom_call" | custom-call | flops 12582912 | bytes 655360 | tf_op jit(solution)/shard_map/pallas_call | solution.py:91
  72.7 0.9 %broadcast_select_fusion = f32[8,16,128]{2,1,0:T(8,128)S(1)} fusion(f32[8,16,128]{2,1,0:T(8,128)} %shard_map.107, pred[8]{0:T(512)(128)(4,1)S(1)} %gt.51), kind=kLoop, calls=%fused_computation.85 | loop fusion | flops 16384 | bytes 131080 | tf_op jit(solution)/shard_map/jit(_where)/select_n | solution.py:195
  73.6 3.3 %collective-permute-start.17 = (f32[2,16,128]{2,1,0:T(8,128)S(1)}, f32[2,16,128]{2,1,0:T(8,128)S(1)}, u32[]{:S(2)}, u32[]{:S(2)}) collective-permute-start(f32[2,16,128]{2,1,0:T(8,128)S(1)} %get-tuple-element.23), channel_id=1, source_target_pairs={{0,12},{4,0},{8,4},{12,8},{1,13},{5,1},{9,5},{13,9},{2,14},{6,2},{... | collective-permute-start | bytes 49160 | tf_op jit(solution)/shard_map/ppermute | solution.py:119
  76.9 0.2 collective-permute-start.16
  77.2 0.4 collective-permute-start.15
  77.6 0.8 collective-permute-done.17
  78.4 3.2 %collective-permute-done.16 = f32[2,16,128]{2,1,0:T(8,128)S(1)} collective-permute-done((f32[2,16,128]{2,1,0:T(8,128)S(1)}, f32[2,16,128]{2,1,0:T(8,128)S(1)}, u32[]{:S(2)}, u32[]{:S(2)}) %collective-permute-start.16) | collective-permute-done | bytes 16416 | tf_op jit(solution)/shard_map/ppermute | solution.py:119
  81.6 1.1 %collective-permute-done.15 = f32[2,16,128]{2,1,0:T(8,128)S(1)} collective-permute-done((f32[2,16,128]{2,1,0:T(8,128)S(1)}, f32[2,16,128]{2,1,0:T(8,128)S(1)}, u32[]{:S(2)}, u32[]{:S(2)}) %collective-permute-start.15) | collective-permute-done | bytes 16416 | tf_op jit(solution)/shard_map/ppermute | solution.py:119
  82.8 0.2 select_reduce_fusion.2
  83.3 1.3 %collective-permute-done.18 = f32[2,16,8,128]{3,2,1,0:T(8,128)S(1)} collective-permute-done((f32[2,16,8,128]{3,2,1,0:T(8,128)S(1)}, f32[2,16,8,128]{3,2,1,0:T(8,128)S(1)}, u32[]{:S(2)}, u32[]{:S(2)}) %collective-permute-start.18) | collective-permute-done | bytes 131104 | tf_op jit(solution)/shard_map/ppermute | solution.py:107
  84.6 0.8 fusion.11
  (86 shorter events, 3.4 us)
Async XLA Ops:
  0.6 0.7 copy-start.9
  1.3 0.7 copy-start.8
  1.3 0.7 copy-start.7
  2.4 9.9 %collective-permute-start = (s32[2]{0:T(128)S(1)}, s32[2]{0:T(128)S(1)}, u32[]{:S(2)}, u32[]{:S(2)}) collective-permute-start(s32[2]{0:T(128)S(1)} %get-tuple-element.13), channel_id=1, source_target_pairs={{0,4},{4,8},{8,12},{12,0},{1,5},{5,9},{9,13},{13,1},{2,6},{6,10},{... | collective-permute-start | bytes 32 | tf_op jit(solution)/shard_map/ppermute | solution.py:119
  5.5 6.9 %collective-permute-start.2 = (s32[2]{0:T(128)S(1)}, s32[2]{0:T(128)S(1)}, u32[]{:S(2)}, u32[]{:S(2)}) collective-permute-start(s32[2]{0:T(128)S(1)} %get-tuple-element.12), channel_id=1, source_target_pairs={{0,8},{4,12},{8,0},{12,4},{1,9},{5,13},{9,1},{13,5},{2,10},{6,14},... | collective-permute-start | bytes 32 | tf_op jit(solution)/shard_map/ppermute | solution.py:119
  8.1 4.4 %collective-permute-start.4 = (s32[2]{0:T(128)S(1)}, s32[2]{0:T(128)S(1)}, u32[]{:S(2)}, u32[]{:S(2)}) collective-permute-start(s32[2]{0:T(128)S(1)} %get-tuple-element.11), channel_id=1, source_target_pairs={{0,12},{4,0},{8,4},{12,8},{1,13},{5,1},{9,5},{13,9},{2,14},{6,2},{... | collective-permute-start | bytes 32 | tf_op jit(solution)/shard_map/ppermute | solution.py:119
  9.7 1.0 %copy-start.5 = (s32[1024]{0:T(1024)S(1)}, s32[1024]{0:T(1024)}, u32[]{:S(2)}) copy-start(s32[1024]{0:T(1024)} %param.12) | copy-start | bytes 12292
  9.7 1.1 %copy-start.4 = (bf16[64,1024]{1,0:T(8,128)(2,1)S(1)}, bf16[64,1024]{1,0:T(8,128)(2,1)}, u32[]{:S(2)}) copy-start(bf16[64,1024]{1,0:T(8,128)(2,1)} %param.10) | copy-start | bytes 393220
  11.5 0.7 copy-start.6
  13.3 5.9 %collective-permute-start.5 = (bf16[2,65,128]{2,1,0:T(8,128)(2,1)S(1)}, bf16[2,65,128]{2,1,0:T(8,128)(2,1)S(1)}, u32[]{:S(2)}, u32[]{:S(2)}) collective-permute-start(bf16[2,65,128]{2,1,0:T(8,128)(2,1)S(1)} %get-tuple-element.5), channel_id=1, source_target_pairs={{0,4},{4,8},{8,12},{12,0},{1,5},{5,9},{9,13},{13,1},{2,6},{6,10},{... | collective-permute-start | bytes 99848 | tf_op jit(solution)/shard_map/ppermute | solution.py:126
  14.0 5.8 %collective-permute-start.3 = (bf16[2,65,128]{2,1,0:T(8,128)(2,1)S(1)}, bf16[2,65,128]{2,1,0:T(8,128)(2,1)S(1)}, u32[]{:S(2)}, u32[]{:S(2)}) collective-permute-start(bf16[2,65,128]{2,1,0:T(8,128)(2,1)S(1)} %get-tuple-element.4), channel_id=1, source_target_pairs={{0,8},{4,12},{8,0},{12,4},{1,9},{5,13},{9,1},{13,5},{2,10},{6,14},... | collective-permute-start | bytes 99848 | tf_op jit(solution)/shard_map/ppermute | solution.py:126
  16.2 4.0 %collective-permute-start.1 = (bf16[2,65,128]{2,1,0:T(8,128)(2,1)S(1)}, bf16[2,65,128]{2,1,0:T(8,128)(2,1)S(1)}, u32[]{:S(2)}, u32[]{:S(2)}) collective-permute-start(bf16[2,65,128]{2,1,0:T(8,128)(2,1)S(1)} %get-tuple-element.3), channel_id=1, source_target_pairs={{0,12},{4,0},{8,4},{12,8},{1,13},{5,1},{9,5},{13,9},{2,14},{6,2},{... | collective-permute-start | bytes 99848 | tf_op jit(solution)/shard_map/ppermute | solution.py:126
  29.4 0.8 copy-start.3
  30.5 0.8 copy-start
  30.5 1.4 %collective-permute-start.6 = (f32[2,16,8,128]{3,2,1,0:T(8,128)S(1)}, f32[2,16,8,128]{3,2,1,0:T(8,128)S(1)}, u32[]{:S(2)}, u32[]{:S(2)}) collective-permute-start(f32[2,16,8,128]{3,2,1,0:T(8,128)S(1)} %pad_maximum_fusion.1), channel_id=1, source_target_pairs={{0,1},{1,0},{2,3},{3,2},{4,5},{5,4},{6,7},{7,6},{8,9},{9,8},{10,11... | collective-permute-start | bytes 393224 | tf_op jit(solution)/shard_map/ppermute | solution.py:107
  39.4 4.2 %collective-permute-start.9 = (f32[2,16,128]{2,1,0:T(8,128)S(1)}, f32[2,16,128]{2,1,0:T(8,128)S(1)}, u32[]{:S(2)}, u32[]{:S(2)}) collective-permute-start(f32[2,16,128]{2,1,0:T(8,128)S(1)} %get-tuple-element.27), channel_id=1, source_target_pairs={{0,12},{4,0},{8,4},{12,8},{1,13},{5,1},{9,5},{13,9},{2,14},{6,2},{... | collective-permute-start | bytes 49160 | tf_op jit(solution)/shard_map/ppermute | solution.py:119
  42.2 4.6 %collective-permute-start.8 = (f32[2,16,128]{2,1,0:T(8,128)S(1)}, f32[2,16,128]{2,1,0:T(8,128)S(1)}, u32[]{:S(2)}, u32[]{:S(2)}) collective-permute-start(f32[2,16,128]{2,1,0:T(8,128)S(1)} %get-tuple-element.28), channel_id=1, source_target_pairs={{0,8},{4,12},{8,0},{12,4},{1,9},{5,13},{9,1},{13,5},{2,10},{6,14},... | collective-permute-start | bytes 49160 | tf_op jit(solution)/shard_map/ppermute | solution.py:119
  42.4 5.5 %collective-permute-start.7 = (f32[2,16,128]{2,1,0:T(8,128)S(1)}, f32[2,16,128]{2,1,0:T(8,128)S(1)}, u32[]{:S(2)}, u32[]{:S(2)}) collective-permute-start(f32[2,16,128]{2,1,0:T(8,128)S(1)} %get-tuple-element.29), channel_id=1, source_target_pairs={{0,4},{4,8},{8,12},{12,0},{1,5},{5,9},{9,13},{13,1},{2,6},{6,10},{... | collective-permute-start | bytes 49160 | tf_op jit(solution)/shard_map/ppermute | solution.py:119
  48.5 0.8 copy-start.1
  48.5 1.4 %collective-permute-start.10 = (f32[2,16,8,128]{3,2,1,0:T(8,128)S(1)}, f32[2,16,8,128]{3,2,1,0:T(8,128)S(1)}, u32[]{:S(2)}, u32[]{:S(2)}) collective-permute-start(f32[2,16,8,128]{3,2,1,0:T(8,128)S(1)} %pad_maximum_fusion.2), channel_id=1, source_target_pairs={{0,1},{1,0},{2,3},{3,2},{4,5},{5,4},{6,7},{7,6},{8,9},{9,8},{10,11... | collective-permute-start | bytes 393224 | tf_op jit(solution)/shard_map/ppermute | solution.py:107
  50.2 5.6 %collective-permute-start.13 = (f32[2,16,128]{2,1,0:T(8,128)S(1)}, f32[2,16,128]{2,1,0:T(8,128)S(1)}, u32[]{:S(2)}, u32[]{:S(2)}) collective-permute-start(f32[2,16,128]{2,1,0:T(8,128)S(1)} %get-tuple-element.9), channel_id=1, source_target_pairs={{0,4},{4,8},{8,12},{12,0},{1,5},{5,9},{9,13},{13,1},{2,6},{6,10},{... | collective-permute-start | bytes 49160 | tf_op jit(solution)/shard_map/ppermute | solution.py:126
  50.2 5.5 %collective-permute-start.12 = (f32[2,16,128]{2,1,0:T(8,128)S(1)}, f32[2,16,128]{2,1,0:T(8,128)S(1)}, u32[]{:S(2)}, u32[]{:S(2)}) collective-permute-start(f32[2,16,128]{2,1,0:T(8,128)S(1)} %get-tuple-element.8), channel_id=1, source_target_pairs={{0,8},{4,12},{8,0},{12,4},{1,9},{5,13},{9,1},{13,5},{2,10},{6,14},... | collective-permute-start | bytes 49160 | tf_op jit(solution)/shard_map/ppermute | solution.py:126
  51.2 5.1 %collective-permute-start.11 = (f32[2,16,128]{2,1,0:T(8,128)S(1)}, f32[2,16,128]{2,1,0:T(8,128)S(1)}, u32[]{:S(2)}, u32[]{:S(2)}) collective-permute-start(f32[2,16,128]{2,1,0:T(8,128)S(1)} %get-tuple-element.7), channel_id=1, source_target_pairs={{0,12},{4,0},{8,4},{12,8},{1,13},{5,1},{9,5},{13,9},{2,14},{6,2},{... | collective-permute-start | bytes 49160 | tf_op jit(solution)/shard_map/ppermute | solution.py:126
  63.7 0.8 copy-start.2
  64.7 1.4 %collective-permute-start.14 = (f32[2,16,8,128]{3,2,1,0:T(8,128)S(1)}, f32[2,16,8,128]{3,2,1,0:T(8,128)S(1)}, u32[]{:S(2)}, u32[]{:S(2)}) collective-permute-start(f32[2,16,8,128]{3,2,1,0:T(8,128)S(1)} %pad_maximum_fusion.3), channel_id=1, source_target_pairs={{0,1},{1,0},{2,3},{3,2},{4,5},{5,4},{6,7},{7,6},{8,9},{9,8},{10,11... | collective-permute-start | bytes 393224 | tf_op jit(solution)/shard_map/ppermute | solution.py:107
  73.6 4.8 %collective-permute-start.17 = (f32[2,16,128]{2,1,0:T(8,128)S(1)}, f32[2,16,128]{2,1,0:T(8,128)S(1)}, u32[]{:S(2)}, u32[]{:S(2)}) collective-permute-start(f32[2,16,128]{2,1,0:T(8,128)S(1)} %get-tuple-element.23), channel_id=1, source_target_pairs={{0,12},{4,0},{8,4},{12,8},{1,13},{5,1},{9,5},{13,9},{2,14},{6,2},{... | collective-permute-start | bytes 49160 | tf_op jit(solution)/shard_map/ppermute | solution.py:119
  76.9 4.6 %collective-permute-start.16 = (f32[2,16,128]{2,1,0:T(8,128)S(1)}, f32[2,16,128]{2,1,0:T(8,128)S(1)}, u32[]{:S(2)}, u32[]{:S(2)}) collective-permute-start(f32[2,16,128]{2,1,0:T(8,128)S(1)} %get-tuple-element.24), channel_id=1, source_target_pairs={{0,8},{4,12},{8,0},{12,4},{1,9},{5,13},{9,1},{13,5},{2,10},{6,14},... | collective-permute-start | bytes 49160 | tf_op jit(solution)/shard_map/ppermute | solution.py:119
  77.2 5.5 %collective-permute-start.15 = (f32[2,16,128]{2,1,0:T(8,128)S(1)}, f32[2,16,128]{2,1,0:T(8,128)S(1)}, u32[]{:S(2)}, u32[]{:S(2)}) collective-permute-start(f32[2,16,128]{2,1,0:T(8,128)S(1)} %get-tuple-element.25), channel_id=1, source_target_pairs={{0,4},{4,8},{8,12},{12,0},{1,5},{5,9},{9,13},{13,1},{2,6},{6,10},{... | collective-permute-start | bytes 49160 | tf_op jit(solution)/shard_map/ppermute | solution.py:119
  83.2 1.4 %collective-permute-start.18 = (f32[2,16,8,128]{3,2,1,0:T(8,128)S(1)}, f32[2,16,8,128]{3,2,1,0:T(8,128)S(1)}, u32[]{:S(2)}, u32[]{:S(2)}) collective-permute-start(f32[2,16,8,128]{3,2,1,0:T(8,128)S(1)} %pad_maximum_fusion.4), channel_id=1, source_target_pairs={{0,1},{1,0},{2,3},{3,2},{4,5},{5,4},{6,7},{7,6},{8,9},{9,8},{10,11... | collective-permute-start | bytes 393224 | tf_op jit(solution)/shard_map/ppermute | solution.py:107

commit v5 on v3

--- a/solution.py
+++ b/solution.py
@@ -147,7 +147,7 @@
         real_pot = jnp.zeros((marginals, blocks, BLOCK), jnp.float32)
         for sweep_index in range(ITERS):
             if sweep_index == 0:
-                panel = jnp.zeros((slot_count, marginals, BLOCK), jnp.float32)
+                panel = jnp.zeros((slot_count, 1, BLOCK), jnp.float32)
             else:
                 panel = jnp.concatenate(
                     send_down(

time: 71.8 us -> 71.5 us (level)
    sub x1 -> x0, other arithmetic: 0.75 us -> none  [shards(): scores = (panel / SMOOTH)[:, :, :, None] - cost_rows[:, None]]
    reduce_max x4, other arithmetic: 7.72 us -> 8.47 us  [lse_parts(): highest = jnp.max(scores, axis=axis)]
  transfers between devices with their start and end apart: 19 -> 19, of which waited for: 15 -> 14; matrix products, arithmetic and copies ran while one was open for 7% -> 7% of each run, Pallas kernels for 0% -> 0%
where the time goes in v5:
time: 71.5 us; the launch traced here: 71.2 us
  other arithmetic  24.9 us (35%)
  starting transfers between devices  21.7 us (30%)
  waiting for transfers between devices  19.6 us (27%)
  local copies, waits for them, and re-layouts  3.56 us (5%)
  between operations  1.14 us (2%)
    ppermute x9, starting transfers between devices, send_up(): moved.append(lax.ppermute(chunks[offset], 'blk', perm))  13.9 us
    ppermute x6, waiting for transfers between devices, send_down(): moved.append(lax.ppermute(chunks[offset], 'blk', perm))  10.1 us
    reduce_max x4, other arithmetic, lse_parts(): highest = jnp.max(scores, axis=axis)  8.47 us
    reduce_sum x4, other arithmetic, lse_parts(): jnp.sum(jnp.exp(scores - jnp.expand_dims(highest, axis)), axis=axis)  8.13 us
    ppermute x6, starting transfers between devices, send_down(): moved.append(lax.ppermute(chunks[offset], 'blk', perm))  7.57 us
    ppermute x9, waiting for transfers between devices, send_up(): moved.append(lax.ppermute(chunks[offset], 'blk', perm))  4.87 us
    ppermute x4, waiting for transfers between devices, sub_join(): other = lax.ppermute(jnp.stack(parts), 'sub', [(0, 1), (1, 0)])  4.64 us
    reduce_sum x10, other arithmetic, pick_rows(): return jnp.sum(chosen, axis=2, dtype=values.dtype)  2.97 us
  transfers between devices with their start and end apart: 19, of which 14 were waited for; matrix products, arithmetic and copies ran while one was open for 7% of the time, Pallas kernels for 0%

profile of v5, /device:TPU:0, one launch (start us, length us, event | category | flops | bytes accessed | tf_op | source)
XLA Modules:
  0.0 71.2 jit_solution(12690619783034824480)
XLA Ops:
  0.7 0.7 fusion.34
  1.4 0.7 %fusion.35 = (s32[4,2]{0,1:T(2,128)S(1)}, s32[4,2]{0,1:T(2,128)S(1)}) fusion(s32[4,2]{0,1:T(2,128)} %param.16, s32[4]{0:T(128)} %param.17, s32[4,2]{0,1:T(2,128)} %param.15), kind=kLoop, calls=%fused_computation.132 | loop fusion | flops 24 | bytes 144 | tf_op jit(solution)/shard_map/jit(_where)/select_n | solution.py:129
  2.1 0.2 select_reduce_fusion.25
  2.3 0.2 slice_reduce_fusion.3
  2.5 5.1 %collective-permute-start.2 = (s32[2]{0:T(128)S(1)}, s32[2]{0:T(128)S(1)}, u32[]{:S(2)}, u32[]{:S(2)}) collective-permute-start(s32[2]{0:T(128)S(1)} %get-tuple-element.11), channel_id=1, source_target_pairs={{0,12},{4,0},{8,4},{12,8},{1,13},{5,1},{9,5},{13,9},{2,14},{6,2},{... | collective-permute-start | bytes 32 | tf_op jit(solution)/shard_map/ppermute | solution.py:91
  7.6 1.0 %collective-permute-start = (s32[2]{0:T(128)S(1)}, s32[2]{0:T(128)S(1)}, u32[]{:S(2)}, u32[]{:S(2)}) collective-permute-start(s32[2]{0:T(128)S(1)} %get-tuple-element.13), channel_id=1, source_target_pairs={{0,4},{4,8},{8,12},{12,0},{1,5},{5,9},{9,13},{13,1},{2,6},{6,10},{... | collective-permute-start | bytes 32 | tf_op jit(solution)/shard_map/ppermute | solution.py:91
  8.7 0.9 %copy.47 = bf16[8,8,8,128]{3,2,1,0:T(8,128)(2,1)S(1)} copy(bf16[8,8,8,128]{3,1,2,0:T(8,128)(2,1)} %bitcast.202) | data formatting | bytes 262144
  9.6 0.7 convert_bitcast_fusion.1
  10.3 0.1 copy.34
  10.6 0.9 %copy.46 = bf16[8,8,8,128]{3,2,1,0:T(8,128)(2,1)S(1)} copy(bf16[8,8,8,128]{3,1,2,0:T(8,128)(2,1)} %bitcast.203) | data formatting | bytes 262144
  11.5 0.8 %select_reduce_fusion = bf16[8,64,128]{2,1,0:T(8,128)(2,1)S(1)} fusion(pred[8,8]{1,0:T(8,128)(4,1)S(1)} %iota_compare_fusion.1, bf16[64,8,128]{2,1,0:T(8,128)(2,1)S(1)} %bitcast.196), kind=kLoop, calls=%fused_computation.12 | loop fusion | flops 983040 | bytes 262208 | tf_op jit(solution)/shard_map/reduce_sum | solution.py:26
  12.6 0.4 collective-permute-done
  13.0 0.8 %select_reduce_fusion.15 = (bf16[2,65,128]{2,1,0:T(8,128)(2,1)S(1)}, bf16[2,65,128]{2,1,0:T(8,128)(2,1)S(1)}, bf16[2,65,128]{2,1,0:T(8,128)(2,1)S(1)}, bf16[2,65,128]{2,1,0:T(8,128)(2,1)S(1)}) fusion(pred[2,8]{1,0:T(4,128)(4,1)S(1)} %iota_compare_fusion.6, bf16[65,8,128]{2,1,0:T(8,128)(2,1)S(1)} %maximum_bitcast_fusion, ...), kind=kLoop, calls=%fused_computation.33 | loop fusion | flops 998400 | bytes 266304 | tf_op jit(solution)/shard_map/reduce_sum | solution.py:26
  13.8 2.5 %collective-permute-start.3 = (bf16[2,65,128]{2,1,0:T(8,128)(2,1)S(1)}, bf16[2,65,128]{2,1,0:T(8,128)(2,1)S(1)}, u32[]{:S(2)}, u32[]{:S(2)}) collective-permute-start(bf16[2,65,128]{2,1,0:T(8,128)(2,1)S(1)} %get-tuple-element.3), channel_id=1, source_target_pairs={{0,12},{4,0},{8,4},{12,8},{1,13},{5,1},{9,5},{13,9},{2,14},{6,2},{... | collective-permute-start | bytes 99848 | tf_op jit(solution)/shard_map/ppermute | solution.py:98
  16.3 1.1 %collective-permute-start.4 = (bf16[2,65,128]{2,1,0:T(8,128)(2,1)S(1)}, bf16[2,65,128]{2,1,0:T(8,128)(2,1)S(1)}, u32[]{:S(2)}, u32[]{:S(2)}) collective-permute-start(bf16[2,65,128]{2,1,0:T(8,128)(2,1)S(1)} %get-tuple-element.4), channel_id=1, source_target_pairs={{0,8},{4,12},{8,0},{12,4},{1,9},{5,13},{9,1},{13,5},{2,10},{6,14},... | collective-permute-start | bytes 99848 | tf_op jit(solution)/shard_map/ppermute | solution.py:98
  17.5 0.1 copy.35
  17.7 0.1 copy.36
  18.0 3.1 %collective-permute-done.4 = bf16[2,65,128]{2,1,0:T(8,128)(2,1)S(1)} collective-permute-done((bf16[2,65,128]{2,1,0:T(8,128)(2,1)S(1)}, bf16[2,65,128]{2,1,0:T(8,128)(2,1)S(1)}, u32[]{:S(2)}, u32[]{:S(2)}) %collective-permute-start.4) | collective-permute-done | bytes 33312 | tf_op jit(solution)/shard_map/ppermute | solution.py:98
  21.1 2.0 %collective-permute-done.5 = bf16[2,65,128]{2,1,0:T(8,128)(2,1)S(1)} collective-permute-done((bf16[2,65,128]{2,1,0:T(8,128)(2,1)S(1)}, bf16[2,65,128]{2,1,0:T(8,128)(2,1)S(1)}, u32[]{:S(2)}, u32[]{:S(2)}) %collective-permute-start.5) | collective-permute-done | bytes 33312 | tf_op jit(solution)/shard_map/ppermute | solution.py:98
  23.2 0.3 fusion.8
  23.5 0.2 copy.40
  23.8 1.0 %subtract_reduce_fusion.3 = (f32[8,128]{1,0:T(8,128)S(1)}, f32[8,128,128]{1,2,0:T(8,128)S(1)}, f32[8,128,128]{1,2,0:T(8,128)S(1)}) fusion(bf16[8,128]{1,0:T(8,128)(2,1)S(1)} %bitcast.206, bf16[8,128]{1,0:T(8,128)(2,1)S(1)} %select_reduce_fusion.23, f32[8,128,128]{2,1,0:T(8,128)S(1)} %copy.40, f32[8,128]{1,0:T(8,128)S(1)} %broadcast_multiply_fusion.2, ...), kind=kLoop, calls=%fused_computation.29 | loop fusion | flops 1833984 | bytes 2113536 | tf_op jit(solution)/shard_map/reduce_max | solution.py:71
  24.7 0.4 exponential_reduce_fusion
  25.7 0.1 copy.39
  25.9 0.2 copy.41
  26.1 0.7 collective-permute-done.6
  26.8 0.2 select_reduce_fusion.11
  27.1 2.5 %subtract_reduce_fusion.2 = f32[8,16,128]{2,1,0:T(8,128)S(1)} fusion(f32[8,128,128]{2,1,0:T(8,128)S(1)} %copy.41, f32[8,16,128]{2,1,0:T(8,128)S(1)} %broadcast_multiply_fusion.1), kind=kLoop, calls=%fused_computation.5 | loop fusion | flops 4177920 | bytes 655360 | tf_op jit(solution)/shard_map/reduce_max | solution.py:71
  29.6 2.6 %fusion.1 = f32[8,16,128]{2,1,0:T(8,128)S(1)} fusion(f32[8,16,128]{2,1,0:T(8,128)S(1)} %subtract_reduce_fusion.2, f32[8,128,128]{2,1,0:T(8,128)S(1)} %copy.41, f32[8,16,128]{2,1,0:T(8,128)S(1)} %broadcast_multiply_fusion.1), kind=kLoop, calls=%fused_computation.7 | loop fusion | flops 6275072 | bytes 720896 | tf_op jit(solution)/shard_map/reduce_sum | solution.py:72
  32.3 0.3 collective-permute-start.8
  32.6 3.6 %collective-permute-start.9 = (f32[2,16,128]{2,1,0:T(8,128)S(1)}, f32[2,16,128]{2,1,0:T(8,128)S(1)}, u32[]{:S(2)}, u32[]{:S(2)}) collective-permute-start(f32[2,16,128]{2,1,0:T(8,128)S(1)} %get-tuple-element.29), channel_id=1, source_target_pairs={{0,12},{4,0},{8,4},{12,8},{1,13},{5,1},{9,5},{13,9},{2,14},{6,2},{... | collective-permute-start | bytes 49160 | tf_op jit(solution)/shard_map/ppermute | solution.py:91
  36.2 1.6 %collective-permute-done.7 = f32[2,16,128]{2,1,0:T(8,128)S(1)} collective-permute-done((f32[2,16,128]{2,1,0:T(8,128)S(1)}, f32[2,16,128]{2,1,0:T(8,128)S(1)}, u32[]{:S(2)}, u32[]{:S(2)}) %collective-permute-start.7) | collective-permute-done | bytes 16416 | tf_op jit(solution)/shard_map/ppermute | solution.py:91
  37.9 0.6 collective-permute-done.9
  38.4 0.1 select_reduce_fusion.10
  38.6 0.2 select_reduce_fusion.9
  38.8 0.1 select_reduce_fusion.8
  39.1 1.3 %collective-permute-done.10 = f32[2,16,8,128]{3,2,1,0:T(8,128)S(1)} collective-permute-done((f32[2,16,8,128]{3,2,1,0:T(8,128)S(1)}, f32[2,16,8,128]{3,2,1,0:T(8,128)S(1)}, u32[]{:S(2)}, u32[]{:S(2)}) %collective-permute-start.10) | collective-permute-done | bytes 131104 | tf_op jit(solution)/shard_map/ppermute | solution.py:79
  40.4 0.2 select_reduce_fusion.19
  40.6 3.3 %collective-permute-start.11 = (f32[2,16,128]{2,1,0:T(8,128)S(1)}, f32[2,16,128]{2,1,0:T(8,128)S(1)}, u32[]{:S(2)}, u32[]{:S(2)}) collective-permute-start(f32[2,16,128]{2,1,0:T(8,128)S(1)} %get-tuple-element.7), channel_id=1, source_target_pairs={{0,12},{4,0},{8,4},{12,8},{1,13},{5,1},{9,5},{13,9},{2,14},{6,2},{... | collective-permute-start | bytes 49160 | tf_op jit(solution)/shard_map/ppermute | solution.py:98
  43.9 0.2 collective-permute-start.12
  44.2 0.4 collective-permute-start.13
  44.6 0.2 copy.42
  44.8 0.6 collective-permute-done.11
  45.4 3.2 %collective-permute-done.12 = f32[2,16,128]{2,1,0:T(8,128)S(1)} collective-permute-done((f32[2,16,128]{2,1,0:T(8,128)S(1)}, f32[2,16,128]{2,1,0:T(8,128)S(1)}, u32[]{:S(2)}, u32[]{:S(2)}) %collective-permute-start.12) | collective-permute-done | bytes 16416 | tf_op jit(solution)/shard_map/ppermute | solution.py:98
  48.6 1.1 %collective-permute-done.13 = f32[2,16,128]{2,1,0:T(8,128)S(1)} collective-permute-done((f32[2,16,128]{2,1,0:T(8,128)S(1)}, f32[2,16,128]{2,1,0:T(8,128)S(1)}, u32[]{:S(2)}, u32[]{:S(2)}) %collective-permute-start.13) | collective-permute-done | bytes 16416 | tf_op jit(solution)/shard_map/ppermute | solution.py:98
  49.7 2.5 %subtract_reduce_fusion.1 = f32[8,16,128]{2,1,0:T(8,128)S(1)} fusion(f32[8,128,128]{2,1,0:T(8,128)S(1)} %copy.42, f32[8,16,128]{2,1,0:T(8,128)S(1)} %maximum_multiply_fusion), kind=kLoop, calls=%fused_computation.3 | loop fusion | flops 4177920 | bytes 655360 | tf_op jit(solution)/shard_map/reduce_max | solution.py:71
  52.2 2.6 %fusion.3 = f32[8,16,128]{2,1,0:T(8,128)S(1)} fusion(f32[8,16,128]{2,1,0:T(8,128)S(1)} %subtract_reduce_fusion.1, f32[8,128,128]{2,1,0:T(8,128)S(1)} %copy.42, f32[8,16,128]{2,1,0:T(8,128)S(1)} %maximum_multiply_fusion), kind=kLoop, calls=%fused_computation.9 | loop fusion | flops 6275072 | bytes 720896 | tf_op jit(solution)/shard_map/reduce_sum | solution.py:72
  54.9 0.1 select_reduce_fusion.7
  55.0 0.2 select_reduce_fusion.6
  55.2 0.1 exponential_multiply_fusion
  55.3 0.1 select_reduce_fusion.5
  55.5 1.3 %collective-permute-done.14 = f32[2,16,8,128]{3,2,1,0:T(8,128)S(1)} collective-permute-done((f32[2,16,8,128]{3,2,1,0:T(8,128)S(1)}, f32[2,16,8,128]{3,2,1,0:T(8,128)S(1)}, u32[]{:S(2)}, u32[]{:S(2)}) %collective-permute-start.14) | collective-permute-done | bytes 131104 | tf_op jit(solution)/shard_map/ppermute | solution.py:79
  56.9 0.2 select_reduce_fusion.4
  57.2 2.5 %subtract_reduce_fusion = f32[8,16,128]{2,1,0:T(8,128)S(1)} fusion(f32[8,16,128]{2,1,0:T(8,128)S(1)} %broadcast_multiply_fusion, f32[8,128,128]{2,1,0:T(8,128)S(1)} %copy.41), kind=kLoop, calls=%fused_computation.1 | loop fusion | flops 4177920 | bytes 655360 | tf_op jit(solution)/shard_map/reduce_max | solution.py:71
  59.7 2.6 %fusion.5 = f32[8,16,128]{2,1,0:T(8,128)S(1)} fusion(f32[8,16,128]{2,1,0:T(8,128)S(1)} %subtract_reduce_fusion, f32[8,16,128]{2,1,0:T(8,128)S(1)} %broadcast_multiply_fusion, f32[8,128,128]{2,1,0:T(8,128)S(1)} %copy.41), kind=kLoop, calls=%fused_computation.11 | loop fusion | flops 6275072 | bytes 720896 | tf_op jit(solution)/shard_map/reduce_sum | solution.py:72
  62.4 1.0 %collective-permute-start.16 = (f32[2,16,128]{2,1,0:T(8,128)S(1)}, f32[2,16,128]{2,1,0:T(8,128)S(1)}, u32[]{:S(2)}, u32[]{:S(2)}) collective-permute-start(f32[2,16,128]{2,1,0:T(8,128)S(1)} %get-tuple-element.26), channel_id=1, source_target_pairs={{0,8},{4,12},{8,0},{12,4},{1,9},{5,13},{9,1},{13,5},{2,10},{6,14},... | collective-permute-start | bytes 49160 | tf_op jit(solution)/shard_map/ppermute | solution.py:91
  63.4 2.8 %collective-permute-start.17 = (f32[2,16,128]{2,1,0:T(8,128)S(1)}, f32[2,16,128]{2,1,0:T(8,128)S(1)}, u32[]{:S(2)}, u32[]{:S(2)}) collective-permute-start(f32[2,16,128]{2,1,0:T(8,128)S(1)} %get-tuple-element.25), channel_id=1, source_target_pairs={{0,12},{4,0},{8,4},{12,8},{1,13},{5,1},{9,5},{13,9},{2,14},{6,2},{... | collective-permute-start | bytes 49160 | tf_op jit(solution)/shard_map/ppermute | solution.py:91
  66.2 1.7 %collective-permute-done.15 = f32[2,16,128]{2,1,0:T(8,128)S(1)} collective-permute-done((f32[2,16,128]{2,1,0:T(8,128)S(1)}, f32[2,16,128]{2,1,0:T(8,128)S(1)}, u32[]{:S(2)}, u32[]{:S(2)}) %collective-permute-start.15) | collective-permute-done | bytes 16416 | tf_op jit(solution)/shard_map/ppermute | solution.py:91
  67.9 0.6 collective-permute-done.17
  68.5 0.1 select_reduce_fusion.3
  68.6 0.2 select_reduce_fusion.2
  68.9 0.1 select_reduce_fusion.1
  69.1 1.3 %collective-permute-done.18 = f32[2,16,8,128]{3,2,1,0:T(8,128)S(1)} collective-permute-done((f32[2,16,8,128]{3,2,1,0:T(8,128)S(1)}, f32[2,16,8,128]{3,2,1,0:T(8,128)S(1)}, u32[]{:S(2)}, u32[]{:S(2)}) %collective-permute-start.18) | collective-permute-done | bytes 131104 | tf_op jit(solution)/shard_map/ppermute | solution.py:79
  70.4 0.8 %fusion.17 = (f32[16,1024]{1,0:T(8,128)}, f32[16,1024]{1,0:T(8,128)}) fusion(f32[2,8,8,128]{3,2,1,0:T(8,128)S(1)} %bitcast.198, f32[2,8,8,128]{3,2,1,0:T(8,128)S(1)} %bitcast.192, f32[2,8,8,128]{3,2,1,0:T(8,128)S(1)} %bitcast.197, f32[2,8,8,128]{3,2,1,0:T(8,128)S(1)} %bitcast.187, s32[16,1024]{1,0:T(8,128)S(1)} %copy-done.1, ...), kind=kLoop, calls=%fused_computation.58 | loop fusion | flops 491520 | bytes 786432 | tf_op jit(solution)/shard_map/sub | solution.py:57
  (74 shorter events, 2.7 us)
Async XLA Ops:
  0.6 11.7 %copy-start.2 = (s32[1024]{0:T(1024)S(1)}, s32[1024]{0:T(1024)}, u32[]{:S(2)}) copy-start(s32[1024]{0:T(1024)} %param.11) | copy-start | bytes 12292
  0.6 11.7 %copy-start = (s32[16,1024]{1,0:T(8,128)S(1)}, s32[16,1024]{1,0:T(8,128)}, u32[]{:S(2)}) copy-start(s32[16,1024]{1,0:T(8,128)} %param.13) | copy-start | bytes 196612
  2.5 9.9 %collective-permute-start.2 = (s32[2]{0:T(128)S(1)}, s32[2]{0:T(128)S(1)}, u32[]{:S(2)}, u32[]{:S(2)}) collective-permute-start(s32[2]{0:T(128)S(1)} %get-tuple-element.11), channel_id=1, source_target_pairs={{0,12},{4,0},{8,4},{12,8},{1,13},{5,1},{9,5},{13,9},{2,14},{6,2},{... | collective-permute-start | bytes 32 | tf_op jit(solution)/shard_map/ppermute | solution.py:91
  7.6 4.9 %collective-permute-start.1 = (s32[2]{0:T(128)S(1)}, s32[2]{0:T(128)S(1)}, u32[]{:S(2)}, u32[]{:S(2)}) collective-permute-start(s32[2]{0:T(128)S(1)} %get-tuple-element.12), channel_id=1, source_target_pairs={{0,8},{4,12},{8,0},{12,4},{1,9},{5,13},{9,1},{13,5},{2,10},{6,14},... | collective-permute-start | bytes 32 | tf_op jit(solution)/shard_map/ppermute | solution.py:91
  7.6 5.3 %collective-permute-start = (s32[2]{0:T(128)S(1)}, s32[2]{0:T(128)S(1)}, u32[]{:S(2)}, u32[]{:S(2)}) collective-permute-start(s32[2]{0:T(128)S(1)} %get-tuple-element.13), channel_id=1, source_target_pairs={{0,4},{4,8},{8,12},{12,0},{1,5},{5,9},{9,13},{13,1},{2,6},{6,10},{... | collective-permute-start | bytes 32 | tf_op jit(solution)/shard_map/ppermute | solution.py:91
  13.8 4.2 %collective-permute-start.3 = (bf16[2,65,128]{2,1,0:T(8,128)(2,1)S(1)}, bf16[2,65,128]{2,1,0:T(8,128)(2,1)S(1)}, u32[]{:S(2)}, u32[]{:S(2)}) collective-permute-start(bf16[2,65,128]{2,1,0:T(8,128)(2,1)S(1)} %get-tuple-element.3), channel_id=1, source_target_pairs={{0,12},{4,0},{8,4},{12,8},{1,13},{5,1},{9,5},{13,9},{2,14},{6,2},{... | collective-permute-start | bytes 99848 | tf_op jit(solution)/shard_map/ppermute | solution.py:98
  16.3 4.9 %collective-permute-start.4 = (bf16[2,65,128]{2,1,0:T(8,128)(2,1)S(1)}, bf16[2,65,128]{2,1,0:T(8,128)(2,1)S(1)}, u32[]{:S(2)}, u32[]{:S(2)}) collective-permute-start(bf16[2,65,128]{2,1,0:T(8,128)(2,1)S(1)} %get-tuple-element.4), channel_id=1, source_target_pairs={{0,8},{4,12},{8,0},{12,4},{1,9},{5,13},{9,1},{13,5},{2,10},{6,14},... | collective-permute-start | bytes 99848 | tf_op jit(solution)/shard_map/ppermute | solution.py:98
  17.4 5.8 %collective-permute-start.5 = (bf16[2,65,128]{2,1,0:T(8,128)(2,1)S(1)}, bf16[2,65,128]{2,1,0:T(8,128)(2,1)S(1)}, u32[]{:S(2)}, u32[]{:S(2)}) collective-permute-start(bf16[2,65,128]{2,1,0:T(8,128)(2,1)S(1)} %get-tuple-element.5), channel_id=1, source_target_pairs={{0,4},{4,8},{8,12},{12,0},{1,5},{5,9},{9,13},{13,1},{2,6},{6,10},{... | collective-permute-start | bytes 99848 | tf_op jit(solution)/shard_map/ppermute | solution.py:98
  25.6 1.2 %collective-permute-start.6 = (f32[2,1,8,128]{3,2,1,0:T(8,128)S(1)}, f32[2,1,8,128]{3,2,1,0:T(8,128)S(1)}, u32[]{:S(2)}, u32[]{:S(2)}) collective-permute-start(f32[2,1,8,128]{3,2,1,0:T(8,128)S(1)} %pad_maximum_fusion.6), channel_id=1, source_target_pairs={{0,1},{1,0},{2,3},{3,2},{4,5},{5,4},{6,7},{7,6},{8,9},{9,8},{10,11... | collective-permute-start | bytes 24584 | tf_op jit(solution)/shard_map/ppermute | solution.py:79
  32.3 6.7 %copy-start.1 = (s32[16,1024]{1,0:T(8,128)S(1)}, s32[16,1024]{1,0:T(8,128)}, u32[]{:S(2)}) copy-start(s32[16,1024]{1,0:T(8,128)} %param.14) | copy-start | bytes 196612
  32.3 5.6 %collective-permute-start.7 = (f32[2,16,128]{2,1,0:T(8,128)S(1)}, f32[2,16,128]{2,1,0:T(8,128)S(1)}, u32[]{:S(2)}, u32[]{:S(2)}) collective-permute-start(f32[2,16,128]{2,1,0:T(8,128)S(1)} %get-tuple-element.31), channel_id=1, source_target_pairs={{0,4},{4,8},{8,12},{12,0},{1,5},{5,9},{9,13},{13,1},{2,6},{6,10},{... | collective-permute-start | bytes 49160 | tf_op jit(solution)/shard_map/ppermute | solution.py:91
  32.3 5.5 %collective-permute-start.8 = (f32[2,16,128]{2,1,0:T(8,128)S(1)}, f32[2,16,128]{2,1,0:T(8,128)S(1)}, u32[]{:S(2)}, u32[]{:S(2)}) collective-permute-start(f32[2,16,128]{2,1,0:T(8,128)S(1)} %get-tuple-element.30), channel_id=1, source_target_pairs={{0,8},{4,12},{8,0},{12,4},{1,9},{5,13},{9,1},{13,5},{2,10},{6,14},... | collective-permute-start | bytes 49160 | tf_op jit(solution)/shard_map/ppermute | solution.py:91
  32.6 5.8 %collective-permute-start.9 = (f32[2,16,128]{2,1,0:T(8,128)S(1)}, f32[2,16,128]{2,1,0:T(8,128)S(1)}, u32[]{:S(2)}, u32[]{:S(2)}) collective-permute-start(f32[2,16,128]{2,1,0:T(8,128)S(1)} %get-tuple-element.29), channel_id=1, source_target_pairs={{0,12},{4,0},{8,4},{12,8},{1,13},{5,1},{9,5},{13,9},{2,14},{6,2},{... | collective-permute-start | bytes 49160 | tf_op jit(solution)/shard_map/ppermute | solution.py:91
  38.9 1.4 %collective-permute-start.10 = (f32[2,16,8,128]{3,2,1,0:T(8,128)S(1)}, f32[2,16,8,128]{3,2,1,0:T(8,128)S(1)}, u32[]{:S(2)}, u32[]{:S(2)}) collective-permute-start(f32[2,16,8,128]{3,2,1,0:T(8,128)S(1)} %pad_maximum_fusion.1), channel_id=1, source_target_pairs={{0,1},{1,0},{2,3},{3,2},{4,5},{5,4},{6,7},{7,6},{8,9},{9,8},{10,11... | collective-permute-start | bytes 393224 | tf_op jit(solution)/shard_map/ppermute | solution.py:79
  40.6 4.8 %collective-permute-start.11 = (f32[2,16,128]{2,1,0:T(8,128)S(1)}, f32[2,16,128]{2,1,0:T(8,128)S(1)}, u32[]{:S(2)}, u32[]{:S(2)}) collective-permute-start(f32[2,16,128]{2,1,0:T(8,128)S(1)} %get-tuple-element.7), channel_id=1, source_target_pairs={{0,12},{4,0},{8,4},{12,8},{1,13},{5,1},{9,5},{13,9},{2,14},{6,2},{... | collective-permute-start | bytes 49160 | tf_op jit(solution)/shard_map/ppermute | solution.py:98
  43.9 4.6 %collective-permute-start.12 = (f32[2,16,128]{2,1,0:T(8,128)S(1)}, f32[2,16,128]{2,1,0:T(8,128)S(1)}, u32[]{:S(2)}, u32[]{:S(2)}) collective-permute-start(f32[2,16,128]{2,1,0:T(8,128)S(1)} %get-tuple-element.8), channel_id=1, source_target_pairs={{0,8},{4,12},{8,0},{12,4},{1,9},{5,13},{9,1},{13,5},{2,10},{6,14},... | collective-permute-start | bytes 49160 | tf_op jit(solution)/shard_map/ppermute | solution.py:98
  44.2 5.5 %collective-permute-start.13 = (f32[2,16,128]{2,1,0:T(8,128)S(1)}, f32[2,16,128]{2,1,0:T(8,128)S(1)}, u32[]{:S(2)}, u32[]{:S(2)}) collective-permute-start(f32[2,16,128]{2,1,0:T(8,128)S(1)} %get-tuple-element.9), channel_id=1, source_target_pairs={{0,4},{4,8},{8,12},{12,0},{1,5},{5,9},{9,13},{13,1},{2,6},{6,10},{... | collective-permute-start | bytes 49160 | tf_op jit(solution)/shard_map/ppermute | solution.py:98
  55.5 1.4 %collective-permute-start.14 = (f32[2,16,8,128]{3,2,1,0:T(8,128)S(1)}, f32[2,16,8,128]{3,2,1,0:T(8,128)S(1)}, u32[]{:S(2)}, u32[]{:S(2)}) collective-permute-start(f32[2,16,8,128]{3,2,1,0:T(8,128)S(1)} %pad_maximum_fusion.2), channel_id=1, source_target_pairs={{0,1},{1,0},{2,3},{3,2},{4,5},{5,4},{6,7},{7,6},{8,9},{9,8},{10,11... | collective-permute-start | bytes 393224 | tf_op jit(solution)/shard_map/ppermute | solution.py:79
  62.4 5.6 %collective-permute-start.15 = (f32[2,16,128]{2,1,0:T(8,128)S(1)}, f32[2,16,128]{2,1,0:T(8,128)S(1)}, u32[]{:S(2)}, u32[]{:S(2)}) collective-permute-start(f32[2,16,128]{2,1,0:T(8,128)S(1)} %get-tuple-element.27), channel_id=1, source_target_pairs={{0,4},{4,8},{8,12},{12,0},{1,5},{5,9},{9,13},{13,1},{2,6},{6,10},{... | collective-permute-start | bytes 49160 | tf_op jit(solution)/shard_map/ppermute | solution.py:91
  62.4 5.5 %collective-permute-start.16 = (f32[2,16,128]{2,1,0:T(8,128)S(1)}, f32[2,16,128]{2,1,0:T(8,128)S(1)}, u32[]{:S(2)}, u32[]{:S(2)}) collective-permute-start(f32[2,16,128]{2,1,0:T(8,128)S(1)} %get-tuple-element.26), channel_id=1, source_target_pairs={{0,8},{4,12},{8,0},{12,4},{1,9},{5,13},{9,1},{13,5},{2,10},{6,14},... | collective-permute-start | bytes 49160 | tf_op jit(solution)/shard_map/ppermute | solution.py:91
  63.4 5.1 %collective-permute-start.17 = (f32[2,16,128]{2,1,0:T(8,128)S(1)}, f32[2,16,128]{2,1,0:T(8,128)S(1)}, u32[]{:S(2)}, u32[]{:S(2)}) collective-permute-start(f32[2,16,128]{2,1,0:T(8,128)S(1)} %get-tuple-element.25), channel_id=1, source_target_pairs={{0,12},{4,0},{8,4},{12,8},{1,13},{5,1},{9,5},{13,9},{2,14},{6,2},{... | collective-permute-start | bytes 49160 | tf_op jit(solution)/shard_map/ppermute | solution.py:91
  69.0 1.4 %collective-permute-start.18 = (f32[2,16,8,128]{3,2,1,0:T(8,128)S(1)}, f32[2,16,8,128]{3,2,1,0:T(8,128)S(1)}, u32[]{:S(2)}, u32[]{:S(2)}) collective-permute-start(f32[2,16,8,128]{3,2,1,0:T(8,128)S(1)} %pad_maximum_fusion.3), channel_id=1, source_target_pairs={{0,1},{1,0},{2,3},{3,2},{4,5},{5,4},{6,7},{7,6},{8,9},{9,8},{10,11... | collective-permute-start | bytes 393224 | tf_op jit(solution)/shard_map/ppermute | solution.py:79

commit v6 on v5

--- a/solution.py
+++ b/solution.py
@@ -74,15 +74,8 @@
 
 
 def make_shards(n_blk, n_sub):
-    def sub_join(parts):
-        if n_sub == 2:
-            other = lax.ppermute(jnp.stack(parts), "sub", [(0, 1), (1, 0)])
-            return join_parts(parts, (other[0], other[1]))
-        pieces = lax.all_gather(jnp.stack(parts), "sub")
-        subtotal = (pieces[0, 0], pieces[0, 1])
-        for index in range(1, n_sub):
-            subtotal = join_parts(subtotal, (pieces[index, 0], pieces[index, 1]))
-        return subtotal
+    def swap(value):
+        return lax.ppermute(value, "sub", [(0, 1), (1, 0)])
 
     def send_up(chunks):
         moved = [chunks[0]]
@@ -112,29 +105,40 @@
         features, point_count = real_points.shape
         blocks = point_count // BLOCK
         marginals = real_weight.shape[0]
+        half = marginals // n_sub
         peer_count, capacity = pair_block.shape
-        slot_count = peer_count * capacity
+        wide = n_sub * capacity
+        slot_count = peer_count * wide
         my_blk = lax.axis_index("blk")
+        my_sub = lax.axis_index("sub")
         own_real = real_points.reshape(features, blocks, BLOCK)
         real_tags = real_cluster.reshape(1, blocks, BLOCK).astype(jnp.bfloat16)
         own_synth = jnp.concatenate(
             [synth_points, synth_cluster.astype(jnp.bfloat16)[None, :]], axis=0
         ).reshape(features + 1, blocks, BLOCK)
-        log_real = jnp.log(real_weight.astype(jnp.float32) + 0.5).reshape(marginals, blocks, BLOCK)
-        log_synth = jnp.log(synth_weight.astype(jnp.float32) + 0.5).reshape(marginals, blocks, BLOCK)
+        log_real = jnp.log(
+            lax.dynamic_slice_in_dim(real_weight, my_sub * half, half, 0).astype(jnp.float32) + 0.5
+        ).reshape(half, blocks, BLOCK)
+        log_synth = jnp.log(
+            lax.dynamic_slice_in_dim(synth_weight, my_sub * half, half, 0).astype(jnp.float32) + 0.5
+        ).reshape(half, blocks, BLOCK)
 
         peers = (my_blk + jnp.arange(peer_count, dtype=jnp.int32)) % peer_count
-        listed = lax.broadcasted_iota(jnp.int32, (peer_count, capacity), 1) < pair_count[:, None]
-        wanted = pick_lead(jnp.where(listed, pair_block, 0), peers)
-        rows_used = pick_lead(jnp.where(listed, pair_row, 0), peers).reshape(slot_count)
-        usable = pick_lead(listed.astype(jnp.int32), peers).reshape(slot_count)[:, None, None] > 0
-
-        requested = jnp.stack(send_up([wanted[offset] for offset in range(peer_count)]))
-        far = jnp.concatenate(
-            send_down([pick_rows(own_synth, requested[offset], blocks) for offset in range(peer_count)]),
-            axis=0,
+        lists = jnp.stack([pair_block, pair_row, jnp.broadcast_to(pair_count[:, None], pair_block.shape)])
+        lists = jnp.stack([lists, swap(lists)], axis=1)
+        listed = lax.broadcasted_iota(jnp.int32, lists.shape[1:], 2) < lists[2]
+        wanted = pick_lead(jnp.transpose(jnp.where(listed, lists[0], 0), (1, 0, 2)), peers)
+        rows_used = pick_lead(jnp.transpose(jnp.where(listed, lists[1], 0), (1, 0, 2)), peers)
+        usable = pick_lead(jnp.transpose(listed.astype(jnp.int32), (1, 0, 2)), peers)
+        rows_used = rows_used.reshape(slot_count)
+        usable = usable.reshape(slot_count)[:, None, None] > 0
+
+        requested = jnp.stack(send_up([wanted[offset, 0] for offset in range(peer_count)]))
+        far = jnp.stack(
+            send_down([pick_rows(own_synth, requested[offset], blocks) for offset in range(peer_count)])
         )
-        requested = requested.reshape(slot_count)
+        requested = jnp.stack([requested, swap(requested)], axis=1).reshape(slot_count)
+        far = jnp.stack([far, swap(far)], axis=1).reshape(slot_count, features + 1, BLOCK)
         far_y = far[:, :features]
         far_tags = far[:, features]
         slot_x = pick_rows(own_real, rows_used, blocks)
@@ -143,8 +147,8 @@
         cost_cols = cost / SMOOTH
         cost_rows = jnp.transpose(cost_cols, (0, 2, 1))
 
-        synth_pot = jnp.zeros((marginals, blocks, BLOCK), jnp.float32)
-        real_pot = jnp.zeros((marginals, blocks, BLOCK), jnp.float32)
+        synth_pot = jnp.zeros((half, blocks, BLOCK), jnp.float32)
+        real_pot = jnp.zeros((half, blocks, BLOCK), jnp.float32)
         for sweep_index in range(ITERS):
             if sweep_index == 0:
                 panel = jnp.zeros((slot_count, 1, BLOCK), jnp.float32)
@@ -152,7 +156,7 @@
                 panel = jnp.concatenate(
                     send_down(
                         [
-                            pick_rows(synth_pot, requested[offset * capacity : (offset + 1) * capacity], blocks)
+                            pick_rows(synth_pot, requested[offset * wide : (offset + 1) * wide], blocks)
                             for offset in range(peer_count)
                         ]
                     ),
@@ -163,7 +167,6 @@
             highest = jnp.where(usable, highest, SENTINEL)
             mass_sum = jnp.where(usable, mass_sum, 0.0)
             block_top, summed = fold_blocks(highest, mass_sum, rows_used, blocks)
-            block_top, summed = sub_join((block_top, summed))
             real_pot = finish(log_real, block_top, summed)
 
             own_rows = pick_rows(real_pot, rows_used, blocks)
@@ -171,13 +174,19 @@
             highest, mass_sum = lse_parts(scores, 2)
             lse = jnp.where(usable, highest + jnp.log(mass_sum), SENTINEL)
             back = jnp.concatenate(
-                send_up([lse[offset * capacity : (offset + 1) * capacity] for offset in range(peer_count)]),
+                send_up([lse[offset * wide : (offset + 1) * wide] for offset in range(peer_count)]),
                 axis=0,
             )
             block_top, summed = fold_lse(back, requested, blocks)
-            block_top, summed = sub_join((block_top, summed))
             synth_pot = finish(log_synth, block_top, summed)
-        return (real_pot.reshape(marginals, point_count), synth_pot.reshape(marginals, point_count))
+
+        def both_halves(mine):
+            other = swap(mine)
+            first = jnp.where(my_sub == 0, mine, other)
+            second = jnp.where(my_sub == 0, other, mine)
+            return jnp.concatenate([first, second], axis=0).reshape(marginals, point_count)
+
+        return (both_halves(real_pot), both_halves(synth_pot))
 
     return shards
 

time: 71.5 us -> 75.5 us (1.056)
  other arithmetic: 24.9 us -> 28.8 us
  local copies, waits for them, and re-layouts: 3.56 us -> 7.38 us
  starting transfers between devices: 21.7 us -> 18.4 us
    ppermute x9, waiting for transfers between devices: 4.87 us -> 11 us  [send_up(): moved.append(lax.ppermute(chunks[offset], 'blk', perm))]
    ppermute x6, waiting for transfers between devices: 10.1 us -> 6.24 us  [send_down(): moved.append(lax.ppermute(chunks[offset], 'blk', perm))]
    ppermute x4 -> x5, waiting for transfers between devices: 4.64 us -> 1.8 us  [swap(): return lax.ppermute(value, 'sub', [(0, 1), (1, 0)])]
    ppermute x9, starting transfers between devices: 13.9 us -> 11.6 us  [send_up(): moved.append(lax.ppermute(chunks[offset], 'blk', perm))]
    unnamed x2, other arithmetic: 0.04 us -> 1.55 us
    div x2, local copies, waits for them, and re-layouts: 0.39 us -> 1.88 us  [shards(): cost_cols = cost / SMOOTH]
    reduce_max x4, other arithmetic: 8.47 us -> 9.89 us  [lse_parts(): highest = jnp.max(scores, axis=axis)]
    ppermute x6, starting transfers between devices: 7.57 us -> 6.21 us  [send_down(): moved.append(lax.ppermute(chunks[offset], 'blk', perm))]
  transfers between devices with their start and end apart: 19 -> 20, of which waited for: 14 -> 15; matrix products, arithmetic and copies ran while one was open for 7% -> 13% of each run, Pallas kernels for 0% -> 0%
where the time goes in v6:
time: 75.5 us; the launch traced here: 75.1 us
  other arithmetic  28.8 us (38%)
  waiting for transfers between devices  19.1 us (25%)
  starting transfers between devices  18.4 us (24%)
  local copies, waits for them, and re-layouts  7.38 us (10%)
  between operations  1.15 us (2%)
    ppermute x9, starting transfers between devices, send_up(): moved.append(lax.ppermute(chunks[offset], 'blk', perm))  11.6 us
    ppermute x9, waiting for transfers between devices, send_up(): moved.append(lax.ppermute(chunks[offset], 'blk', perm))  11 us
    reduce_max x4, other arithmetic, lse_parts(): highest = jnp.max(scores, axis=axis)  9.89 us
    reduce_sum x4, other arithmetic, lse_parts(): jnp.sum(jnp.exp(scores - jnp.expand_dims(highest, axis)), axis=axis)  8.57 us
    ppermute x6, waiting for transfers between devices, send_down(): moved.append(lax.ppermute(chunks[offset], 'blk', perm))  6.24 us
    ppermute x6, starting transfers between devices, send_down(): moved.append(lax.ppermute(chunks[offset], 'blk', perm))  6.21 us
    reduce_sum x10, other arithmetic, pick_rows(): return jnp.sum(chosen, axis=2, dtype=values.dtype)  3.72 us
    unnamed x5, local copies, waits for them, and re-layouts  3.14 us
  transfers between devices with their start and end apart: 20, of which 15 were waited for; matrix products, arithmetic and copies ran while one was open for 13% of the time, Pallas kernels for 0%

profile of v6, /device:TPU:0, one launch (start us, length us, event | category | flops | bytes accessed | tf_op | source)
XLA Modules:
  0.0 75.1 jit_solution(15871319863909691573)
XLA Ops:
  0.6 0.7 stack_broadcast_in_dim.2
  1.3 0.7 fusion.25
  2.0 0.5 collective-permute-start
  2.5 0.7 convert_bitcast_fusion.1
  3.2 0.7 convert_bitcast_fusion.2
  3.9 0.8 %multiply_bitcast_fusion.1 = f32[1,8,8,128]{3,1,2,0:T(8,128)S(1)} fusion(s32[16,1024]{1,0:T(8,128)} %param.13, s32[]{:T(128)S(6)} %select_n.254), kind=kLoop, calls=%fused_computation.69 | loop fusion | flops 24576 | bytes 65540
  4.7 0.8 %multiply_bitcast_fusion = f32[1,8,8,128]{3,1,2,0:T(8,128)S(1)} fusion(s32[16,1024]{1,0:T(8,128)} %param.14, s32[]{:T(128)S(6)} %select_n.254), kind=kLoop, calls=%fused_computation.68 | loop fusion | flops 24576 | bytes 65540
  5.5 0.9 %copy.61 = bf16[8,8,8,128]{3,2,1,0:T(8,128)(2,1)S(1)} copy(bf16[8,8,8,128]{3,1,2,0:T(8,128)(2,1)} %bitcast.87) | data formatting | bytes 262144
  6.4 0.9 %copy.60 = bf16[8,8,8,128]{3,2,1,0:T(8,128)(2,1)S(1)} copy(bf16[8,8,8,128]{3,1,2,0:T(8,128)(2,1)} %bitcast.88) | data formatting | bytes 262144
  7.4 0.3 select_reduce_fusion.25
  7.7 0.1 copy.49
  7.9 0.2 slice_reduce_fusion.3
  8.5 4.6 %collective-permute-start.3 = (s32[2]{0:T(128)S(1)}, s32[2]{0:T(128)S(1)}, u32[]{:S(2)}, u32[]{:S(2)}) collective-permute-start(s32[2]{0:T(128)S(1)} %get-tuple-element.15), channel_id=1, source_target_pairs={{0,12},{4,0},{8,4},{12,8},{1,13},{5,1},{9,5},{13,9},{2,14},{6,2},{... | collective-permute-start | bytes 32 | tf_op jit(solution)/shard_map/ppermute | solution.py:84
  13.1 1.0 %collective-permute-start.1 = (s32[2]{0:T(128)S(1)}, s32[2]{0:T(128)S(1)}, u32[]{:S(2)}, u32[]{:S(2)}) collective-permute-start(s32[2]{0:T(128)S(1)} %get-tuple-element.17), channel_id=1, source_target_pairs={{0,4},{4,8},{8,12},{12,0},{1,5},{5,9},{9,13},{13,1},{2,6},{6,10},{... | collective-permute-start | bytes 32 | tf_op jit(solution)/shard_map/ppermute | solution.py:84
  14.2 1.4 %select_reduce_fusion = bf16[16,64,128]{2,1,0:T(8,128)(2,1)S(1)} fusion(pred[16,8]{1,0:T(8,128)(4,1)S(1)} %iota_compare_fusion.1, bf16[64,8,128]{2,1,0:T(8,128)(2,1)S(1)} %bitcast.81), kind=kLoop, calls=%fused_computation.12 | loop fusion | flops 1966080 | bytes 393344 | tf_op jit(solution)/shard_map/reduce_sum | solution.py:26
  15.7 1.8 %collective-permute-done.2 = s32[2]{0:T(128)S(1)} collective-permute-done((s32[2]{0:T(128)S(1)}, s32[2]{0:T(128)S(1)}, u32[]{:S(2)}, u32[]{:S(2)}) %collective-permute-start.2) | collective-permute-done | bytes 40 | tf_op jit(solution)/shard_map/ppermute | solution.py:84
  17.5 0.9 %collective-permute-done.1 = s32[2]{0:T(128)S(1)} collective-permute-done((s32[2]{0:T(128)S(1)}, s32[2]{0:T(128)S(1)}, u32[]{:S(2)}, u32[]{:S(2)}) %collective-permute-start.1) | collective-permute-done | bytes 40 | tf_op jit(solution)/shard_map/ppermute | solution.py:84
  18.8 0.8 %select_reduce_fusion.15 = (bf16[2,65,128]{2,1,0:T(8,128)(2,1)S(1)}, bf16[2,65,128]{2,1,0:T(8,128)(2,1)S(1)}, bf16[2,65,128]{2,1,0:T(8,128)(2,1)S(1)}, bf16[2,65,128]{2,1,0:T(8,128)(2,1)S(1)}) fusion(pred[2,8]{1,0:T(4,128)(4,1)S(1)} %iota_compare_fusion.10, bf16[65,8,128]{2,1,0:T(8,128)(2,1)S(1)} %maximum_bitcast_fusion, ...), kind=kLoop, calls=%fused_computation.36 | loop fusion | flops 998400 | bytes 266304 | tf_op jit(solution)/shard_map/reduce_sum | solution.py:26
  19.5 0.6 collective-permute-start.5
  20.1 0.7 collective-permute-start.6
  20.9 1.9 %collective-permute-start.7 = (bf16[2,65,128]{2,1,0:T(8,128)(2,1)S(1)}, bf16[2,65,128]{2,1,0:T(8,128)(2,1)S(1)}, u32[]{:S(2)}, u32[]{:S(2)}) collective-permute-start(bf16[2,65,128]{2,1,0:T(8,128)(2,1)S(1)} %get-tuple-element.5), channel_id=1, source_target_pairs={{0,4},{4,8},{8,12},{12,0},{1,5},{5,9},{9,13},{13,1},{2,6},{6,10},{... | collective-permute-start | bytes 99848 | tf_op jit(solution)/shard_map/ppermute | solution.py:91
  23.1 0.3 fusion.11
  23.7 1.7 %collective-permute-done.6 = bf16[2,65,128]{2,1,0:T(8,128)(2,1)S(1)} collective-permute-done((bf16[2,65,128]{2,1,0:T(8,128)(2,1)S(1)}, bf16[2,65,128]{2,1,0:T(8,128)(2,1)S(1)}, u32[]{:S(2)}, u32[]{:S(2)}) %collective-permute-start.6) | collective-permute-done | bytes 33312 | tf_op jit(solution)/shard_map/ppermute | solution.py:91
  25.4 1.2 %collective-permute-done.7 = bf16[2,65,128]{2,1,0:T(8,128)(2,1)S(1)} collective-permute-done((bf16[2,65,128]{2,1,0:T(8,128)(2,1)S(1)}, bf16[2,65,128]{2,1,0:T(8,128)(2,1)S(1)}, u32[]{:S(2)}, u32[]{:S(2)}) %collective-permute-start.7) | collective-permute-done | bytes 33312 | tf_op jit(solution)/shard_map/ppermute | solution.py:91
  26.8 1.3 %collective-permute-done.8 = bf16[4,2,65,128]{3,2,1,0:T(8,128)(2,1)S(1)} collective-permute-done((bf16[4,2,65,128]{3,2,1,0:T(8,128)(2,1)S(1)}, bf16[4,2,65,128]{3,2,1,0:T(8,128)(2,1)S(1)}, u32[]{:S(2)}, u32[]{:S(2)}) %collective-permute-start.8) | collective-permute-done | bytes 133152 | tf_op jit(solution)/shard_map/ppermute | solution.py:78
  28.2 0.4 fusion.8
  28.6 0.3 copy.54
  29.0 2.3 %subtract_reduce_fusion.3 = (f32[16,128]{1,0:T(8,128)S(1)}, f32[16,128,128]{1,2,0:T(8,128)S(1)}, f32[16,128,128]{1,2,0:T(8,128)}) fusion(bf16[16,128]{1,0:T(8,128)(2,1)S(1)} %bitcast.91, bf16[16,128]{1,0:T(8,128)(2,1)S(1)} %select_reduce_fusion.23, f32[16,128,128]{2,1,0:T(8,128)S(1)} %copy.54, f32[16,128]{1,0:T(8,128)S(1)} %get-tuple-element.42, ...), kind=kLoop, calls=%fused_computation.18 | loop fusion | flops 3667968 | bytes 4227072 | tf_op jit(solution)/shard_map/reduce_max | solution.py:71
  31.3 1.6 %copy.55 = f32[16,128,128]{2,1,0:T(8,128)S(1)} copy(f32[16,128,128]{1,2,0:T(8,128)} %get-tuple-element.39) | data formatting | bytes 2097152 | tf_op jit(solution)/shard_map/div | solution.py:147
  32.8 0.6 exponential_reduce_fusion
  34.0 0.2 select_reduce_fusion.11
  34.2 2.5 %subtract_reduce_fusion.2 = f32[16,8,128]{2,1,0:T(8,128)S(1)} fusion(f32[16,128,128]{2,1,0:T(8,128)S(1)} %copy.55, f32[16,8,128]{2,1,0:T(8,128)S(1)} %broadcast_multiply_fusion.1), kind=kLoop, calls=%fused_computation.5 | loop fusion | flops 4177920 | bytes 1179648 | tf_op jit(solution)/shard_map/reduce_max | solution.py:71
  36.7 2.6 %fusion.1 = f32[16,8,128]{2,1,0:T(8,128)S(1)} fusion(f32[16,8,128]{2,1,0:T(8,128)S(1)} %subtract_reduce_fusion.2, f32[16,128,128]{2,1,0:T(8,128)S(1)} %copy.55, f32[16,8,128]{2,1,0:T(8,128)S(1)} %broadcast_multiply_fusion.1), kind=kLoop, calls=%fused_computation.7 | loop fusion | flops 6275072 | bytes 1245184 | tf_op jit(solution)/shard_map/reduce_sum | solution.py:72
  39.5 1.5 %collective-permute-start.11 = (f32[4,8,128]{2,1,0:T(8,128)S(1)}, f32[4,8,128]{2,1,0:T(8,128)S(1)}, u32[]{:S(2)}, u32[]{:S(2)}) collective-permute-start(f32[4,8,128]{2,1,0:T(8,128)S(1)} %get-tuple-element.36), channel_id=1, source_target_pairs={{0,12},{4,0},{8,4},{12,8},{1,13},{5,1},{9,5},{13,9},{2,14},{6,2},{... | collective-permute-start | bytes 49160 | tf_op jit(solution)/shard_map/ppermute | solution.py:84
  41.0 0.2 collective-permute-start.10
  41.2 1.2 %collective-permute-start.9 = (f32[4,8,128]{2,1,0:T(8,128)S(1)}, f32[4,8,128]{2,1,0:T(8,128)S(1)}, u32[]{:S(2)}, u32[]{:S(2)}) collective-permute-start(f32[4,8,128]{2,1,0:T(8,128)S(1)} %get-tuple-element.38), channel_id=1, source_target_pairs={{0,4},{4,8},{8,12},{12,0},{1,5},{5,9},{9,13},{13,1},{2,6},{6,10},{... | collective-permute-start | bytes 49160 | tf_op jit(solution)/shard_map/ppermute | solution.py:84
  42.4 0.9 %collective-permute-done.11 = f32[4,8,128]{2,1,0:T(8,128)S(1)} collective-permute-done((f32[4,8,128]{2,1,0:T(8,128)S(1)}, f32[4,8,128]{2,1,0:T(8,128)S(1)}, u32[]{:S(2)}, u32[]{:S(2)}) %collective-permute-start.11) | collective-permute-done | bytes 16416 | tf_op jit(solution)/shard_map/ppermute | solution.py:84
  43.3 2.5 %collective-permute-done.10 = f32[4,8,128]{2,1,0:T(8,128)S(1)} collective-permute-done((f32[4,8,128]{2,1,0:T(8,128)S(1)}, f32[4,8,128]{2,1,0:T(8,128)S(1)}, u32[]{:S(2)}, u32[]{:S(2)}) %collective-permute-start.10) | collective-permute-done | bytes 16416 | tf_op jit(solution)/shard_map/ppermute | solution.py:84
  45.8 0.9 %collective-permute-done.9 = f32[4,8,128]{2,1,0:T(8,128)S(1)} collective-permute-done((f32[4,8,128]{2,1,0:T(8,128)S(1)}, f32[4,8,128]{2,1,0:T(8,128)S(1)}, u32[]{:S(2)}, u32[]{:S(2)}) %collective-permute-start.9) | collective-permute-done | bytes 16416 | tf_op jit(solution)/shard_map/ppermute | solution.py:84
  46.7 0.1 select_reduce_fusion.10
  46.8 0.2 select_reduce_fusion.9
  47.2 0.2 select_reduce_fusion.19
  47.5 1.0 %collective-permute-start.12 = (f32[4,8,128]{2,1,0:T(8,128)S(1)}, f32[4,8,128]{2,1,0:T(8,128)S(1)}, u32[]{:S(2)}, u32[]{:S(2)}) collective-permute-start(f32[4,8,128]{2,1,0:T(8,128)S(1)} %get-tuple-element.7), channel_id=1, source_target_pairs={{0,12},{4,0},{8,4},{12,8},{1,13},{5,1},{9,5},{13,9},{2,14},{6,2},{... | collective-permute-start | bytes 49160 | tf_op jit(solution)/shard_map/ppermute | solution.py:91
  48.6 1.9 %collective-permute-start.14 = (f32[4,8,128]{2,1,0:T(8,128)S(1)}, f32[4,8,128]{2,1,0:T(8,128)S(1)}, u32[]{:S(2)}, u32[]{:S(2)}) collective-permute-start(f32[4,8,128]{2,1,0:T(8,128)S(1)} %get-tuple-element.9), channel_id=1, source_target_pairs={{0,4},{4,8},{8,12},{12,0},{1,5},{5,9},{9,13},{13,1},{2,6},{6,10},{... | collective-permute-start | bytes 49160 | tf_op jit(solution)/shard_map/ppermute | solution.py:91
  50.5 0.3 copy.56
  50.8 0.4 collective-permute-done.12
  51.2 1.9 %collective-permute-done.13 = f32[4,8,128]{2,1,0:T(8,128)S(1)} collective-permute-done((f32[4,8,128]{2,1,0:T(8,128)S(1)}, f32[4,8,128]{2,1,0:T(8,128)S(1)}, u32[]{:S(2)}, u32[]{:S(2)}) %collective-permute-start.13) | collective-permute-done | bytes 16416 | tf_op jit(solution)/shard_map/ppermute | solution.py:91
  53.1 1.0 %collective-permute-done.14 = f32[4,8,128]{2,1,0:T(8,128)S(1)} collective-permute-done((f32[4,8,128]{2,1,0:T(8,128)S(1)}, f32[4,8,128]{2,1,0:T(8,128)S(1)}, u32[]{:S(2)}, u32[]{:S(2)}) %collective-permute-start.14) | collective-permute-done | bytes 16416 | tf_op jit(solution)/shard_map/ppermute | solution.py:91
  54.1 2.5 %subtract_reduce_fusion.1 = f32[16,8,128]{2,1,0:T(8,128)S(1)} fusion(f32[16,128,128]{2,1,0:T(8,128)S(1)} %copy.56, f32[16,8,128]{2,1,0:T(8,128)S(1)} %maximum_multiply_fusion), kind=kLoop, calls=%fused_computation.3 | loop fusion | flops 4177920 | bytes 1179648 | tf_op jit(solution)/shard_map/reduce_max | solution.py:71
  56.7 2.6 %fusion.3 = f32[16,8,128]{2,1,0:T(8,128)S(1)} fusion(f32[16,8,128]{2,1,0:T(8,128)S(1)} %subtract_reduce_fusion.1, f32[16,128,128]{2,1,0:T(8,128)S(1)} %copy.56, f32[16,8,128]{2,1,0:T(8,128)S(1)} %maximum_multiply_fusion), kind=kLoop, calls=%fused_computation.9 | loop fusion | flops 6275072 | bytes 1245184 | tf_op jit(solution)/shard_map/reduce_sum | solution.py:72
  59.4 0.1 select_reduce_fusion.7
  59.5 0.2 select_reduce_fusion.6
  60.0 0.2 select_reduce_fusion.4
  60.2 2.5 %subtract_reduce_fusion = f32[16,8,128]{2,1,0:T(8,128)S(1)} fusion(f32[16,8,128]{2,1,0:T(8,128)S(1)} %broadcast_multiply_fusion, f32[16,128,128]{2,1,0:T(8,128)S(1)} %copy.55), kind=kLoop, calls=%fused_computation.1 | loop fusion | flops 4177920 | bytes 1179648 | tf_op jit(solution)/shard_map/reduce_max | solution.py:71
  62.8 2.6 %fusion.5 = f32[16,8,128]{2,1,0:T(8,128)S(1)} fusion(f32[16,8,128]{2,1,0:T(8,128)S(1)} %subtract_reduce_fusion, f32[16,8,128]{2,1,0:T(8,128)S(1)} %broadcast_multiply_fusion, f32[16,128,128]{2,1,0:T(8,128)S(1)} %copy.55), kind=kLoop, calls=%fused_computation.11 | loop fusion | flops 6275072 | bytes 1245184 | tf_op jit(solution)/shard_map/reduce_sum | solution.py:72
  65.5 1.6 %collective-permute-start.18 = (f32[4,8,128]{2,1,0:T(8,128)S(1)}, f32[4,8,128]{2,1,0:T(8,128)S(1)}, u32[]{:S(2)}, u32[]{:S(2)}) collective-permute-start(f32[4,8,128]{2,1,0:T(8,128)S(1)} %get-tuple-element.30), channel_id=1, source_target_pairs={{0,12},{4,0},{8,4},{12,8},{1,13},{5,1},{9,5},{13,9},{2,14},{6,2},{... | collective-permute-start | bytes 49160 | tf_op jit(solution)/shard_map/ppermute | solution.py:84
  67.1 1.5 %collective-permute-start.16 = (f32[4,8,128]{2,1,0:T(8,128)S(1)}, f32[4,8,128]{2,1,0:T(8,128)S(1)}, u32[]{:S(2)}, u32[]{:S(2)}) collective-permute-start(f32[4,8,128]{2,1,0:T(8,128)S(1)} %get-tuple-element.32), channel_id=1, source_target_pairs={{0,4},{4,8},{8,12},{12,0},{1,5},{5,9},{9,13},{13,1},{2,6},{6,10},{... | collective-permute-start | bytes 49160 | tf_op jit(solution)/shard_map/ppermute | solution.py:84
  68.6 0.7 collective-permute-done.18
  69.3 2.5 %collective-permute-done.17 = f32[4,8,128]{2,1,0:T(8,128)S(1)} collective-permute-done((f32[4,8,128]{2,1,0:T(8,128)S(1)}, f32[4,8,128]{2,1,0:T(8,128)S(1)}, u32[]{:S(2)}, u32[]{:S(2)}) %collective-permute-start.17) | collective-permute-done | bytes 16416 | tf_op jit(solution)/shard_map/ppermute | solution.py:84
  71.9 0.8 %collective-permute-done.16 = f32[4,8,128]{2,1,0:T(8,128)S(1)} collective-permute-done((f32[4,8,128]{2,1,0:T(8,128)S(1)}, f32[4,8,128]{2,1,0:T(8,128)S(1)}, u32[]{:S(2)}, u32[]{:S(2)}) %collective-permute-start.16) | collective-permute-done | bytes 16416 | tf_op jit(solution)/shard_map/ppermute | solution.py:84
  72.8 0.2 select_reduce_fusion.2
  73.3 0.6 copy.72
  73.9 0.5 collective-permute-done.19
  74.5 0.6 copy.71
  (80 shorter events, 3.7 us)
Async XLA Ops:
  2.0 5.4 %collective-permute-start = (s32[3,4,2]{1,2,0:T(2,128)S(1)}, s32[3,4,2]{1,2,0:T(2,128)S(1)}, u32[]{:S(2)}, u32[]{:S(2)}) collective-permute-start(s32[3,4,2]{1,2,0:T(2,128)S(1)} %get-tuple-element.41), channel_id=1, source_target_pairs={{0,1},{1,0},{2,3},{3,2},{4,5},{5,4},{6,7},{7,6},{8,9},{9,8},{10,11... | collective-permute-start | bytes 296 | tf_op jit(solution)/shard_map/ppermute | solution.py:78
  8.5 7.3 %collective-permute-start.3 = (s32[2]{0:T(128)S(1)}, s32[2]{0:T(128)S(1)}, u32[]{:S(2)}, u32[]{:S(2)}) collective-permute-start(s32[2]{0:T(128)S(1)} %get-tuple-element.15), channel_id=1, source_target_pairs={{0,12},{4,0},{8,4},{12,8},{1,13},{5,1},{9,5},{13,9},{2,14},{6,2},{... | collective-permute-start | bytes 32 | tf_op jit(solution)/shard_map/ppermute | solution.py:84
  13.1 4.4 %collective-permute-start.2 = (s32[2]{0:T(128)S(1)}, s32[2]{0:T(128)S(1)}, u32[]{:S(2)}, u32[]{:S(2)}) collective-permute-start(s32[2]{0:T(128)S(1)} %get-tuple-element.16), channel_id=1, source_target_pairs={{0,8},{4,12},{8,0},{12,4},{1,9},{5,13},{9,1},{13,5},{2,10},{6,14},... | collective-permute-start | bytes 32 | tf_op jit(solution)/shard_map/ppermute | solution.py:84
  13.1 5.3 %collective-permute-start.1 = (s32[2]{0:T(128)S(1)}, s32[2]{0:T(128)S(1)}, u32[]{:S(2)}, u32[]{:S(2)}) collective-permute-start(s32[2]{0:T(128)S(1)} %get-tuple-element.17), channel_id=1, source_target_pairs={{0,4},{4,8},{8,12},{12,0},{1,5},{5,9},{9,13},{13,1},{2,6},{6,10},{... | collective-permute-start | bytes 32 | tf_op jit(solution)/shard_map/ppermute | solution.py:84
  18.5 4.2 %collective-permute-start.4 = (s32[4,2]{1,0:T(4,128)S(1)}, s32[4,2]{1,0:T(4,128)S(1)}, u32[]{:S(2)}, u32[]{:S(2)}) collective-permute-start(s32[4,2]{1,0:T(4,128)S(1)} %pad_add_fusion.3), channel_id=1, source_target_pairs={{0,1},{1,0},{2,3},{3,2},{4,5},{5,4},{6,7},{7,6},{8,9},{9,8},{10,11... | collective-permute-start | bytes 104 | tf_op jit(solution)/shard_map/ppermute | solution.py:78
  19.5 4.2 %collective-permute-start.5 = (bf16[2,65,128]{2,1,0:T(8,128)(2,1)S(1)}, bf16[2,65,128]{2,1,0:T(8,128)(2,1)S(1)}, u32[]{:S(2)}, u32[]{:S(2)}) collective-permute-start(bf16[2,65,128]{2,1,0:T(8,128)(2,1)S(1)} %get-tuple-element.3), channel_id=1, source_target_pairs={{0,12},{4,0},{8,4},{12,8},{1,13},{5,1},{9,5},{13,9},{2,14},{6,2},{... | collective-permute-start | bytes 99848 | tf_op jit(solution)/shard_map/ppermute | solution.py:91
  20.1 5.3 %collective-permute-start.6 = (bf16[2,65,128]{2,1,0:T(8,128)(2,1)S(1)}, bf16[2,65,128]{2,1,0:T(8,128)(2,1)S(1)}, u32[]{:S(2)}, u32[]{:S(2)}) collective-permute-start(bf16[2,65,128]{2,1,0:T(8,128)(2,1)S(1)} %get-tuple-element.4), channel_id=1, source_target_pairs={{0,8},{4,12},{8,0},{12,4},{1,9},{5,13},{9,1},{13,5},{2,10},{6,14},... | collective-permute-start | bytes 99848 | tf_op jit(solution)/shard_map/ppermute | solution.py:91
  20.9 5.8 %collective-permute-start.7 = (bf16[2,65,128]{2,1,0:T(8,128)(2,1)S(1)}, bf16[2,65,128]{2,1,0:T(8,128)(2,1)S(1)}, u32[]{:S(2)}, u32[]{:S(2)}) collective-permute-start(bf16[2,65,128]{2,1,0:T(8,128)(2,1)S(1)} %get-tuple-element.5), channel_id=1, source_target_pairs={{0,4},{4,8},{8,12},{12,0},{1,5},{5,9},{9,13},{13,1},{2,6},{6,10},{... | collective-permute-start | bytes 99848 | tf_op jit(solution)/shard_map/ppermute | solution.py:91
  26.6 1.4 %collective-permute-start.8 = (bf16[4,2,65,128]{3,2,1,0:T(8,128)(2,1)S(1)}, bf16[4,2,65,128]{3,2,1,0:T(8,128)(2,1)S(1)}, u32[]{:S(2)}, u32[]{:S(2)}) collective-permute-start(bf16[4,2,65,128]{3,2,1,0:T(8,128)(2,1)S(1)} %get-tuple-element.26), channel_id=1, source_target_pairs={{0,1},{1,0},{2,3},{3,2},{4,5},{5,4},{6,7},{7,6},{8,9},{9,8},{10,11... | collective-permute-start | bytes 399368 | tf_op jit(solution)/shard_map/ppermute | solution.py:78
  39.5 3.8 %collective-permute-start.11 = (f32[4,8,128]{2,1,0:T(8,128)S(1)}, f32[4,8,128]{2,1,0:T(8,128)S(1)}, u32[]{:S(2)}, u32[]{:S(2)}) collective-permute-start(f32[4,8,128]{2,1,0:T(8,128)S(1)} %get-tuple-element.36), channel_id=1, source_target_pairs={{0,12},{4,0},{8,4},{12,8},{1,13},{5,1},{9,5},{13,9},{2,14},{6,2},{... | collective-permute-start | bytes 49160 | tf_op jit(solution)/shard_map/ppermute | solution.py:84
  41.0 4.8 %collective-permute-start.10 = (f32[4,8,128]{2,1,0:T(8,128)S(1)}, f32[4,8,128]{2,1,0:T(8,128)S(1)}, u32[]{:S(2)}, u32[]{:S(2)}) collective-permute-start(f32[4,8,128]{2,1,0:T(8,128)S(1)} %get-tuple-element.37), channel_id=1, source_target_pairs={{0,8},{4,12},{8,0},{12,4},{1,9},{5,13},{9,1},{13,5},{2,10},{6,14},... | collective-permute-start | bytes 49160 | tf_op jit(solution)/shard_map/ppermute | solution.py:84
  41.2 5.5 %collective-permute-start.9 = (f32[4,8,128]{2,1,0:T(8,128)S(1)}, f32[4,8,128]{2,1,0:T(8,128)S(1)}, u32[]{:S(2)}, u32[]{:S(2)}) collective-permute-start(f32[4,8,128]{2,1,0:T(8,128)S(1)} %get-tuple-element.38), channel_id=1, source_target_pairs={{0,4},{4,8},{8,12},{12,0},{1,5},{5,9},{9,13},{13,1},{2,6},{6,10},{... | collective-permute-start | bytes 49160 | tf_op jit(solution)/shard_map/ppermute | solution.py:84
  47.5 3.8 %collective-permute-start.12 = (f32[4,8,128]{2,1,0:T(8,128)S(1)}, f32[4,8,128]{2,1,0:T(8,128)S(1)}, u32[]{:S(2)}, u32[]{:S(2)}) collective-permute-start(f32[4,8,128]{2,1,0:T(8,128)S(1)} %get-tuple-element.7), channel_id=1, source_target_pairs={{0,12},{4,0},{8,4},{12,8},{1,13},{5,1},{9,5},{13,9},{2,14},{6,2},{... | collective-permute-start | bytes 49160 | tf_op jit(solution)/shard_map/ppermute | solution.py:91
  48.5 4.6 %collective-permute-start.13 = (f32[4,8,128]{2,1,0:T(8,128)S(1)}, f32[4,8,128]{2,1,0:T(8,128)S(1)}, u32[]{:S(2)}, u32[]{:S(2)}) collective-permute-start(f32[4,8,128]{2,1,0:T(8,128)S(1)} %get-tuple-element.8), channel_id=1, source_target_pairs={{0,8},{4,12},{8,0},{12,4},{1,9},{5,13},{9,1},{13,5},{2,10},{6,14},... | collective-permute-start | bytes 49160 | tf_op jit(solution)/shard_map/ppermute | solution.py:91
  48.6 5.5 %collective-permute-start.14 = (f32[4,8,128]{2,1,0:T(8,128)S(1)}, f32[4,8,128]{2,1,0:T(8,128)S(1)}, u32[]{:S(2)}, u32[]{:S(2)}) collective-permute-start(f32[4,8,128]{2,1,0:T(8,128)S(1)} %get-tuple-element.9), channel_id=1, source_target_pairs={{0,4},{4,8},{8,12},{12,0},{1,5},{5,9},{9,13},{13,1},{2,6},{6,10},{... | collective-permute-start | bytes 49160 | tf_op jit(solution)/shard_map/ppermute | solution.py:91
  65.5 3.8 %collective-permute-start.18 = (f32[4,8,128]{2,1,0:T(8,128)S(1)}, f32[4,8,128]{2,1,0:T(8,128)S(1)}, u32[]{:S(2)}, u32[]{:S(2)}) collective-permute-start(f32[4,8,128]{2,1,0:T(8,128)S(1)} %get-tuple-element.30), channel_id=1, source_target_pairs={{0,12},{4,0},{8,4},{12,8},{1,13},{5,1},{9,5},{13,9},{2,14},{6,2},{... | collective-permute-start | bytes 49160 | tf_op jit(solution)/shard_map/ppermute | solution.py:84
  67.1 4.8 %collective-permute-start.17 = (f32[4,8,128]{2,1,0:T(8,128)S(1)}, f32[4,8,128]{2,1,0:T(8,128)S(1)}, u32[]{:S(2)}, u32[]{:S(2)}) collective-permute-start(f32[4,8,128]{2,1,0:T(8,128)S(1)} %get-tuple-element.31), channel_id=1, source_target_pairs={{0,8},{4,12},{8,0},{12,4},{1,9},{5,13},{9,1},{13,5},{2,10},{6,14},... | collective-permute-start | bytes 49160 | tf_op jit(solution)/shard_map/ppermute | solution.py:84
  67.1 5.5 %collective-permute-start.16 = (f32[4,8,128]{2,1,0:T(8,128)S(1)}, f32[4,8,128]{2,1,0:T(8,128)S(1)}, u32[]{:S(2)}, u32[]{:S(2)}) collective-permute-start(f32[4,8,128]{2,1,0:T(8,128)S(1)} %get-tuple-element.32), channel_id=1, source_target_pairs={{0,4},{4,8},{8,12},{12,0},{1,5},{5,9},{9,13},{13,1},{2,6},{6,10},{... | collective-permute-start | bytes 49160 | tf_op jit(solution)/shard_map/ppermute | solution.py:84
  68.6 4.6 %collective-permute-start.15 = (f32[8,8,128]{2,1,0:T(8,128)S(1)}, f32[8,8,128]{2,1,0:T(8,128)S(1)}, u32[]{:S(2)}, u32[]{:S(2)}) collective-permute-start(f32[8,8,128]{2,1,0:T(8,128)S(1)} %bitcast_subtract_fusion.3), channel_id=1, source_target_pairs={{0,1},{1,0},{2,3},{3,2},{4,5},{5,4},{6,7},{7,6},{8,9},{9,8},{10,11... | collective-permute-start | bytes 98312 | tf_op jit(solution)/shard_map/ppermute | solution.py:78
  73.2 1.3 %collective-permute-start.19 = (f32[8,8,128]{2,1,0:T(8,128)S(1)}, f32[8,8,128]{2,1,0:T(8,128)S(1)}, u32[]{:S(2)}, u32[]{:S(2)}) collective-permute-start(f32[8,8,128]{2,1,0:T(8,128)S(1)} %bitcast_subtract_fusion.1), channel_id=1, source_target_pairs={{0,1},{1,0},{2,3},{3,2},{4,5},{5,4},{6,7},{7,6},{8,9},{9,8},{10,11... | collective-permute-start | bytes 98312 | tf_op jit(solution)/shard_map/ppermute | solution.py:78

commit v7 on v6

--- a/solution.py
+++ b/solution.py
@@ -124,16 +124,17 @@
         ).reshape(half, blocks, BLOCK)
 
         peers = (my_blk + jnp.arange(peer_count, dtype=jnp.int32)) % peer_count
+        own_listed = lax.broadcasted_iota(jnp.int32, (peer_count, capacity), 1) < pair_count[:, None]
+        own_wanted = pick_lead(jnp.where(own_listed, pair_block, 0), peers)
+        requested = jnp.stack(send_up([own_wanted[offset] for offset in range(peer_count)]))
         lists = jnp.stack([pair_block, pair_row, jnp.broadcast_to(pair_count[:, None], pair_block.shape)])
         lists = jnp.stack([lists, swap(lists)], axis=1)
         listed = lax.broadcasted_iota(jnp.int32, lists.shape[1:], 2) < lists[2]
-        wanted = pick_lead(jnp.transpose(jnp.where(listed, lists[0], 0), (1, 0, 2)), peers)
         rows_used = pick_lead(jnp.transpose(jnp.where(listed, lists[1], 0), (1, 0, 2)), peers)
         usable = pick_lead(jnp.transpose(listed.astype(jnp.int32), (1, 0, 2)), peers)
         rows_used = rows_used.reshape(slot_count)
         usable = usable.reshape(slot_count)[:, None, None] > 0
 
-        requested = jnp.stack(send_up([wanted[offset, 0] for offset in range(peer_count)]))
         far = jnp.stack(
             send_down([pick_rows(own_synth, requested[offset], blocks) for offset in range(peer_count)])
         )
@@ -143,9 +144,8 @@
         far_tags = far[:, features]
         slot_x = pick_rows(own_real, rows_used, blocks)
         slot_tags = pick_rows(real_tags, rows_used, blocks)[:, 0]
-        cost = slot_costs(slot_x, slot_tags, far_y, far_tags)
-        cost_cols = cost / SMOOTH
-        cost_rows = jnp.transpose(cost_cols, (0, 2, 1))
+        cost_cols = slot_costs(slot_x, slot_tags, far_y, far_tags) / SMOOTH
+        cost_rows = slot_costs(far_y, far_tags, slot_x, slot_tags) / SMOOTH
 
         synth_pot = jnp.zeros((half, blocks, BLOCK), jnp.float32)
         real_pot = jnp.zeros((half, blocks, BLOCK), jnp.float32)

time: 75.5 us -> 72.7 us (0.963)
  waiting for transfers between devices: 19.1 us -> 13.4 us
  starting transfers between devices: 18.4 us -> 23.2 us
  local copies, waits for them, and re-layouts: 7.38 us -> 5.26 us
  matrix products: 0.36 us -> 2.37 us
  other arithmetic: 28.8 us -> 27 us
    ppermute x6, waiting for transfers between devices: 6.24 us -> 2.28 us  [send_down(): moved.append(lax.ppermute(chunks[offset], 'blk', perm))]
    ppermute x9, starting transfers between devices: 11.6 us -> 14.6 us  [send_up(): moved.append(lax.ppermute(chunks[offset], 'blk', perm))]
    ppermute x9, waiting for transfers between devices: 11 us -> 8.64 us  [send_up(): moved.append(lax.ppermute(chunks[offset], 'blk', perm))]
    reduce_max x4 -> x3, other arithmetic: 9.89 us -> 7.57 us  [lse_parts(): highest = jnp.max(scores, axis=axis)]
    dot_general x1 -> x2, matrix products: 0.36 us -> 2.37 us  [slot_costs(): jnp.einsum('gdi,gdj->gij', slot_real, slot_synth, preferred_element_type=...]
    div x2 -> x0, local copies, waits for them, and re-layouts: 1.88 us -> none  [shards(): cost_cols = cost / SMOOTH]
    ppermute x6, starting transfers between devices: 6.21 us -> 7.76 us  [send_down(): moved.append(lax.ppermute(chunks[offset], 'blk', perm))]
  transfers between devices with their start and end apart: 20 -> 20, of which waited for: 15 -> 10; matrix products, arithmetic and copies ran while one was open for 13% -> 16% of each run, Pallas kernels for 0% -> 0%
where the time goes in v7:
time: 72.7 us; the launch traced here: 72.3 us
  other arithmetic  27 us (37%)
  starting transfers between devices  23.2 us (32%)
  waiting for transfers between devices  13.4 us (18%)
  local copies, waits for them, and re-layouts  5.26 us (7%)
  matrix products  2.37 us (3%)
  between operations  1.15 us (2%)
    ppermute x9, starting transfers between devices, send_up(): moved.append(lax.ppermute(chunks[offset], 'blk', perm))  14.6 us
    ppermute x9, waiting for transfers between devices, send_up(): moved.append(lax.ppermute(chunks[offset], 'blk', perm))  8.64 us
    reduce_sum x4, other arithmetic, lse_parts(): jnp.sum(jnp.exp(scores - jnp.expand_dims(highest, axis)), axis=axis)  8.13 us
    ppermute x6, starting transfers between devices, send_down(): moved.append(lax.ppermute(chunks[offset], 'blk', perm))  7.76 us
    reduce_max x3, other arithmetic, lse_parts(): highest = jnp.max(scores, axis=axis)  7.57 us
    reduce_sum x10, other arithmetic, pick_rows(): return jnp.sum(chosen, axis=2, dtype=values.dtype)  3.73 us
    unnamed x5, local copies, waits for them, and re-layouts  3.14 us
    ppermute x5, waiting for transfers between devices, swap(): return lax.ppermute(value, 'sub', [(0, 1), (1, 0)])  2.43 us
  transfers between devices with their start and end apart: 20, of which 10 were waited for; matrix products, arithmetic and copies ran while one was open for 16% of the time, Pallas kernels for 0%

profile of v7, /device:TPU:0, one launch (start us, length us, event | category | flops | bytes accessed | tf_op | source)
XLA Modules:
  0.0 72.3 jit_solution(13222955600076643301)
XLA Ops:
  0.6 0.7 stack_broadcast_in_dim.2
  1.3 0.7 fusion.25
  2.0 0.5 collective-permute-start
  2.4 0.7 compare_select_fusion.2
  3.2 0.1 select_reduce_fusion.26
  3.4 0.2 slice_reduce_fusion.3
  3.6 2.6 %collective-permute-start.1 = (s32[2]{0:T(128)S(1)}, s32[2]{0:T(128)S(1)}, u32[]{:S(2)}, u32[]{:S(2)}) collective-permute-start(s32[2]{0:T(128)S(1)} %get-tuple-element.17), channel_id=1, source_target_pairs={{0,4},{4,8},{8,12},{12,0},{1,5},{5,9},{9,13},{13,1},{2,6},{6,10},{... | collective-permute-start | bytes 32 | tf_op jit(solution)/shard_map/ppermute | solution.py:84
  6.2 2.6 %collective-permute-start.2 = (s32[2]{0:T(128)S(1)}, s32[2]{0:T(128)S(1)}, u32[]{:S(2)}, u32[]{:S(2)}) collective-permute-start(s32[2]{0:T(128)S(1)} %get-tuple-element.16), channel_id=1, source_target_pairs={{0,8},{4,12},{8,0},{12,4},{1,9},{5,13},{9,1},{13,5},{2,10},{6,14},... | collective-permute-start | bytes 32 | tf_op jit(solution)/shard_map/ppermute | solution.py:84
  8.8 1.3 %collective-permute-start.3 = (s32[2]{0:T(128)S(1)}, s32[2]{0:T(128)S(1)}, u32[]{:S(2)}, u32[]{:S(2)}) collective-permute-start(s32[2]{0:T(128)S(1)} %get-tuple-element.15), channel_id=1, source_target_pairs={{0,12},{4,0},{8,4},{12,8},{1,13},{5,1},{9,5},{13,9},{2,14},{6,2},{... | collective-permute-start | bytes 32 | tf_op jit(solution)/shard_map/ppermute | solution.py:84
  10.1 0.7 convert_bitcast_fusion.1
  10.9 0.7 convert_bitcast_fusion.2
  11.6 0.9 %copy.50 = bf16[8,8,8,128]{3,2,1,0:T(8,128)(2,1)S(1)} copy(bf16[8,8,8,128]{3,1,2,0:T(8,128)(2,1)} %bitcast.81) | data formatting | bytes 262144
  12.5 0.9 %copy.51 = bf16[8,8,8,128]{3,2,1,0:T(8,128)(2,1)S(1)} copy(bf16[8,8,8,128]{3,1,2,0:T(8,128)(2,1)} %bitcast.82) | data formatting | bytes 262144
  13.5 0.8 %multiply_bitcast_fusion.1 = f32[1,8,8,128]{3,1,2,0:T(8,128)S(1)} fusion(s32[16,1024]{1,0:T(8,128)} %param.13, s32[]{:T(128)S(6)} %select_n.256), kind=kLoop, calls=%fused_computation.71 | loop fusion | flops 24576 | bytes 65540
  14.2 0.8 %multiply_bitcast_fusion = f32[1,8,8,128]{3,1,2,0:T(8,128)S(1)} fusion(s32[16,1024]{1,0:T(8,128)} %param.14, s32[]{:T(128)S(6)} %select_n.256), kind=kLoop, calls=%fused_computation.70 | loop fusion | flops 24576 | bytes 65540
  15.7 0.8 %select_reduce_fusion.15 = (bf16[2,65,128]{2,1,0:T(8,128)(2,1)S(1)}, bf16[2,65,128]{2,1,0:T(8,128)(2,1)S(1)}, bf16[2,65,128]{2,1,0:T(8,128)(2,1)S(1)}, bf16[2,65,128]{2,1,0:T(8,128)(2,1)S(1)}) fusion(pred[2,8]{1,0:T(4,128)(4,1)S(1)} %iota_compare_fusion.10, bf16[65,8,128]{2,1,0:T(8,128)(2,1)S(1)} %maximum_bitcast_fusion, ...), kind=kLoop, calls=%fused_computation.38 | loop fusion | flops 998400 | bytes 266304 | tf_op jit(solution)/shard_map/reduce_sum | solution.py:26
  16.5 0.7 %collective-permute-start.7 = (bf16[2,65,128]{2,1,0:T(8,128)(2,1)S(1)}, bf16[2,65,128]{2,1,0:T(8,128)(2,1)S(1)}, u32[]{:S(2)}, u32[]{:S(2)}) collective-permute-start(bf16[2,65,128]{2,1,0:T(8,128)(2,1)S(1)} %get-tuple-element.5), channel_id=1, source_target_pairs={{0,4},{4,8},{8,12},{12,0},{1,5},{5,9},{9,13},{13,1},{2,6},{6,10},{... | collective-permute-start | bytes 99848 | tf_op jit(solution)/shard_map/ppermute | solution.py:91
  17.2 0.3 collective-permute-start.6
  17.6 2.8 %collective-permute-start.5 = (bf16[2,65,128]{2,1,0:T(8,128)(2,1)S(1)}, bf16[2,65,128]{2,1,0:T(8,128)(2,1)S(1)}, u32[]{:S(2)}, u32[]{:S(2)}) collective-permute-start(bf16[2,65,128]{2,1,0:T(8,128)(2,1)S(1)} %get-tuple-element.3), channel_id=1, source_target_pairs={{0,12},{4,0},{8,4},{12,8},{1,13},{5,1},{9,5},{13,9},{2,14},{6,2},{... | collective-permute-start | bytes 99848 | tf_op jit(solution)/shard_map/ppermute | solution.py:91
  20.4 1.1 %collective-permute-done.4 = s32[4,2]{0,1:T(2,128)S(1)} collective-permute-done((s32[4,2]{0,1:T(2,128)S(1)}, s32[4,2]{0,1:T(2,128)S(1)}, u32[]{:S(2)}, u32[]{:S(2)}) %collective-permute-start.4) | collective-permute-done | bytes 64 | tf_op jit(solution)/shard_map/ppermute | solution.py:78
  21.5 0.3 fusion.13
  22.5 0.2 select_reduce_fusion.24
  23.0 1.4 %select_reduce_fusion = bf16[16,64,128]{2,1,0:T(8,128)(2,1)S(1)} fusion(pred[16,8]{1,0:T(8,128)(4,1)S(1)} %iota_compare_fusion.1, bf16[64,8,128]{2,1,0:T(8,128)(2,1)S(1)} %bitcast.75), kind=kLoop, calls=%fused_computation.12 | loop fusion | flops 1966080 | bytes 393344 | tf_op jit(solution)/shard_map/reduce_sum | solution.py:26
  24.5 0.3 collective-permute-start.8
  24.8 0.1 copy.41
  25.1 0.8 %collective-permute-done.8 = bf16[4,2,65,128]{3,2,1,0:T(8,128)(2,1)S(1)} collective-permute-done((bf16[4,2,65,128]{3,2,1,0:T(8,128)(2,1)S(1)}, bf16[4,2,65,128]{3,2,1,0:T(8,128)(2,1)S(1)}, u32[]{:S(2)}, u32[]{:S(2)}) %collective-permute-start.8) | collective-permute-done | bytes 133152 | tf_op jit(solution)/shard_map/ppermute | solution.py:78
  26.1 1.2 %subtract_reduce_fusion.3 = (f32[16,128]{1,0:T(8,128)S(1)}, f32[16,128,128]{2,1,0:T(8,128)S(1)}) fusion(bf16[16,128]{1,0:T(8,128)(2,1)S(1)} %select_reduce_fusion.23, bf16[16,128]{1,0:T(8,128)(2,1)S(1)} %bitcast.90, bf16[16,64,128]{2,1,0:T(8,128)(2,1)S(1)} %select_reduce_fusion, bf16[16,65,128]{2,1,0:T(8,128)(2,1)S(1)} %bitcast.73, ...), kind=kOutput, calls=%fused_computation.20 | convolution fusion | flops 35649536 | bytes 1605632 | tf_op jit(solution)/shard_map/gdi,gdj->gij/dot_general | solution.py:61
  27.3 1.1 %fusion.9 = f32[16,128,128]{2,1,0:T(8,128)S(1)} fusion(bf16[16,64,128]{2,1,0:T(8,128)(2,1)S(1)} %select_reduce_fusion, f32[16,128]{1,0:T(8,128)S(1)} %get-tuple-element.40, f32[16,128]{1,0:T(8,128)S(1)} %get-tuple-element.39, bf16[16,128]{1,0:T(8,128)(2,1)S(1)} %bitcast.91, bf16[16,128]{1,0:T(8,128)(2,1)S(1)} %select_reduce_fusion.23, ...), kind=kOutput, calls=%fused_computation.18 | convolution fusion | flops 35127296 | bytes 1597440 | tf_op jit(solution)/shard_map/gdi,gdj->gij/dot_general | solution.py:61
  28.8 0.2 exponential_reduce_fusion
  29.2 0.2 select_reduce_fusion.11
  29.4 2.5 %subtract_reduce_fusion.2 = f32[16,8,128]{2,1,0:T(8,128)S(1)} fusion(f32[16,128,128]{2,1,0:T(8,128)S(1)} %fusion.9, f32[16,8,128]{2,1,0:T(8,128)S(1)} %broadcast_multiply_fusion.1), kind=kLoop, calls=%fused_computation.5 | loop fusion | flops 4177920 | bytes 1179648 | tf_op jit(solution)/shard_map/reduce_max | solution.py:71
  32.0 2.6 %fusion.1 = f32[16,8,128]{2,1,0:T(8,128)S(1)} fusion(f32[16,8,128]{2,1,0:T(8,128)S(1)} %subtract_reduce_fusion.2, f32[16,128,128]{2,1,0:T(8,128)S(1)} %fusion.9, f32[16,8,128]{2,1,0:T(8,128)S(1)} %broadcast_multiply_fusion.1), kind=kLoop, calls=%fused_computation.7 | loop fusion | flops 6275072 | bytes 1245184 | tf_op jit(solution)/shard_map/reduce_sum | solution.py:72
  34.7 1.7 %collective-permute-start.11 = (f32[4,8,128]{2,1,0:T(8,128)S(1)}, f32[4,8,128]{2,1,0:T(8,128)S(1)}, u32[]{:S(2)}, u32[]{:S(2)}) collective-permute-start(f32[4,8,128]{2,1,0:T(8,128)S(1)} %get-tuple-element.31), channel_id=1, source_target_pairs={{0,12},{4,0},{8,4},{12,8},{1,13},{5,1},{9,5},{13,9},{2,14},{6,2},{... | collective-permute-start | bytes 49160 | tf_op jit(solution)/shard_map/ppermute | solution.py:84
  36.4 0.4 collective-permute-start.10
  36.9 1.9 %collective-permute-start.9 = (f32[4,8,128]{2,1,0:T(8,128)S(1)}, f32[4,8,128]{2,1,0:T(8,128)S(1)}, u32[]{:S(2)}, u32[]{:S(2)}) collective-permute-start(f32[4,8,128]{2,1,0:T(8,128)S(1)} %get-tuple-element.33), channel_id=1, source_target_pairs={{0,4},{4,8},{8,12},{12,0},{1,5},{5,9},{9,13},{13,1},{2,6},{6,10},{... | collective-permute-start | bytes 49160 | tf_op jit(solution)/shard_map/ppermute | solution.py:84
  38.9 2.2 %collective-permute-done.10 = f32[4,8,128]{2,1,0:T(8,128)S(1)} collective-permute-done((f32[4,8,128]{2,1,0:T(8,128)S(1)}, f32[4,8,128]{2,1,0:T(8,128)S(1)}, u32[]{:S(2)}, u32[]{:S(2)}) %collective-permute-start.10) | collective-permute-done | bytes 16416 | tf_op jit(solution)/shard_map/ppermute | solution.py:84
  41.1 1.3 %collective-permute-done.9 = f32[4,8,128]{2,1,0:T(8,128)S(1)} collective-permute-done((f32[4,8,128]{2,1,0:T(8,128)S(1)}, f32[4,8,128]{2,1,0:T(8,128)S(1)}, u32[]{:S(2)}, u32[]{:S(2)}) %collective-permute-start.9) | collective-permute-done | bytes 16416 | tf_op jit(solution)/shard_map/ppermute | solution.py:84
  42.4 0.1 select_reduce_fusion.10
  42.5 0.2 select_reduce_fusion.9
  42.8 0.1 select_reduce_fusion.8
  42.9 0.2 select_reduce_fusion.19
  43.2 0.2 collective-permute-start.14
  43.4 1.1 %collective-permute-start.13 = (f32[4,8,128]{2,1,0:T(8,128)S(1)}, f32[4,8,128]{2,1,0:T(8,128)S(1)}, u32[]{:S(2)}, u32[]{:S(2)}) collective-permute-start(f32[4,8,128]{2,1,0:T(8,128)S(1)} %get-tuple-element.8), channel_id=1, source_target_pairs={{0,8},{4,12},{8,0},{12,4},{1,9},{5,13},{9,1},{13,5},{2,10},{6,14},... | collective-permute-start | bytes 49160 | tf_op jit(solution)/shard_map/ppermute | solution.py:91
  44.4 2.6 %collective-permute-start.12 = (f32[4,8,128]{2,1,0:T(8,128)S(1)}, f32[4,8,128]{2,1,0:T(8,128)S(1)}, u32[]{:S(2)}, u32[]{:S(2)}) collective-permute-start(f32[4,8,128]{2,1,0:T(8,128)S(1)} %get-tuple-element.7), channel_id=1, source_target_pairs={{0,12},{4,0},{8,4},{12,8},{1,13},{5,1},{9,5},{13,9},{2,14},{6,2},{... | collective-permute-start | bytes 49160 | tf_op jit(solution)/shard_map/ppermute | solution.py:91
  47.0 1.7 %collective-permute-done.14 = f32[4,8,128]{2,1,0:T(8,128)S(1)} collective-permute-done((f32[4,8,128]{2,1,0:T(8,128)S(1)}, f32[4,8,128]{2,1,0:T(8,128)S(1)}, u32[]{:S(2)}, u32[]{:S(2)}) %collective-permute-start.14) | collective-permute-done | bytes 16416 | tf_op jit(solution)/shard_map/ppermute | solution.py:91
  48.7 0.6 collective-permute-done.12
  49.3 2.5 %subtract_reduce_fusion.1 = f32[16,8,128]{2,1,0:T(8,128)S(1)} fusion(f32[16,128,128]{2,1,0:T(8,128)S(1)} %get-tuple-element.38, f32[16,8,128]{2,1,0:T(8,128)S(1)} %maximum_multiply_fusion), kind=kLoop, calls=%fused_computation.3 | loop fusion | flops 4177920 | bytes 1179648 | tf_op jit(solution)/shard_map/reduce_max | solution.py:71
  51.9 2.6 %fusion.3 = f32[16,8,128]{2,1,0:T(8,128)S(1)} fusion(f32[16,8,128]{2,1,0:T(8,128)S(1)} %subtract_reduce_fusion.1, f32[16,128,128]{2,1,0:T(8,128)S(1)} %get-tuple-element.38, f32[16,8,128]{2,1,0:T(8,128)S(1)} %maximum_multiply_fusion), kind=kLoop, calls=%fused_computation.9 | loop fusion | flops 6275072 | bytes 1245184 | tf_op jit(solution)/shard_map/reduce_sum | solution.py:72
  54.6 0.1 select_reduce_fusion.7
  54.7 0.2 select_reduce_fusion.6
  55.2 0.2 select_reduce_fusion.4
  55.4 2.5 %subtract_reduce_fusion = f32[16,8,128]{2,1,0:T(8,128)S(1)} fusion(f32[16,8,128]{2,1,0:T(8,128)S(1)} %broadcast_multiply_fusion, f32[16,128,128]{2,1,0:T(8,128)S(1)} %fusion.9), kind=kLoop, calls=%fused_computation.1 | loop fusion | flops 4177920 | bytes 1179648 | tf_op jit(solution)/shard_map/reduce_max | solution.py:71
  58.0 2.6 %fusion.5 = f32[16,8,128]{2,1,0:T(8,128)S(1)} fusion(f32[16,8,128]{2,1,0:T(8,128)S(1)} %subtract_reduce_fusion, f32[16,8,128]{2,1,0:T(8,128)S(1)} %broadcast_multiply_fusion, f32[16,128,128]{2,1,0:T(8,128)S(1)} %fusion.9), kind=kLoop, calls=%fused_computation.11 | loop fusion | flops 6275072 | bytes 1245184 | tf_op jit(solution)/shard_map/reduce_sum | solution.py:72
  60.7 3.3 %collective-permute-start.18 = (f32[4,8,128]{2,1,0:T(8,128)S(1)}, f32[4,8,128]{2,1,0:T(8,128)S(1)}, u32[]{:S(2)}, u32[]{:S(2)}) collective-permute-start(f32[4,8,128]{2,1,0:T(8,128)S(1)} %get-tuple-element.25), channel_id=1, source_target_pairs={{0,12},{4,0},{8,4},{12,8},{1,13},{5,1},{9,5},{13,9},{2,14},{6,2},{... | collective-permute-start | bytes 49160 | tf_op jit(solution)/shard_map/ppermute | solution.py:84
  64.0 0.2 collective-permute-start.17
  64.3 0.4 collective-permute-start.16
  64.7 0.8 %collective-permute-done.18 = f32[4,8,128]{2,1,0:T(8,128)S(1)} collective-permute-done((f32[4,8,128]{2,1,0:T(8,128)S(1)}, f32[4,8,128]{2,1,0:T(8,128)S(1)}, u32[]{:S(2)}, u32[]{:S(2)}) %collective-permute-start.18) | collective-permute-done | bytes 16416 | tf_op jit(solution)/shard_map/ppermute | solution.py:84
  65.5 3.2 %collective-permute-done.17 = f32[4,8,128]{2,1,0:T(8,128)S(1)} collective-permute-done((f32[4,8,128]{2,1,0:T(8,128)S(1)}, f32[4,8,128]{2,1,0:T(8,128)S(1)}, u32[]{:S(2)}, u32[]{:S(2)}) %collective-permute-start.17) | collective-permute-done | bytes 16416 | tf_op jit(solution)/shard_map/ppermute | solution.py:84
  68.7 1.1 %collective-permute-done.16 = f32[4,8,128]{2,1,0:T(8,128)S(1)} collective-permute-done((f32[4,8,128]{2,1,0:T(8,128)S(1)}, f32[4,8,128]{2,1,0:T(8,128)S(1)}, u32[]{:S(2)}, u32[]{:S(2)}) %collective-permute-start.16) | collective-permute-done | bytes 16416 | tf_op jit(solution)/shard_map/ppermute | solution.py:84
  69.8 0.1 select_reduce_fusion.3
  69.9 0.2 select_reduce_fusion.2
  70.4 0.6 copy.62
  71.1 0.5 collective-permute-done.19
  71.6 0.6 copy.61
  (80 shorter events, 3.6 us)
Async XLA Ops:
  2.0 20.4 %collective-permute-start = (s32[3,4,2]{1,2,0:T(2,128)S(1)}, s32[3,4,2]{1,2,0:T(2,128)S(1)}, u32[]{:S(2)}, u32[]{:S(2)}) collective-permute-start(s32[3,4,2]{1,2,0:T(2,128)S(1)} %get-tuple-element.35), channel_id=1, source_target_pairs={{0,1},{1,0},{2,3},{3,2},{4,5},{5,4},{6,7},{7,6},{8,9},{9,8},{10,11... | collective-permute-start | bytes 296 | tf_op jit(solution)/shard_map/ppermute | solution.py:78
  3.6 11.7 %collective-permute-start.1 = (s32[2]{0:T(128)S(1)}, s32[2]{0:T(128)S(1)}, u32[]{:S(2)}, u32[]{:S(2)}) collective-permute-start(s32[2]{0:T(128)S(1)} %get-tuple-element.17), channel_id=1, source_target_pairs={{0,4},{4,8},{8,12},{12,0},{1,5},{5,9},{9,13},{13,1},{2,6},{6,10},{... | collective-permute-start | bytes 32 | tf_op jit(solution)/shard_map/ppermute | solution.py:84
  6.2 8.9 %collective-permute-start.2 = (s32[2]{0:T(128)S(1)}, s32[2]{0:T(128)S(1)}, u32[]{:S(2)}, u32[]{:S(2)}) collective-permute-start(s32[2]{0:T(128)S(1)} %get-tuple-element.16), channel_id=1, source_target_pairs={{0,8},{4,12},{8,0},{12,4},{1,9},{5,13},{9,1},{13,5},{2,10},{6,14},... | collective-permute-start | bytes 32 | tf_op jit(solution)/shard_map/ppermute | solution.py:84
  8.8 6.2 %collective-permute-start.3 = (s32[2]{0:T(128)S(1)}, s32[2]{0:T(128)S(1)}, u32[]{:S(2)}, u32[]{:S(2)}) collective-permute-start(s32[2]{0:T(128)S(1)} %get-tuple-element.15), channel_id=1, source_target_pairs={{0,12},{4,0},{8,4},{12,8},{1,13},{5,1},{9,5},{13,9},{2,14},{6,2},{... | collective-permute-start | bytes 32 | tf_op jit(solution)/shard_map/ppermute | solution.py:84
  16.5 7.9 %collective-permute-start.7 = (bf16[2,65,128]{2,1,0:T(8,128)(2,1)S(1)}, bf16[2,65,128]{2,1,0:T(8,128)(2,1)S(1)}, u32[]{:S(2)}, u32[]{:S(2)}) collective-permute-start(bf16[2,65,128]{2,1,0:T(8,128)(2,1)S(1)} %get-tuple-element.5), channel_id=1, source_target_pairs={{0,4},{4,8},{8,12},{12,0},{1,5},{5,9},{9,13},{13,1},{2,6},{6,10},{... | collective-permute-start | bytes 99848 | tf_op jit(solution)/shard_map/ppermute | solution.py:91
  17.2 7.2 %collective-permute-start.6 = (bf16[2,65,128]{2,1,0:T(8,128)(2,1)S(1)}, bf16[2,65,128]{2,1,0:T(8,128)(2,1)S(1)}, u32[]{:S(2)}, u32[]{:S(2)}) collective-permute-start(bf16[2,65,128]{2,1,0:T(8,128)(2,1)S(1)} %get-tuple-element.4), channel_id=1, source_target_pairs={{0,8},{4,12},{8,0},{12,4},{1,9},{5,13},{9,1},{13,5},{2,10},{6,14},... | collective-permute-start | bytes 99848 | tf_op jit(solution)/shard_map/ppermute | solution.py:91
  17.6 6.9 %collective-permute-start.5 = (bf16[2,65,128]{2,1,0:T(8,128)(2,1)S(1)}, bf16[2,65,128]{2,1,0:T(8,128)(2,1)S(1)}, u32[]{:S(2)}, u32[]{:S(2)}) collective-permute-start(bf16[2,65,128]{2,1,0:T(8,128)(2,1)S(1)} %get-tuple-element.3), channel_id=1, source_target_pairs={{0,12},{4,0},{8,4},{12,8},{1,13},{5,1},{9,5},{13,9},{2,14},{6,2},{... | collective-permute-start | bytes 99848 | tf_op jit(solution)/shard_map/ppermute | solution.py:91
  20.4 1.1 %collective-permute-start.4 = (s32[4,2]{0,1:T(2,128)S(1)}, s32[4,2]{0,1:T(2,128)S(1)}, u32[]{:S(2)}, u32[]{:S(2)}) collective-permute-start(s32[4,2]{0,1:T(2,128)S(1)} %pad_add_fusion.3), channel_id=1, source_target_pairs={{0,1},{1,0},{2,3},{3,2},{4,5},{5,4},{6,7},{7,6},{8,9},{9,8},{10,11... | collective-permute-start | bytes 104 | tf_op jit(solution)/shard_map/ppermute | solution.py:78
  24.5 1.4 %collective-permute-start.8 = (bf16[4,2,65,128]{3,2,1,0:T(8,128)(2,1)S(1)}, bf16[4,2,65,128]{3,2,1,0:T(8,128)(2,1)S(1)}, u32[]{:S(2)}, u32[]{:S(2)}) collective-permute-start(bf16[4,2,65,128]{3,2,1,0:T(8,128)(2,1)S(1)} %get-tuple-element.21), channel_id=1, source_target_pairs={{0,1},{1,0},{2,3},{3,2},{4,5},{5,4},{6,7},{7,6},{8,9},{9,8},{10,11... | collective-permute-start | bytes 399368 | tf_op jit(solution)/shard_map/ppermute | solution.py:78
  34.7 4.2 %collective-permute-start.11 = (f32[4,8,128]{2,1,0:T(8,128)S(1)}, f32[4,8,128]{2,1,0:T(8,128)S(1)}, u32[]{:S(2)}, u32[]{:S(2)}) collective-permute-start(f32[4,8,128]{2,1,0:T(8,128)S(1)} %get-tuple-element.31), channel_id=1, source_target_pairs={{0,12},{4,0},{8,4},{12,8},{1,13},{5,1},{9,5},{13,9},{2,14},{6,2},{... | collective-permute-start | bytes 49160 | tf_op jit(solution)/shard_map/ppermute | solution.py:84
  36.4 4.6 %collective-permute-start.10 = (f32[4,8,128]{2,1,0:T(8,128)S(1)}, f32[4,8,128]{2,1,0:T(8,128)S(1)}, u32[]{:S(2)}, u32[]{:S(2)}) collective-permute-start(f32[4,8,128]{2,1,0:T(8,128)S(1)} %get-tuple-element.32), channel_id=1, source_target_pairs={{0,8},{4,12},{8,0},{12,4},{1,9},{5,13},{9,1},{13,5},{2,10},{6,14},... | collective-permute-start | bytes 49160 | tf_op jit(solution)/shard_map/ppermute | solution.py:84
  36.9 5.5 %collective-permute-start.9 = (f32[4,8,128]{2,1,0:T(8,128)S(1)}, f32[4,8,128]{2,1,0:T(8,128)S(1)}, u32[]{:S(2)}, u32[]{:S(2)}) collective-permute-start(f32[4,8,128]{2,1,0:T(8,128)S(1)} %get-tuple-element.33), channel_id=1, source_target_pairs={{0,4},{4,8},{8,12},{12,0},{1,5},{5,9},{9,13},{13,1},{2,6},{6,10},{... | collective-permute-start | bytes 49160 | tf_op jit(solution)/shard_map/ppermute | solution.py:84
  43.2 5.6 %collective-permute-start.14 = (f32[4,8,128]{2,1,0:T(8,128)S(1)}, f32[4,8,128]{2,1,0:T(8,128)S(1)}, u32[]{:S(2)}, u32[]{:S(2)}) collective-permute-start(f32[4,8,128]{2,1,0:T(8,128)S(1)} %get-tuple-element.9), channel_id=1, source_target_pairs={{0,4},{4,8},{8,12},{12,0},{1,5},{5,9},{9,13},{13,1},{2,6},{6,10},{... | collective-permute-start | bytes 49160 | tf_op jit(solution)/shard_map/ppermute | solution.py:91
  43.4 5.4 %collective-permute-start.13 = (f32[4,8,128]{2,1,0:T(8,128)S(1)}, f32[4,8,128]{2,1,0:T(8,128)S(1)}, u32[]{:S(2)}, u32[]{:S(2)}) collective-permute-start(f32[4,8,128]{2,1,0:T(8,128)S(1)} %get-tuple-element.8), channel_id=1, source_target_pairs={{0,8},{4,12},{8,0},{12,4},{1,9},{5,13},{9,1},{13,5},{2,10},{6,14},... | collective-permute-start | bytes 49160 | tf_op jit(solution)/shard_map/ppermute | solution.py:91
  44.4 4.9 %collective-permute-start.12 = (f32[4,8,128]{2,1,0:T(8,128)S(1)}, f32[4,8,128]{2,1,0:T(8,128)S(1)}, u32[]{:S(2)}, u32[]{:S(2)}) collective-permute-start(f32[4,8,128]{2,1,0:T(8,128)S(1)} %get-tuple-element.7), channel_id=1, source_target_pairs={{0,12},{4,0},{8,4},{12,8},{1,13},{5,1},{9,5},{13,9},{2,14},{6,2},{... | collective-permute-start | bytes 49160 | tf_op jit(solution)/shard_map/ppermute | solution.py:91
  60.7 4.8 %collective-permute-start.18 = (f32[4,8,128]{2,1,0:T(8,128)S(1)}, f32[4,8,128]{2,1,0:T(8,128)S(1)}, u32[]{:S(2)}, u32[]{:S(2)}) collective-permute-start(f32[4,8,128]{2,1,0:T(8,128)S(1)} %get-tuple-element.25), channel_id=1, source_target_pairs={{0,12},{4,0},{8,4},{12,8},{1,13},{5,1},{9,5},{13,9},{2,14},{6,2},{... | collective-permute-start | bytes 49160 | tf_op jit(solution)/shard_map/ppermute | solution.py:84
  64.0 4.6 %collective-permute-start.17 = (f32[4,8,128]{2,1,0:T(8,128)S(1)}, f32[4,8,128]{2,1,0:T(8,128)S(1)}, u32[]{:S(2)}, u32[]{:S(2)}) collective-permute-start(f32[4,8,128]{2,1,0:T(8,128)S(1)} %get-tuple-element.26), channel_id=1, source_target_pairs={{0,8},{4,12},{8,0},{12,4},{1,9},{5,13},{9,1},{13,5},{2,10},{6,14},... | collective-permute-start | bytes 49160 | tf_op jit(solution)/shard_map/ppermute | solution.py:84
  64.3 5.5 %collective-permute-start.16 = (f32[4,8,128]{2,1,0:T(8,128)S(1)}, f32[4,8,128]{2,1,0:T(8,128)S(1)}, u32[]{:S(2)}, u32[]{:S(2)}) collective-permute-start(f32[4,8,128]{2,1,0:T(8,128)S(1)} %get-tuple-element.27), channel_id=1, source_target_pairs={{0,4},{4,8},{8,12},{12,0},{1,5},{5,9},{9,13},{13,1},{2,6},{6,10},{... | collective-permute-start | bytes 49160 | tf_op jit(solution)/shard_map/ppermute | solution.py:84
  64.7 5.7 %collective-permute-start.15 = (f32[8,8,128]{2,1,0:T(8,128)S(1)}, f32[8,8,128]{2,1,0:T(8,128)S(1)}, u32[]{:S(2)}, u32[]{:S(2)}) collective-permute-start(f32[8,8,128]{2,1,0:T(8,128)S(1)} %bitcast_subtract_fusion.2), channel_id=1, source_target_pairs={{0,1},{1,0},{2,3},{3,2},{4,5},{5,4},{6,7},{7,6},{8,9},{9,8},{10,11... | collective-permute-start | bytes 98312 | tf_op jit(solution)/shard_map/ppermute | solution.py:78
  70.3 1.3 %collective-permute-start.19 = (f32[8,8,128]{2,1,0:T(8,128)S(1)}, f32[8,8,128]{2,1,0:T(8,128)S(1)}, u32[]{:S(2)}, u32[]{:S(2)}) collective-permute-start(f32[8,8,128]{2,1,0:T(8,128)S(1)} %bitcast_subtract_fusion), channel_id=1, source_target_pairs={{0,1},{1,0},{2,3},{3,2},{4,5},{5,4},{6,7},{7,6},{8,9},{9,8},{10,11... | collective-permute-start | bytes 98312 | tf_op jit(solution)/shard_map/ppermute | solution.py:78

commit v8 on v7

--- a/solution.py
+++ b/solution.py
@@ -124,22 +124,19 @@
         ).reshape(half, blocks, BLOCK)
 
         peers = (my_blk + jnp.arange(peer_count, dtype=jnp.int32)) % peer_count
-        own_listed = lax.broadcasted_iota(jnp.int32, (peer_count, capacity), 1) < pair_count[:, None]
-        own_wanted = pick_lead(jnp.where(own_listed, pair_block, 0), peers)
-        requested = jnp.stack(send_up([own_wanted[offset] for offset in range(peer_count)]))
+        everything = send_down([own_synth] * peer_count)
         lists = jnp.stack([pair_block, pair_row, jnp.broadcast_to(pair_count[:, None], pair_block.shape)])
         lists = jnp.stack([lists, swap(lists)], axis=1)
         listed = lax.broadcasted_iota(jnp.int32, lists.shape[1:], 2) < lists[2]
+        wanted = pick_lead(jnp.transpose(jnp.where(listed, lists[0], 0), (1, 0, 2)), peers)
         rows_used = pick_lead(jnp.transpose(jnp.where(listed, lists[1], 0), (1, 0, 2)), peers)
         usable = pick_lead(jnp.transpose(listed.astype(jnp.int32), (1, 0, 2)), peers)
+        wanted = wanted.reshape(peer_count, wide)
         rows_used = rows_used.reshape(slot_count)
         usable = usable.reshape(slot_count)[:, None, None] > 0
-
-        far = jnp.stack(
-            send_down([pick_rows(own_synth, requested[offset], blocks) for offset in range(peer_count)])
+        far = jnp.concatenate(
+            [pick_rows(everything[offset], wanted[offset], blocks) for offset in range(peer_count)], axis=0
         )
-        requested = jnp.stack([requested, swap(requested)], axis=1).reshape(slot_count)
-        far = jnp.stack([far, swap(far)], axis=1).reshape(slot_count, features + 1, BLOCK)
         far_y = far[:, :features]
         far_tags = far[:, features]
         slot_x = pick_rows(own_real, rows_used, blocks)
@@ -173,10 +170,16 @@
             scores = (own_rows / SMOOTH)[:, :, :, None] - cost_cols[:, None]
             highest, mass_sum = lse_parts(scores, 2)
             lse = jnp.where(usable, highest + jnp.log(mass_sum), SENTINEL)
+            if sweep_index == 0:
+                block_ids = jnp.broadcast_to(wanted.reshape(slot_count, 1, 1).astype(jnp.float32), (slot_count, 1, BLOCK))
+                lse = jnp.concatenate([lse, block_ids], axis=1)
             back = jnp.concatenate(
                 send_up([lse[offset * wide : (offset + 1) * wide] for offset in range(peer_count)]),
                 axis=0,
             )
+            if sweep_index == 0:
+                requested = back[:, half, 0].astype(jnp.int32)
+                back = back[:, :half]
             block_top, summed = fold_lse(back, requested, blocks)
             synth_pot = finish(log_synth, block_top, summed)
 

time: 72.7 us -> 67.3 us (0.926)
  starting transfers between devices: 23.2 us -> 20.4 us
  waiting for transfers between devices: 13.4 us -> 12.4 us
  local copies, waits for them, and re-layouts: 5.26 us -> 4.32 us
  other arithmetic: 27 us -> 26.2 us
    ppermute x9 -> x6, starting transfers between devices: 14.6 us -> 9.26 us  [send_up(): moved.append(lax.ppermute(chunks[offset], 'blk', perm))]
    ppermute x6, starting transfers between devices: 7.76 us -> 11.1 us  [send_down(): moved.append(lax.ppermute(chunks[offset], 'blk', perm))]
    ppermute x5 -> x3, waiting for transfers between devices: 2.43 us -> 0.51 us  [swap(): return lax.ppermute(value, 'sub', [(0, 1), (1, 0)])]
    ppermute x9 -> x6, waiting for transfers between devices: 8.64 us -> 9.81 us  [send_up(): moved.append(lax.ppermute(chunks[offset], 'blk', perm))]
    unnamed x5 -> x8, local copies, waits for them, and re-layouts: 3.14 us -> 2.26 us
    reduce_sum x10 -> x13, other arithmetic: 3.73 us -> 4.56 us  [pick_rows(): return jnp.sum(chosen, axis=2, dtype=values.dtype)]
    unnamed x2 -> x1, other arithmetic: 1.55 us -> 0.8 us
  transfers between devices with their start and end apart: 20 -> 15, of which waited for: 10 -> 10; matrix products, arithmetic and copies ran while one was open for 16% -> 13% of each run, Pallas kernels for 0% -> 0%
where the time goes in v8:
time: 67.3 us; the launch traced here: 67 us
  other arithmetic  26.2 us (39%)
  starting transfers between devices  20.4 us (30%)
  waiting for transfers between devices  12.4 us (18%)
  local copies, waits for them, and re-layouts  4.32 us (6%)
  matrix products  2.37 us (4%)
  between operations  1.18 us (2%)
    ppermute x6, starting transfers between devices, send_down(): moved.append(lax.ppermute(chunks[offset], 'blk', perm))  11.1 us
    ppermute x6, waiting for transfers between devices, send_up(): moved.append(lax.ppermute(chunks[offset], 'blk', perm))  9.81 us
    ppermute x6, starting transfers between devices, send_up(): moved.append(lax.ppermute(chunks[offset], 'blk', perm))  9.26 us
    reduce_sum x4, other arithmetic, lse_parts(): jnp.sum(jnp.exp(scores - jnp.expand_dims(highest, axis)), axis=axis)  8.13 us
    reduce_max x3, other arithmetic, lse_parts(): highest = jnp.max(scores, axis=axis)  7.57 us
    reduce_sum x13, other arithmetic, pick_rows(): return jnp.sum(chosen, axis=2, dtype=values.dtype)  4.56 us
    dot_general x2, matrix products, slot_costs(): jnp.einsum('gdi,gdj->gij', slot_real, slot_synth, preferred_element_type=...  2.37 us
    unnamed x8, local copies, waits for them, and re-layouts  2.26 us
  transfers between devices with their start and end apart: 15, of which 10 were waited for; matrix products, arithmetic and copies ran while one was open for 13% of the time, Pallas kernels for 0%

profile of v8, /device:TPU:0, one launch (start us, length us, event | category | flops | bytes accessed | tf_op | source)
XLA Modules:
  0.0 67.0 jit_solution(15816610467239242390)
XLA Ops:
  0.6 0.7 %convert_bitcast_fusion.3 = (bf16[1,1,8,128]{3,2,1,0:T(8,128)(2,1)S(1)}, bf16[1,8,128]{2,1,0:T(8,128)(2,1)S(1)}) fusion(s32[1024]{0:T(1024)} %param.12), kind=kLoop, calls=%fused_computation.138 | loop fusion | flops 1024 | bytes 8192 | tf_op jit(solution)/shard_map/concatenate | solution.py:116
  1.4 0.9 %copy.98 = bf16[8,8,8,128]{3,2,1,0:T(8,128)(2,1)S(1)} copy(bf16[8,8,8,128]{3,1,2,0:T(8,128)(2,1)} %bitcast.67) | data formatting | bytes 262144
  2.3 3.1 %collective-permute-start.3 = (bf16[65,8,128]{2,1,0:T(8,128)(2,1)S(1)}, bf16[65,8,128]{2,1,0:T(8,128)(2,1)S(1)}, u32[]{:S(2)}, u32[]{:S(2)}) collective-permute-start(bf16[65,8,128]{2,1,0:T(8,128)(2,1)S(1)} %pad_maximum_fusion.1), channel_id=1, source_target_pairs={{0,4},{4,8},{8,12},{12,0},{1,5},{5,9},{9,13},{13,1},{2,6},{6,10},{... | collective-permute-start | bytes 399368 | tf_op jit(solution)/shard_map/ppermute | solution.py:91
  5.4 2.6 %collective-permute-start.2 = (bf16[65,8,128]{2,1,0:T(8,128)(2,1)S(1)}, bf16[65,8,128]{2,1,0:T(8,128)(2,1)S(1)}, u32[]{:S(2)}, u32[]{:S(2)}) collective-permute-start(bf16[65,8,128]{2,1,0:T(8,128)(2,1)S(1)} %pad_maximum_fusion.1), channel_id=1, source_target_pairs={{0,8},{4,12},{8,0},{12,4},{1,9},{5,13},{9,1},{13,5},{2,10},{6,14},... | collective-permute-start | bytes 399368 | tf_op jit(solution)/shard_map/ppermute | solution.py:91
  8.0 1.3 %collective-permute-start.1 = (bf16[65,8,128]{2,1,0:T(8,128)(2,1)S(1)}, bf16[65,8,128]{2,1,0:T(8,128)(2,1)S(1)}, u32[]{:S(2)}, u32[]{:S(2)}) collective-permute-start(bf16[65,8,128]{2,1,0:T(8,128)(2,1)S(1)} %pad_maximum_fusion.1), channel_id=1, source_target_pairs={{0,12},{4,0},{8,4},{12,8},{1,13},{5,1},{9,5},{13,9},{2,14},{6,2},{... | collective-permute-start | bytes 399368 | tf_op jit(solution)/shard_map/ppermute | solution.py:91
  9.3 0.7 stack_broadcast_in_dim.2
  10.0 0.7 %fusion.22 = (s32[3,1,4,2]{2,3,0,1:T(2,128)S(1)}, s32[3,4,2]{1,2,0:T(2,128)S(1)}) fusion(s32[1,4,2]{1,2,0:T(2,128)S(1)} %stack_broadcast_in_dim.2, s32[1,4,2]{1,2,0:T(2,128)} %bitcast.75, s32[1,4,2]{1,2,0:T(2,128)} %bitcast.76), kind=kLoop, calls=%fused_computation.141 | loop fusion | flops 48 | bytes 288 | tf_op jit(solution)/shard_map/stack | solution.py:129
  10.8 0.7 %convert_bitcast_fusion.1 = bf16[8,128]{1,0:T(8,128)(2,1)S(1)} fusion(s32[1024]{0:T(1024)} %param.11), kind=kLoop, calls=%fused_computation.130 | loop fusion | flops 1024 | bytes 6144 | tf_op jit(solution)/shard_map/convert_element_type | solution.py:115
  11.5 0.8 %multiply_bitcast_fusion = (f32[1,8,8,128]{3,1,2,0:T(8,128)S(1)}, f32[1,8,8,128]{3,1,2,0:T(8,128)S(1)}) fusion(s32[16,1024]{1,0:T(8,128)} %param.14, s32[]{:T(128)S(6)} %select_n.250, s32[16,1024]{1,0:T(8,128)} %param.13), kind=kLoop, calls=%fused_computation.74 | loop fusion | flops 49152 | bytes 131076
  12.4 0.3 select_reduce_fusion.25
  12.7 0.3 slice_reduce_fusion.7
  12.9 0.1 copy.90
  13.8 0.1 select_reduce_fusion.23
  13.9 1.4 %select_reduce_fusion = bf16[16,64,128]{2,1,0:T(8,128)(2,1)S(1)} fusion(pred[16,8]{1,0:T(8,128)(4,1)S(1)} %iota_compare_fusion.1, bf16[64,8,128]{2,1,0:T(8,128)(2,1)S(1)} %bitcast.64), kind=kLoop, calls=%fused_computation.12 | loop fusion | flops 1966080 | bytes 393344 | tf_op jit(solution)/shard_map/reduce_sum | solution.py:26
  15.5 0.1 copy.91
  15.6 0.1 gt.46
  15.7 0.1 copy.92
  15.9 0.4 select_reduce_fusion.4
  16.3 0.4 select_reduce_fusion.1
  16.8 0.4 select_reduce_fusion.2
  17.2 0.4 select_reduce_fusion.3
  17.7 1.2 %subtract_reduce_fusion.3 = (f32[16,128]{1,0:T(8,128)S(1)}, f32[16,128,128]{2,1,0:T(8,128)S(1)}) fusion(bf16[16,128]{1,0:T(8,128)(2,1)S(1)} %select_reduce_fusion.23, bf16[16,128]{1,0:T(8,128)(2,1)S(1)} %bitcast.73, bf16[16,64,128]{2,1,0:T(8,128)(2,1)S(1)} %select_reduce_fusion, bf16[16,65,128]{2,1,0:T(8,128)(2,1)S(1)} %pad_maximum_fusion, ...), kind=kOutput, calls=%fused_computation.20 | convolution fusion | flops 35649536 | bytes 1605632 | tf_op jit(solution)/shard_map/gdi,gdj->gij/dot_general | solution.py:61
  19.0 1.1 %fusion.9 = f32[16,128,128]{2,1,0:T(8,128)S(1)} fusion(bf16[16,64,128]{2,1,0:T(8,128)(2,1)S(1)} %select_reduce_fusion, f32[16,128]{1,0:T(8,128)S(1)} %broadcast_multiply_fusion.3, f32[16,128]{1,0:T(8,128)S(1)} %broadcast_multiply_fusion.2, bf16[16,128]{1,0:T(8,128)(2,1)S(1)} %bitcast.74, bf16[16,128]{1,0:T(8,128)(2,1)S(1)} %select_reduce_fusion.23, ...), kind=kOutput, calls=%fused_computation.18 | convolution fusion | flops 35127296 | bytes 1597440 | tf_op jit(solution)/shard_map/gdi,gdj->gij/dot_general | solution.py:61
  20.3 0.1 select_reduce_fusion.21
  20.4 0.2 exponential_reduce_fusion
  20.7 0.1 select_reduce_fusion.20
  20.8 0.2 select_reduce_fusion.15
  21.0 2.5 %subtract_reduce_fusion.2 = f32[16,8,128]{2,1,0:T(8,128)S(1)} fusion(f32[16,128,128]{2,1,0:T(8,128)S(1)} %fusion.9, f32[16,8,128]{2,1,0:T(8,128)S(1)} %broadcast_multiply_fusion.1), kind=kLoop, calls=%fused_computation.5 | loop fusion | flops 4177920 | bytes 1179648 | tf_op jit(solution)/shard_map/reduce_max | solution.py:71
  23.6 2.6 %fusion.1 = f32[16,8,128]{2,1,0:T(8,128)S(1)} fusion(f32[16,8,128]{2,1,0:T(8,128)S(1)} %subtract_reduce_fusion.2, f32[16,128,128]{2,1,0:T(8,128)S(1)} %fusion.9, f32[16,8,128]{2,1,0:T(8,128)S(1)} %broadcast_multiply_fusion.1), kind=kLoop, calls=%fused_computation.7 | loop fusion | flops 6275072 | bytes 1245184 | tf_op jit(solution)/shard_map/reduce_sum | solution.py:72
  26.4 4.4 %collective-permute-start.6 = (f32[4,9,128]{2,0,1:T(4,128)S(1)}, f32[4,9,128]{2,0,1:T(4,128)S(1)}, u32[]{:S(2)}, u32[]{:S(2)}) collective-permute-start(f32[4,9,128]{2,0,1:T(4,128)S(1)} %get-tuple-element.23), channel_id=1, source_target_pairs={{0,12},{4,0},{8,4},{12,8},{1,13},{5,1},{9,5},{13,9},{2,14},{6,2},{... | collective-permute-start | bytes 55304 | tf_op jit(solution)/shard_map/ppermute | solution.py:84
  30.9 0.6 collective-permute-start.4
  31.5 0.8 %collective-permute-done.6 = f32[4,9,128]{2,0,1:T(4,128)S(1)} collective-permute-done((f32[4,9,128]{2,0,1:T(4,128)S(1)}, f32[4,9,128]{2,0,1:T(4,128)S(1)}, u32[]{:S(2)}, u32[]{:S(2)}) %collective-permute-start.6) | collective-permute-done | bytes 18464 | tf_op jit(solution)/shard_map/ppermute | solution.py:84
  32.3 3.2 %collective-permute-done.5 = f32[4,9,128]{2,0,1:T(4,128)S(1)} collective-permute-done((f32[4,9,128]{2,0,1:T(4,128)S(1)}, f32[4,9,128]{2,0,1:T(4,128)S(1)}, u32[]{:S(2)}, u32[]{:S(2)}) %collective-permute-start.5) | collective-permute-done | bytes 18464 | tf_op jit(solution)/shard_map/ppermute | solution.py:84
  35.5 0.9 %collective-permute-done.4 = f32[4,9,128]{2,0,1:T(4,128)S(1)} collective-permute-done((f32[4,9,128]{2,0,1:T(4,128)S(1)}, f32[4,9,128]{2,0,1:T(4,128)S(1)}, u32[]{:S(2)}, u32[]{:S(2)}) %collective-permute-start.4) | collective-permute-done | bytes 18464 | tf_op jit(solution)/shard_map/ppermute | solution.py:84
  36.5 0.1 fusion.23
  36.7 0.1 select_reduce_fusion.14
  36.8 0.2 select_reduce_fusion.13
  37.1 0.1 select_reduce_fusion.12
  37.2 0.1 slice_reduce_fusion.3
  37.7 0.2 select_reduce_fusion.19
  37.9 1.2 %collective-permute-start.8 = (f32[4,8,128]{2,1,0:T(8,128)S(1)}, f32[4,8,128]{2,1,0:T(8,128)S(1)}, u32[]{:S(2)}, u32[]{:S(2)}) collective-permute-start(f32[4,8,128]{2,1,0:T(8,128)S(1)} %get-tuple-element.4), channel_id=1, source_target_pairs={{0,8},{4,12},{8,0},{12,4},{1,9},{5,13},{9,1},{13,5},{2,10},{6,14},... | collective-permute-start | bytes 49160 | tf_op jit(solution)/shard_map/ppermute | solution.py:91
  39.1 2.8 %collective-permute-start.7 = (f32[4,8,128]{2,1,0:T(8,128)S(1)}, f32[4,8,128]{2,1,0:T(8,128)S(1)}, u32[]{:S(2)}, u32[]{:S(2)}) collective-permute-start(f32[4,8,128]{2,1,0:T(8,128)S(1)} %get-tuple-element.3), channel_id=1, source_target_pairs={{0,12},{4,0},{8,4},{12,8},{1,13},{5,1},{9,5},{13,9},{2,14},{6,2},{... | collective-permute-start | bytes 49160 | tf_op jit(solution)/shard_map/ppermute | solution.py:91
  42.0 1.5 %collective-permute-done.9 = f32[4,8,128]{2,1,0:T(8,128)S(1)} collective-permute-done((f32[4,8,128]{2,1,0:T(8,128)S(1)}, f32[4,8,128]{2,1,0:T(8,128)S(1)}, u32[]{:S(2)}, u32[]{:S(2)}) %collective-permute-start.9) | collective-permute-done | bytes 16416 | tf_op jit(solution)/shard_map/ppermute | solution.py:91
  43.5 0.6 collective-permute-done.7
  44.0 2.5 %subtract_reduce_fusion.1 = f32[16,8,128]{2,1,0:T(8,128)S(1)} fusion(f32[16,128,128]{2,1,0:T(8,128)S(1)} %get-tuple-element.38, f32[16,8,128]{2,1,0:T(8,128)S(1)} %maximum_multiply_fusion), kind=kLoop, calls=%fused_computation.3 | loop fusion | flops 4177920 | bytes 1179648 | tf_op jit(solution)/shard_map/reduce_max | solution.py:71
  46.7 2.6 %fusion.3 = f32[16,8,128]{2,1,0:T(8,128)S(1)} fusion(f32[16,8,128]{2,1,0:T(8,128)S(1)} %subtract_reduce_fusion.1, f32[16,128,128]{2,1,0:T(8,128)S(1)} %get-tuple-element.38, f32[16,8,128]{2,1,0:T(8,128)S(1)} %maximum_multiply_fusion), kind=kLoop, calls=%fused_computation.9 | loop fusion | flops 6275072 | bytes 1245184 | tf_op jit(solution)/shard_map/reduce_sum | solution.py:72
  49.3 0.1 select_reduce_fusion.11
  49.4 0.2 select_reduce_fusion.10
  49.7 0.1 exponential_multiply_fusion
  49.8 0.1 select_reduce_fusion.9
  49.9 0.2 select_reduce_fusion.8
  50.2 2.5 %subtract_reduce_fusion = f32[16,8,128]{2,1,0:T(8,128)S(1)} fusion(f32[16,8,128]{2,1,0:T(8,128)S(1)} %broadcast_multiply_fusion, f32[16,128,128]{2,1,0:T(8,128)S(1)} %fusion.9), kind=kLoop, calls=%fused_computation.1 | loop fusion | flops 4177920 | bytes 1179648 | tf_op jit(solution)/shard_map/reduce_max | solution.py:71
  52.7 2.6 %fusion.5 = f32[16,8,128]{2,1,0:T(8,128)S(1)} fusion(f32[16,8,128]{2,1,0:T(8,128)S(1)} %subtract_reduce_fusion, f32[16,8,128]{2,1,0:T(8,128)S(1)} %broadcast_multiply_fusion, f32[16,128,128]{2,1,0:T(8,128)S(1)} %fusion.9), kind=kLoop, calls=%fused_computation.11 | loop fusion | flops 6275072 | bytes 1245184 | tf_op jit(solution)/shard_map/reduce_sum | solution.py:72
  55.4 3.5 %collective-permute-start.13 = (f32[4,8,128]{2,1,0:T(8,128)S(1)}, f32[4,8,128]{2,1,0:T(8,128)S(1)}, u32[]{:S(2)}, u32[]{:S(2)}) collective-permute-start(f32[4,8,128]{2,1,0:T(8,128)S(1)} %get-tuple-element.28), channel_id=1, source_target_pairs={{0,12},{4,0},{8,4},{12,8},{1,13},{5,1},{9,5},{13,9},{2,14},{6,2},{... | collective-permute-start | bytes 49160 | tf_op jit(solution)/shard_map/ppermute | solution.py:84
  59.0 0.6 collective-permute-start.11
  59.6 0.8 %collective-permute-done.13 = f32[4,8,128]{2,1,0:T(8,128)S(1)} collective-permute-done((f32[4,8,128]{2,1,0:T(8,128)S(1)}, f32[4,8,128]{2,1,0:T(8,128)S(1)}, u32[]{:S(2)}, u32[]{:S(2)}) %collective-permute-start.13) | collective-permute-done | bytes 16416 | tf_op jit(solution)/shard_map/ppermute | solution.py:84
  60.4 3.2 %collective-permute-done.12 = f32[4,8,128]{2,1,0:T(8,128)S(1)} collective-permute-done((f32[4,8,128]{2,1,0:T(8,128)S(1)}, f32[4,8,128]{2,1,0:T(8,128)S(1)}, u32[]{:S(2)}, u32[]{:S(2)}) %collective-permute-start.12) | collective-permute-done | bytes 16416 | tf_op jit(solution)/shard_map/ppermute | solution.py:84
  63.6 0.9 %collective-permute-done.11 = f32[4,8,128]{2,1,0:T(8,128)S(1)} collective-permute-done((f32[4,8,128]{2,1,0:T(8,128)S(1)}, f32[4,8,128]{2,1,0:T(8,128)S(1)}, u32[]{:S(2)}, u32[]{:S(2)}) %collective-permute-start.11) | collective-permute-done | bytes 16416 | tf_op jit(solution)/shard_map/ppermute | solution.py:84
  64.5 0.1 select_reduce_fusion.7
  64.6 0.2 select_reduce_fusion.6
  64.9 0.1 select_reduce_fusion.5
  65.2 0.6 copy.113
  65.8 0.5 collective-permute-done.14
  66.3 0.6 copy.112
  (74 shorter events, 2.7 us)
Async XLA Ops:
  0.6 11.7 %copy-start = (bf16[64,1024]{1,0:T(8,128)(2,1)S(1)}, bf16[64,1024]{1,0:T(8,128)(2,1)}, u32[]{:S(2)}) copy-start(bf16[64,1024]{1,0:T(8,128)(2,1)} %param.9) | copy-start | bytes 393220
  2.3 14.0 %collective-permute-start.3 = (bf16[65,8,128]{2,1,0:T(8,128)(2,1)S(1)}, bf16[65,8,128]{2,1,0:T(8,128)(2,1)S(1)}, u32[]{:S(2)}, u32[]{:S(2)}) collective-permute-start(bf16[65,8,128]{2,1,0:T(8,128)(2,1)S(1)} %pad_maximum_fusion.1), channel_id=1, source_target_pairs={{0,4},{4,8},{8,12},{12,0},{1,5},{5,9},{9,13},{13,1},{2,6},{6,10},{... | collective-permute-start | bytes 399368 | tf_op jit(solution)/shard_map/ppermute | solution.py:91
  5.4 11.4 %collective-permute-start.2 = (bf16[65,8,128]{2,1,0:T(8,128)(2,1)S(1)}, bf16[65,8,128]{2,1,0:T(8,128)(2,1)S(1)}, u32[]{:S(2)}, u32[]{:S(2)}) collective-permute-start(bf16[65,8,128]{2,1,0:T(8,128)(2,1)S(1)} %pad_maximum_fusion.1), channel_id=1, source_target_pairs={{0,8},{4,12},{8,0},{12,4},{1,9},{5,13},{9,1},{13,5},{2,10},{6,14},... | collective-permute-start | bytes 399368 | tf_op jit(solution)/shard_map/ppermute | solution.py:91
  8.0 9.2 %collective-permute-start.1 = (bf16[65,8,128]{2,1,0:T(8,128)(2,1)S(1)}, bf16[65,8,128]{2,1,0:T(8,128)(2,1)S(1)}, u32[]{:S(2)}, u32[]{:S(2)}) collective-permute-start(bf16[65,8,128]{2,1,0:T(8,128)(2,1)S(1)} %pad_maximum_fusion.1), channel_id=1, source_target_pairs={{0,12},{4,0},{8,4},{12,8},{1,13},{5,1},{9,5},{13,9},{2,14},{6,2},{... | collective-permute-start | bytes 399368 | tf_op jit(solution)/shard_map/ppermute | solution.py:91
  10.7 1.6 %collective-permute-start = (s32[3,4,2]{1,2,0:T(2,128)S(1)}, s32[3,4,2]{1,2,0:T(2,128)S(1)}, u32[]{:S(2)}, u32[]{:S(2)}) collective-permute-start(s32[3,4,2]{1,2,0:T(2,128)S(1)} %get-tuple-element.36), channel_id=1, source_target_pairs={{0,1},{1,0},{2,3},{3,2},{4,5},{5,4},{6,7},{7,6},{8,9},{9,8},{10,11... | collective-permute-start | bytes 296 | tf_op jit(solution)/shard_map/ppermute | solution.py:78
  26.4 5.9 %collective-permute-start.6 = (f32[4,9,128]{2,0,1:T(4,128)S(1)}, f32[4,9,128]{2,0,1:T(4,128)S(1)}, u32[]{:S(2)}, u32[]{:S(2)}) collective-permute-start(f32[4,9,128]{2,0,1:T(4,128)S(1)} %get-tuple-element.23), channel_id=1, source_target_pairs={{0,12},{4,0},{8,4},{12,8},{1,13},{5,1},{9,5},{13,9},{2,14},{6,2},{... | collective-permute-start | bytes 55304 | tf_op jit(solution)/shard_map/ppermute | solution.py:84
  30.9 4.7 %collective-permute-start.5 = (f32[4,9,128]{2,0,1:T(4,128)S(1)}, f32[4,9,128]{2,0,1:T(4,128)S(1)}, u32[]{:S(2)}, u32[]{:S(2)}) collective-permute-start(f32[4,9,128]{2,0,1:T(4,128)S(1)} %get-tuple-element.24), channel_id=1, source_target_pairs={{0,8},{4,12},{8,0},{12,4},{1,9},{5,13},{9,1},{13,5},{2,10},{6,14},... | collective-permute-start | bytes 55304 | tf_op jit(solution)/shard_map/ppermute | solution.py:84
  30.9 5.6 %collective-permute-start.4 = (f32[4,9,128]{2,0,1:T(4,128)S(1)}, f32[4,9,128]{2,0,1:T(4,128)S(1)}, u32[]{:S(2)}, u32[]{:S(2)}) collective-permute-start(f32[4,9,128]{2,0,1:T(4,128)S(1)} %get-tuple-element.22), channel_id=1, source_target_pairs={{0,4},{4,8},{8,12},{12,0},{1,5},{5,9},{9,13},{13,1},{2,6},{6,10},{... | collective-permute-start | bytes 55304 | tf_op jit(solution)/shard_map/ppermute | solution.py:84
  37.9 5.6 %collective-permute-start.9 = (f32[4,8,128]{2,1,0:T(8,128)S(1)}, f32[4,8,128]{2,1,0:T(8,128)S(1)}, u32[]{:S(2)}, u32[]{:S(2)}) collective-permute-start(f32[4,8,128]{2,1,0:T(8,128)S(1)} %get-tuple-element.5), channel_id=1, source_target_pairs={{0,4},{4,8},{8,12},{12,0},{1,5},{5,9},{9,13},{13,1},{2,6},{6,10},{... | collective-permute-start | bytes 49160 | tf_op jit(solution)/shard_map/ppermute | solution.py:91
  37.9 5.5 %collective-permute-start.8 = (f32[4,8,128]{2,1,0:T(8,128)S(1)}, f32[4,8,128]{2,1,0:T(8,128)S(1)}, u32[]{:S(2)}, u32[]{:S(2)}) collective-permute-start(f32[4,8,128]{2,1,0:T(8,128)S(1)} %get-tuple-element.4), channel_id=1, source_target_pairs={{0,8},{4,12},{8,0},{12,4},{1,9},{5,13},{9,1},{13,5},{2,10},{6,14},... | collective-permute-start | bytes 49160 | tf_op jit(solution)/shard_map/ppermute | solution.py:91
  39.1 4.9 %collective-permute-start.7 = (f32[4,8,128]{2,1,0:T(8,128)S(1)}, f32[4,8,128]{2,1,0:T(8,128)S(1)}, u32[]{:S(2)}, u32[]{:S(2)}) collective-permute-start(f32[4,8,128]{2,1,0:T(8,128)S(1)} %get-tuple-element.3), channel_id=1, source_target_pairs={{0,12},{4,0},{8,4},{12,8},{1,13},{5,1},{9,5},{13,9},{2,14},{6,2},{... | collective-permute-start | bytes 49160 | tf_op jit(solution)/shard_map/ppermute | solution.py:91
  55.4 5.0 %collective-permute-start.13 = (f32[4,8,128]{2,1,0:T(8,128)S(1)}, f32[4,8,128]{2,1,0:T(8,128)S(1)}, u32[]{:S(2)}, u32[]{:S(2)}) collective-permute-start(f32[4,8,128]{2,1,0:T(8,128)S(1)} %get-tuple-element.28), channel_id=1, source_target_pairs={{0,12},{4,0},{8,4},{12,8},{1,13},{5,1},{9,5},{13,9},{2,14},{6,2},{... | collective-permute-start | bytes 49160 | tf_op jit(solution)/shard_map/ppermute | solution.py:84
  59.0 4.6 %collective-permute-start.12 = (f32[4,8,128]{2,1,0:T(8,128)S(1)}, f32[4,8,128]{2,1,0:T(8,128)S(1)}, u32[]{:S(2)}, u32[]{:S(2)}) collective-permute-start(f32[4,8,128]{2,1,0:T(8,128)S(1)} %get-tuple-element.29), channel_id=1, source_target_pairs={{0,8},{4,12},{8,0},{12,4},{1,9},{5,13},{9,1},{13,5},{2,10},{6,14},... | collective-permute-start | bytes 49160 | tf_op jit(solution)/shard_map/ppermute | solution.py:84
  59.0 5.5 %collective-permute-start.11 = (f32[4,8,128]{2,1,0:T(8,128)S(1)}, f32[4,8,128]{2,1,0:T(8,128)S(1)}, u32[]{:S(2)}, u32[]{:S(2)}) collective-permute-start(f32[4,8,128]{2,1,0:T(8,128)S(1)} %get-tuple-element.30), channel_id=1, source_target_pairs={{0,4},{4,8},{8,12},{12,0},{1,5},{5,9},{9,13},{13,1},{2,6},{6,10},{... | collective-permute-start | bytes 49160 | tf_op jit(solution)/shard_map/ppermute | solution.py:84
  59.6 5.5 %collective-permute-start.10 = (f32[8,8,128]{2,1,0:T(8,128)S(1)}, f32[8,8,128]{2,1,0:T(8,128)S(1)}, u32[]{:S(2)}, u32[]{:S(2)}) collective-permute-start(f32[8,8,128]{2,1,0:T(8,128)S(1)} %bitcast_subtract_fusion.2), channel_id=1, source_target_pairs={{0,1},{1,0},{2,3},{3,2},{4,5},{5,4},{6,7},{7,6},{8,9},{9,8},{10,11... | collective-permute-start | bytes 98312 | tf_op jit(solution)/shard_map/ppermute | solution.py:78
  65.0 1.3 %collective-permute-start.14 = (f32[8,8,128]{2,1,0:T(8,128)S(1)}, f32[8,8,128]{2,1,0:T(8,128)S(1)}, u32[]{:S(2)}, u32[]{:S(2)}) collective-permute-start(f32[8,8,128]{2,1,0:T(8,128)S(1)} %bitcast_subtract_fusion), channel_id=1, source_target_pairs={{0,1},{1,0},{2,3},{3,2},{4,5},{5,4},{6,7},{7,6},{8,9},{9,8},{10,11... | collective-permute-start | bytes 98312 | tf_op jit(solution)/shard_map/ppermute | solution.py:78

commit v9 on v8

--- a/solution.py
+++ b/solution.py
@@ -159,24 +159,34 @@
                     ),
                     axis=0,
                 )
-            scores = (panel / SMOOTH)[:, :, :, None] - cost_rows[:, None]
-            highest, mass_sum = lse_parts(scores, 2)
+            highest, mass_sum = [], []
+            for offset in range(peer_count):
+                piece = slice(offset * wide, (offset + 1) * wide)
+                scores = (panel[piece] / SMOOTH)[:, :, :, None] - cost_rows[piece, None]
+                parts = lse_parts(scores, 2)
+                highest.append(parts[0])
+                mass_sum.append(parts[1])
+            highest = jnp.concatenate(highest, axis=0)
+            mass_sum = jnp.concatenate(mass_sum, axis=0)
             highest = jnp.where(usable, highest, SENTINEL)
             mass_sum = jnp.where(usable, mass_sum, 0.0)
             block_top, summed = fold_blocks(highest, mass_sum, rows_used, blocks)
             real_pot = finish(log_real, block_top, summed)
 
             own_rows = pick_rows(real_pot, rows_used, blocks)
-            scores = (own_rows / SMOOTH)[:, :, :, None] - cost_cols[:, None]
-            highest, mass_sum = lse_parts(scores, 2)
-            lse = jnp.where(usable, highest + jnp.log(mass_sum), SENTINEL)
-            if sweep_index == 0:
-                block_ids = jnp.broadcast_to(wanted.reshape(slot_count, 1, 1).astype(jnp.float32), (slot_count, 1, BLOCK))
-                lse = jnp.concatenate([lse, block_ids], axis=1)
-            back = jnp.concatenate(
-                send_up([lse[offset * wide : (offset + 1) * wide] for offset in range(peer_count)]),
-                axis=0,
-            )
+            chunks = [None] * peer_count
+            for offset in list(range(1, peer_count)) + [0]:
+                piece = slice(offset * wide, (offset + 1) * wide)
+                scores = (own_rows[piece] / SMOOTH)[:, :, :, None] - cost_cols[piece, None]
+                highest, mass_sum = lse_parts(scores, 2)
+                lse = jnp.where(usable[piece], highest + jnp.log(mass_sum), SENTINEL)
+                if sweep_index == 0:
+                    block_ids = jnp.broadcast_to(
+                        wanted[offset].reshape(wide, 1, 1).astype(jnp.float32), (wide, 1, BLOCK)
+                    )
+                    lse = jnp.concatenate([lse, block_ids], axis=1)
+                chunks[offset] = lse
+            back = jnp.concatenate(send_up(chunks), axis=0)
             if sweep_index == 0:
                 requested = back[:, half, 0].astype(jnp.int32)
                 back = back[:, :half]

time: 67.3 us -> 63.4 us (0.942)
  waiting for transfers between devices: 12.4 us -> 6.88 us
  other arithmetic: 26.2 us -> 28.6 us
  starting transfers between devices: 20.4 us -> 18.8 us
    ppermute x6, waiting for transfers between devices: 9.81 us -> 6.23 us  [send_up(): moved.append(lax.ppermute(chunks[offset], 'blk', perm))]
    ppermute x6, waiting for transfers between devices: 2.11 us -> 0.14 us  [send_down(): moved.append(lax.ppermute(chunks[offset], 'blk', perm))]
    ppermute x6, starting transfers between devices: 9.26 us -> 7.62 us  [send_up(): moved.append(lax.ppermute(chunks[offset], 'blk', perm))]
    reduce_sum x4 -> x14, other arithmetic: 8.13 us -> 9.27 us  [lse_parts(): jnp.sum(jnp.exp(scores - jnp.expand_dims(highest, axis)), axis=axis)]
    unnamed x1 -> x2, other arithmetic: 0.8 us -> 1.55 us
    reduce_max x3 -> x11, other arithmetic: 7.57 us -> 7.55 us  [lse_parts(): highest = jnp.max(scores, axis=axis)]
  transfers between devices with their start and end apart: 15 -> 15, of which waited for: 10 -> 5; matrix products, arithmetic and copies ran while one was open for 13% -> 38% of each run, Pallas kernels for 0% -> 0%
where the time goes in v9:
time: 63.4 us; the launch traced here: 63 us
  other arithmetic  28.6 us (45%)
  starting transfers between devices  18.8 us (30%)
  waiting for transfers between devices  6.88 us (11%)
  local copies, waits for them, and re-layouts  4.99 us (8%)
  matrix products  2.35 us (4%)
  between operations  1.36 us (2%)
    ppermute x6, starting transfers between devices, send_down(): moved.append(lax.ppermute(chunks[offset], 'blk', perm))  11.1 us
    reduce_sum x14, other arithmetic, lse_parts(): jnp.sum(jnp.exp(scores - jnp.expand_dims(highest, axis)), axis=axis)  9.27 us
    ppermute x6, starting transfers between devices, send_up(): moved.append(lax.ppermute(chunks[offset], 'blk', perm))  7.62 us
    reduce_max x11, other arithmetic, lse_parts(): highest = jnp.max(scores, axis=axis)  7.55 us
    ppermute x6, waiting for transfers between devices, send_up(): moved.append(lax.ppermute(chunks[offset], 'blk', perm))  6.23 us
    reduce_sum x13, other arithmetic, pick_rows(): return jnp.sum(chosen, axis=2, dtype=values.dtype)  4.56 us
    dot_general x2, matrix products, slot_costs(): jnp.einsum('gdi,gdj->gij', slot_real, slot_synth, preferred_element_type=...  2.35 us
    unnamed x8, local copies, waits for them, and re-layouts  2.26 us
  transfers between devices with their start and end apart: 15, of which 5 were waited for; matrix products, arithmetic and copies ran while one was open for 38% of the time, Pallas kernels for 0%

profile of v9, /device:TPU:0, one launch (start us, length us, event | category | flops | bytes accessed | tf_op | source)
XLA Modules:
  0.0 63.0 jit_solution(13807182968976425944)
XLA Ops:
  0.6 0.7 %convert_bitcast_fusion.3 = (bf16[1,1,8,128]{3,2,1,0:T(8,128)(2,1)S(1)}, bf16[1,8,128]{2,1,0:T(8,128)(2,1)S(1)}) fusion(s32[1024]{0:T(1024)} %param.12), kind=kLoop, calls=%fused_computation.192 | loop fusion | flops 1024 | bytes 8192 | tf_op jit(solution)/shard_map/concatenate | solution.py:116
  1.4 0.9 %copy.134 = bf16[8,8,8,128]{3,2,1,0:T(8,128)(2,1)S(1)} copy(bf16[8,8,8,128]{3,1,2,0:T(8,128)(2,1)} %bitcast.69) | data formatting | bytes 262144
  2.3 3.1 %collective-permute-start.3 = (bf16[65,8,128]{2,1,0:T(8,128)(2,1)S(1)}, bf16[65,8,128]{2,1,0:T(8,128)(2,1)S(1)}, u32[]{:S(2)}, u32[]{:S(2)}) collective-permute-start(bf16[65,8,128]{2,1,0:T(8,128)(2,1)S(1)} %pad_maximum_fusion.1), channel_id=1, source_target_pairs={{0,4},{4,8},{8,12},{12,0},{1,5},{5,9},{9,13},{13,1},{2,6},{6,10},{... | collective-permute-start | bytes 399368 | tf_op jit(solution)/shard_map/ppermute | solution.py:91
  5.4 2.6 %collective-permute-start.2 = (bf16[65,8,128]{2,1,0:T(8,128)(2,1)S(1)}, bf16[65,8,128]{2,1,0:T(8,128)(2,1)S(1)}, u32[]{:S(2)}, u32[]{:S(2)}) collective-permute-start(bf16[65,8,128]{2,1,0:T(8,128)(2,1)S(1)} %pad_maximum_fusion.1), channel_id=1, source_target_pairs={{0,8},{4,12},{8,0},{12,4},{1,9},{5,13},{9,1},{13,5},{2,10},{6,14},... | collective-permute-start | bytes 399368 | tf_op jit(solution)/shard_map/ppermute | solution.py:91
  8.0 1.3 %collective-permute-start.1 = (bf16[65,8,128]{2,1,0:T(8,128)(2,1)S(1)}, bf16[65,8,128]{2,1,0:T(8,128)(2,1)S(1)}, u32[]{:S(2)}, u32[]{:S(2)}) collective-permute-start(bf16[65,8,128]{2,1,0:T(8,128)(2,1)S(1)} %pad_maximum_fusion.1), channel_id=1, source_target_pairs={{0,12},{4,0},{8,4},{12,8},{1,13},{5,1},{9,5},{13,9},{2,14},{6,2},{... | collective-permute-start | bytes 399368 | tf_op jit(solution)/shard_map/ppermute | solution.py:91
  9.3 0.7 %stack_broadcast_in_dim.2 = s32[1,4,2]{1,2,0:T(2,128)S(1)} broadcast(s32[4]{0:T(128)} %param.17), dimensions={1} | broadcast | bytes 48 | tf_op jit(solution)/shard_map/stack;broadcast_in_dim | solution.py:128
  10.0 0.7 %fusion.40 = (s32[3,1,4,2]{2,3,0,1:T(2,128)S(1)}, s32[3,4,2]{1,2,0:T(2,128)S(1)}) fusion(s32[1,4,2]{1,2,0:T(2,128)S(1)} %stack_broadcast_in_dim.2, s32[1,4,2]{1,2,0:T(2,128)} %bitcast.77, s32[1,4,2]{1,2,0:T(2,128)} %bitcast.78), kind=kLoop, calls=%fused_computation.197 | loop fusion | flops 48 | bytes 288 | tf_op jit(solution)/shard_map/stack | solution.py:129
  10.8 0.7 %convert_bitcast_fusion.1 = bf16[8,128]{1,0:T(8,128)(2,1)S(1)} fusion(s32[1024]{0:T(1024)} %param.11), kind=kLoop, calls=%fused_computation.184 | loop fusion | flops 1024 | bytes 6144 | tf_op jit(solution)/shard_map/convert_element_type | solution.py:115
  11.5 0.8 %multiply_bitcast_fusion.1 = f32[1,8,8,128]{3,1,2,0:T(8,128)S(1)} fusion(s32[16,1024]{1,0:T(8,128)} %param.13, s32[]{:T(128)S(6)} %select_n.272), kind=kLoop, calls=%fused_computation.109 | loop fusion | flops 24576 | bytes 65540
  12.2 0.8 %multiply_bitcast_fusion = f32[1,8,8,128]{3,1,2,0:T(8,128)S(1)} fusion(s32[16,1024]{1,0:T(8,128)} %param.14, s32[]{:T(128)S(6)} %select_n.272), kind=kLoop, calls=%fused_computation.107 | loop fusion | flops 24576 | bytes 65540
  13.1 0.3 select_reduce_fusion.25
  13.4 0.3 slice_reduce_fusion.11
  13.9 0.1 copy.125
  14.0 0.3 slice_reduce_fusion.3
  15.0 1.5 %select_reduce_fusion = bf16[16,64,128]{2,1,0:T(8,128)(2,1)S(1)} fusion(pred[16,8]{1,0:T(8,128)(4,1)S(1)} %iota_compare_fusion.1, bf16[64,8,128]{2,1,0:T(8,128)(2,1)S(1)} %bitcast.66), kind=kLoop, calls=%fused_computation.48 | loop fusion | flops 1966080 | bytes 393344 | tf_op jit(solution)/shard_map/reduce_sum | solution.py:26
  17.1 0.4 select_reduce_fusion.4
  17.5 0.4 select_reduce_fusion.1
  17.9 0.4 select_reduce_fusion.2
  18.3 0.4 select_reduce_fusion.3
  18.9 1.2 %fusion.26 = f32[16,128,128]{2,1,0:T(8,128)S(1)} fusion(bf16[16,64,128]{2,1,0:T(8,128)(2,1)S(1)} %select_reduce_fusion, f32[16,128]{1,0:T(8,128)S(1)} %broadcast_multiply_fusion.4, f32[16,128]{1,0:T(8,128)S(1)} %broadcast_multiply_fusion.5, bf16[16,128]{1,0:T(8,128)(2,1)S(1)} %select_reduce_fusion.23, bf16[16,128]{1,0:T(8,128)(2,1)S(1)} %bitcast.75, ...), kind=kOutput, calls=%fused_computation.53 | convolution fusion | flops 35127296 | bytes 1597440 | tf_op jit(solution)/shard_map/gdi,gdj->gij/dot_general | solution.py:61
  20.1 1.1 %fusion.27 = f32[16,128,128]{2,1,0:T(8,128)S(1)} fusion(bf16[16,64,128]{2,1,0:T(8,128)(2,1)S(1)} %select_reduce_fusion, f32[16,128]{1,0:T(8,128)S(1)} %broadcast_multiply_fusion.5, f32[16,128]{1,0:T(8,128)S(1)} %broadcast_multiply_fusion.4, bf16[16,128]{1,0:T(8,128)(2,1)S(1)} %bitcast.76, bf16[16,128]{1,0:T(8,128)(2,1)S(1)} %select_reduce_fusion.23, ...), kind=kOutput, calls=%fused_computation.54 | convolution fusion | flops 35127296 | bytes 1597440 | tf_op jit(solution)/shard_map/gdi,gdj->gij/dot_general | solution.py:61
  21.5 0.2 exponential_reduce_fusion.2
  22.2 0.2 select_reduce_fusion.15
  22.4 1.3 %subtract_reduce_fusion.8 = (f32[4,8,128]{2,1,0:T(8,128)S(1)}, f32[4,8,128]{2,1,0:T(8,128)S(1)}) fusion(f32[4,128,128]{2,1,0:T(8,128)S(1)} %get-tuple-element.34, f32[4,8,128]{2,1,0:T(8,128)S(1)} %get-tuple-element.47, f32[4,128,128]{2,1,0:T(8,128)S(1)} %get-tuple-element.35, f32[4,8,128]{2,1,0:T(8,128)S(1)} %get-tuple-element.48), kind=kLoop, calls=%fused_computation.17 | loop fusion | flops 2088960 | bytes 589824 | tf_op jit(solution)/shard_map/reduce_max | solution.py:71
  23.7 0.7 %fusion.7 = f32[4,8,128]{2,1,0:T(8,128)S(1)} fusion(f32[4,8,128]{2,1,0:T(8,128)S(1)} %get-tuple-element.54, f32[4,128,128]{2,1,0:T(8,128)S(1)} %get-tuple-element.34, f32[4,8,128]{2,1,0:T(8,128)S(1)} %get-tuple-element.47), kind=kLoop, calls=%fused_computation.31 | loop fusion | flops 1568768 | bytes 311296 | tf_op jit(solution)/shard_map/reduce_sum | solution.py:72
  24.6 3.3 %collective-permute-start.6 = (f32[4,9,128]{2,0,1:T(4,128)S(1)}, f32[4,9,128]{2,0,1:T(4,128)S(1)}, u32[]{:S(2)}, u32[]{:S(2)}) collective-permute-start(f32[4,9,128]{2,0,1:T(4,128)S(1)} %pad_maximum_fusion.8), channel_id=1, source_target_pairs={{0,12},{4,0},{8,4},{12,8},{1,13},{5,1},{9,5},{13,9},{2,14},{6,2},{... | collective-permute-start | bytes 55304 | tf_op jit(solution)/shard_map/ppermute | solution.py:84
  27.9 0.7 %fusion.5 = f32[4,8,128]{2,1,0:T(8,128)S(1)} fusion(f32[4,8,128]{2,1,0:T(8,128)S(1)} %get-tuple-element.55, f32[4,128,128]{2,1,0:T(8,128)S(1)} %get-tuple-element.35, f32[4,8,128]{2,1,0:T(8,128)S(1)} %get-tuple-element.48), kind=kLoop, calls=%fused_computation.29 | loop fusion | flops 1568768 | bytes 311296 | tf_op jit(solution)/shard_map/reduce_sum | solution.py:72
  28.8 1.3 %subtract_reduce_fusion.10 = (f32[4,8,128]{2,1,0:T(8,128)S(1)}, f32[4,8,128]{2,1,0:T(8,128)S(1)}) fusion(f32[4,128,128]{2,1,0:T(8,128)S(1)} %get-tuple-element.36, f32[4,8,128]{2,1,0:T(8,128)S(1)} %get-tuple-element.49, f32[4,128,128]{2,1,0:T(8,128)S(1)} %get-tuple-element.33, f32[4,8,128]{2,1,0:T(8,128)S(1)} %get-tuple-element.46), kind=kLoop, calls=%fused_computation.21 | loop fusion | flops 2088960 | bytes 589824 | tf_op jit(solution)/shard_map/reduce_max | solution.py:71
  30.1 0.7 %fusion.3 = f32[4,8,128]{2,1,0:T(8,128)S(1)} fusion(f32[4,8,128]{2,1,0:T(8,128)S(1)} %get-tuple-element.56, f32[4,128,128]{2,1,0:T(8,128)S(1)} %get-tuple-element.36, f32[4,8,128]{2,1,0:T(8,128)S(1)} %get-tuple-element.49), kind=kLoop, calls=%fused_computation.27 | loop fusion | flops 1568768 | bytes 311296 | tf_op jit(solution)/shard_map/reduce_sum | solution.py:72
  31.0 0.6 collective-permute-start.4
  31.6 0.7 %fusion.1 = f32[4,8,128]{2,1,0:T(8,128)S(1)} fusion(f32[4,8,128]{2,1,0:T(8,128)S(1)} %get-tuple-element.57, f32[4,128,128]{2,1,0:T(8,128)S(1)} %get-tuple-element.33, f32[4,8,128]{2,1,0:T(8,128)S(1)} %get-tuple-element.46), kind=kLoop, calls=%fused_computation.25 | loop fusion | flops 1568768 | bytes 311296 | tf_op jit(solution)/shard_map/reduce_sum | solution.py:72
  32.4 1.1 %collective-permute-done.5 = f32[4,9,128]{2,0,1:T(4,128)S(1)} collective-permute-done((f32[4,9,128]{2,0,1:T(4,128)S(1)}, f32[4,9,128]{2,0,1:T(4,128)S(1)}, u32[]{:S(2)}, u32[]{:S(2)}) %collective-permute-start.5) | collective-permute-done | bytes 18464 | tf_op jit(solution)/shard_map/ppermute | solution.py:84
  33.5 3.1 %collective-permute-done.4 = f32[4,9,128]{2,0,1:T(4,128)S(1)} collective-permute-done((f32[4,9,128]{2,0,1:T(4,128)S(1)}, f32[4,9,128]{2,0,1:T(4,128)S(1)}, u32[]{:S(2)}, u32[]{:S(2)}) %collective-permute-start.4) | collective-permute-done | bytes 18464 | tf_op jit(solution)/shard_map/ppermute | solution.py:84
  37.0 0.2 select_reduce_fusion.13
  37.4 0.1 slice_reduce_fusion.7
  37.9 0.2 select_reduce_fusion.19
  38.2 1.2 %collective-permute-start.8 = (f32[4,8,128]{2,1,0:T(8,128)S(1)}, f32[4,8,128]{2,1,0:T(8,128)S(1)}, u32[]{:S(2)}, u32[]{:S(2)}) collective-permute-start(f32[4,8,128]{2,1,0:T(8,128)S(1)} %get-tuple-element.11), channel_id=1, source_target_pairs={{0,8},{4,12},{8,0},{12,4},{1,9},{5,13},{9,1},{13,5},{2,10},{6,14},... | collective-permute-start | bytes 49160 | tf_op jit(solution)/shard_map/ppermute | solution.py:91
  39.3 2.8 %collective-permute-start.7 = (f32[4,8,128]{2,1,0:T(8,128)S(1)}, f32[4,8,128]{2,1,0:T(8,128)S(1)}, u32[]{:S(2)}, u32[]{:S(2)}) collective-permute-start(f32[4,8,128]{2,1,0:T(8,128)S(1)} %get-tuple-element.10), channel_id=1, source_target_pairs={{0,12},{4,0},{8,4},{12,8},{1,13},{5,1},{9,5},{13,9},{2,14},{6,2},{... | collective-permute-start | bytes 49160 | tf_op jit(solution)/shard_map/ppermute | solution.py:91
  42.2 0.6 subtract_reduce_fusion.7
  42.8 0.7 %fusion.9 = f32[4,8,128]{2,1,0:T(8,128)S(1)} fusion(f32[4,8,128]{2,1,0:T(8,128)S(1)} %subtract_reduce_fusion.7, f32[4,128,128]{2,1,0:T(8,128)S(1)} %get-tuple-element.30, f32[4,8,128]{2,1,0:T(8,128)S(1)} %broadcast_multiply_fusion.3), kind=kLoop, calls=%fused_computation.33 | loop fusion | flops 1568768 | bytes 311296 | tf_op jit(solution)/shard_map/reduce_sum | solution.py:72
  43.7 0.6 subtract_reduce_fusion.4
  44.3 0.7 %fusion.15 = f32[4,8,128]{2,1,0:T(8,128)S(1)} fusion(f32[4,8,128]{2,1,0:T(8,128)S(1)} %subtract_reduce_fusion.4, f32[4,128,128]{2,1,0:T(8,128)S(1)} %get-tuple-element.37, f32[4,8,128]{2,1,0:T(8,128)S(1)} %broadcast_multiply_fusion), kind=kLoop, calls=%fused_computation.39 | loop fusion | flops 1568768 | bytes 311296 | tf_op jit(solution)/shard_map/reduce_sum | solution.py:72
  45.1 0.6 subtract_reduce_fusion.5
  45.7 0.7 %fusion.13 = f32[4,8,128]{2,1,0:T(8,128)S(1)} fusion(f32[4,8,128]{2,1,0:T(8,128)S(1)} %subtract_reduce_fusion.5, f32[4,128,128]{2,1,0:T(8,128)S(1)} %get-tuple-element.32, f32[4,8,128]{2,1,0:T(8,128)S(1)} %broadcast_multiply_fusion.1), kind=kLoop, calls=%fused_computation.37 | loop fusion | flops 1568768 | bytes 311296 | tf_op jit(solution)/shard_map/reduce_sum | solution.py:72
  46.5 0.6 subtract_reduce_fusion.6
  47.2 0.7 %fusion.11 = f32[4,8,128]{2,1,0:T(8,128)S(1)} fusion(f32[4,8,128]{2,1,0:T(8,128)S(1)} %subtract_reduce_fusion.6, f32[4,128,128]{2,1,0:T(8,128)S(1)} %get-tuple-element.31, f32[4,8,128]{2,1,0:T(8,128)S(1)} %broadcast_multiply_fusion.2), kind=kLoop, calls=%fused_computation.35 | loop fusion | flops 1568768 | bytes 311296 | tf_op jit(solution)/shard_map/reduce_sum | solution.py:72
  48.1 0.2 select_reduce_fusion.10
  48.7 0.2 select_reduce_fusion.8
  48.9 0.6 subtract_reduce_fusion
  49.5 0.7 %fusion.23 = f32[4,8,128]{2,1,0:T(8,128)S(1)} fusion(f32[4,8,128]{2,1,0:T(8,128)S(1)} %subtract_reduce_fusion, f32[4,8,128]{2,1,0:T(8,128)S(1)} %get-tuple-element.41, f32[4,128,128]{2,1,0:T(8,128)S(1)} %get-tuple-element.34), kind=kLoop, calls=%fused_computation.47 | loop fusion | flops 1568768 | bytes 311296 | tf_op jit(solution)/shard_map/reduce_sum | solution.py:72
  50.4 1.5 %collective-permute-start.13 = (f32[4,8,128]{2,1,0:T(8,128)S(1)}, f32[4,8,128]{2,1,0:T(8,128)S(1)}, u32[]{:S(2)}, u32[]{:S(2)}) collective-permute-start(f32[4,8,128]{2,1,0:T(8,128)S(1)} %add_select_fusion), channel_id=1, source_target_pairs={{0,12},{4,0},{8,4},{12,8},{1,13},{5,1},{9,5},{13,9},{2,14},{6,2},{... | collective-permute-start | bytes 49160 | tf_op jit(solution)/shard_map/ppermute | solution.py:84
  51.9 0.6 subtract_reduce_fusion.1
  52.5 0.7 %fusion.21 = f32[4,8,128]{2,1,0:T(8,128)S(1)} fusion(f32[4,8,128]{2,1,0:T(8,128)S(1)} %subtract_reduce_fusion.1, f32[4,8,128]{2,1,0:T(8,128)S(1)} %get-tuple-element.42, f32[4,128,128]{2,1,0:T(8,128)S(1)} %get-tuple-element.35), kind=kLoop, calls=%fused_computation.45 | loop fusion | flops 1568768 | bytes 311296 | tf_op jit(solution)/shard_map/reduce_sum | solution.py:72
  53.3 0.2 collective-permute-start.12
  53.6 0.6 subtract_reduce_fusion.2
  54.2 0.7 %fusion.19 = f32[4,8,128]{2,1,0:T(8,128)S(1)} fusion(f32[4,8,128]{2,1,0:T(8,128)S(1)} %subtract_reduce_fusion.2, f32[4,8,128]{2,1,0:T(8,128)S(1)} %get-tuple-element.43, f32[4,128,128]{2,1,0:T(8,128)S(1)} %get-tuple-element.36), kind=kLoop, calls=%fused_computation.43 | loop fusion | flops 1568768 | bytes 311296 | tf_op jit(solution)/shard_map/reduce_sum | solution.py:72
  55.0 2.0 %collective-permute-start.11 = (f32[4,8,128]{2,1,0:T(8,128)S(1)}, f32[4,8,128]{2,1,0:T(8,128)S(1)}, u32[]{:S(2)}, u32[]{:S(2)}) collective-permute-start(f32[4,8,128]{2,1,0:T(8,128)S(1)} %add_select_fusion.2), channel_id=1, source_target_pairs={{0,4},{4,8},{8,12},{12,0},{1,5},{5,9},{9,13},{13,1},{2,6},{6,10},{... | collective-permute-start | bytes 49160 | tf_op jit(solution)/shard_map/ppermute | solution.py:84
  57.0 0.6 subtract_reduce_fusion.3
  57.7 0.7 %fusion.17 = f32[4,8,128]{2,1,0:T(8,128)S(1)} fusion(f32[4,8,128]{2,1,0:T(8,128)S(1)} %subtract_reduce_fusion.3, f32[4,8,128]{2,1,0:T(8,128)S(1)} %get-tuple-element.40, f32[4,128,128]{2,1,0:T(8,128)S(1)} %get-tuple-element.33), kind=kLoop, calls=%fused_computation.41 | loop fusion | flops 1568768 | bytes 311296 | tf_op jit(solution)/shard_map/reduce_sum | solution.py:72
  58.5 2.1 %collective-permute-done.11 = f32[4,8,128]{2,1,0:T(8,128)S(1)} collective-permute-done((f32[4,8,128]{2,1,0:T(8,128)S(1)}, f32[4,8,128]{2,1,0:T(8,128)S(1)}, u32[]{:S(2)}, u32[]{:S(2)}) %collective-permute-start.11) | collective-permute-done | bytes 16416 | tf_op jit(solution)/shard_map/ppermute | solution.py:84
  60.7 0.2 select_reduce_fusion.6
  61.2 0.6 %copy.149 = f32[2,8,8,128]{3,1,2,0:T(8,128)} copy(f32[2,8,8,128]{3,2,1,0:T(8,128)S(1)} %bitcast.67) | data formatting | bytes 131072
  61.9 0.5 collective-permute-done.14
  62.4 0.6 %copy.148 = f32[2,8,8,128]{3,1,2,0:T(8,128)} copy(f32[2,8,8,128]{3,2,1,0:T(8,128)S(1)} %bitcast.68) | data formatting | bytes 131072
  (118 shorter events, 5.3 us)
Async XLA Ops:
  0.6 12.4 %copy-start = (bf16[64,1024]{1,0:T(8,128)(2,1)S(1)}, bf16[64,1024]{1,0:T(8,128)(2,1)}, u32[]{:S(2)}) copy-start(bf16[64,1024]{1,0:T(8,128)(2,1)} %param.9) | copy-start | bytes 393220
  2.3 15.2 %collective-permute-start.3 = (bf16[65,8,128]{2,1,0:T(8,128)(2,1)S(1)}, bf16[65,8,128]{2,1,0:T(8,128)(2,1)S(1)}, u32[]{:S(2)}, u32[]{:S(2)}) collective-permute-start(bf16[65,8,128]{2,1,0:T(8,128)(2,1)S(1)} %pad_maximum_fusion.1), channel_id=1, source_target_pairs={{0,4},{4,8},{8,12},{12,0},{1,5},{5,9},{9,13},{13,1},{2,6},{6,10},{... | collective-permute-start | bytes 399368 | tf_op jit(solution)/shard_map/ppermute | solution.py:91
  5.4 12.5 %collective-permute-start.2 = (bf16[65,8,128]{2,1,0:T(8,128)(2,1)S(1)}, bf16[65,8,128]{2,1,0:T(8,128)(2,1)S(1)}, u32[]{:S(2)}, u32[]{:S(2)}) collective-permute-start(bf16[65,8,128]{2,1,0:T(8,128)(2,1)S(1)} %pad_maximum_fusion.1), channel_id=1, source_target_pairs={{0,8},{4,12},{8,0},{12,4},{1,9},{5,13},{9,1},{13,5},{2,10},{6,14},... | collective-permute-start | bytes 399368 | tf_op jit(solution)/shard_map/ppermute | solution.py:91
  8.0 10.3 %collective-permute-start.1 = (bf16[65,8,128]{2,1,0:T(8,128)(2,1)S(1)}, bf16[65,8,128]{2,1,0:T(8,128)(2,1)S(1)}, u32[]{:S(2)}, u32[]{:S(2)}) collective-permute-start(bf16[65,8,128]{2,1,0:T(8,128)(2,1)S(1)} %pad_maximum_fusion.1), channel_id=1, source_target_pairs={{0,12},{4,0},{8,4},{12,8},{1,13},{5,1},{9,5},{13,9},{2,14},{6,2},{... | collective-permute-start | bytes 399368 | tf_op jit(solution)/shard_map/ppermute | solution.py:91
  10.7 2.4 %collective-permute-start = (s32[3,4,2]{1,2,0:T(2,128)S(1)}, s32[3,4,2]{1,2,0:T(2,128)S(1)}, u32[]{:S(2)}, u32[]{:S(2)}) collective-permute-start(s32[3,4,2]{1,2,0:T(2,128)S(1)} %get-tuple-element.53), channel_id=1, source_target_pairs={{0,1},{1,0},{2,3},{3,2},{4,5},{5,4},{6,7},{7,6},{8,9},{9,8},{10,11... | collective-permute-start | bytes 296 | tf_op jit(solution)/shard_map/ppermute | solution.py:78
  24.6 7.8 %collective-permute-start.6 = (f32[4,9,128]{2,0,1:T(4,128)S(1)}, f32[4,9,128]{2,0,1:T(4,128)S(1)}, u32[]{:S(2)}, u32[]{:S(2)}) collective-permute-start(f32[4,9,128]{2,0,1:T(4,128)S(1)} %pad_maximum_fusion.8), channel_id=1, source_target_pairs={{0,12},{4,0},{8,4},{12,8},{1,13},{5,1},{9,5},{13,9},{2,14},{6,2},{... | collective-permute-start | bytes 55304 | tf_op jit(solution)/shard_map/ppermute | solution.py:84
  28.8 4.7 %collective-permute-start.5 = (f32[4,9,128]{2,0,1:T(4,128)S(1)}, f32[4,9,128]{2,0,1:T(4,128)S(1)}, u32[]{:S(2)}, u32[]{:S(2)}) collective-permute-start(f32[4,9,128]{2,0,1:T(4,128)S(1)} %pad_maximum_fusion.7), channel_id=1, source_target_pairs={{0,8},{4,12},{8,0},{12,4},{1,9},{5,13},{9,1},{13,5},{2,10},{6,14},... | collective-permute-start | bytes 55304 | tf_op jit(solution)/shard_map/ppermute | solution.py:84
  31.0 5.6 %collective-permute-start.4 = (f32[4,9,128]{2,0,1:T(4,128)S(1)}, f32[4,9,128]{2,0,1:T(4,128)S(1)}, u32[]{:S(2)}, u32[]{:S(2)}) collective-permute-start(f32[4,9,128]{2,0,1:T(4,128)S(1)} %pad_maximum_fusion.6), channel_id=1, source_target_pairs={{0,4},{4,8},{8,12},{12,0},{1,5},{5,9},{9,13},{13,1},{2,6},{6,10},{... | collective-permute-start | bytes 55304 | tf_op jit(solution)/shard_map/ppermute | solution.py:84
  38.1 5.6 %collective-permute-start.9 = (f32[4,8,128]{2,1,0:T(8,128)S(1)}, f32[4,8,128]{2,1,0:T(8,128)S(1)}, u32[]{:S(2)}, u32[]{:S(2)}) collective-permute-start(f32[4,8,128]{2,1,0:T(8,128)S(1)} %get-tuple-element.12), channel_id=1, source_target_pairs={{0,4},{4,8},{8,12},{12,0},{1,5},{5,9},{9,13},{13,1},{2,6},{6,10},{... | collective-permute-start | bytes 49160 | tf_op jit(solution)/shard_map/ppermute | solution.py:91
  38.2 6.9 %collective-permute-start.8 = (f32[4,8,128]{2,1,0:T(8,128)S(1)}, f32[4,8,128]{2,1,0:T(8,128)S(1)}, u32[]{:S(2)}, u32[]{:S(2)}) collective-permute-start(f32[4,8,128]{2,1,0:T(8,128)S(1)} %get-tuple-element.11), channel_id=1, source_target_pairs={{0,8},{4,12},{8,0},{12,4},{1,9},{5,13},{9,1},{13,5},{2,10},{6,14},... | collective-permute-start | bytes 49160 | tf_op jit(solution)/shard_map/ppermute | solution.py:91
  39.3 7.2 %collective-permute-start.7 = (f32[4,8,128]{2,1,0:T(8,128)S(1)}, f32[4,8,128]{2,1,0:T(8,128)S(1)}, u32[]{:S(2)}, u32[]{:S(2)}) collective-permute-start(f32[4,8,128]{2,1,0:T(8,128)S(1)} %get-tuple-element.10), channel_id=1, source_target_pairs={{0,12},{4,0},{8,4},{12,8},{1,13},{5,1},{9,5},{13,9},{2,14},{6,2},{... | collective-permute-start | bytes 49160 | tf_op jit(solution)/shard_map/ppermute | solution.py:91
  48.6 12.6 %collective-permute-start.10 = (f32[8,8,128]{2,1,0:T(8,128)S(1)}, f32[8,8,128]{2,1,0:T(8,128)S(1)}, u32[]{:S(2)}, u32[]{:S(2)}) collective-permute-start(f32[8,8,128]{2,1,0:T(8,128)S(1)} %bitcast_subtract_fusion.2), channel_id=1, source_target_pairs={{0,1},{1,0},{2,3},{3,2},{4,5},{5,4},{6,7},{7,6},{8,9},{9,8},{10,11... | collective-permute-start | bytes 98312 | tf_op jit(solution)/shard_map/ppermute | solution.py:78
  50.4 8.1 %collective-permute-start.13 = (f32[4,8,128]{2,1,0:T(8,128)S(1)}, f32[4,8,128]{2,1,0:T(8,128)S(1)}, u32[]{:S(2)}, u32[]{:S(2)}) collective-permute-start(f32[4,8,128]{2,1,0:T(8,128)S(1)} %add_select_fusion), channel_id=1, source_target_pairs={{0,12},{4,0},{8,4},{12,8},{1,13},{5,1},{9,5},{13,9},{2,14},{6,2},{... | collective-permute-start | bytes 49160 | tf_op jit(solution)/shard_map/ppermute | solution.py:84
  53.3 5.2 %collective-permute-start.12 = (f32[4,8,128]{2,1,0:T(8,128)S(1)}, f32[4,8,128]{2,1,0:T(8,128)S(1)}, u32[]{:S(2)}, u32[]{:S(2)}) collective-permute-start(f32[4,8,128]{2,1,0:T(8,128)S(1)} %add_select_fusion.1), channel_id=1, source_target_pairs={{0,8},{4,12},{8,0},{12,4},{1,9},{5,13},{9,1},{13,5},{2,10},{6,14},... | collective-permute-start | bytes 49160 | tf_op jit(solution)/shard_map/ppermute | solution.py:84
  55.0 5.5 %collective-permute-start.11 = (f32[4,8,128]{2,1,0:T(8,128)S(1)}, f32[4,8,128]{2,1,0:T(8,128)S(1)}, u32[]{:S(2)}, u32[]{:S(2)}) collective-permute-start(f32[4,8,128]{2,1,0:T(8,128)S(1)} %add_select_fusion.2), channel_id=1, source_target_pairs={{0,4},{4,8},{8,12},{12,0},{1,5},{5,9},{9,13},{13,1},{2,6},{6,10},{... | collective-permute-start | bytes 49160 | tf_op jit(solution)/shard_map/ppermute | solution.py:84
  61.1 1.3 %collective-permute-start.14 = (f32[8,8,128]{2,1,0:T(8,128)S(1)}, f32[8,8,128]{2,1,0:T(8,128)S(1)}, u32[]{:S(2)}, u32[]{:S(2)}) collective-permute-start(f32[8,8,128]{2,1,0:T(8,128)S(1)} %bitcast_subtract_fusion), channel_id=1, source_target_pairs={{0,1},{1,0},{2,3},{3,2},{4,5},{5,4},{6,7},{7,6},{8,9},{9,8},{10,11... | collective-permute-start | bytes 98312 | tf_op jit(solution)/shard_map/ppermute | solution.py:78

commit v10 on v9

--- a/solution.py
+++ b/solution.py
@@ -134,8 +134,10 @@
         wanted = wanted.reshape(peer_count, wide)
         rows_used = rows_used.reshape(slot_count)
         usable = usable.reshape(slot_count)[:, None, None] > 0
-        far = jnp.concatenate(
-            [pick_rows(everything[offset], wanted[offset], blocks) for offset in range(peer_count)], axis=0
+        far = pick_rows(
+            jnp.concatenate(everything, axis=1),
+            (wanted + blocks * jnp.arange(peer_count, dtype=jnp.int32)[:, None]).reshape(slot_count),
+            peer_count * blocks,
         )
         far_y = far[:, :features]
         far_tags = far[:, features]
@@ -143,6 +145,12 @@
         slot_tags = pick_rows(real_tags, rows_used, blocks)[:, 0]
         cost_cols = slot_costs(slot_x, slot_tags, far_y, far_tags) / SMOOTH
         cost_rows = slot_costs(far_y, far_tags, slot_x, slot_tags) / SMOOTH
+
+        def both_halves(mine):
+            other = swap(mine)
+            first = jnp.where(my_sub == 0, mine, other)
+            second = jnp.where(my_sub == 0, other, mine)
+            return jnp.concatenate([first, second], axis=0).reshape(marginals, point_count)
 
         synth_pot = jnp.zeros((half, blocks, BLOCK), jnp.float32)
         real_pot = jnp.zeros((half, blocks, BLOCK), jnp.float32)
@@ -177,7 +185,10 @@
             chunks = [None] * peer_count
             for offset in list(range(1, peer_count)) + [0]:
                 piece = slice(offset * wide, (offset + 1) * wide)
-                scores = (own_rows[piece] / SMOOTH)[:, :, :, None] - cost_cols[piece, None]
+                rows_here = own_rows[piece]
+                if sweep_index == ITERS - 1 and offset == 0:
+                    real_out, rows_here = lax.optimization_barrier((both_halves(real_pot), rows_here))
+                scores = (rows_here / SMOOTH)[:, :, :, None] - cost_cols[piece, None]
                 highest, mass_sum = lse_parts(scores, 2)
                 lse = jnp.where(usable[piece], highest + jnp.log(mass_sum), SENTINEL)
                 if sweep_index == 0:
@@ -193,13 +204,7 @@
             block_top, summed = fold_lse(back, requested, blocks)
             synth_pot = finish(log_synth, block_top, summed)
 
-        def both_halves(mine):
-            other = swap(mine)
-            first = jnp.where(my_sub == 0, mine, other)
-            second = jnp.where(my_sub == 0, other, mine)
-            return jnp.concatenate([first, second], axis=0).reshape(marginals, point_count)
-
-        return (both_halves(real_pot), both_halves(synth_pot))
+        return (real_out, both_halves(synth_pot))
 
     return shards
 

time: 63.4 us -> 66.4 us (1.047)
  other arithmetic: 28.6 us -> 30.4 us
  local copies, waits for them, and re-layouts: 4.99 us -> 5.99 us
    reduce_sum x13 -> x10, other arithmetic: 4.56 us -> 6.42 us  [pick_rows(): return jnp.sum(chosen, axis=2, dtype=values.dtype)]
    unnamed x8 -> x6, local copies, waits for them, and re-layouts: 2.26 us -> 3.16 us
    ppermute x3, waiting for transfers between devices: 0.51 us -> 1.2 us  [swap(): return lax.ppermute(value, 'sub', [(0, 1), (1, 0)])]
  transfers between devices with their start and end apart: 15 -> 15, of which waited for: 5 -> 5; matrix products, arithmetic and copies ran while one was open for 38% -> 35% of each run, Pallas kernels for 0% -> 0%
where the time goes in v10:
time: 66.4 us; the launch traced here: 66 us
  other arithmetic  30.4 us (46%)
  starting transfers between devices  18.6 us (28%)
  waiting for transfers between devices  7.45 us (11%)
  local copies, waits for them, and re-layouts  5.99 us (9%)
  matrix products  2.35 us (4%)
  between operations  1.35 us (2%)
    ppermute x6, starting transfers between devices, send_down(): moved.append(lax.ppermute(chunks[offset], 'blk', perm))  10.9 us
    reduce_sum x14, other arithmetic, lse_parts(): jnp.sum(jnp.exp(scores - jnp.expand_dims(highest, axis)), axis=axis)  9.27 us
    reduce_max x11, other arithmetic, lse_parts(): highest = jnp.max(scores, axis=axis)  7.54 us
    ppermute x6, starting transfers between devices, send_up(): moved.append(lax.ppermute(chunks[offset], 'blk', perm))  7.52 us
    reduce_sum x10, other arithmetic, pick_rows(): return jnp.sum(chosen, axis=2, dtype=values.dtype)  6.42 us
    ppermute x6, waiting for transfers between devices, send_up(): moved.append(lax.ppermute(chunks[offset], 'blk', perm))  5.92 us
    unnamed x6, local copies, waits for them, and re-layouts  3.16 us
    dot_general x2, matrix products, slot_costs(): jnp.einsum('gdi,gdj->gij', slot_real, slot_synth, preferred_element_type=...  2.35 us
  transfers between devices with their start and end apart: 15, of which 5 were waited for; matrix products, arithmetic and copies ran while one was open for 35% of the time, Pallas kernels for 0%

profile of v10, /device:TPU:0, one launch (start us, length us, event | category | flops | bytes accessed | tf_op | source)
XLA Modules:
  0.0 66.0 jit_solution(16615741820839754787)
XLA Ops:
  0.6 0.7 %convert_bitcast_fusion.2 = bf16[1,8,128]{2,1,0:T(8,128)(2,1)S(1)} fusion(s32[1024]{0:T(1024)} %param.12), kind=kLoop, calls=%fused_computation.185 | loop fusion | flops 1024 | bytes 6144 | tf_op jit(solution)/shard_map/concatenate | solution.py:116
  1.3 0.9 %copy.136 = bf16[8,8,8,128]{3,2,1,0:T(8,128)(2,1)S(1)} copy(bf16[8,8,8,128]{3,1,2,0:T(8,128)(2,1)} %bitcast.60) | data formatting | bytes 262144
  2.3 3.1 %collective-permute-start.3 = (bf16[65,8,128]{2,1,0:T(8,128)(2,1)S(1)}, bf16[65,8,128]{2,1,0:T(8,128)(2,1)S(1)}, u32[]{:S(2)}, u32[]{:S(2)}) collective-permute-start(bf16[65,8,128]{2,1,0:T(8,128)(2,1)S(1)} %pad_maximum_fusion.1), channel_id=1, source_target_pairs={{0,4},{4,8},{8,12},{12,0},{1,5},{5,9},{9,13},{13,1},{2,6},{6,10},{... | collective-permute-start | bytes 399368 | tf_op jit(solution)/shard_map/ppermute | solution.py:91
  5.3 2.6 %collective-permute-start.2 = (bf16[65,8,128]{2,1,0:T(8,128)(2,1)S(1)}, bf16[65,8,128]{2,1,0:T(8,128)(2,1)S(1)}, u32[]{:S(2)}, u32[]{:S(2)}) collective-permute-start(bf16[65,8,128]{2,1,0:T(8,128)(2,1)S(1)} %pad_maximum_fusion.1), channel_id=1, source_target_pairs={{0,8},{4,12},{8,0},{12,4},{1,9},{5,13},{9,1},{13,5},{2,10},{6,14},... | collective-permute-start | bytes 399368 | tf_op jit(solution)/shard_map/ppermute | solution.py:91
  7.9 1.3 %collective-permute-start.1 = (bf16[65,8,128]{2,1,0:T(8,128)(2,1)S(1)}, bf16[65,8,128]{2,1,0:T(8,128)(2,1)S(1)}, u32[]{:S(2)}, u32[]{:S(2)}) collective-permute-start(bf16[65,8,128]{2,1,0:T(8,128)(2,1)S(1)} %pad_maximum_fusion.1), channel_id=1, source_target_pairs={{0,12},{4,0},{8,4},{12,8},{1,13},{5,1},{9,5},{13,9},{2,14},{6,2},{... | collective-permute-start | bytes 399368 | tf_op jit(solution)/shard_map/ppermute | solution.py:91
  9.3 0.7 stack_broadcast_in_dim.2
  9.9 0.7 %fusion.44 = (s32[3,1,4,2]{2,3,0,1:T(2,128)S(1)}, s32[3,4,2]{1,2,0:T(2,128)S(1)}) fusion(s32[1,4,2]{1,2,0:T(2,128)S(1)} %stack_broadcast_in_dim.2, s32[1,4,2]{1,2,0:T(2,128)} %bitcast.68, s32[1,4,2]{1,2,0:T(2,128)} %bitcast.69), kind=kLoop, calls=%fused_computation.192 | loop fusion | flops 48 | bytes 288 | tf_op jit(solution)/shard_map/stack | solution.py:129
  10.7 0.9 %copy.137 = bf16[8,8,8,128]{3,2,1,0:T(8,128)(2,1)S(1)} copy(bf16[8,8,8,128]{3,1,2,0:T(8,128)(2,1)} %bitcast.61) | data formatting | bytes 262144
  11.7 0.7 %convert_bitcast_fusion.1 = bf16[8,128]{1,0:T(8,128)(2,1)S(1)} fusion(s32[1024]{0:T(1024)} %param.11), kind=kLoop, calls=%fused_computation.184 | loop fusion | flops 1024 | bytes 6144 | tf_op jit(solution)/shard_map/convert_element_type | solution.py:115
  12.4 0.8 %multiply_bitcast_fusion.1 = f32[1,8,8,128]{3,1,2,0:T(8,128)S(1)} fusion(s32[16,1024]{1,0:T(8,128)} %param.13, s32[]{:T(128)S(6)} %select_n.263), kind=kLoop, calls=%fused_computation.105 | loop fusion | flops 24576 | bytes 65540
  13.1 0.8 %multiply_bitcast_fusion = f32[1,8,8,128]{3,1,2,0:T(8,128)S(1)} fusion(s32[16,1024]{1,0:T(8,128)} %param.14, s32[]{:T(128)S(6)} %select_n.263), kind=kLoop, calls=%fused_computation.103 | loop fusion | flops 24576 | bytes 65540
  14.1 0.3 select_reduce_fusion.22
  14.7 1.5 %select_reduce_fusion.1 = bf16[16,64,128]{2,1,0:T(8,128)(2,1)S(1)} fusion(pred[16,8]{1,0:T(8,128)(4,1)S(1)} %iota_compare_fusion.2, bf16[64,8,128]{2,1,0:T(8,128)(2,1)S(1)} %bitcast.57), kind=kLoop, calls=%fused_computation.49 | loop fusion | flops 1966080 | bytes 393344 | tf_op jit(solution)/shard_map/reduce_sum | solution.py:26
  16.5 0.3 slice_reduce_fusion.3
  16.8 0.1 fusion.37
  16.9 0.1 copy.126
  18.1 3.4 %select_reduce_fusion = bf16[16,65,128]{2,1,0:T(8,128)(2,1)S(1)} fusion(pred[16,32]{1,0:T(8,128)(4,1)S(1)} %iota_compare_fusion.1, bf16[65,32,128]{2,1,0:T(8,128)(2,1)S(1)} %pad_maximum_fusion), kind=kLoop, calls=%fused_computation | loop fusion | flops 8386560 | bytes 799232 | tf_op jit(solution)/shard_map/reduce_sum | solution.py:26
  21.6 1.2 %fusion.26 = f32[16,128,128]{2,1,0:T(8,128)S(1)} fusion(bf16[16,64,128]{2,1,0:T(8,128)(2,1)S(1)} %select_reduce_fusion.1, f32[16,128]{1,0:T(8,128)S(1)} %broadcast_multiply_fusion.5, f32[16,128]{1,0:T(8,128)S(1)} %broadcast_multiply_fusion.6, bf16[16,128]{1,0:T(8,128)(2,1)S(1)} %select_reduce_fusion.20, bf16[16,128]{1,0:T(8,128)(2,1)S(1)} %bitcast.66, ...), kind=kOutput, calls=%fused_computation.54 | convolution fusion | flops 35127296 | bytes 1597440 | tf_op jit(solution)/shard_map/gdi,gdj->gij/dot_general | solution.py:61
  22.8 1.1 %fusion.27 = f32[16,128,128]{2,1,0:T(8,128)S(1)} fusion(bf16[16,64,128]{2,1,0:T(8,128)(2,1)S(1)} %select_reduce_fusion.1, f32[16,128]{1,0:T(8,128)S(1)} %broadcast_multiply_fusion.6, f32[16,128]{1,0:T(8,128)S(1)} %broadcast_multiply_fusion.5, bf16[16,128]{1,0:T(8,128)(2,1)S(1)} %bitcast.67, bf16[16,128]{1,0:T(8,128)(2,1)S(1)} %select_reduce_fusion.20, ...), kind=kOutput, calls=%fused_computation.55 | convolution fusion | flops 35127296 | bytes 1597440 | tf_op jit(solution)/shard_map/gdi,gdj->gij/dot_general | solution.py:61
  24.2 0.2 exponential_reduce_fusion.2
  24.9 0.2 select_reduce_fusion.12
  25.2 1.3 %subtract_reduce_fusion.8 = (f32[4,8,128]{2,1,0:T(8,128)S(1)}, f32[4,8,128]{2,1,0:T(8,128)S(1)}) fusion(f32[4,128,128]{2,1,0:T(8,128)S(1)} %get-tuple-element.38, f32[4,8,128]{2,1,0:T(8,128)S(1)} %get-tuple-element.51, f32[4,128,128]{2,1,0:T(8,128)S(1)} %get-tuple-element.39, f32[4,8,128]{2,1,0:T(8,128)S(1)} %get-tuple-element.52), kind=kLoop, calls=%fused_computation.18 | loop fusion | flops 2088960 | bytes 589824 | tf_op jit(solution)/shard_map/reduce_max | solution.py:71
  26.5 0.7 %fusion.7 = f32[4,8,128]{2,1,0:T(8,128)S(1)} fusion(f32[4,8,128]{2,1,0:T(8,128)S(1)} %get-tuple-element.56, f32[4,128,128]{2,1,0:T(8,128)S(1)} %get-tuple-element.38, f32[4,8,128]{2,1,0:T(8,128)S(1)} %get-tuple-element.51), kind=kLoop, calls=%fused_computation.32 | loop fusion | flops 1568768 | bytes 311296 | tf_op jit(solution)/shard_map/reduce_sum | solution.py:72
  27.4 3.1 %collective-permute-start.6 = (f32[4,9,128]{2,0,1:T(4,128)S(1)}, f32[4,9,128]{2,0,1:T(4,128)S(1)}, u32[]{:S(2)}, u32[]{:S(2)}) collective-permute-start(f32[4,9,128]{2,0,1:T(4,128)S(1)} %pad_maximum_fusion.8), channel_id=1, source_target_pairs={{0,12},{4,0},{8,4},{12,8},{1,13},{5,1},{9,5},{13,9},{2,14},{6,2},{... | collective-permute-start | bytes 55304 | tf_op jit(solution)/shard_map/ppermute | solution.py:84
  30.5 0.7 %fusion.5 = f32[4,8,128]{2,1,0:T(8,128)S(1)} fusion(f32[4,8,128]{2,1,0:T(8,128)S(1)} %get-tuple-element.57, f32[4,128,128]{2,1,0:T(8,128)S(1)} %get-tuple-element.39, f32[4,8,128]{2,1,0:T(8,128)S(1)} %get-tuple-element.52), kind=kLoop, calls=%fused_computation.30 | loop fusion | flops 1568768 | bytes 311296 | tf_op jit(solution)/shard_map/reduce_sum | solution.py:72
  31.4 0.4 collective-permute-start.5
  31.8 1.3 %subtract_reduce_fusion.10 = (f32[4,8,128]{2,1,0:T(8,128)S(1)}, f32[4,8,128]{2,1,0:T(8,128)S(1)}) fusion(f32[4,128,128]{2,1,0:T(8,128)S(1)} %get-tuple-element.40, f32[4,8,128]{2,1,0:T(8,128)S(1)} %get-tuple-element.53, f32[4,128,128]{2,1,0:T(8,128)S(1)} %get-tuple-element.37, f32[4,8,128]{2,1,0:T(8,128)S(1)} %get-tuple-element.50), kind=kLoop, calls=%fused_computation.22 | loop fusion | flops 2088960 | bytes 589824 | tf_op jit(solution)/shard_map/reduce_max | solution.py:71
  33.1 0.7 %fusion.3 = f32[4,8,128]{2,1,0:T(8,128)S(1)} fusion(f32[4,8,128]{2,1,0:T(8,128)S(1)} %get-tuple-element.58, f32[4,128,128]{2,1,0:T(8,128)S(1)} %get-tuple-element.40, f32[4,8,128]{2,1,0:T(8,128)S(1)} %get-tuple-element.53), kind=kLoop, calls=%fused_computation.28 | loop fusion | flops 1568768 | bytes 311296 | tf_op jit(solution)/shard_map/reduce_sum | solution.py:72
  34.0 0.2 collective-permute-start.4
  34.2 0.7 %fusion.1 = f32[4,8,128]{2,1,0:T(8,128)S(1)} fusion(f32[4,8,128]{2,1,0:T(8,128)S(1)} %get-tuple-element.59, f32[4,128,128]{2,1,0:T(8,128)S(1)} %get-tuple-element.37, f32[4,8,128]{2,1,0:T(8,128)S(1)} %get-tuple-element.50), kind=kLoop, calls=%fused_computation.26 | loop fusion | flops 1568768 | bytes 311296 | tf_op jit(solution)/shard_map/reduce_sum | solution.py:72
  35.1 1.1 %collective-permute-done.5 = f32[4,9,128]{2,0,1:T(4,128)S(1)} collective-permute-done((f32[4,9,128]{2,0,1:T(4,128)S(1)}, f32[4,9,128]{2,0,1:T(4,128)S(1)}, u32[]{:S(2)}, u32[]{:S(2)}) %collective-permute-start.5) | collective-permute-done | bytes 18464 | tf_op jit(solution)/shard_map/ppermute | solution.py:84
  36.1 3.5 %collective-permute-done.4 = f32[4,9,128]{2,0,1:T(4,128)S(1)} collective-permute-done((f32[4,9,128]{2,0,1:T(4,128)S(1)}, f32[4,9,128]{2,0,1:T(4,128)S(1)}, u32[]{:S(2)}, u32[]{:S(2)}) %collective-permute-start.4) | collective-permute-done | bytes 18464 | tf_op jit(solution)/shard_map/ppermute | solution.py:84
  40.0 0.2 select_reduce_fusion.10
  40.4 0.1 slice_reduce_fusion.7
  40.9 0.2 select_reduce_fusion.16
  41.2 0.8 %collective-permute-start.8 = (f32[4,8,128]{2,1,0:T(8,128)S(1)}, f32[4,8,128]{2,1,0:T(8,128)S(1)}, u32[]{:S(2)}, u32[]{:S(2)}) collective-permute-start(f32[4,8,128]{2,1,0:T(8,128)S(1)} %get-tuple-element.15), channel_id=1, source_target_pairs={{0,8},{4,12},{8,0},{12,4},{1,9},{5,13},{9,1},{13,5},{2,10},{6,14},... | collective-permute-start | bytes 49160 | tf_op jit(solution)/shard_map/ppermute | solution.py:91
  42.0 3.0 %collective-permute-start.7 = (f32[4,8,128]{2,1,0:T(8,128)S(1)}, f32[4,8,128]{2,1,0:T(8,128)S(1)}, u32[]{:S(2)}, u32[]{:S(2)}) collective-permute-start(f32[4,8,128]{2,1,0:T(8,128)S(1)} %get-tuple-element.14), channel_id=1, source_target_pairs={{0,12},{4,0},{8,4},{12,8},{1,13},{5,1},{9,5},{13,9},{2,14},{6,2},{... | collective-permute-start | bytes 49160 | tf_op jit(solution)/shard_map/ppermute | solution.py:91
  45.0 0.6 subtract_reduce_fusion.7
  45.6 0.7 %fusion.9 = f32[4,8,128]{2,1,0:T(8,128)S(1)} fusion(f32[4,8,128]{2,1,0:T(8,128)S(1)} %subtract_reduce_fusion.7, f32[4,128,128]{2,1,0:T(8,128)S(1)} %get-tuple-element.34, f32[4,8,128]{2,1,0:T(8,128)S(1)} %broadcast_multiply_fusion.4), kind=kLoop, calls=%fused_computation.34 | loop fusion | flops 1568768 | bytes 311296 | tf_op jit(solution)/shard_map/reduce_sum | solution.py:72
  46.4 0.3 collective-permute-done.9
  46.7 0.6 subtract_reduce_fusion.4
  47.3 0.7 %fusion.15 = f32[4,8,128]{2,1,0:T(8,128)S(1)} fusion(f32[4,8,128]{2,1,0:T(8,128)S(1)} %subtract_reduce_fusion.4, f32[4,128,128]{2,1,0:T(8,128)S(1)} %get-tuple-element.41, f32[4,8,128]{2,1,0:T(8,128)S(1)} %broadcast_multiply_fusion.1), kind=kLoop, calls=%fused_computation.40 | loop fusion | flops 1568768 | bytes 311296 | tf_op jit(solution)/shard_map/reduce_sum | solution.py:72
  48.1 0.6 subtract_reduce_fusion.5
  48.8 0.7 %fusion.13 = f32[4,8,128]{2,1,0:T(8,128)S(1)} fusion(f32[4,8,128]{2,1,0:T(8,128)S(1)} %subtract_reduce_fusion.5, f32[4,128,128]{2,1,0:T(8,128)S(1)} %get-tuple-element.36, f32[4,8,128]{2,1,0:T(8,128)S(1)} %broadcast_multiply_fusion.2), kind=kLoop, calls=%fused_computation.38 | loop fusion | flops 1568768 | bytes 311296 | tf_op jit(solution)/shard_map/reduce_sum | solution.py:72
  49.5 0.6 subtract_reduce_fusion.6
  50.3 0.7 %fusion.11 = f32[4,8,128]{2,1,0:T(8,128)S(1)} fusion(f32[4,8,128]{2,1,0:T(8,128)S(1)} %subtract_reduce_fusion.6, f32[4,128,128]{2,1,0:T(8,128)S(1)} %get-tuple-element.35, f32[4,8,128]{2,1,0:T(8,128)S(1)} %broadcast_multiply_fusion.3), kind=kLoop, calls=%fused_computation.36 | loop fusion | flops 1568768 | bytes 311296 | tf_op jit(solution)/shard_map/reduce_sum | solution.py:72
  51.1 0.2 select_reduce_fusion.7
  51.7 0.2 select_reduce_fusion.5
  51.9 0.6 subtract_reduce_fusion
  52.6 0.7 %fusion.23 = f32[4,8,128]{2,1,0:T(8,128)S(1)} fusion(f32[4,8,128]{2,1,0:T(8,128)S(1)} %subtract_reduce_fusion, f32[4,8,128]{2,1,0:T(8,128)S(1)} %get-tuple-element.45, f32[4,128,128]{2,1,0:T(8,128)S(1)} %get-tuple-element.38), kind=kLoop, calls=%fused_computation.48 | loop fusion | flops 1568768 | bytes 311296 | tf_op jit(solution)/shard_map/reduce_sum | solution.py:72
  53.4 1.5 %collective-permute-start.13 = (f32[4,8,128]{2,1,0:T(8,128)S(1)}, f32[4,8,128]{2,1,0:T(8,128)S(1)}, u32[]{:S(2)}, u32[]{:S(2)}) collective-permute-start(f32[4,8,128]{2,1,0:T(8,128)S(1)} %add_select_fusion), channel_id=1, source_target_pairs={{0,12},{4,0},{8,4},{12,8},{1,13},{5,1},{9,5},{13,9},{2,14},{6,2},{... | collective-permute-start | bytes 49160 | tf_op jit(solution)/shard_map/ppermute | solution.py:84
  54.9 0.6 subtract_reduce_fusion.1
  55.5 0.7 %fusion.21 = f32[4,8,128]{2,1,0:T(8,128)S(1)} fusion(f32[4,8,128]{2,1,0:T(8,128)S(1)} %subtract_reduce_fusion.1, f32[4,8,128]{2,1,0:T(8,128)S(1)} %get-tuple-element.46, f32[4,128,128]{2,1,0:T(8,128)S(1)} %get-tuple-element.39), kind=kLoop, calls=%fused_computation.46 | loop fusion | flops 1568768 | bytes 311296 | tf_op jit(solution)/shard_map/reduce_sum | solution.py:72
  56.4 0.2 collective-permute-start.12
  56.6 0.6 subtract_reduce_fusion.2
  57.2 0.7 %fusion.19 = f32[4,8,128]{2,1,0:T(8,128)S(1)} fusion(f32[4,8,128]{2,1,0:T(8,128)S(1)} %subtract_reduce_fusion.2, f32[4,8,128]{2,1,0:T(8,128)S(1)} %get-tuple-element.44, f32[4,128,128]{2,1,0:T(8,128)S(1)} %get-tuple-element.40), kind=kLoop, calls=%fused_computation.44 | loop fusion | flops 1568768 | bytes 311296 | tf_op jit(solution)/shard_map/reduce_sum | solution.py:72
  58.0 2.0 %collective-permute-start.11 = (f32[4,8,128]{2,1,0:T(8,128)S(1)}, f32[4,8,128]{2,1,0:T(8,128)S(1)}, u32[]{:S(2)}, u32[]{:S(2)}) collective-permute-start(f32[4,8,128]{2,1,0:T(8,128)S(1)} %add_select_fusion.2), channel_id=1, source_target_pairs={{0,4},{4,8},{8,12},{12,0},{1,5},{5,9},{9,13},{13,1},{2,6},{6,10},{... | collective-permute-start | bytes 49160 | tf_op jit(solution)/shard_map/ppermute | solution.py:84
  60.1 0.6 copy.150
  60.7 0.6 subtract_reduce_fusion.3
  61.4 0.7 %fusion.17 = f32[4,8,128]{2,1,0:T(8,128)S(1)} fusion(f32[4,8,128]{2,1,0:T(8,128)S(1)} %subtract_reduce_fusion.3, f32[4,8,128]{2,1,0:T(8,128)S(1)} %broadcast_multiply_fusion, f32[4,128,128]{2,1,0:T(8,128)S(1)} %get-tuple-element.37), kind=kLoop, calls=%fused_computation.42 | loop fusion | flops 1568768 | bytes 311296 | tf_op jit(solution)/shard_map/reduce_sum | solution.py:72
  62.2 1.4 %collective-permute-done.11 = f32[4,8,128]{2,1,0:T(8,128)S(1)} collective-permute-done((f32[4,8,128]{2,1,0:T(8,128)S(1)}, f32[4,8,128]{2,1,0:T(8,128)S(1)}, u32[]{:S(2)}, u32[]{:S(2)}) %collective-permute-start.11) | collective-permute-done | bytes 16416 | tf_op jit(solution)/shard_map/ppermute | solution.py:84
  63.7 0.2 select_reduce_fusion.3
  64.2 1.2 %collective-permute-done.14 = f32[8,8,128]{2,1,0:T(8,128)S(1)} collective-permute-done((f32[8,8,128]{2,1,0:T(8,128)S(1)}, f32[8,8,128]{2,1,0:T(8,128)S(1)}, u32[]{:S(2)}, u32[]{:S(2)}) %collective-permute-start.14) | collective-permute-done | bytes 32800 | tf_op jit(solution)/shard_map/ppermute | solution.py:78
  65.4 0.6 copy.149
  (112 shorter events, 5.3 us)
Async XLA Ops:
  2.3 15.7 %collective-permute-start.3 = (bf16[65,8,128]{2,1,0:T(8,128)(2,1)S(1)}, bf16[65,8,128]{2,1,0:T(8,128)(2,1)S(1)}, u32[]{:S(2)}, u32[]{:S(2)}) collective-permute-start(bf16[65,8,128]{2,1,0:T(8,128)(2,1)S(1)} %pad_maximum_fusion.1), channel_id=1, source_target_pairs={{0,4},{4,8},{8,12},{12,0},{1,5},{5,9},{9,13},{13,1},{2,6},{6,10},{... | collective-permute-start | bytes 399368 | tf_op jit(solution)/shard_map/ppermute | solution.py:91
  5.3 12.6 %collective-permute-start.2 = (bf16[65,8,128]{2,1,0:T(8,128)(2,1)S(1)}, bf16[65,8,128]{2,1,0:T(8,128)(2,1)S(1)}, u32[]{:S(2)}, u32[]{:S(2)}) collective-permute-start(bf16[65,8,128]{2,1,0:T(8,128)(2,1)S(1)} %pad_maximum_fusion.1), channel_id=1, source_target_pairs={{0,8},{4,12},{8,0},{12,4},{1,9},{5,13},{9,1},{13,5},{2,10},{6,14},... | collective-permute-start | bytes 399368 | tf_op jit(solution)/shard_map/ppermute | solution.py:91
  7.9 10.0 %collective-permute-start.1 = (bf16[65,8,128]{2,1,0:T(8,128)(2,1)S(1)}, bf16[65,8,128]{2,1,0:T(8,128)(2,1)S(1)}, u32[]{:S(2)}, u32[]{:S(2)}) collective-permute-start(bf16[65,8,128]{2,1,0:T(8,128)(2,1)S(1)} %pad_maximum_fusion.1), channel_id=1, source_target_pairs={{0,12},{4,0},{8,4},{12,8},{1,13},{5,1},{9,5},{13,9},{2,14},{6,2},{... | collective-permute-start | bytes 399368 | tf_op jit(solution)/shard_map/ppermute | solution.py:91
  10.6 3.4 %collective-permute-start = (s32[3,4,2]{1,2,0:T(2,128)S(1)}, s32[3,4,2]{1,2,0:T(2,128)S(1)}, u32[]{:S(2)}, u32[]{:S(2)}) collective-permute-start(s32[3,4,2]{1,2,0:T(2,128)S(1)} %get-tuple-element.55), channel_id=1, source_target_pairs={{0,1},{1,0},{2,3},{3,2},{4,5},{5,4},{6,7},{7,6},{8,9},{9,8},{10,11... | collective-permute-start | bytes 296 | tf_op jit(solution)/shard_map/ppermute | solution.py:78
  27.4 7.7 %collective-permute-start.6 = (f32[4,9,128]{2,0,1:T(4,128)S(1)}, f32[4,9,128]{2,0,1:T(4,128)S(1)}, u32[]{:S(2)}, u32[]{:S(2)}) collective-permute-start(f32[4,9,128]{2,0,1:T(4,128)S(1)} %pad_maximum_fusion.8), channel_id=1, source_target_pairs={{0,12},{4,0},{8,4},{12,8},{1,13},{5,1},{9,5},{13,9},{2,14},{6,2},{... | collective-permute-start | bytes 55304 | tf_op jit(solution)/shard_map/ppermute | solution.py:84
  31.4 4.7 %collective-permute-start.5 = (f32[4,9,128]{2,0,1:T(4,128)S(1)}, f32[4,9,128]{2,0,1:T(4,128)S(1)}, u32[]{:S(2)}, u32[]{:S(2)}) collective-permute-start(f32[4,9,128]{2,0,1:T(4,128)S(1)} %pad_maximum_fusion.7), channel_id=1, source_target_pairs={{0,8},{4,12},{8,0},{12,4},{1,9},{5,13},{9,1},{13,5},{2,10},{6,14},... | collective-permute-start | bytes 55304 | tf_op jit(solution)/shard_map/ppermute | solution.py:84
  34.0 5.6 %collective-permute-start.4 = (f32[4,9,128]{2,0,1:T(4,128)S(1)}, f32[4,9,128]{2,0,1:T(4,128)S(1)}, u32[]{:S(2)}, u32[]{:S(2)}) collective-permute-start(f32[4,9,128]{2,0,1:T(4,128)S(1)} %pad_maximum_fusion.6), channel_id=1, source_target_pairs={{0,4},{4,8},{8,12},{12,0},{1,5},{5,9},{9,13},{13,1},{2,6},{6,10},{... | collective-permute-start | bytes 55304 | tf_op jit(solution)/shard_map/ppermute | solution.py:84
  41.1 5.6 %collective-permute-start.9 = (f32[4,8,128]{2,1,0:T(8,128)S(1)}, f32[4,8,128]{2,1,0:T(8,128)S(1)}, u32[]{:S(2)}, u32[]{:S(2)}) collective-permute-start(f32[4,8,128]{2,1,0:T(8,128)S(1)} %get-tuple-element.16), channel_id=1, source_target_pairs={{0,4},{4,8},{8,12},{12,0},{1,5},{5,9},{9,13},{13,1},{2,6},{6,10},{... | collective-permute-start | bytes 49160 | tf_op jit(solution)/shard_map/ppermute | solution.py:91
  41.2 6.9 %collective-permute-start.8 = (f32[4,8,128]{2,1,0:T(8,128)S(1)}, f32[4,8,128]{2,1,0:T(8,128)S(1)}, u32[]{:S(2)}, u32[]{:S(2)}) collective-permute-start(f32[4,8,128]{2,1,0:T(8,128)S(1)} %get-tuple-element.15), channel_id=1, source_target_pairs={{0,8},{4,12},{8,0},{12,4},{1,9},{5,13},{9,1},{13,5},{2,10},{6,14},... | collective-permute-start | bytes 49160 | tf_op jit(solution)/shard_map/ppermute | solution.py:91
  42.0 7.5 %collective-permute-start.7 = (f32[4,8,128]{2,1,0:T(8,128)S(1)}, f32[4,8,128]{2,1,0:T(8,128)S(1)}, u32[]{:S(2)}, u32[]{:S(2)}) collective-permute-start(f32[4,8,128]{2,1,0:T(8,128)S(1)} %get-tuple-element.14), channel_id=1, source_target_pairs={{0,12},{4,0},{8,4},{12,8},{1,13},{5,1},{9,5},{13,9},{2,14},{6,2},{... | collective-permute-start | bytes 49160 | tf_op jit(solution)/shard_map/ppermute | solution.py:91
  51.6 8.5 %collective-permute-start.10 = (f32[8,8,128]{2,1,0:T(8,128)S(1)}, f32[8,8,128]{2,1,0:T(8,128)S(1)}, u32[]{:S(2)}, u32[]{:S(2)}) collective-permute-start(f32[8,8,128]{2,1,0:T(8,128)S(1)} %bitcast_subtract_fusion.2), channel_id=1, source_target_pairs={{0,1},{1,0},{2,3},{3,2},{4,5},{5,4},{6,7},{7,6},{8,9},{9,8},{10,11... | collective-permute-start | bytes 98312 | tf_op jit(solution)/shard_map/ppermute | solution.py:78
  53.4 8.8 %collective-permute-start.13 = (f32[4,8,128]{2,1,0:T(8,128)S(1)}, f32[4,8,128]{2,1,0:T(8,128)S(1)}, u32[]{:S(2)}, u32[]{:S(2)}) collective-permute-start(f32[4,8,128]{2,1,0:T(8,128)S(1)} %add_select_fusion), channel_id=1, source_target_pairs={{0,12},{4,0},{8,4},{12,8},{1,13},{5,1},{9,5},{13,9},{2,14},{6,2},{... | collective-permute-start | bytes 49160 | tf_op jit(solution)/shard_map/ppermute | solution.py:84
  56.4 5.8 %collective-permute-start.12 = (f32[4,8,128]{2,1,0:T(8,128)S(1)}, f32[4,8,128]{2,1,0:T(8,128)S(1)}, u32[]{:S(2)}, u32[]{:S(2)}) collective-permute-start(f32[4,8,128]{2,1,0:T(8,128)S(1)} %add_select_fusion.1), channel_id=1, source_target_pairs={{0,8},{4,12},{8,0},{12,4},{1,9},{5,13},{9,1},{13,5},{2,10},{6,14},... | collective-permute-start | bytes 49160 | tf_op jit(solution)/shard_map/ppermute | solution.py:84
  58.0 5.5 %collective-permute-start.11 = (f32[4,8,128]{2,1,0:T(8,128)S(1)}, f32[4,8,128]{2,1,0:T(8,128)S(1)}, u32[]{:S(2)}, u32[]{:S(2)}) collective-permute-start(f32[4,8,128]{2,1,0:T(8,128)S(1)} %add_select_fusion.2), channel_id=1, source_target_pairs={{0,4},{4,8},{8,12},{12,0},{1,5},{5,9},{9,13},{13,1},{2,6},{6,10},{... | collective-permute-start | bytes 49160 | tf_op jit(solution)/shard_map/ppermute | solution.py:84
  64.1 1.3 %collective-permute-start.14 = (f32[8,8,128]{2,1,0:T(8,128)S(1)}, f32[8,8,128]{2,1,0:T(8,128)S(1)}, u32[]{:S(2)}, u32[]{:S(2)}) collective-permute-start(f32[8,8,128]{2,1,0:T(8,128)S(1)} %bitcast_subtract_fusion), channel_id=1, source_target_pairs={{0,1},{1,0},{2,3},{3,2},{4,5},{5,4},{6,7},{7,6},{8,9},{9,8},{10,11... | collective-permute-start | bytes 98312 | tf_op jit(solution)/shard_map/ppermute | solution.py:78

commit v11 on v9

--- a/solution.py
+++ b/solution.py
@@ -77,19 +77,26 @@
     def swap(value):
         return lax.ppermute(value, "sub", [(0, 1), (1, 0)])
 
-    def send_up(chunks):
+    def partner(index, offset):
+        if n_blk & (n_blk - 1) == 0:
+            return index ^ offset
+        return (index + offset) % n_blk
+
+    def exchange(chunks, upward):
         moved = [chunks[0]]
         for offset in range(1, n_blk):
-            perm = [(index, (index + offset) % n_blk) for index in range(n_blk)]
+            if upward:
+                perm = [(index, partner(index, offset)) for index in range(n_blk)]
+            else:
+                perm = [(partner(index, offset), index) for index in range(n_blk)]
             moved.append(lax.ppermute(chunks[offset], "blk", perm))
         return moved
 
+    def send_up(chunks):
+        return exchange(chunks, True)
+
     def send_down(chunks):
-        moved = [chunks[0]]
-        for offset in range(1, n_blk):
-            perm = [(index, (index - offset) % n_blk) for index in range(n_blk)]
-            moved.append(lax.ppermute(chunks[offset], "blk", perm))
-        return moved
+        return exchange(chunks, False)
 
     def shards(
         real_points,
@@ -123,7 +130,11 @@
             lax.dynamic_slice_in_dim(synth_weight, my_sub * half, half, 0).astype(jnp.float32) + 0.5
         ).reshape(half, blocks, BLOCK)
 
-        peers = (my_blk + jnp.arange(peer_count, dtype=jnp.int32)) % peer_count
+        offsets = jnp.arange(peer_count, dtype=jnp.int32)
+        if peer_count & (peer_count - 1) == 0:
+            peers = jnp.bitwise_xor(my_blk, offsets)
+        else:
+            peers = (my_blk + offsets) % peer_count
         everything = send_down([own_synth] * peer_count)
         lists = jnp.stack([pair_block, pair_row, jnp.broadcast_to(pair_count[:, None], pair_block.shape)])
         lists = jnp.stack([lists, swap(lists)], axis=1)

time: 63.4 us -> 61.2 us (0.965)
  waiting for transfers between devices: 6.88 us -> 3.96 us
    ppermute x12, waiting for transfers between devices: 6.37 us -> 3.45 us  [exchange(): moved.append(lax.ppermute(chunks[offset], 'blk', perm))]
  transfers between devices with their start and end apart: 15 -> 15, of which waited for: 5 -> 4; matrix products, arithmetic and copies ran while one was open for 38% -> 40% of each run, Pallas kernels for 0% -> 0%
where the time goes in v11:
time: 61.2 us; the launch traced here: 60.9 us
  other arithmetic  28.8 us (47%)
  starting transfers between devices  19.2 us (31%)
  local copies, waits for them, and re-layouts  4.99 us (8%)
  waiting for transfers between devices  3.96 us (6%)
  matrix products  2.53 us (4%)
  between operations  1.37 us (2%)
    ppermute x12, starting transfers between devices, exchange(): moved.append(lax.ppermute(chunks[offset], 'blk', perm))  19.1 us
    reduce_sum x14, other arithmetic, lse_parts(): jnp.sum(jnp.exp(scores - jnp.expand_dims(highest, axis)), axis=axis)  9.49 us
    reduce_max x11, other arithmetic, lse_parts(): highest = jnp.max(scores, axis=axis)  7.55 us
    reduce_sum x13, other arithmetic, pick_rows(): return jnp.sum(chosen, axis=2, dtype=values.dtype)  4.56 us
    ppermute x12, waiting for transfers between devices, exchange(): moved.append(lax.ppermute(chunks[offset], 'blk', perm))  3.45 us
    dot_general x2, matrix products, slot_costs(): jnp.einsum('gdi,gdj->gij', slot_real, slot_synth, preferred_element_type=...  2.53 us
    unnamed x8, local copies, waits for them, and re-layouts  2.26 us
    unnamed x2, other arithmetic  1.55 us
  transfers between devices with their start and end apart: 15, of which 4 were waited for; matrix products, arithmetic and copies ran while one was open for 40% of the time, Pallas kernels for 0%

profile of v11, /device:TPU:0, one launch (start us, length us, event | category | flops | bytes accessed | tf_op | source)
XLA Modules:
  0.0 60.9 jit_solution(8335601247416763500)
XLA Ops:
  0.6 0.7 %convert_bitcast_fusion.3 = (bf16[1,1,8,128]{3,2,1,0:T(8,128)(2,1)S(1)}, bf16[1,8,128]{2,1,0:T(8,128)(2,1)S(1)}) fusion(s32[1024]{0:T(1024)} %param.12), kind=kLoop, calls=%fused_computation.189 | loop fusion | flops 1024 | bytes 8192 | tf_op jit(solution)/shard_map/concatenate | solution.py:123
  1.4 0.9 %copy.134 = bf16[8,8,8,128]{3,2,1,0:T(8,128)(2,1)S(1)} copy(bf16[8,8,8,128]{3,1,2,0:T(8,128)(2,1)} %bitcast.69) | data formatting | bytes 262144
  2.3 5.1 %collective-permute-start.3 = (bf16[65,8,128]{2,1,0:T(8,128)(2,1)S(1)}, bf16[65,8,128]{2,1,0:T(8,128)(2,1)S(1)}, u32[]{:S(2)}, u32[]{:S(2)}) collective-permute-start(bf16[65,8,128]{2,1,0:T(8,128)(2,1)S(1)} %pad_maximum_fusion.1), channel_id=1, source_target_pairs={{12,0},{8,4},{4,8},{0,12},{13,1},{9,5},{5,9},{1,13},{14,2},{10,6},... | collective-permute-start | bytes 399368 | tf_op jit(solution)/shard_map/ppermute | solution.py:92
  7.4 0.6 %collective-permute-start.1 = (bf16[65,8,128]{2,1,0:T(8,128)(2,1)S(1)}, bf16[65,8,128]{2,1,0:T(8,128)(2,1)S(1)}, u32[]{:S(2)}, u32[]{:S(2)}) collective-permute-start(bf16[65,8,128]{2,1,0:T(8,128)(2,1)S(1)} %pad_maximum_fusion.1), channel_id=1, source_target_pairs={{4,0},{0,4},{12,8},{8,12},{5,1},{1,5},{13,9},{9,13},{6,2},{2,6},{1... | collective-permute-start | bytes 399368 | tf_op jit(solution)/shard_map/ppermute | solution.py:92
  8.1 0.7 %stack_broadcast_in_dim.2 = s32[1,4,2]{1,2,0:T(2,128)S(1)} broadcast(s32[4]{0:T(128)} %param.17), dimensions={1} | broadcast | bytes 48 | tf_op jit(solution)/shard_map/stack;broadcast_in_dim | solution.py:139
  8.7 0.7 %fusion.39 = (s32[3,1,4,2]{2,3,0,1:T(2,128)S(1)}, s32[3,4,2]{1,2,0:T(2,128)S(1)}) fusion(s32[1,4,2]{1,2,0:T(2,128)S(1)} %stack_broadcast_in_dim.2, s32[1,4,2]{1,2,0:T(2,128)} %bitcast.77, s32[1,4,2]{1,2,0:T(2,128)} %bitcast.78), kind=kLoop, calls=%fused_computation.194 | loop fusion | flops 48 | bytes 288 | tf_op jit(solution)/shard_map/stack | solution.py:140
  9.5 0.7 %convert_bitcast_fusion.1 = bf16[8,128]{1,0:T(8,128)(2,1)S(1)} fusion(s32[1024]{0:T(1024)} %param.11), kind=kLoop, calls=%fused_computation.182 | loop fusion | flops 1024 | bytes 6144 | tf_op jit(solution)/shard_map/convert_element_type | solution.py:122
  10.2 0.8 %multiply_bitcast_fusion.1 = f32[1,8,8,128]{3,1,2,0:T(8,128)S(1)} fusion(s32[16,1024]{1,0:T(8,128)} %param.13, s32[]{:T(128)S(6)} %select_n.261), kind=kLoop, calls=%fused_computation.109 | loop fusion | flops 24576 | bytes 65540
  11.0 0.8 %multiply_bitcast_fusion = f32[1,8,8,128]{3,1,2,0:T(8,128)S(1)} fusion(s32[16,1024]{1,0:T(8,128)} %param.14, s32[]{:T(128)S(6)} %select_n.261), kind=kLoop, calls=%fused_computation.107 | loop fusion | flops 24576 | bytes 65540
  11.9 0.3 select_reduce_fusion.25
  12.2 0.3 slice_reduce_fusion.11
  12.6 0.1 copy.125
  12.7 0.3 slice_reduce_fusion.3
  13.7 1.5 %select_reduce_fusion = bf16[16,64,128]{2,1,0:T(8,128)(2,1)S(1)} fusion(pred[16,8]{1,0:T(8,128)(4,1)S(1)} %iota_compare_fusion.1, bf16[64,8,128]{2,1,0:T(8,128)(2,1)S(1)} %bitcast.66), kind=kLoop, calls=%fused_computation.48 | loop fusion | flops 1966080 | bytes 393344 | tf_op jit(solution)/shard_map/reduce_sum | solution.py:26
  15.8 0.4 select_reduce_fusion.4
  16.2 0.4 select_reduce_fusion.1
  16.6 2.1 %collective-permute-done.2 = bf16[65,8,128]{2,1,0:T(8,128)(2,1)S(1)} collective-permute-done((bf16[65,8,128]{2,1,0:T(8,128)(2,1)S(1)}, bf16[65,8,128]{2,1,0:T(8,128)(2,1)S(1)}, u32[]{:S(2)}, u32[]{:S(2)}) %collective-permute-start.2) | collective-permute-done | bytes 133152 | tf_op jit(solution)/shard_map/ppermute | solution.py:92
  18.7 0.4 select_reduce_fusion.2
  19.1 0.4 select_reduce_fusion.3
  19.6 1.4 %fusion.26 = f32[16,128,128]{2,1,0:T(8,128)S(1)} fusion(bf16[16,64,128]{2,1,0:T(8,128)(2,1)S(1)} %select_reduce_fusion, f32[16,128]{1,0:T(8,128)S(1)} %broadcast_multiply_fusion.4, f32[16,128]{1,0:T(8,128)S(1)} %broadcast_multiply_fusion.5, bf16[16,128]{1,0:T(8,128)(2,1)S(1)} %select_reduce_fusion.23, bf16[16,128]{1,0:T(8,128)(2,1)S(1)} %bitcast.75, ...), kind=kOutput, calls=%fused_computation.53 | convolution fusion | flops 35127296 | bytes 1597440 | tf_op jit(solution)/shard_map/gdi,gdj->gij/dot_general | solution.py:61
  21.0 1.1 %fusion.27 = f32[16,128,128]{2,1,0:T(8,128)S(1)} fusion(bf16[16,64,128]{2,1,0:T(8,128)(2,1)S(1)} %select_reduce_fusion, f32[16,128]{1,0:T(8,128)S(1)} %broadcast_multiply_fusion.5, f32[16,128]{1,0:T(8,128)S(1)} %broadcast_multiply_fusion.4, bf16[16,128]{1,0:T(8,128)(2,1)S(1)} %bitcast.76, bf16[16,128]{1,0:T(8,128)(2,1)S(1)} %select_reduce_fusion.23, ...), kind=kOutput, calls=%fused_computation.54 | convolution fusion | flops 35127296 | bytes 1597440 | tf_op jit(solution)/shard_map/gdi,gdj->gij/dot_general | solution.py:61
  22.2 0.1 exponential_reduce_fusion.3
  22.4 0.2 exponential_reduce_fusion.2
  23.1 0.2 select_reduce_fusion.15
  23.4 1.3 %subtract_reduce_fusion.8 = (f32[4,8,128]{2,1,0:T(8,128)S(1)}, f32[4,8,128]{2,1,0:T(8,128)S(1)}) fusion(f32[4,128,128]{2,1,0:T(8,128)S(1)} %get-tuple-element.34, f32[4,8,128]{2,1,0:T(8,128)S(1)} %get-tuple-element.47, f32[4,128,128]{2,1,0:T(8,128)S(1)} %get-tuple-element.35, f32[4,8,128]{2,1,0:T(8,128)S(1)} %get-tuple-element.48), kind=kLoop, calls=%fused_computation.17 | loop fusion | flops 2088960 | bytes 589824 | tf_op jit(solution)/shard_map/reduce_max | solution.py:71
  24.7 0.7 %fusion.7 = f32[4,8,128]{2,1,0:T(8,128)S(1)} fusion(f32[4,8,128]{2,1,0:T(8,128)S(1)} %get-tuple-element.54, f32[4,128,128]{2,1,0:T(8,128)S(1)} %get-tuple-element.34, f32[4,8,128]{2,1,0:T(8,128)S(1)} %get-tuple-element.47), kind=kLoop, calls=%fused_computation.31 | loop fusion | flops 1568768 | bytes 311296 | tf_op jit(solution)/shard_map/reduce_sum | solution.py:72
  25.6 2.5 %collective-permute-start.6 = (f32[4,9,128]{2,0,1:T(4,128)S(1)}, f32[4,9,128]{2,0,1:T(4,128)S(1)}, u32[]{:S(2)}, u32[]{:S(2)}) collective-permute-start(f32[4,9,128]{2,0,1:T(4,128)S(1)} %pad_maximum_fusion.8), channel_id=1, source_target_pairs={{0,12},{4,8},{8,4},{12,0},{1,13},{5,9},{9,5},{13,1},{2,14},{6,10},... | collective-permute-start | bytes 55304 | tf_op jit(solution)/shard_map/ppermute | solution.py:92
  28.1 0.7 %fusion.5 = f32[4,8,128]{2,1,0:T(8,128)S(1)} fusion(f32[4,8,128]{2,1,0:T(8,128)S(1)} %get-tuple-element.55, f32[4,128,128]{2,1,0:T(8,128)S(1)} %get-tuple-element.35, f32[4,8,128]{2,1,0:T(8,128)S(1)} %get-tuple-element.48), kind=kLoop, calls=%fused_computation.29 | loop fusion | flops 1568768 | bytes 311296 | tf_op jit(solution)/shard_map/reduce_sum | solution.py:72
  29.0 1.3 %subtract_reduce_fusion.10 = (f32[4,8,128]{2,1,0:T(8,128)S(1)}, f32[4,8,128]{2,1,0:T(8,128)S(1)}) fusion(f32[4,128,128]{2,1,0:T(8,128)S(1)} %get-tuple-element.36, f32[4,8,128]{2,1,0:T(8,128)S(1)} %get-tuple-element.49, f32[4,128,128]{2,1,0:T(8,128)S(1)} %get-tuple-element.33, f32[4,8,128]{2,1,0:T(8,128)S(1)} %get-tuple-element.46), kind=kLoop, calls=%fused_computation.21 | loop fusion | flops 2088960 | bytes 589824 | tf_op jit(solution)/shard_map/reduce_max | solution.py:71
  30.3 0.7 %fusion.3 = f32[4,8,128]{2,1,0:T(8,128)S(1)} fusion(f32[4,8,128]{2,1,0:T(8,128)S(1)} %get-tuple-element.56, f32[4,128,128]{2,1,0:T(8,128)S(1)} %get-tuple-element.36, f32[4,8,128]{2,1,0:T(8,128)S(1)} %get-tuple-element.49), kind=kLoop, calls=%fused_computation.27 | loop fusion | flops 1568768 | bytes 311296 | tf_op jit(solution)/shard_map/reduce_sum | solution.py:72
  31.2 1.9 %collective-permute-start.4 = (f32[4,9,128]{2,0,1:T(4,128)S(1)}, f32[4,9,128]{2,0,1:T(4,128)S(1)}, u32[]{:S(2)}, u32[]{:S(2)}) collective-permute-start(f32[4,9,128]{2,0,1:T(4,128)S(1)} %pad_maximum_fusion.6), channel_id=1, source_target_pairs={{0,4},{4,0},{8,12},{12,8},{1,5},{5,1},{9,13},{13,9},{2,6},{6,2},{1... | collective-permute-start | bytes 55304 | tf_op jit(solution)/shard_map/ppermute | solution.py:92
  33.1 0.7 %fusion.1 = f32[4,8,128]{2,1,0:T(8,128)S(1)} fusion(f32[4,8,128]{2,1,0:T(8,128)S(1)} %get-tuple-element.57, f32[4,128,128]{2,1,0:T(8,128)S(1)} %get-tuple-element.33, f32[4,8,128]{2,1,0:T(8,128)S(1)} %get-tuple-element.46), kind=kLoop, calls=%fused_computation.25 | loop fusion | flops 1568768 | bytes 311296 | tf_op jit(solution)/shard_map/reduce_sum | solution.py:72
  34.0 1.0 %collective-permute-done.4 = f32[4,9,128]{2,0,1:T(4,128)S(1)} collective-permute-done((f32[4,9,128]{2,0,1:T(4,128)S(1)}, f32[4,9,128]{2,0,1:T(4,128)S(1)}, u32[]{:S(2)}, u32[]{:S(2)}) %collective-permute-start.4) | collective-permute-done | bytes 18464 | tf_op jit(solution)/shard_map/ppermute | solution.py:92
  35.5 0.2 select_reduce_fusion.13
  35.8 0.1 slice_reduce_fusion.7
  36.3 0.2 select_reduce_fusion.19
  36.5 2.4 %collective-permute-start.9 = (f32[4,8,128]{2,1,0:T(8,128)S(1)}, f32[4,8,128]{2,1,0:T(8,128)S(1)}, u32[]{:S(2)}, u32[]{:S(2)}) collective-permute-start(f32[4,8,128]{2,1,0:T(8,128)S(1)} %get-tuple-element.12), channel_id=1, source_target_pairs={{12,0},{8,4},{4,8},{0,12},{13,1},{9,5},{5,9},{1,13},{14,2},{10,6},... | collective-permute-start | bytes 49160 | tf_op jit(solution)/shard_map/ppermute | solution.py:92
  38.9 1.0 %collective-permute-start.8 = (f32[4,8,128]{2,1,0:T(8,128)S(1)}, f32[4,8,128]{2,1,0:T(8,128)S(1)}, u32[]{:S(2)}, u32[]{:S(2)}) collective-permute-start(f32[4,8,128]{2,1,0:T(8,128)S(1)} %get-tuple-element.11), channel_id=1, source_target_pairs={{8,0},{12,4},{0,8},{4,12},{9,1},{13,5},{1,9},{5,13},{10,2},{14,6},... | collective-permute-start | bytes 49160 | tf_op jit(solution)/shard_map/ppermute | solution.py:92
  39.9 1.1 %collective-permute-start.7 = (f32[4,8,128]{2,1,0:T(8,128)S(1)}, f32[4,8,128]{2,1,0:T(8,128)S(1)}, u32[]{:S(2)}, u32[]{:S(2)}) collective-permute-start(f32[4,8,128]{2,1,0:T(8,128)S(1)} %get-tuple-element.10), channel_id=1, source_target_pairs={{4,0},{0,4},{12,8},{8,12},{5,1},{1,5},{13,9},{9,13},{6,2},{2,6},{1... | collective-permute-start | bytes 49160 | tf_op jit(solution)/shard_map/ppermute | solution.py:92
  41.0 0.6 %subtract_reduce_fusion.7 = f32[4,8,128]{2,1,0:T(8,128)S(1)} fusion(f32[4,128,128]{2,1,0:T(8,128)S(1)} %get-tuple-element.30, f32[4,8,128]{2,1,0:T(8,128)S(1)} %broadcast_multiply_fusion.3), kind=kLoop, calls=%fused_computation.15 | loop fusion | flops 1044480 | bytes 294912 | tf_op jit(solution)/shard_map/reduce_max | solution.py:71
  41.6 0.7 %fusion.9 = f32[4,8,128]{2,1,0:T(8,128)S(1)} fusion(f32[4,8,128]{2,1,0:T(8,128)S(1)} %subtract_reduce_fusion.7, f32[4,128,128]{2,1,0:T(8,128)S(1)} %get-tuple-element.30, f32[4,8,128]{2,1,0:T(8,128)S(1)} %broadcast_multiply_fusion.3), kind=kLoop, calls=%fused_computation.33 | loop fusion | flops 1568768 | bytes 311296 | tf_op jit(solution)/shard_map/reduce_sum | solution.py:72
  42.4 0.6 %subtract_reduce_fusion.4 = f32[4,8,128]{2,1,0:T(8,128)S(1)} fusion(f32[4,128,128]{2,1,0:T(8,128)S(1)} %get-tuple-element.37, f32[4,8,128]{2,1,0:T(8,128)S(1)} %broadcast_multiply_fusion), kind=kLoop, calls=%fused_computation.9 | loop fusion | flops 1044480 | bytes 294912 | tf_op jit(solution)/shard_map/reduce_max | solution.py:71
  43.0 0.7 %fusion.15 = f32[4,8,128]{2,1,0:T(8,128)S(1)} fusion(f32[4,8,128]{2,1,0:T(8,128)S(1)} %subtract_reduce_fusion.4, f32[4,128,128]{2,1,0:T(8,128)S(1)} %get-tuple-element.37, f32[4,8,128]{2,1,0:T(8,128)S(1)} %broadcast_multiply_fusion), kind=kLoop, calls=%fused_computation.39 | loop fusion | flops 1568768 | bytes 311296 | tf_op jit(solution)/shard_map/reduce_sum | solution.py:72
  43.8 0.6 %subtract_reduce_fusion.5 = f32[4,8,128]{2,1,0:T(8,128)S(1)} fusion(f32[4,128,128]{2,1,0:T(8,128)S(1)} %get-tuple-element.32, f32[4,8,128]{2,1,0:T(8,128)S(1)} %broadcast_multiply_fusion.1), kind=kLoop, calls=%fused_computation.11 | loop fusion | flops 1044480 | bytes 294912 | tf_op jit(solution)/shard_map/reduce_max | solution.py:71
  44.4 0.7 %fusion.13 = f32[4,8,128]{2,1,0:T(8,128)S(1)} fusion(f32[4,8,128]{2,1,0:T(8,128)S(1)} %subtract_reduce_fusion.5, f32[4,128,128]{2,1,0:T(8,128)S(1)} %get-tuple-element.32, f32[4,8,128]{2,1,0:T(8,128)S(1)} %broadcast_multiply_fusion.1), kind=kLoop, calls=%fused_computation.37 | loop fusion | flops 1568768 | bytes 311296 | tf_op jit(solution)/shard_map/reduce_sum | solution.py:72
  45.2 0.6 %subtract_reduce_fusion.6 = f32[4,8,128]{2,1,0:T(8,128)S(1)} fusion(f32[4,128,128]{2,1,0:T(8,128)S(1)} %get-tuple-element.31, f32[4,8,128]{2,1,0:T(8,128)S(1)} %broadcast_multiply_fusion.2), kind=kLoop, calls=%fused_computation.13 | loop fusion | flops 1044480 | bytes 294912 | tf_op jit(solution)/shard_map/reduce_max | solution.py:71
  45.9 0.7 %fusion.11 = f32[4,8,128]{2,1,0:T(8,128)S(1)} fusion(f32[4,8,128]{2,1,0:T(8,128)S(1)} %subtract_reduce_fusion.6, f32[4,128,128]{2,1,0:T(8,128)S(1)} %get-tuple-element.31, f32[4,8,128]{2,1,0:T(8,128)S(1)} %broadcast_multiply_fusion.2), kind=kLoop, calls=%fused_computation.35 | loop fusion | flops 1568768 | bytes 311296 | tf_op jit(solution)/shard_map/reduce_sum | solution.py:72
  46.8 0.2 select_reduce_fusion.10
  47.4 0.2 select_reduce_fusion.8
  47.6 0.6 %subtract_reduce_fusion = f32[4,8,128]{2,1,0:T(8,128)S(1)} fusion(f32[4,8,128]{2,1,0:T(8,128)S(1)} %get-tuple-element.41, f32[4,128,128]{2,1,0:T(8,128)S(1)} %get-tuple-element.34), kind=kLoop, calls=%fused_computation.1 | loop fusion | flops 1044480 | bytes 294912 | tf_op jit(solution)/shard_map/reduce_max | solution.py:71
  48.2 0.7 %fusion.23 = f32[4,8,128]{2,1,0:T(8,128)S(1)} fusion(f32[4,8,128]{2,1,0:T(8,128)S(1)} %subtract_reduce_fusion, f32[4,8,128]{2,1,0:T(8,128)S(1)} %get-tuple-element.41, f32[4,128,128]{2,1,0:T(8,128)S(1)} %get-tuple-element.34), kind=kLoop, calls=%fused_computation.47 | loop fusion | flops 1568768 | bytes 311296 | tf_op jit(solution)/shard_map/reduce_sum | solution.py:72
  49.1 2.4 %collective-permute-start.13 = (f32[4,8,128]{2,1,0:T(8,128)S(1)}, f32[4,8,128]{2,1,0:T(8,128)S(1)}, u32[]{:S(2)}, u32[]{:S(2)}) collective-permute-start(f32[4,8,128]{2,1,0:T(8,128)S(1)} %add_select_fusion), channel_id=1, source_target_pairs={{0,12},{4,8},{8,4},{12,0},{1,13},{5,9},{9,5},{13,1},{2,14},{6,10},... | collective-permute-start | bytes 49160 | tf_op jit(solution)/shard_map/ppermute | solution.py:92
  51.4 0.6 %subtract_reduce_fusion.1 = f32[4,8,128]{2,1,0:T(8,128)S(1)} fusion(f32[4,8,128]{2,1,0:T(8,128)S(1)} %get-tuple-element.42, f32[4,128,128]{2,1,0:T(8,128)S(1)} %get-tuple-element.35), kind=kLoop, calls=%fused_computation.3 | loop fusion | flops 1044480 | bytes 294912 | tf_op jit(solution)/shard_map/reduce_max | solution.py:71
  52.1 1.0 %fusion.21 = f32[4,8,128]{2,1,0:T(8,128)S(1)} fusion(f32[4,8,128]{2,1,0:T(8,128)S(1)} %subtract_reduce_fusion.1, f32[4,8,128]{2,1,0:T(8,128)S(1)} %get-tuple-element.42, f32[4,128,128]{2,1,0:T(8,128)S(1)} %get-tuple-element.35), kind=kLoop, calls=%fused_computation.45 | loop fusion | flops 1568768 | bytes 311296 | tf_op jit(solution)/shard_map/reduce_sum | solution.py:72
  53.2 0.6 %subtract_reduce_fusion.2 = f32[4,8,128]{2,1,0:T(8,128)S(1)} fusion(f32[4,8,128]{2,1,0:T(8,128)S(1)} %get-tuple-element.43, f32[4,128,128]{2,1,0:T(8,128)S(1)} %get-tuple-element.36), kind=kLoop, calls=%fused_computation.5 | loop fusion | flops 1044480 | bytes 294912 | tf_op jit(solution)/shard_map/reduce_max | solution.py:71
  53.8 0.7 %fusion.19 = f32[4,8,128]{2,1,0:T(8,128)S(1)} fusion(f32[4,8,128]{2,1,0:T(8,128)S(1)} %subtract_reduce_fusion.2, f32[4,8,128]{2,1,0:T(8,128)S(1)} %get-tuple-element.43, f32[4,128,128]{2,1,0:T(8,128)S(1)} %get-tuple-element.36), kind=kLoop, calls=%fused_computation.43 | loop fusion | flops 1568768 | bytes 311296 | tf_op jit(solution)/shard_map/reduce_sum | solution.py:72
  54.7 2.0 %collective-permute-start.11 = (f32[4,8,128]{2,1,0:T(8,128)S(1)}, f32[4,8,128]{2,1,0:T(8,128)S(1)}, u32[]{:S(2)}, u32[]{:S(2)}) collective-permute-start(f32[4,8,128]{2,1,0:T(8,128)S(1)} %add_select_fusion.2), channel_id=1, source_target_pairs={{0,4},{4,0},{8,12},{12,8},{1,5},{5,1},{9,13},{13,9},{2,6},{6,2},{1... | collective-permute-start | bytes 49160 | tf_op jit(solution)/shard_map/ppermute | solution.py:92
  56.6 0.6 %subtract_reduce_fusion.3 = f32[4,8,128]{2,1,0:T(8,128)S(1)} fusion(f32[4,8,128]{2,1,0:T(8,128)S(1)} %get-tuple-element.40, f32[4,128,128]{2,1,0:T(8,128)S(1)} %get-tuple-element.33), kind=kLoop, calls=%fused_computation.7 | loop fusion | flops 1044480 | bytes 294912 | tf_op jit(solution)/shard_map/reduce_max | solution.py:71
  57.3 0.7 %fusion.17 = f32[4,8,128]{2,1,0:T(8,128)S(1)} fusion(f32[4,8,128]{2,1,0:T(8,128)S(1)} %subtract_reduce_fusion.3, f32[4,8,128]{2,1,0:T(8,128)S(1)} %get-tuple-element.40, f32[4,128,128]{2,1,0:T(8,128)S(1)} %get-tuple-element.33), kind=kLoop, calls=%fused_computation.41 | loop fusion | flops 1568768 | bytes 311296 | tf_op jit(solution)/shard_map/reduce_sum | solution.py:72
  58.1 0.3 collective-permute-done.11
  58.5 0.2 select_reduce_fusion.6
  59.1 0.6 %copy.149 = f32[2,8,8,128]{3,1,2,0:T(8,128)} copy(f32[2,8,8,128]{3,2,1,0:T(8,128)S(1)} %bitcast.67) | data formatting | bytes 131072
  59.7 0.5 collective-permute-done.14
  60.2 0.6 %copy.148 = f32[2,8,8,128]{3,1,2,0:T(8,128)} copy(f32[2,8,8,128]{3,2,1,0:T(8,128)S(1)} %bitcast.68) | data formatting | bytes 131072
  (118 shorter events, 5.1 us)
Async XLA Ops:
  0.6 11.1 %copy-start = (bf16[64,1024]{1,0:T(8,128)(2,1)S(1)}, bf16[64,1024]{1,0:T(8,128)(2,1)}, u32[]{:S(2)}) copy-start(bf16[64,1024]{1,0:T(8,128)(2,1)} %param.9) | copy-start | bytes 393220
  2.3 13.9 %collective-permute-start.3 = (bf16[65,8,128]{2,1,0:T(8,128)(2,1)S(1)}, bf16[65,8,128]{2,1,0:T(8,128)(2,1)S(1)}, u32[]{:S(2)}, u32[]{:S(2)}) collective-permute-start(bf16[65,8,128]{2,1,0:T(8,128)(2,1)S(1)} %pad_maximum_fusion.1), channel_id=1, source_target_pairs={{12,0},{8,4},{4,8},{0,12},{13,1},{9,5},{5,9},{1,13},{14,2},{10,6},... | collective-permute-start | bytes 399368 | tf_op jit(solution)/shard_map/ppermute | solution.py:92
  7.4 11.2 %collective-permute-start.2 = (bf16[65,8,128]{2,1,0:T(8,128)(2,1)S(1)}, bf16[65,8,128]{2,1,0:T(8,128)(2,1)S(1)}, u32[]{:S(2)}, u32[]{:S(2)}) collective-permute-start(bf16[65,8,128]{2,1,0:T(8,128)(2,1)S(1)} %pad_maximum_fusion.1), channel_id=1, source_target_pairs={{8,0},{12,4},{0,8},{4,12},{9,1},{13,5},{1,9},{5,13},{10,2},{14,6},... | collective-permute-start | bytes 399368 | tf_op jit(solution)/shard_map/ppermute | solution.py:92
  7.4 11.6 %collective-permute-start.1 = (bf16[65,8,128]{2,1,0:T(8,128)(2,1)S(1)}, bf16[65,8,128]{2,1,0:T(8,128)(2,1)S(1)}, u32[]{:S(2)}, u32[]{:S(2)}) collective-permute-start(bf16[65,8,128]{2,1,0:T(8,128)(2,1)S(1)} %pad_maximum_fusion.1), channel_id=1, source_target_pairs={{4,0},{0,4},{12,8},{8,12},{5,1},{1,5},{13,9},{9,13},{6,2},{2,6},{1... | collective-permute-start | bytes 399368 | tf_op jit(solution)/shard_map/ppermute | solution.py:92
  9.4 2.4 %collective-permute-start = (s32[3,4,2]{1,2,0:T(2,128)S(1)}, s32[3,4,2]{1,2,0:T(2,128)S(1)}, u32[]{:S(2)}, u32[]{:S(2)}) collective-permute-start(s32[3,4,2]{1,2,0:T(2,128)S(1)} %get-tuple-element.53), channel_id=1, source_target_pairs={{0,1},{1,0},{2,3},{3,2},{4,5},{5,4},{6,7},{7,6},{8,9},{9,8},{10,11... | collective-permute-start | bytes 296 | tf_op jit(solution)/shard_map/ppermute | solution.py:78
  25.6 8.4 %collective-permute-start.6 = (f32[4,9,128]{2,0,1:T(4,128)S(1)}, f32[4,9,128]{2,0,1:T(4,128)S(1)}, u32[]{:S(2)}, u32[]{:S(2)}) collective-permute-start(f32[4,9,128]{2,0,1:T(4,128)S(1)} %pad_maximum_fusion.8), channel_id=1, source_target_pairs={{0,12},{4,8},{8,4},{12,0},{1,13},{5,9},{9,5},{13,1},{2,14},{6,10},... | collective-permute-start | bytes 55304 | tf_op jit(solution)/shard_map/ppermute | solution.py:92
  29.0 5.0 %collective-permute-start.5 = (f32[4,9,128]{2,0,1:T(4,128)S(1)}, f32[4,9,128]{2,0,1:T(4,128)S(1)}, u32[]{:S(2)}, u32[]{:S(2)}) collective-permute-start(f32[4,9,128]{2,0,1:T(4,128)S(1)} %pad_maximum_fusion.7), channel_id=1, source_target_pairs={{0,8},{4,12},{8,0},{12,4},{1,9},{5,13},{9,1},{13,5},{2,10},{6,14},... | collective-permute-start | bytes 55304 | tf_op jit(solution)/shard_map/ppermute | solution.py:92
  31.2 3.8 %collective-permute-start.4 = (f32[4,9,128]{2,0,1:T(4,128)S(1)}, f32[4,9,128]{2,0,1:T(4,128)S(1)}, u32[]{:S(2)}, u32[]{:S(2)}) collective-permute-start(f32[4,9,128]{2,0,1:T(4,128)S(1)} %pad_maximum_fusion.6), channel_id=1, source_target_pairs={{0,4},{4,0},{8,12},{12,8},{1,5},{5,1},{9,13},{13,9},{2,6},{6,2},{1... | collective-permute-start | bytes 55304 | tf_op jit(solution)/shard_map/ppermute | solution.py:92
  36.5 5.8 %collective-permute-start.9 = (f32[4,8,128]{2,1,0:T(8,128)S(1)}, f32[4,8,128]{2,1,0:T(8,128)S(1)}, u32[]{:S(2)}, u32[]{:S(2)}) collective-permute-start(f32[4,8,128]{2,1,0:T(8,128)S(1)} %get-tuple-element.12), channel_id=1, source_target_pairs={{12,0},{8,4},{4,8},{0,12},{13,1},{9,5},{5,9},{1,13},{14,2},{10,6},... | collective-permute-start | bytes 49160 | tf_op jit(solution)/shard_map/ppermute | solution.py:92
  38.9 4.9 %collective-permute-start.8 = (f32[4,8,128]{2,1,0:T(8,128)S(1)}, f32[4,8,128]{2,1,0:T(8,128)S(1)}, u32[]{:S(2)}, u32[]{:S(2)}) collective-permute-start(f32[4,8,128]{2,1,0:T(8,128)S(1)} %get-tuple-element.11), channel_id=1, source_target_pairs={{8,0},{12,4},{0,8},{4,12},{9,1},{13,5},{1,9},{5,13},{10,2},{14,6},... | collective-permute-start | bytes 49160 | tf_op jit(solution)/shard_map/ppermute | solution.py:92
  39.9 5.3 %collective-permute-start.7 = (f32[4,8,128]{2,1,0:T(8,128)S(1)}, f32[4,8,128]{2,1,0:T(8,128)S(1)}, u32[]{:S(2)}, u32[]{:S(2)}) collective-permute-start(f32[4,8,128]{2,1,0:T(8,128)S(1)} %get-tuple-element.10), channel_id=1, source_target_pairs={{4,0},{0,4},{12,8},{8,12},{5,1},{1,5},{13,9},{9,13},{6,2},{2,6},{1... | collective-permute-start | bytes 49160 | tf_op jit(solution)/shard_map/ppermute | solution.py:92
  47.3 11.7 %collective-permute-start.10 = (f32[8,8,128]{2,1,0:T(8,128)S(1)}, f32[8,8,128]{2,1,0:T(8,128)S(1)}, u32[]{:S(2)}, u32[]{:S(2)}) collective-permute-start(f32[8,8,128]{2,1,0:T(8,128)S(1)} %bitcast_subtract_fusion.2), channel_id=1, source_target_pairs={{0,1},{1,0},{2,3},{3,2},{4,5},{5,4},{6,7},{7,6},{8,9},{9,8},{10,11... | collective-permute-start | bytes 98312 | tf_op jit(solution)/shard_map/ppermute | solution.py:78
  49.1 9.0 %collective-permute-start.13 = (f32[4,8,128]{2,1,0:T(8,128)S(1)}, f32[4,8,128]{2,1,0:T(8,128)S(1)}, u32[]{:S(2)}, u32[]{:S(2)}) collective-permute-start(f32[4,8,128]{2,1,0:T(8,128)S(1)} %add_select_fusion), channel_id=1, source_target_pairs={{0,12},{4,8},{8,4},{12,0},{1,13},{5,9},{9,5},{13,1},{2,14},{6,10},... | collective-permute-start | bytes 49160 | tf_op jit(solution)/shard_map/ppermute | solution.py:92
  53.1 5.0 %collective-permute-start.12 = (f32[4,8,128]{2,1,0:T(8,128)S(1)}, f32[4,8,128]{2,1,0:T(8,128)S(1)}, u32[]{:S(2)}, u32[]{:S(2)}) collective-permute-start(f32[4,8,128]{2,1,0:T(8,128)S(1)} %add_select_fusion.1), channel_id=1, source_target_pairs={{0,8},{4,12},{8,0},{12,4},{1,9},{5,13},{9,1},{13,5},{2,10},{6,14},... | collective-permute-start | bytes 49160 | tf_op jit(solution)/shard_map/ppermute | solution.py:92
  54.7 3.8 %collective-permute-start.11 = (f32[4,8,128]{2,1,0:T(8,128)S(1)}, f32[4,8,128]{2,1,0:T(8,128)S(1)}, u32[]{:S(2)}, u32[]{:S(2)}) collective-permute-start(f32[4,8,128]{2,1,0:T(8,128)S(1)} %add_select_fusion.2), channel_id=1, source_target_pairs={{0,4},{4,0},{8,12},{12,8},{1,5},{5,1},{9,13},{13,9},{2,6},{6,2},{1... | collective-permute-start | bytes 49160 | tf_op jit(solution)/shard_map/ppermute | solution.py:92
  58.9 1.3 %collective-permute-start.14 = (f32[8,8,128]{2,1,0:T(8,128)S(1)}, f32[8,8,128]{2,1,0:T(8,128)S(1)}, u32[]{:S(2)}, u32[]{:S(2)}) collective-permute-start(f32[8,8,128]{2,1,0:T(8,128)S(1)} %bitcast_subtract_fusion), channel_id=1, source_target_pairs={{0,1},{1,0},{2,3},{3,2},{4,5},{5,4},{6,7},{7,6},{8,9},{9,8},{10,11... | collective-permute-start | bytes 98312 | tf_op jit(solution)/shard_map/ppermute | solution.py:78

commit v12 on v11

--- a/solution.py
+++ b/solution.py
@@ -145,15 +145,16 @@
         wanted = wanted.reshape(peer_count, wide)
         rows_used = rows_used.reshape(slot_count)
         usable = usable.reshape(slot_count)[:, None, None] > 0
-        far = jnp.concatenate(
-            [pick_rows(everything[offset], wanted[offset], blocks) for offset in range(peer_count)], axis=0
-        )
-        far_y = far[:, :features]
-        far_tags = far[:, features]
-        slot_x = pick_rows(own_real, rows_used, blocks)
-        slot_tags = pick_rows(real_tags, rows_used, blocks)[:, 0]
-        cost_cols = slot_costs(slot_x, slot_tags, far_y, far_tags) / SMOOTH
-        cost_rows = slot_costs(far_y, far_tags, slot_x, slot_tags) / SMOOTH
+        cost_cols, cost_rows = [], []
+        for offset in range(peer_count):
+            piece = slice(offset * wide, (offset + 1) * wide)
+            far = pick_rows(everything[offset], wanted[offset], blocks)
+            far_y = far[:, :features]
+            far_tags = far[:, features]
+            slot_x = pick_rows(own_real, rows_used[piece], blocks)
+            slot_tags = pick_rows(real_tags, rows_used[piece], blocks)[:, 0]
+            cost_cols.append(slot_costs(slot_x, slot_tags, far_y, far_tags) / SMOOTH)
+            cost_rows.append(slot_costs(far_y, far_tags, slot_x, slot_tags) / SMOOTH)
 
         synth_pot = jnp.zeros((half, blocks, BLOCK), jnp.float32)
         real_pot = jnp.zeros((half, blocks, BLOCK), jnp.float32)
@@ -173,7 +174,7 @@
             highest, mass_sum = [], []
             for offset in range(peer_count):
                 piece = slice(offset * wide, (offset + 1) * wide)
-                scores = (panel[piece] / SMOOTH)[:, :, :, None] - cost_rows[piece, None]
+                scores = (panel[piece] / SMOOTH)[:, :, :, None] - cost_rows[offset][:, None]
                 parts = lse_parts(scores, 2)
                 highest.append(parts[0])
                 mass_sum.append(parts[1])
@@ -188,7 +189,7 @@
             chunks = [None] * peer_count
             for offset in list(range(1, peer_count)) + [0]:
                 piece = slice(offset * wide, (offset + 1) * wide)
-                scores = (own_rows[piece] / SMOOTH)[:, :, :, None] - cost_cols[piece, None]
+                scores = (own_rows[piece] / SMOOTH)[:, :, :, None] - cost_cols[offset][:, None]
                 highest, mass_sum = lse_parts(scores, 2)
                 lse = jnp.where(usable[piece], highest + jnp.log(mass_sum), SENTINEL)
                 if sweep_index == 0:

time: 61.2 us -> 67.1 us (1.096)
  waiting for transfers between devices: 3.96 us -> 13 us
  other arithmetic: 28.8 us -> 26.1 us
    ppermute x12, waiting for transfers between devices: 3.45 us -> 11.5 us  [exchange(): moved.append(lax.ppermute(chunks[offset], 'blk', perm))]
    unnamed x2 -> x1, other arithmetic: 1.55 us -> 0.03 us
    ppermute x3, waiting for transfers between devices: 0.51 us -> 1.45 us  [swap(): return lax.ppermute(value, 'sub', [(0, 1), (1, 0)])]
    another operation x1, other arithmetic: 0.7 us -> 0.01 us  [shards(): lists = jnp.stack([lists, swap(lists)], axis=1)]
    convert_element_type x1, other arithmetic: 0.69 us -> 0.01 us  [shards(): real_tags = real_cluster.reshape(1, blocks, BLOCK).astype(jnp.bfloat16)]
    dot_general x2 -> x8, matrix products: 2.53 us -> 2.29 us  [slot_costs(): jnp.einsum('gdi,gdj->gij', slot_real, slot_synth, preferred_element_type=...]
    unnamed x8 -> x23, local copies, waits for them, and re-layouts: 2.26 us -> 2.35 us
    reduce_max x11 -> x12, other arithmetic: 7.55 us -> 7.47 us  [lse_parts(): highest = jnp.max(scores, axis=axis)]
  transfers between devices with their start and end apart: 15 -> 15, of which waited for: 4 -> 8; matrix products, arithmetic and copies ran while one was open for 40% -> 26% of each run, Pallas kernels for 0% -> 0%
where the time goes in v12:
time: 67.1 us; the launch traced here: 67 us
  other arithmetic  26.1 us (39%)
  starting transfers between devices  19.3 us (29%)
  waiting for transfers between devices  13 us (19%)
  local copies, waits for them, and re-layouts  4.83 us (7%)
  matrix products  2.29 us (3%)
  between operations  1.48 us (2%)
    ppermute x12, starting transfers between devices, exchange(): moved.append(lax.ppermute(chunks[offset], 'blk', perm))  19.1 us
    ppermute x12, waiting for transfers between devices, exchange(): moved.append(lax.ppermute(chunks[offset], 'blk', perm))  11.5 us
    reduce_sum x16, other arithmetic, lse_parts(): jnp.sum(jnp.exp(scores - jnp.expand_dims(highest, axis)), axis=axis)  9.41 us
    reduce_max x12, other arithmetic, lse_parts(): highest = jnp.max(scores, axis=axis)  7.47 us
    reduce_sum x13, other arithmetic, pick_rows(): return jnp.sum(chosen, axis=2, dtype=values.dtype)  4.55 us
    unnamed x23, local copies, waits for them, and re-layouts  2.35 us
    dot_general x8, matrix products, slot_costs(): jnp.einsum('gdi,gdj->gij', slot_real, slot_synth, preferred_element_type=...  2.29 us
    ppermute x3, waiting for transfers between devices, swap(): return lax.ppermute(value, 'sub', [(0, 1), (1, 0)])  1.45 us
  transfers between devices with their start and end apart: 15, of which 8 were waited for; matrix products, arithmetic and copies ran while one was open for 26% of the time, Pallas kernels for 0%

profile of v12, /device:TPU:0, one launch (start us, length us, event | category | flops | bytes accessed | tf_op | source)
XLA Modules:
  0.0 67.0 jit_solution(12056978427970236154)
XLA Ops:
  0.6 0.7 %convert_bitcast_fusion.3 = (bf16[1,1,8,128]{3,2,1,0:T(8,128)(2,1)S(1)}, bf16[1,8,128]{2,1,0:T(8,128)(2,1)S(1)}) fusion(s32[1024]{0:T(1024)} %param.12), kind=kLoop, calls=%fused_computation.240 | loop fusion | flops 1024 | bytes 8192 | tf_op jit(solution)/shard_map/concatenate | solution.py:123
  1.3 1.0 %copy.137 = bf16[8,8,8,128]{3,2,1,0:T(8,128)(2,1)S(1)} copy(bf16[8,8,8,128]{3,1,2,0:T(8,128)(2,1)} %bitcast.84) | data formatting | bytes 262144
  2.4 5.1 %collective-permute-start.3 = (bf16[65,8,128]{2,1,0:T(8,128)(2,1)S(1)}, bf16[65,8,128]{2,1,0:T(8,128)(2,1)S(1)}, u32[]{:S(2)}, u32[]{:S(2)}) collective-permute-start(bf16[65,8,128]{2,1,0:T(8,128)(2,1)S(1)} %pad_maximum_fusion), channel_id=1, source_target_pairs={{12,0},{8,4},{4,8},{0,12},{13,1},{9,5},{5,9},{1,13},{14,2},{10,6},... | collective-permute-start | bytes 399368 | tf_op jit(solution)/shard_map/ppermute | solution.py:92
  7.5 0.6 collective-permute-start.1
  8.4 0.9 %collective-permute-done = s32[3,4,2]{1,2,0:T(2,128)S(1)} collective-permute-done((s32[3,4,2]{1,2,0:T(2,128)S(1)}, s32[3,4,2]{1,2,0:T(2,128)S(1)}, u32[]{:S(2)}, u32[]{:S(2)}) %collective-permute-start) | collective-permute-done | bytes 128 | tf_op jit(solution)/shard_map/ppermute | solution.py:78
  9.4 0.3 select_reduce_fusion.31
  9.8 0.4 slice_reduce_fusion.14
  10.4 0.4 select_reduce_fusion.3
  11.6 1.4 %select_reduce_fusion.18 = (bf16[4,64,128]{2,1,0:T(8,128)(2,1)S(1)}, bf16[4,64,128]{2,1,0:T(8,128)(2,1)S(1)}, bf16[4,64,128]{2,1,0:T(8,128)(2,1)S(1)}, bf16[4,64,128]{2,1,0:T(8,128)(2,1)S(1)}) fusion(pred[4,8]{1,0:T(4,128)(4,1)S(1)} %iota_compare_fusion.12, bf16[64,8,128]{2,1,0:T(8,128)(2,1)S(1)} %bitcast.81, pred[4,8]{1,0:T(4,128)(4,1)S(1)} %iota_compare_fusion.10, ...), kind=kLoop, calls=%fused_computation.90 | loop fusion | flops 1966080 | bytes 393344 | tf_op jit(solution)/shard_map/reduce_sum | solution.py:26
  13.1 0.3 fusion.31
  13.3 0.3 subtract_reduce_fusion.15
  14.4 0.3 slice_reduce_fusion.3
  15.3 0.4 select_reduce_fusion
  15.7 3.0 %collective-permute-done.2 = bf16[65,8,128]{2,1,0:T(8,128)(2,1)S(1)} collective-permute-done((bf16[65,8,128]{2,1,0:T(8,128)(2,1)S(1)}, bf16[65,8,128]{2,1,0:T(8,128)(2,1)S(1)}, u32[]{:S(2)}, u32[]{:S(2)}) %collective-permute-start.2) | collective-permute-done | bytes 133152 | tf_op jit(solution)/shard_map/ppermute | solution.py:92
  18.7 0.4 select_reduce_fusion.1
  19.2 0.4 select_reduce_fusion.2
  19.7 0.3 fusion.29
  20.0 0.3 subtract_reduce_fusion.14
  20.3 0.3 fusion.27
  20.6 0.3 subtract_reduce_fusion.13
  20.9 0.3 fusion.25
  21.2 0.3 subtract_reduce_fusion.12
  22.1 0.2 select_reduce_fusion.14
  22.4 0.6 subtract_reduce_fusion.11
  23.0 0.9 %fusion.1 = f32[4,8,128]{2,1,0:T(8,128)S(1)} fusion(f32[4,8,128]{2,1,0:T(8,128)S(1)} %subtract_reduce_fusion.11, f32[4,128,128]{2,1,0:T(8,128)S(1)} %fusion.31, f32[4,8,128]{2,1,0:T(8,128)S(1)} %get-tuple-element.43), kind=kLoop, calls=%fused_computation.25 | loop fusion | flops 1568768 | bytes 311296 | tf_op jit(solution)/shard_map/reduce_sum | solution.py:72
  24.0 0.6 subtract_reduce_fusion.8
  24.6 0.7 %fusion.7 = f32[4,8,128]{2,1,0:T(8,128)S(1)} fusion(f32[4,8,128]{2,1,0:T(8,128)S(1)} %subtract_reduce_fusion.8, f32[4,128,128]{2,1,0:T(8,128)S(1)} %fusion.25, f32[4,8,128]{2,1,0:T(8,128)S(1)} %get-tuple-element.44), kind=kLoop, calls=%fused_computation.31 | loop fusion | flops 1568768 | bytes 311296 | tf_op jit(solution)/shard_map/reduce_sum | solution.py:72
  25.4 0.6 subtract_reduce_fusion.9
  26.0 0.7 %fusion.5 = f32[4,8,128]{2,1,0:T(8,128)S(1)} fusion(f32[4,8,128]{2,1,0:T(8,128)S(1)} %subtract_reduce_fusion.9, f32[4,128,128]{2,1,0:T(8,128)S(1)} %fusion.27, f32[4,8,128]{2,1,0:T(8,128)S(1)} %get-tuple-element.45), kind=kLoop, calls=%fused_computation.29 | loop fusion | flops 1568768 | bytes 311296 | tf_op jit(solution)/shard_map/reduce_sum | solution.py:72
  26.9 0.6 subtract_reduce_fusion.10
  27.5 0.7 %fusion.3 = f32[4,8,128]{2,1,0:T(8,128)S(1)} fusion(f32[4,8,128]{2,1,0:T(8,128)S(1)} %subtract_reduce_fusion.10, f32[4,128,128]{2,1,0:T(8,128)S(1)} %fusion.29, f32[4,8,128]{2,1,0:T(8,128)S(1)} %get-tuple-element.46), kind=kLoop, calls=%fused_computation.27 | loop fusion | flops 1568768 | bytes 311296 | tf_op jit(solution)/shard_map/reduce_sum | solution.py:72
  28.5 3.0 %collective-permute-start.5 = (f32[4,9,128]{2,0,1:T(4,128)S(1)}, f32[4,9,128]{2,0,1:T(4,128)S(1)}, u32[]{:S(2)}, u32[]{:S(2)}) collective-permute-start(f32[4,9,128]{2,0,1:T(4,128)S(1)} %pad_maximum_fusion.6), channel_id=1, source_target_pairs={{0,8},{4,12},{8,0},{12,4},{1,9},{5,13},{9,1},{13,5},{2,10},{6,14},... | collective-permute-start | bytes 55304 | tf_op jit(solution)/shard_map/ppermute | solution.py:92
  31.7 1.4 %collective-permute-start.6 = (f32[4,9,128]{2,0,1:T(4,128)S(1)}, f32[4,9,128]{2,0,1:T(4,128)S(1)}, u32[]{:S(2)}, u32[]{:S(2)}) collective-permute-start(f32[4,9,128]{2,0,1:T(4,128)S(1)} %pad_maximum_fusion.7), channel_id=1, source_target_pairs={{0,12},{4,8},{8,4},{12,0},{1,13},{5,9},{9,5},{13,1},{2,14},{6,10},... | collective-permute-start | bytes 55304 | tf_op jit(solution)/shard_map/ppermute | solution.py:92
  33.1 0.2 collective-permute-done.5
  33.3 3.9 %collective-permute-done.6 = f32[4,9,128]{2,0,1:T(4,128)S(1)} collective-permute-done((f32[4,9,128]{2,0,1:T(4,128)S(1)}, f32[4,9,128]{2,0,1:T(4,128)S(1)}, u32[]{:S(2)}, u32[]{:S(2)}) %collective-permute-start.6) | collective-permute-done | bytes 18464 | tf_op jit(solution)/shard_map/ppermute | solution.py:92
  38.1 0.2 select_reduce_fusion.12
  38.6 0.2 select_reduce_fusion.22
  38.8 0.6 subtract_reduce_fusion.7
  39.5 0.7 %fusion.9 = f32[4,8,128]{2,1,0:T(8,128)S(1)} fusion(f32[4,8,128]{2,1,0:T(8,128)S(1)} %subtract_reduce_fusion.7, f32[4,128,128]{2,1,0:T(8,128)S(1)} %get-tuple-element.58, f32[4,8,128]{2,1,0:T(8,128)S(1)} %broadcast_multiply_fusion.3), kind=kLoop, calls=%fused_computation.33 | loop fusion | flops 1568768 | bytes 311296 | tf_op jit(solution)/shard_map/reduce_sum | solution.py:72
  40.3 1.9 %collective-permute-start.8 = (f32[4,8,128]{2,1,0:T(8,128)S(1)}, f32[4,8,128]{2,1,0:T(8,128)S(1)}, u32[]{:S(2)}, u32[]{:S(2)}) collective-permute-start(f32[4,8,128]{2,1,0:T(8,128)S(1)} %get-tuple-element.8), channel_id=1, source_target_pairs={{8,0},{12,4},{0,8},{4,12},{9,1},{13,5},{1,9},{5,13},{10,2},{14,6},... | collective-permute-start | bytes 49160 | tf_op jit(solution)/shard_map/ppermute | solution.py:92
  42.2 2.5 %collective-permute-start.9 = (f32[4,8,128]{2,1,0:T(8,128)S(1)}, f32[4,8,128]{2,1,0:T(8,128)S(1)}, u32[]{:S(2)}, u32[]{:S(2)}) collective-permute-start(f32[4,8,128]{2,1,0:T(8,128)S(1)} %get-tuple-element.9), channel_id=1, source_target_pairs={{12,0},{8,4},{4,8},{0,12},{13,1},{9,5},{5,9},{1,13},{14,2},{10,6},... | collective-permute-start | bytes 49160 | tf_op jit(solution)/shard_map/ppermute | solution.py:92
  44.7 0.6 subtract_reduce_fusion.6
  45.3 0.7 %fusion.11 = f32[4,8,128]{2,1,0:T(8,128)S(1)} fusion(f32[4,8,128]{2,1,0:T(8,128)S(1)} %subtract_reduce_fusion.6, f32[4,128,128]{2,1,0:T(8,128)S(1)} %get-tuple-element.56, f32[4,8,128]{2,1,0:T(8,128)S(1)} %broadcast_multiply_fusion.2), kind=kLoop, calls=%fused_computation.35 | loop fusion | flops 1568768 | bytes 311296 | tf_op jit(solution)/shard_map/reduce_sum | solution.py:72
  46.1 0.6 subtract_reduce_fusion.5
  46.7 0.7 %fusion.13 = f32[4,8,128]{2,1,0:T(8,128)S(1)} fusion(f32[4,8,128]{2,1,0:T(8,128)S(1)} %subtract_reduce_fusion.5, f32[4,128,128]{2,1,0:T(8,128)S(1)} %get-tuple-element.54, f32[4,8,128]{2,1,0:T(8,128)S(1)} %broadcast_multiply_fusion.1), kind=kLoop, calls=%fused_computation.37 | loop fusion | flops 1568768 | bytes 311296 | tf_op jit(solution)/shard_map/reduce_sum | solution.py:72
  47.5 0.2 collective-permute-done.9
  47.7 0.6 subtract_reduce_fusion.4
  48.4 0.7 %fusion.15 = f32[4,8,128]{2,1,0:T(8,128)S(1)} fusion(f32[4,8,128]{2,1,0:T(8,128)S(1)} %subtract_reduce_fusion.4, f32[4,128,128]{2,1,0:T(8,128)S(1)} %get-tuple-element.52, f32[4,8,128]{2,1,0:T(8,128)S(1)} %broadcast_multiply_fusion), kind=kLoop, calls=%fused_computation.39 | loop fusion | flops 1568768 | bytes 311296 | tf_op jit(solution)/shard_map/reduce_sum | solution.py:72
  50.1 0.6 subtract_reduce_fusion.3
  50.8 0.7 %fusion.17 = f32[4,8,128]{2,1,0:T(8,128)S(1)} fusion(f32[4,8,128]{2,1,0:T(8,128)S(1)} %subtract_reduce_fusion.3, f32[4,8,128]{2,1,0:T(8,128)S(1)} %get-tuple-element.37, f32[4,128,128]{2,1,0:T(8,128)S(1)} %fusion.31), kind=kLoop, calls=%fused_computation.41 | loop fusion | flops 1568768 | bytes 311296 | tf_op jit(solution)/shard_map/reduce_sum | solution.py:72
  51.5 0.6 subtract_reduce_fusion
  52.1 0.7 %fusion.23 = f32[4,8,128]{2,1,0:T(8,128)S(1)} fusion(f32[4,8,128]{2,1,0:T(8,128)S(1)} %subtract_reduce_fusion, f32[4,8,128]{2,1,0:T(8,128)S(1)} %get-tuple-element.38, f32[4,128,128]{2,1,0:T(8,128)S(1)} %fusion.25), kind=kLoop, calls=%fused_computation.47 | loop fusion | flops 1568768 | bytes 311296 | tf_op jit(solution)/shard_map/reduce_sum | solution.py:72
  53.0 0.6 subtract_reduce_fusion.1
  53.6 0.7 %fusion.21 = f32[4,8,128]{2,1,0:T(8,128)S(1)} fusion(f32[4,8,128]{2,1,0:T(8,128)S(1)} %subtract_reduce_fusion.1, f32[4,8,128]{2,1,0:T(8,128)S(1)} %get-tuple-element.39, f32[4,128,128]{2,1,0:T(8,128)S(1)} %fusion.27), kind=kLoop, calls=%fused_computation.45 | loop fusion | flops 1568768 | bytes 311296 | tf_op jit(solution)/shard_map/reduce_sum | solution.py:72
  54.4 0.6 subtract_reduce_fusion.2
  55.1 0.7 %fusion.19 = f32[4,8,128]{2,1,0:T(8,128)S(1)} fusion(f32[4,8,128]{2,1,0:T(8,128)S(1)} %subtract_reduce_fusion.2, f32[4,8,128]{2,1,0:T(8,128)S(1)} %get-tuple-element.40, f32[4,128,128]{2,1,0:T(8,128)S(1)} %fusion.29), kind=kLoop, calls=%fused_computation.43 | loop fusion | flops 1568768 | bytes 311296 | tf_op jit(solution)/shard_map/reduce_sum | solution.py:72
  55.9 0.6 collective-permute-start.11
  56.5 2.4 %collective-permute-start.12 = (f32[4,8,128]{2,1,0:T(8,128)S(1)}, f32[4,8,128]{2,1,0:T(8,128)S(1)}, u32[]{:S(2)}, u32[]{:S(2)}) collective-permute-start(f32[4,8,128]{2,1,0:T(8,128)S(1)} %add_select_fusion.1), channel_id=1, source_target_pairs={{0,8},{4,12},{8,0},{12,4},{1,9},{5,13},{9,1},{13,5},{2,10},{6,14},... | collective-permute-start | bytes 49160 | tf_op jit(solution)/shard_map/ppermute | solution.py:92
  59.0 1.3 %collective-permute-start.13 = (f32[4,8,128]{2,1,0:T(8,128)S(1)}, f32[4,8,128]{2,1,0:T(8,128)S(1)}, u32[]{:S(2)}, u32[]{:S(2)}) collective-permute-start(f32[4,8,128]{2,1,0:T(8,128)S(1)} %add_select_fusion), channel_id=1, source_target_pairs={{0,12},{4,8},{8,4},{12,0},{1,13},{5,9},{9,5},{13,1},{2,14},{6,10},... | collective-permute-start | bytes 49160 | tf_op jit(solution)/shard_map/ppermute | solution.py:92
  60.4 0.8 %collective-permute-done.12 = f32[4,8,128]{2,1,0:T(8,128)S(1)} collective-permute-done((f32[4,8,128]{2,1,0:T(8,128)S(1)}, f32[4,8,128]{2,1,0:T(8,128)S(1)}, u32[]{:S(2)}, u32[]{:S(2)}) %collective-permute-start.12) | collective-permute-done | bytes 16416 | tf_op jit(solution)/shard_map/ppermute | solution.py:92
  61.2 3.3 %collective-permute-done.13 = f32[4,8,128]{2,1,0:T(8,128)S(1)} collective-permute-done((f32[4,8,128]{2,1,0:T(8,128)S(1)}, f32[4,8,128]{2,1,0:T(8,128)S(1)}, u32[]{:S(2)}, u32[]{:S(2)}) %collective-permute-start.13) | collective-permute-done | bytes 16416 | tf_op jit(solution)/shard_map/ppermute | solution.py:92
  65.1 0.6 copy.155
  65.8 0.5 collective-permute-done.14
  66.3 0.6 copy.154
  (162 shorter events, 7.0 us)
Async XLA Ops:
  1.3 6.8 %copy-start.6 = (s32[4]{0:T(128)S(1)}, s32[4]{0:T(128)}, u32[]{:S(2)}) copy-start(s32[4]{0:T(128)} %param.17) | copy-start | bytes 52
  1.3 6.8 %copy-start.4 = (s32[4,2]{0,1:T(2,128)S(1)}, s32[4,2]{0,1:T(2,128)}, u32[]{:S(2)}) copy-start(s32[4,2]{0,1:T(2,128)} %param.16) | copy-start | bytes 100
  1.3 6.8 %copy-start.5 = (s32[4,2]{0,1:T(2,128)S(1)}, s32[4,2]{0,1:T(2,128)}, u32[]{:S(2)}) copy-start(s32[4,2]{0,1:T(2,128)} %param.15) | copy-start | bytes 100
  1.3 7.0 %copy-start.3 = (s32[1024]{0:T(1024)S(1)}, s32[1024]{0:T(1024)}, u32[]{:S(2)}) copy-start(s32[1024]{0:T(1024)} %param.11) | copy-start | bytes 12292
  2.3 6.0 %copy-start.1 = (s32[16,1024]{1,0:T(8,128)S(1)}, s32[16,1024]{1,0:T(8,128)}, u32[]{:S(2)}) copy-start(s32[16,1024]{1,0:T(8,128)} %param.14) | copy-start | bytes 196612
  2.3 6.0 %copy-start.2 = (s32[16,1024]{1,0:T(8,128)S(1)}, s32[16,1024]{1,0:T(8,128)}, u32[]{:S(2)}) copy-start(s32[16,1024]{1,0:T(8,128)} %param.13) | copy-start | bytes 196612
  2.4 6.0 %copy-start = (bf16[64,1024]{1,0:T(8,128)(2,1)S(1)}, bf16[64,1024]{1,0:T(8,128)(2,1)}, u32[]{:S(2)}) copy-start(bf16[64,1024]{1,0:T(8,128)(2,1)} %param.9) | copy-start | bytes 393220
  2.4 12.9 %collective-permute-start.3 = (bf16[65,8,128]{2,1,0:T(8,128)(2,1)S(1)}, bf16[65,8,128]{2,1,0:T(8,128)(2,1)S(1)}, u32[]{:S(2)}, u32[]{:S(2)}) collective-permute-start(bf16[65,8,128]{2,1,0:T(8,128)(2,1)S(1)} %pad_maximum_fusion), channel_id=1, source_target_pairs={{12,0},{8,4},{4,8},{0,12},{13,1},{9,5},{5,9},{1,13},{14,2},{10,6},... | collective-permute-start | bytes 399368 | tf_op jit(solution)/shard_map/ppermute | solution.py:92
  7.5 11.2 %collective-permute-start.2 = (bf16[65,8,128]{2,1,0:T(8,128)(2,1)S(1)}, bf16[65,8,128]{2,1,0:T(8,128)(2,1)S(1)}, u32[]{:S(2)}, u32[]{:S(2)}) collective-permute-start(bf16[65,8,128]{2,1,0:T(8,128)(2,1)S(1)} %pad_maximum_fusion), channel_id=1, source_target_pairs={{8,0},{12,4},{0,8},{4,12},{9,1},{13,5},{1,9},{5,13},{10,2},{14,6},... | collective-permute-start | bytes 399368 | tf_op jit(solution)/shard_map/ppermute | solution.py:92
  7.5 11.7 %collective-permute-start.1 = (bf16[65,8,128]{2,1,0:T(8,128)(2,1)S(1)}, bf16[65,8,128]{2,1,0:T(8,128)(2,1)S(1)}, u32[]{:S(2)}, u32[]{:S(2)}) collective-permute-start(bf16[65,8,128]{2,1,0:T(8,128)(2,1)S(1)} %pad_maximum_fusion), channel_id=1, source_target_pairs={{4,0},{0,4},{12,8},{8,12},{5,1},{1,5},{13,9},{9,13},{6,2},{2,6},{1... | collective-permute-start | bytes 399368 | tf_op jit(solution)/shard_map/ppermute | solution.py:92
  8.2 1.2 %collective-permute-start = (s32[3,4,2]{1,2,0:T(2,128)S(1)}, s32[3,4,2]{1,2,0:T(2,128)S(1)}, u32[]{:S(2)}, u32[]{:S(2)}) collective-permute-start(s32[3,4,2]{1,2,0:T(2,128)S(1)} %get-tuple-element.50), channel_id=1, source_target_pairs={{0,1},{1,0},{2,3},{3,2},{4,5},{5,4},{6,7},{7,6},{8,9},{9,8},{10,11... | collective-permute-start | bytes 296 | tf_op jit(solution)/shard_map/ppermute | solution.py:78
  28.4 4.7 %collective-permute-start.4 = (f32[4,9,128]{2,0,1:T(4,128)S(1)}, f32[4,9,128]{2,0,1:T(4,128)S(1)}, u32[]{:S(2)}, u32[]{:S(2)}) collective-permute-start(f32[4,9,128]{2,0,1:T(4,128)S(1)} %pad_maximum_fusion.5), channel_id=1, source_target_pairs={{0,4},{4,0},{8,12},{12,8},{1,5},{5,1},{9,13},{13,9},{2,6},{6,2},{1... | collective-permute-start | bytes 55304 | tf_op jit(solution)/shard_map/ppermute | solution.py:92
  28.5 4.8 %collective-permute-start.5 = (f32[4,9,128]{2,0,1:T(4,128)S(1)}, f32[4,9,128]{2,0,1:T(4,128)S(1)}, u32[]{:S(2)}, u32[]{:S(2)}) collective-permute-start(f32[4,9,128]{2,0,1:T(4,128)S(1)} %pad_maximum_fusion.6), channel_id=1, source_target_pairs={{0,8},{4,12},{8,0},{12,4},{1,9},{5,13},{9,1},{13,5},{2,10},{6,14},... | collective-permute-start | bytes 55304 | tf_op jit(solution)/shard_map/ppermute | solution.py:92
  31.7 5.6 %collective-permute-start.6 = (f32[4,9,128]{2,0,1:T(4,128)S(1)}, f32[4,9,128]{2,0,1:T(4,128)S(1)}, u32[]{:S(2)}, u32[]{:S(2)}) collective-permute-start(f32[4,9,128]{2,0,1:T(4,128)S(1)} %pad_maximum_fusion.7), channel_id=1, source_target_pairs={{0,12},{4,8},{8,4},{12,0},{1,13},{5,9},{9,5},{13,1},{2,14},{6,10},... | collective-permute-start | bytes 55304 | tf_op jit(solution)/shard_map/ppermute | solution.py:92
  39.4 5.3 %collective-permute-start.7 = (f32[4,8,128]{2,1,0:T(8,128)S(1)}, f32[4,8,128]{2,1,0:T(8,128)S(1)}, u32[]{:S(2)}, u32[]{:S(2)}) collective-permute-start(f32[4,8,128]{2,1,0:T(8,128)S(1)} %get-tuple-element.7), channel_id=1, source_target_pairs={{4,0},{0,4},{12,8},{8,12},{5,1},{1,5},{13,9},{9,13},{6,2},{2,6},{1... | collective-permute-start | bytes 49160 | tf_op jit(solution)/shard_map/ppermute | solution.py:92
  40.3 5.8 %collective-permute-start.8 = (f32[4,8,128]{2,1,0:T(8,128)S(1)}, f32[4,8,128]{2,1,0:T(8,128)S(1)}, u32[]{:S(2)}, u32[]{:S(2)}) collective-permute-start(f32[4,8,128]{2,1,0:T(8,128)S(1)} %get-tuple-element.8), channel_id=1, source_target_pairs={{8,0},{12,4},{0,8},{4,12},{9,1},{13,5},{1,9},{5,13},{10,2},{14,6},... | collective-permute-start | bytes 49160 | tf_op jit(solution)/shard_map/ppermute | solution.py:92
  42.2 5.5 %collective-permute-start.9 = (f32[4,8,128]{2,1,0:T(8,128)S(1)}, f32[4,8,128]{2,1,0:T(8,128)S(1)}, u32[]{:S(2)}, u32[]{:S(2)}) collective-permute-start(f32[4,8,128]{2,1,0:T(8,128)S(1)} %get-tuple-element.9), channel_id=1, source_target_pairs={{12,0},{8,4},{4,8},{0,12},{13,1},{9,5},{5,9},{1,13},{14,2},{10,6},... | collective-permute-start | bytes 49160 | tf_op jit(solution)/shard_map/ppermute | solution.py:92
  49.8 15.3 %collective-permute-start.10 = (f32[8,8,128]{2,1,0:T(8,128)S(1)}, f32[8,8,128]{2,1,0:T(8,128)S(1)}, u32[]{:S(2)}, u32[]{:S(2)}) collective-permute-start(f32[8,8,128]{2,1,0:T(8,128)S(1)} %bitcast_subtract_fusion.2), channel_id=1, source_target_pairs={{0,1},{1,0},{2,3},{3,2},{4,5},{5,4},{6,7},{7,6},{8,9},{9,8},{10,11... | collective-permute-start | bytes 98312 | tf_op jit(solution)/shard_map/ppermute | solution.py:78
  55.9 4.5 %collective-permute-start.11 = (f32[4,8,128]{2,1,0:T(8,128)S(1)}, f32[4,8,128]{2,1,0:T(8,128)S(1)}, u32[]{:S(2)}, u32[]{:S(2)}) collective-permute-start(f32[4,8,128]{2,1,0:T(8,128)S(1)} %add_select_fusion.2), channel_id=1, source_target_pairs={{0,4},{4,0},{8,12},{12,8},{1,5},{5,1},{9,13},{13,9},{2,6},{6,2},{1... | collective-permute-start | bytes 49160 | tf_op jit(solution)/shard_map/ppermute | solution.py:92
  56.5 4.6 %collective-permute-start.12 = (f32[4,8,128]{2,1,0:T(8,128)S(1)}, f32[4,8,128]{2,1,0:T(8,128)S(1)}, u32[]{:S(2)}, u32[]{:S(2)}) collective-permute-start(f32[4,8,128]{2,1,0:T(8,128)S(1)} %add_select_fusion.1), channel_id=1, source_target_pairs={{0,8},{4,12},{8,0},{12,4},{1,9},{5,13},{9,1},{13,5},{2,10},{6,14},... | collective-permute-start | bytes 49160 | tf_op jit(solution)/shard_map/ppermute | solution.py:92
  59.0 5.5 %collective-permute-start.13 = (f32[4,8,128]{2,1,0:T(8,128)S(1)}, f32[4,8,128]{2,1,0:T(8,128)S(1)}, u32[]{:S(2)}, u32[]{:S(2)}) collective-permute-start(f32[4,8,128]{2,1,0:T(8,128)S(1)} %add_select_fusion), channel_id=1, source_target_pairs={{0,12},{4,8},{8,4},{12,0},{1,13},{5,9},{9,5},{13,1},{2,14},{6,10},... | collective-permute-start | bytes 49160 | tf_op jit(solution)/shard_map/ppermute | solution.py:92
  65.0 1.3 %collective-permute-start.14 = (f32[8,8,128]{2,1,0:T(8,128)S(1)}, f32[8,8,128]{2,1,0:T(8,128)S(1)}, u32[]{:S(2)}, u32[]{:S(2)}) collective-permute-start(f32[8,8,128]{2,1,0:T(8,128)S(1)} %bitcast_subtract_fusion), channel_id=1, source_target_pairs={{0,1},{1,0},{2,3},{3,2},{4,5},{5,4},{6,7},{7,6},{8,9},{9,8},{10,11... | collective-permute-start | bytes 98312 | tf_op jit(solution)/shard_map/ppermute | solution.py:78

commit v13 on v11

--- a/solution.py
+++ b/solution.py
@@ -120,15 +120,15 @@
         my_sub = lax.axis_index("sub")
         own_real = real_points.reshape(features, blocks, BLOCK)
         real_tags = real_cluster.reshape(1, blocks, BLOCK).astype(jnp.bfloat16)
-        own_synth = jnp.concatenate(
-            [synth_points, synth_cluster.astype(jnp.bfloat16)[None, :]], axis=0
-        ).reshape(features + 1, blocks, BLOCK)
-        log_real = jnp.log(
+        own_synth = jnp.concatenate([synth_points, synth_cluster.astype(jnp.bfloat16)[None, :]], axis=0)
+        log_real_flat = jnp.log(
             lax.dynamic_slice_in_dim(real_weight, my_sub * half, half, 0).astype(jnp.float32) + 0.5
-        ).reshape(half, blocks, BLOCK)
-        log_synth = jnp.log(
+        )
+        log_synth_flat = jnp.log(
             lax.dynamic_slice_in_dim(synth_weight, my_sub * half, half, 0).astype(jnp.float32) + 0.5
-        ).reshape(half, blocks, BLOCK)
+        )
+        log_real = log_real_flat.reshape(half, blocks, BLOCK)
+        log_synth = log_synth_flat.reshape(half, blocks, BLOCK)
 
         offsets = jnp.arange(peer_count, dtype=jnp.int32)
         if peer_count & (peer_count - 1) == 0:
@@ -146,7 +146,11 @@
         rows_used = rows_used.reshape(slot_count)
         usable = usable.reshape(slot_count)[:, None, None] > 0
         far = jnp.concatenate(
-            [pick_rows(everything[offset], wanted[offset], blocks) for offset in range(peer_count)], axis=0
+            [
+                pick_rows(everything[offset].reshape(features + 1, blocks, BLOCK), wanted[offset], blocks)
+                for offset in range(peer_count)
+            ],
+            axis=0,
         )
         far_y = far[:, :features]
         far_tags = far[:, features]
@@ -182,7 +186,13 @@
             highest = jnp.where(usable, highest, SENTINEL)
             mass_sum = jnp.where(usable, mass_sum, 0.0)
             block_top, summed = fold_blocks(highest, mass_sum, rows_used, blocks)
-            real_pot = finish(log_real, block_top, summed)
+            if sweep_index == ITERS - 1:
+                real_flat = finish(
+                    log_real_flat, block_top.reshape(half, point_count), summed.reshape(half, point_count)
+                )
+                real_pot = real_flat.reshape(half, blocks, BLOCK)
+            else:
+                real_pot = finish(log_real, block_top, summed)
 
             own_rows = pick_rows(real_pot, rows_used, blocks)
             chunks = [None] * peer_count
@@ -202,15 +212,20 @@
                 requested = back[:, half, 0].astype(jnp.int32)
                 back = back[:, :half]
             block_top, summed = fold_lse(back, requested, blocks)
-            synth_pot = finish(log_synth, block_top, summed)
+            if sweep_index == ITERS - 1:
+                synth_flat = finish(
+                    log_synth_flat, block_top.reshape(half, point_count), summed.reshape(half, point_count)
+                )
+            else:
+                synth_pot = finish(log_synth, block_top, summed)
 
         def both_halves(mine):
             other = swap(mine)
             first = jnp.where(my_sub == 0, mine, other)
             second = jnp.where(my_sub == 0, other, mine)
-            return jnp.concatenate([first, second], axis=0).reshape(marginals, point_count)
-
-        return (both_halves(real_pot), both_halves(synth_pot))
+            return jnp.concatenate([first, second], axis=0)
+
+        return (both_halves(real_flat), both_halves(synth_flat))
 
     return shards
 

time: 61.2 us -> 62.8 us (1.026)
  other arithmetic: 28.8 us -> 29.8 us
  local copies, waits for them, and re-layouts: 4.99 us -> 5.82 us
    concatenate x3, other arithmetic: 0.06 us -> 1.31 us  [the longest x2 1.27 us: both_halves(): return jnp.concatenate([first, second], axis=0)]
    unnamed x8 -> x12, local copies, waits for them, and re-layouts: 2.26 us -> 3.03 us
    unnamed x2 -> x3, other arithmetic: 1.55 us -> 0.81 us
    convert_element_type x0 -> x1, other arithmetic: none -> 0.69 us  [shards(): synth_cluster.astype(jnp.bfloat16)[None, :]]
    reduce_sum x13 -> x11, other arithmetic: 4.56 us -> 4.42 us  [pick_rows(): return jnp.sum(chosen, axis=2, dtype=values.dtype)]
    reduce_max x11 -> x13, other arithmetic: 7.55 us -> 7.49 us  [lse_parts(): highest = jnp.max(scores, axis=axis)]
  transfers between devices with their start and end apart: 15 -> 15, of which waited for: 4 -> 4; matrix products, arithmetic and copies ran while one was open for 40% -> 41% of each run, Pallas kernels for 0% -> 0%
where the time goes in v13:
time: 62.8 us; the launch traced here: 62.4 us
  other arithmetic  29.8 us (47%)
  starting transfers between devices  19.2 us (31%)
  local copies, waits for them, and re-layouts  5.82 us (9%)
  waiting for transfers between devices  3.58 us (6%)
  matrix products  2.53 us (4%)
  between operations  1.44 us (2%)
    ppermute x12, starting transfers between devices, exchange(): moved.append(lax.ppermute(chunks[offset], 'blk', perm))  19.1 us
    reduce_sum x14, other arithmetic, lse_parts(): jnp.sum(jnp.exp(scores - jnp.expand_dims(highest, axis)), axis=axis)  9.53 us
    reduce_max x13, other arithmetic, lse_parts(): highest = jnp.max(scores, axis=axis)  7.49 us
    reduce_sum x11, other arithmetic, pick_rows(): return jnp.sum(chosen, axis=2, dtype=values.dtype)  4.42 us
    ppermute x12, waiting for transfers between devices, exchange(): moved.append(lax.ppermute(chunks[offset], 'blk', perm))  3.05 us
    unnamed x12, local copies, waits for them, and re-layouts  3.03 us
    dot_general x2, matrix products, slot_costs(): jnp.einsum('gdi,gdj->gij', slot_real, slot_synth, preferred_element_type=...  2.53 us
    concatenate x2, other arithmetic, both_halves(): return jnp.concatenate([first, second], axis=0)  1.27 us
  transfers between devices with their start and end apart: 15, of which 4 were waited for; matrix products, arithmetic and copies ran while one was open for 41% of the time, Pallas kernels for 0%

profile of v13, /device:TPU:0, one launch (start us, length us, event | category | flops | bytes accessed | tf_op | source)
XLA Modules:
  0.0 62.4 jit_solution(3377332212224867210)
XLA Ops:
  0.6 0.9 %constant_dynamic-update-slice_fusion.1 = bf16[65,1024]{1,0:T(8,128)(2,1)S(1)} fusion(bf16[64,1024]{1,0:T(8,128)(2,1)} %param.10), kind=kLoop, calls=%fused_computation.152 | loop fusion | bytes 262144
  1.5 0.7 %convert_element_type.75 = bf16[1024]{0:T(1024)(128)(2,1)S(1)} convert(s32[1024]{0:T(1024)} %param.12) | non-fusion elementwise | flops 1024 | bytes 6144 | tf_op jit(solution)/shard_map/convert_element_type | solution.py:123
  2.3 5.1 %collective-permute-start.3 = (bf16[65,1024]{1,0:T(8,128)(2,1)S(1)}, bf16[65,1024]{1,0:T(8,128)(2,1)S(1)}, u32[]{:S(2)}, u32[]{:S(2)}) collective-permute-start(bf16[65,1024]{1,0:T(8,128)(2,1)S(1)} %constant_dynamic-update-slice_fusion), channel_id=1, source_target_pairs={{12,0},{8,4},{4,8},{0,12},{13,1},{9,5},{5,9},{1,13},{14,2},{10,6},... | collective-permute-start | bytes 399368 | tf_op jit(solution)/shard_map/ppermute | solution.py:92
  7.4 0.6 %collective-permute-start.1 = (bf16[65,1024]{1,0:T(8,128)(2,1)S(1)}, bf16[65,1024]{1,0:T(8,128)(2,1)S(1)}, u32[]{:S(2)}, u32[]{:S(2)}) collective-permute-start(bf16[65,1024]{1,0:T(8,128)(2,1)S(1)} %constant_dynamic-update-slice_fusion), channel_id=1, source_target_pairs={{4,0},{0,4},{12,8},{8,12},{5,1},{1,5},{13,9},{9,13},{6,2},{2,6},{1... | collective-permute-start | bytes 399368 | tf_op jit(solution)/shard_map/ppermute | solution.py:92
  8.0 0.7 %stack_broadcast_in_dim.2 = s32[1,4,2]{1,2,0:T(2,128)S(1)} broadcast(s32[4]{0:T(128)} %param.17), dimensions={1} | broadcast | bytes 48 | tf_op jit(solution)/shard_map/stack;broadcast_in_dim | solution.py:139
  8.7 0.7 %fusion.40 = (s32[3,1,4,2]{2,3,0,1:T(2,128)S(1)}, s32[3,4,2]{1,2,0:T(2,128)S(1)}) fusion(s32[1,4,2]{1,2,0:T(2,128)S(1)} %stack_broadcast_in_dim.2, s32[1,4,2]{1,2,0:T(2,128)} %bitcast.81, s32[1,4,2]{1,2,0:T(2,128)} %bitcast.82), kind=kLoop, calls=%fused_computation.194 | loop fusion | flops 48 | bytes 288 | tf_op jit(solution)/shard_map/stack | solution.py:140
  9.4 0.7 %convert_bitcast_fusion.3 = bf16[1,1,8,128]{3,2,1,0:T(8,128)(2,1)S(1)} fusion(s32[1024]{0:T(1024)} %param.12), kind=kLoop, calls=%fused_computation.196 | loop fusion | flops 1024 | bytes 6144 | tf_op jit(solution)/shard_map/concatenate | solution.py:123
  10.1 0.9 %copy.145 = bf16[8,8,8,128]{3,2,1,0:T(8,128)(2,1)S(1)} copy(bf16[8,8,8,128]{3,1,2,0:T(8,128)(2,1)} %bitcast.70) | data formatting | bytes 262144
  11.1 0.7 %convert_bitcast_fusion.1 = bf16[8,128]{1,0:T(8,128)(2,1)S(1)} fusion(s32[1024]{0:T(1024)} %param.11), kind=kLoop, calls=%fused_computation.184 | loop fusion | flops 1024 | bytes 6144 | tf_op jit(solution)/shard_map/convert_element_type | solution.py:122
  11.8 0.8 %fusion.31 = f32[1,8,8,128]{3,1,2,0:T(8,128)S(1)} fusion(s32[16,1024]{1,0:T(8,128)} %param.14, s32[]{:T(128)S(6)} %select_n.264), kind=kLoop, calls=%fused_computation.109 | loop fusion | flops 24576 | bytes 65540
  12.6 0.9 %copy.149 = bf16[8,8,8,128]{3,2,1,0:T(8,128)(2,1)S(1)} copy(bf16[8,8,8,128]{3,1,2,0:T(8,128)(2,1)} %bitcast.76) | data formatting | bytes 262144
  13.5 0.3 select_reduce_fusion.25
  13.8 0.3 slice_reduce_fusion.11
  14.5 1.5 %select_reduce_fusion = bf16[16,64,128]{2,1,0:T(8,128)(2,1)S(1)} fusion(pred[16,8]{1,0:T(8,128)(4,1)S(1)} %iota_compare_fusion.1, bf16[64,8,128]{2,1,0:T(8,128)(2,1)S(1)} %bitcast.69), kind=kLoop, calls=%fused_computation.48 | loop fusion | flops 1966080 | bytes 393344 | tf_op jit(solution)/shard_map/reduce_sum | solution.py:26
  16.5 0.3 slice_reduce_fusion.3
  17.5 2.3 %collective-permute-done.2 = bf16[65,1024]{1,0:T(8,128)(2,1)S(1)} collective-permute-done((bf16[65,1024]{1,0:T(8,128)(2,1)S(1)}, bf16[65,1024]{1,0:T(8,128)(2,1)S(1)}, u32[]{:S(2)}, u32[]{:S(2)}) %collective-permute-start.2) | collective-permute-done | bytes 133152 | tf_op jit(solution)/shard_map/ppermute | solution.py:92
  20.0 0.7 %select_reduce_fusion.1 = (bf16[4,65,128]{2,1,0:T(8,128)(2,1)S(1)}, bf16[4,65,128]{2,1,0:T(8,128)(2,1)S(1)}) fusion(pred[4,8]{1,0:T(4,128)(4,1)S(1)} %iota_compare_fusion.6, bf16[65,8,128]{2,1,0:T(8,128)(2,1)S(1)} %slice.217, bf16[65,8,128]{2,1,0:T(8,128)(2,1)S(1)} %slice.216, pred[4,8]{1,0:T(4,128)(4,1)S(1)} %iota_compare_fusion.7), kind=kLoop, calls=%fused_computation.55 | loop fusion | flops 998400 | bytes 399424 | tf_op jit(solution)/shard_map/reduce_sum | solution.py:26
  20.7 0.7 %select_reduce_fusion.3 = (bf16[4,65,128]{2,1,0:T(8,128)(2,1)S(1)}, bf16[4,65,128]{2,1,0:T(8,128)(2,1)S(1)}) fusion(pred[4,8]{1,0:T(4,128)(4,1)S(1)} %iota_compare_fusion.8, bf16[65,8,128]{2,1,0:T(8,128)(2,1)S(1)} %slice.215, bf16[65,8,128]{2,1,0:T(8,128)(2,1)S(1)} %maximum_bitcast_fusion, pred[4,8]{1,0:T(4,128)(4,1)S(1)} %iota_compare_fusion.9), kind=kLoop, calls=%fused_computation.57 | loop fusion | flops 998400 | bytes 399424 | tf_op jit(solution)/shard_map/reduce_sum | solution.py:26
  21.6 1.4 %fusion.26 = f32[16,128,128]{2,1,0:T(8,128)S(1)} fusion(bf16[16,64,128]{2,1,0:T(8,128)(2,1)S(1)} %select_reduce_fusion, f32[16,128]{1,0:T(8,128)S(1)} %broadcast_multiply_fusion.4, f32[16,128]{1,0:T(8,128)S(1)} %broadcast_multiply_fusion.5, bf16[16,128]{1,0:T(8,128)(2,1)S(1)} %select_reduce_fusion.23, bf16[16,128]{1,0:T(8,128)(2,1)S(1)} %bitcast.79, ...), kind=kOutput, calls=%fused_computation.53 | convolution fusion | flops 35127296 | bytes 1597440 | tf_op jit(solution)/shard_map/gdi,gdj->gij/dot_general | solution.py:61
  23.0 1.1 %fusion.27 = f32[16,128,128]{2,1,0:T(8,128)S(1)} fusion(bf16[16,64,128]{2,1,0:T(8,128)(2,1)S(1)} %select_reduce_fusion, f32[16,128]{1,0:T(8,128)S(1)} %broadcast_multiply_fusion.5, f32[16,128]{1,0:T(8,128)S(1)} %broadcast_multiply_fusion.4, bf16[16,128]{1,0:T(8,128)(2,1)S(1)} %bitcast.80, bf16[16,128]{1,0:T(8,128)(2,1)S(1)} %select_reduce_fusion.23, ...), kind=kOutput, calls=%fused_computation.54 | convolution fusion | flops 35127296 | bytes 1597440 | tf_op jit(solution)/shard_map/gdi,gdj->gij/dot_general | solution.py:61
  24.4 0.2 exponential_reduce_fusion.2
  25.1 0.2 copy-done
  25.3 0.2 select_reduce_fusion.15
  25.5 0.6 subtract_reduce_fusion.8
  26.1 0.7 %fusion.7 = f32[4,8,128]{2,1,0:T(8,128)S(1)} fusion(f32[4,8,128]{2,1,0:T(8,128)S(1)} %subtract_reduce_fusion.8, f32[4,128,128]{2,1,0:T(8,128)S(1)} %get-tuple-element.34, f32[4,8,128]{2,1,0:T(8,128)S(1)} %get-tuple-element.47), kind=kLoop, calls=%fused_computation.31 | loop fusion | flops 1568768 | bytes 311296 | tf_op jit(solution)/shard_map/reduce_sum | solution.py:72
  27.0 2.5 %collective-permute-start.6 = (f32[4,9,128]{2,0,1:T(4,128)S(1)}, f32[4,9,128]{2,0,1:T(4,128)S(1)}, u32[]{:S(2)}, u32[]{:S(2)}) collective-permute-start(f32[4,9,128]{2,0,1:T(4,128)S(1)} %pad_maximum_fusion.7), channel_id=1, source_target_pairs={{0,12},{4,8},{8,4},{12,0},{1,13},{5,9},{9,5},{13,1},{2,14},{6,10},... | collective-permute-start | bytes 55304 | tf_op jit(solution)/shard_map/ppermute | solution.py:92
  29.6 0.6 subtract_reduce_fusion.9
  30.2 0.7 %fusion.5 = f32[4,8,128]{2,1,0:T(8,128)S(1)} fusion(f32[4,8,128]{2,1,0:T(8,128)S(1)} %subtract_reduce_fusion.9, f32[4,128,128]{2,1,0:T(8,128)S(1)} %get-tuple-element.35, f32[4,8,128]{2,1,0:T(8,128)S(1)} %get-tuple-element.48), kind=kLoop, calls=%fused_computation.29 | loop fusion | flops 1568768 | bytes 311296 | tf_op jit(solution)/shard_map/reduce_sum | solution.py:72
  31.2 0.6 subtract_reduce_fusion.10
  31.8 0.7 %fusion.3 = f32[4,8,128]{2,1,0:T(8,128)S(1)} fusion(f32[4,8,128]{2,1,0:T(8,128)S(1)} %subtract_reduce_fusion.10, f32[4,128,128]{2,1,0:T(8,128)S(1)} %get-tuple-element.36, f32[4,8,128]{2,1,0:T(8,128)S(1)} %get-tuple-element.49), kind=kLoop, calls=%fused_computation.27 | loop fusion | flops 1568768 | bytes 311296 | tf_op jit(solution)/shard_map/reduce_sum | solution.py:72
  32.7 1.9 %collective-permute-start.4 = (f32[4,9,128]{2,0,1:T(4,128)S(1)}, f32[4,9,128]{2,0,1:T(4,128)S(1)}, u32[]{:S(2)}, u32[]{:S(2)}) collective-permute-start(f32[4,9,128]{2,0,1:T(4,128)S(1)} %pad_maximum_fusion.5), channel_id=1, source_target_pairs={{0,4},{4,0},{8,12},{12,8},{1,5},{5,1},{9,13},{13,9},{2,6},{6,2},{1... | collective-permute-start | bytes 55304 | tf_op jit(solution)/shard_map/ppermute | solution.py:92
  34.6 0.6 subtract_reduce_fusion.11
  35.2 0.7 %fusion.1 = f32[4,8,128]{2,1,0:T(8,128)S(1)} fusion(f32[4,8,128]{2,1,0:T(8,128)S(1)} %subtract_reduce_fusion.11, f32[4,128,128]{2,1,0:T(8,128)S(1)} %get-tuple-element.33, f32[4,8,128]{2,1,0:T(8,128)S(1)} %get-tuple-element.46), kind=kLoop, calls=%fused_computation.25 | loop fusion | flops 1568768 | bytes 311296 | tf_op jit(solution)/shard_map/reduce_sum | solution.py:72
  36.1 0.4 collective-permute-done.4
  36.9 0.2 select_reduce_fusion.13
  37.8 0.2 select_reduce_fusion.19
  38.0 2.4 %collective-permute-start.9 = (f32[4,8,128]{2,1,0:T(8,128)S(1)}, f32[4,8,128]{2,1,0:T(8,128)S(1)}, u32[]{:S(2)}, u32[]{:S(2)}) collective-permute-start(f32[4,8,128]{2,1,0:T(8,128)S(1)} %get-tuple-element.12), channel_id=1, source_target_pairs={{12,0},{8,4},{4,8},{0,12},{13,1},{9,5},{5,9},{1,13},{14,2},{10,6},... | collective-permute-start | bytes 49160 | tf_op jit(solution)/shard_map/ppermute | solution.py:92
  40.4 1.0 %collective-permute-start.8 = (f32[4,8,128]{2,1,0:T(8,128)S(1)}, f32[4,8,128]{2,1,0:T(8,128)S(1)}, u32[]{:S(2)}, u32[]{:S(2)}) collective-permute-start(f32[4,8,128]{2,1,0:T(8,128)S(1)} %get-tuple-element.11), channel_id=1, source_target_pairs={{8,0},{12,4},{0,8},{4,12},{9,1},{13,5},{1,9},{5,13},{10,2},{14,6},... | collective-permute-start | bytes 49160 | tf_op jit(solution)/shard_map/ppermute | solution.py:92
  41.4 1.1 %collective-permute-start.7 = (f32[4,8,128]{2,1,0:T(8,128)S(1)}, f32[4,8,128]{2,1,0:T(8,128)S(1)}, u32[]{:S(2)}, u32[]{:S(2)}) collective-permute-start(f32[4,8,128]{2,1,0:T(8,128)S(1)} %get-tuple-element.10), channel_id=1, source_target_pairs={{4,0},{0,4},{12,8},{8,12},{5,1},{1,5},{13,9},{9,13},{6,2},{2,6},{1... | collective-permute-start | bytes 49160 | tf_op jit(solution)/shard_map/ppermute | solution.py:92
  42.5 0.6 subtract_reduce_fusion.7
  43.1 0.7 %fusion.9 = f32[4,8,128]{2,1,0:T(8,128)S(1)} fusion(f32[4,8,128]{2,1,0:T(8,128)S(1)} %subtract_reduce_fusion.7, f32[4,128,128]{2,1,0:T(8,128)S(1)} %get-tuple-element.30, f32[4,8,128]{2,1,0:T(8,128)S(1)} %broadcast_multiply_fusion.3), kind=kLoop, calls=%fused_computation.33 | loop fusion | flops 1568768 | bytes 311296 | tf_op jit(solution)/shard_map/reduce_sum | solution.py:72
  43.9 0.6 subtract_reduce_fusion.4
  44.5 0.7 %fusion.15 = f32[4,8,128]{2,1,0:T(8,128)S(1)} fusion(f32[4,8,128]{2,1,0:T(8,128)S(1)} %subtract_reduce_fusion.4, f32[4,128,128]{2,1,0:T(8,128)S(1)} %get-tuple-element.37, f32[4,8,128]{2,1,0:T(8,128)S(1)} %broadcast_multiply_fusion), kind=kLoop, calls=%fused_computation.39 | loop fusion | flops 1568768 | bytes 311296 | tf_op jit(solution)/shard_map/reduce_sum | solution.py:72
  45.3 0.6 subtract_reduce_fusion.5
  45.9 0.7 %fusion.13 = f32[4,8,128]{2,1,0:T(8,128)S(1)} fusion(f32[4,8,128]{2,1,0:T(8,128)S(1)} %subtract_reduce_fusion.5, f32[4,128,128]{2,1,0:T(8,128)S(1)} %get-tuple-element.32, f32[4,8,128]{2,1,0:T(8,128)S(1)} %broadcast_multiply_fusion.1), kind=kLoop, calls=%fused_computation.37 | loop fusion | flops 1568768 | bytes 311296 | tf_op jit(solution)/shard_map/reduce_sum | solution.py:72
  46.7 0.6 subtract_reduce_fusion.6
  47.4 0.7 %fusion.11 = f32[4,8,128]{2,1,0:T(8,128)S(1)} fusion(f32[4,8,128]{2,1,0:T(8,128)S(1)} %subtract_reduce_fusion.6, f32[4,128,128]{2,1,0:T(8,128)S(1)} %get-tuple-element.31, f32[4,8,128]{2,1,0:T(8,128)S(1)} %broadcast_multiply_fusion.2), kind=kLoop, calls=%fused_computation.35 | loop fusion | flops 1568768 | bytes 311296 | tf_op jit(solution)/shard_map/reduce_sum | solution.py:72
  48.3 0.2 select_reduce_fusion.10
  48.9 0.2 select_reduce_fusion.8
  49.1 0.6 subtract_reduce_fusion
  49.8 1.0 %fusion.23 = f32[4,8,128]{2,1,0:T(8,128)S(1)} fusion(f32[4,8,128]{2,1,0:T(8,128)S(1)} %subtract_reduce_fusion, f32[4,8,128]{2,1,0:T(8,128)S(1)} %get-tuple-element.41, f32[4,128,128]{2,1,0:T(8,128)S(1)} %get-tuple-element.34), kind=kLoop, calls=%fused_computation.47 | loop fusion | flops 1568768 | bytes 311296 | tf_op jit(solution)/shard_map/reduce_sum | solution.py:72
  50.8 2.4 %collective-permute-start.13 = (f32[4,8,128]{2,1,0:T(8,128)S(1)}, f32[4,8,128]{2,1,0:T(8,128)S(1)}, u32[]{:S(2)}, u32[]{:S(2)}) collective-permute-start(f32[4,8,128]{2,1,0:T(8,128)S(1)} %add_select_fusion), channel_id=1, source_target_pairs={{0,12},{4,8},{8,4},{12,0},{1,13},{5,9},{9,5},{13,1},{2,14},{6,10},... | collective-permute-start | bytes 49160 | tf_op jit(solution)/shard_map/ppermute | solution.py:92
  53.2 0.6 subtract_reduce_fusion.1
  53.8 0.7 %fusion.21 = f32[4,8,128]{2,1,0:T(8,128)S(1)} fusion(f32[4,8,128]{2,1,0:T(8,128)S(1)} %subtract_reduce_fusion.1, f32[4,8,128]{2,1,0:T(8,128)S(1)} %get-tuple-element.42, f32[4,128,128]{2,1,0:T(8,128)S(1)} %get-tuple-element.35), kind=kLoop, calls=%fused_computation.45 | loop fusion | flops 1568768 | bytes 311296 | tf_op jit(solution)/shard_map/reduce_sum | solution.py:72
  54.7 0.6 subtract_reduce_fusion.2
  55.4 0.7 %fusion.19 = f32[4,8,128]{2,1,0:T(8,128)S(1)} fusion(f32[4,8,128]{2,1,0:T(8,128)S(1)} %subtract_reduce_fusion.2, f32[4,8,128]{2,1,0:T(8,128)S(1)} %get-tuple-element.43, f32[4,128,128]{2,1,0:T(8,128)S(1)} %get-tuple-element.36), kind=kLoop, calls=%fused_computation.43 | loop fusion | flops 1568768 | bytes 311296 | tf_op jit(solution)/shard_map/reduce_sum | solution.py:72
  56.2 2.0 %collective-permute-start.11 = (f32[4,8,128]{2,1,0:T(8,128)S(1)}, f32[4,8,128]{2,1,0:T(8,128)S(1)}, u32[]{:S(2)}, u32[]{:S(2)}) collective-permute-start(f32[4,8,128]{2,1,0:T(8,128)S(1)} %add_select_fusion.2), channel_id=1, source_target_pairs={{0,4},{4,0},{8,12},{12,8},{1,5},{5,1},{9,13},{13,9},{2,6},{6,2},{1... | collective-permute-start | bytes 49160 | tf_op jit(solution)/shard_map/ppermute | solution.py:92
  58.2 0.6 subtract_reduce_fusion.3
  58.8 0.7 %fusion.17 = f32[4,8,128]{2,1,0:T(8,128)S(1)} fusion(f32[4,8,128]{2,1,0:T(8,128)S(1)} %subtract_reduce_fusion.3, f32[4,8,128]{2,1,0:T(8,128)S(1)} %get-tuple-element.40, f32[4,128,128]{2,1,0:T(8,128)S(1)} %get-tuple-element.33), kind=kLoop, calls=%fused_computation.41 | loop fusion | flops 1568768 | bytes 311296 | tf_op jit(solution)/shard_map/reduce_sum | solution.py:72
  59.6 0.3 collective-permute-done.11
  60.1 0.2 select_reduce_fusion.6
  60.6 0.6 %pad_maximum_fusion.2 = f32[16,1024]{1,0:T(8,128)} fusion(f32[8,1024]{1,0:T(8,128)S(1)} %get-tuple-element.45, f32[8,1024]{1,0:T(8,128)S(1)} %get-tuple-element.44), kind=kLoop, calls=%fused_computation.92 | loop fusion | flops 16384 | bytes 131072 | tf_op jit(solution)/shard_map/concatenate | solution.py:226
  61.2 0.5 collective-permute-done.14
  61.8 0.6 %pad_maximum_fusion.4 = f32[16,1024]{1,0:T(8,128)} fusion(f32[8,1024]{1,0:T(8,128)S(1)} %get-tuple-element.39, f32[8,1024]{1,0:T(8,128)S(1)} %get-tuple-element.38), kind=kLoop, calls=%fused_computation.94 | loop fusion | flops 16384 | bytes 131072 | tf_op jit(solution)/shard_map/concatenate | solution.py:226
  (129 shorter events, 5.6 us)
Async XLA Ops:
  2.3 15.2 %collective-permute-start.3 = (bf16[65,1024]{1,0:T(8,128)(2,1)S(1)}, bf16[65,1024]{1,0:T(8,128)(2,1)S(1)}, u32[]{:S(2)}, u32[]{:S(2)}) collective-permute-start(bf16[65,1024]{1,0:T(8,128)(2,1)S(1)} %constant_dynamic-update-slice_fusion), channel_id=1, source_target_pairs={{12,0},{8,4},{4,8},{0,12},{13,1},{9,5},{5,9},{1,13},{14,2},{10,6},... | collective-permute-start | bytes 399368 | tf_op jit(solution)/shard_map/ppermute | solution.py:92
  7.4 12.5 %collective-permute-start.2 = (bf16[65,1024]{1,0:T(8,128)(2,1)S(1)}, bf16[65,1024]{1,0:T(8,128)(2,1)S(1)}, u32[]{:S(2)}, u32[]{:S(2)}) collective-permute-start(bf16[65,1024]{1,0:T(8,128)(2,1)S(1)} %constant_dynamic-update-slice_fusion), channel_id=1, source_target_pairs={{8,0},{12,4},{0,8},{4,12},{9,1},{13,5},{1,9},{5,13},{10,2},{14,6},... | collective-permute-start | bytes 399368 | tf_op jit(solution)/shard_map/ppermute | solution.py:92
  7.4 12.5 %collective-permute-start.1 = (bf16[65,1024]{1,0:T(8,128)(2,1)S(1)}, bf16[65,1024]{1,0:T(8,128)(2,1)S(1)}, u32[]{:S(2)}, u32[]{:S(2)}) collective-permute-start(bf16[65,1024]{1,0:T(8,128)(2,1)S(1)} %constant_dynamic-update-slice_fusion), channel_id=1, source_target_pairs={{4,0},{0,4},{12,8},{8,12},{5,1},{1,5},{13,9},{9,13},{6,2},{2,6},{1... | collective-permute-start | bytes 399368 | tf_op jit(solution)/shard_map/ppermute | solution.py:92
  9.4 4.1 %collective-permute-start = (s32[3,4,2]{1,2,0:T(2,128)S(1)}, s32[3,4,2]{1,2,0:T(2,128)S(1)}, u32[]{:S(2)}, u32[]{:S(2)}) collective-permute-start(s32[3,4,2]{1,2,0:T(2,128)S(1)} %get-tuple-element.51), channel_id=1, source_target_pairs={{0,1},{1,0},{2,3},{3,2},{4,5},{5,4},{6,7},{7,6},{8,9},{9,8},{10,11... | collective-permute-start | bytes 296 | tf_op jit(solution)/shard_map/ppermute | solution.py:78
  24.4 0.8 %copy-start = (s32[16,1024]{1,0:T(8,128)S(1)}, s32[16,1024]{1,0:T(8,128)}, u32[]{:S(2)}) copy-start(s32[16,1024]{1,0:T(8,128)} %param.13) | copy-start | bytes 196612
  27.0 9.0 %collective-permute-start.6 = (f32[4,9,128]{2,0,1:T(4,128)S(1)}, f32[4,9,128]{2,0,1:T(4,128)S(1)}, u32[]{:S(2)}, u32[]{:S(2)}) collective-permute-start(f32[4,9,128]{2,0,1:T(4,128)S(1)} %pad_maximum_fusion.7), channel_id=1, source_target_pairs={{0,12},{4,8},{8,4},{12,0},{1,13},{5,9},{9,5},{13,1},{2,14},{6,10},... | collective-permute-start | bytes 55304 | tf_op jit(solution)/shard_map/ppermute | solution.py:92
  31.1 4.9 %collective-permute-start.5 = (f32[4,9,128]{2,0,1:T(4,128)S(1)}, f32[4,9,128]{2,0,1:T(4,128)S(1)}, u32[]{:S(2)}, u32[]{:S(2)}) collective-permute-start(f32[4,9,128]{2,0,1:T(4,128)S(1)} %pad_maximum_fusion.6), channel_id=1, source_target_pairs={{0,8},{4,12},{8,0},{12,4},{1,9},{5,13},{9,1},{13,5},{2,10},{6,14},... | collective-permute-start | bytes 55304 | tf_op jit(solution)/shard_map/ppermute | solution.py:92
  32.7 3.8 %collective-permute-start.4 = (f32[4,9,128]{2,0,1:T(4,128)S(1)}, f32[4,9,128]{2,0,1:T(4,128)S(1)}, u32[]{:S(2)}, u32[]{:S(2)}) collective-permute-start(f32[4,9,128]{2,0,1:T(4,128)S(1)} %pad_maximum_fusion.5), channel_id=1, source_target_pairs={{0,4},{4,0},{8,12},{12,8},{1,5},{5,1},{9,13},{13,9},{2,6},{6,2},{1... | collective-permute-start | bytes 55304 | tf_op jit(solution)/shard_map/ppermute | solution.py:92
  38.0 5.8 %collective-permute-start.9 = (f32[4,8,128]{2,1,0:T(8,128)S(1)}, f32[4,8,128]{2,1,0:T(8,128)S(1)}, u32[]{:S(2)}, u32[]{:S(2)}) collective-permute-start(f32[4,8,128]{2,1,0:T(8,128)S(1)} %get-tuple-element.12), channel_id=1, source_target_pairs={{12,0},{8,4},{4,8},{0,12},{13,1},{9,5},{5,9},{1,13},{14,2},{10,6},... | collective-permute-start | bytes 49160 | tf_op jit(solution)/shard_map/ppermute | solution.py:92
  40.4 4.8 %collective-permute-start.8 = (f32[4,8,128]{2,1,0:T(8,128)S(1)}, f32[4,8,128]{2,1,0:T(8,128)S(1)}, u32[]{:S(2)}, u32[]{:S(2)}) collective-permute-start(f32[4,8,128]{2,1,0:T(8,128)S(1)} %get-tuple-element.11), channel_id=1, source_target_pairs={{8,0},{12,4},{0,8},{4,12},{9,1},{13,5},{1,9},{5,13},{10,2},{14,6},... | collective-permute-start | bytes 49160 | tf_op jit(solution)/shard_map/ppermute | solution.py:92
  41.4 5.3 %collective-permute-start.7 = (f32[4,8,128]{2,1,0:T(8,128)S(1)}, f32[4,8,128]{2,1,0:T(8,128)S(1)}, u32[]{:S(2)}, u32[]{:S(2)}) collective-permute-start(f32[4,8,128]{2,1,0:T(8,128)S(1)} %get-tuple-element.10), channel_id=1, source_target_pairs={{4,0},{0,4},{12,8},{8,12},{5,1},{1,5},{13,9},{9,13},{6,2},{2,6},{1... | collective-permute-start | bytes 49160 | tf_op jit(solution)/shard_map/ppermute | solution.py:92
  48.8 11.8 %collective-permute-start.10 = (f32[8,1024]{1,0:T(8,128)S(1)}, f32[8,1024]{1,0:T(8,128)S(1)}, u32[]{:S(2)}, u32[]{:S(2)}) collective-permute-start(f32[8,1024]{1,0:T(8,128)S(1)} %bitcast_subtract_fusion.1), channel_id=1, source_target_pairs={{0,1},{1,0},{2,3},{3,2},{4,5},{5,4},{6,7},{7,6},{8,9},{9,8},{10,11... | collective-permute-start | bytes 98312 | tf_op jit(solution)/shard_map/ppermute | solution.py:78
  50.8 8.8 %collective-permute-start.13 = (f32[4,8,128]{2,1,0:T(8,128)S(1)}, f32[4,8,128]{2,1,0:T(8,128)S(1)}, u32[]{:S(2)}, u32[]{:S(2)}) collective-permute-start(f32[4,8,128]{2,1,0:T(8,128)S(1)} %add_select_fusion), channel_id=1, source_target_pairs={{0,12},{4,8},{8,4},{12,0},{1,13},{5,9},{9,5},{13,1},{2,14},{6,10},... | collective-permute-start | bytes 49160 | tf_op jit(solution)/shard_map/ppermute | solution.py:92
  54.6 5.0 %collective-permute-start.12 = (f32[4,8,128]{2,1,0:T(8,128)S(1)}, f32[4,8,128]{2,1,0:T(8,128)S(1)}, u32[]{:S(2)}, u32[]{:S(2)}) collective-permute-start(f32[4,8,128]{2,1,0:T(8,128)S(1)} %add_select_fusion.1), channel_id=1, source_target_pairs={{0,8},{4,12},{8,0},{12,4},{1,9},{5,13},{9,1},{13,5},{2,10},{6,14},... | collective-permute-start | bytes 49160 | tf_op jit(solution)/shard_map/ppermute | solution.py:92
  56.1 4.4 %copy-start.1 = (s32[16,1024]{1,0:T(8,128)S(1)}, s32[16,1024]{1,0:T(8,128)}, u32[]{:S(2)}) copy-start(s32[16,1024]{1,0:T(8,128)} %param.14) | copy-start | bytes 196612
  56.2 3.8 %collective-permute-start.11 = (f32[4,8,128]{2,1,0:T(8,128)S(1)}, f32[4,8,128]{2,1,0:T(8,128)S(1)}, u32[]{:S(2)}, u32[]{:S(2)}) collective-permute-start(f32[4,8,128]{2,1,0:T(8,128)S(1)} %add_select_fusion.2), channel_id=1, source_target_pairs={{0,4},{4,0},{8,12},{12,8},{1,5},{5,1},{9,13},{13,9},{2,6},{6,2},{1... | collective-permute-start | bytes 49160 | tf_op jit(solution)/shard_map/ppermute | solution.py:92
  60.5 1.3 %collective-permute-start.14 = (f32[8,1024]{1,0:T(8,128)S(1)}, f32[8,1024]{1,0:T(8,128)S(1)}, u32[]{:S(2)}, u32[]{:S(2)}) collective-permute-start(f32[8,1024]{1,0:T(8,128)S(1)} %bitcast_subtract_fusion), channel_id=1, source_target_pairs={{0,1},{1,0},{2,3},{3,2},{4,5},{5,4},{6,7},{7,6},{8,9},{9,8},{10,11... | collective-permute-start | bytes 98312 | tf_op jit(solution)/shard_map/ppermute | solution.py:78

commit v14 on v11

--- a/solution.py
+++ b/solution.py
@@ -119,10 +119,7 @@
         my_blk = lax.axis_index("blk")
         my_sub = lax.axis_index("sub")
         own_real = real_points.reshape(features, blocks, BLOCK)
-        real_tags = real_cluster.reshape(1, blocks, BLOCK).astype(jnp.bfloat16)
-        own_synth = jnp.concatenate(
-            [synth_points, synth_cluster.astype(jnp.bfloat16)[None, :]], axis=0
-        ).reshape(features + 1, blocks, BLOCK)
+        real_tags = real_cluster.reshape(1, blocks, BLOCK)
         log_real = jnp.log(
             lax.dynamic_slice_in_dim(real_weight, my_sub * half, half, 0).astype(jnp.float32) + 0.5
         ).reshape(half, blocks, BLOCK)
@@ -135,7 +132,8 @@
             peers = jnp.bitwise_xor(my_blk, offsets)
         else:
             peers = (my_blk + offsets) % peer_count
-        everything = send_down([own_synth] * peer_count)
+        everything = send_down([synth_points] * peer_count)
+        everything_tags = send_down([synth_cluster] * peer_count)
         lists = jnp.stack([pair_block, pair_row, jnp.broadcast_to(pair_count[:, None], pair_block.shape)])
         lists = jnp.stack([lists, swap(lists)], axis=1)
         listed = lax.broadcasted_iota(jnp.int32, lists.shape[1:], 2) < lists[2]
@@ -145,11 +143,20 @@
         wanted = wanted.reshape(peer_count, wide)
         rows_used = rows_used.reshape(slot_count)
         usable = usable.reshape(slot_count)[:, None, None] > 0
-        far = jnp.concatenate(
-            [pick_rows(everything[offset], wanted[offset], blocks) for offset in range(peer_count)], axis=0
+        far_y = jnp.concatenate(
+            [
+                pick_rows(everything[offset].reshape(features, blocks, BLOCK), wanted[offset], blocks)
+                for offset in range(peer_count)
+            ],
+            axis=0,
         )
-        far_y = far[:, :features]
-        far_tags = far[:, features]
+        far_tags = jnp.concatenate(
+            [
+                pick_rows(everything_tags[offset].reshape(1, blocks, BLOCK), wanted[offset], blocks)[:, 0]
+                for offset in range(peer_count)
+            ],
+            axis=0,
+        )
         slot_x = pick_rows(own_real, rows_used, blocks)
         slot_tags = pick_rows(real_tags, rows_used, blocks)[:, 0]
         cost_cols = slot_costs(slot_x, slot_tags, far_y, far_tags) / SMOOTH

time: 61.2 us -> 67.4 us (1.10)
  starting transfers between devices: 19.2 us -> 23.8 us
  waiting for transfers between devices: 3.96 us -> 7.65 us
  other arithmetic: 28.8 us -> 26.7 us
  local copies, waits for them, and re-layouts: 4.99 us -> 5.96 us
  matrix products: 2.53 us -> 1.59 us
    ppermute x12 -> x15, starting transfers between devices: 19.1 us -> 23.6 us  [exchange(): moved.append(lax.ppermute(chunks[offset], 'blk', perm))]
    ppermute x12 -> x15, waiting for transfers between devices: 3.45 us -> 7.14 us  [exchange(): moved.append(lax.ppermute(chunks[offset], 'blk', perm))]
    unnamed x8 -> x14, local copies, waits for them, and re-layouts: 2.26 us -> 3.24 us
    dot_general x2, matrix products: 2.53 us -> 1.59 us  [slot_costs(): jnp.einsum('gdi,gdj->gij', slot_real, slot_synth, preferred_element_type=...]
    concatenate x3 -> x1, other arithmetic: 0.78 us -> 0.01 us  [shards(): jnp.concatenate([pick_rows(everything_tags[offset].reshape(1, blocks, BLO...]
    unnamed x2 -> x1, other arithmetic: 1.55 us -> 0.8 us
    convert_element_type x1 -> x0, other arithmetic: 0.69 us -> none  [shards(): real_tags = real_cluster.reshape(1, blocks, BLOCK).astype(jnp.bfloat16)]
    reduce_sum x13 -> x15, other arithmetic: 4.56 us -> 4.75 us  [pick_rows(): return jnp.sum(chosen, axis=2, dtype=values.dtype)]
  transfers between devices with their start and end apart: 15 -> 18, of which waited for: 4 -> 5; matrix products, arithmetic and copies ran while one was open for 40% -> 36% of each run, Pallas kernels for 0% -> 0%
where the time goes in v14:
time: 67.4 us; the launch traced here: 67.1 us
  other arithmetic  26.7 us (40%)
  starting transfers between devices  23.8 us (35%)
  waiting for transfers between devices  7.65 us (11%)
  local copies, waits for them, and re-layouts  5.96 us (9%)
  matrix products  1.59 us (2%)
  between operations  1.41 us (2%)
    ppermute x15, starting transfers between devices, exchange(): moved.append(lax.ppermute(chunks[offset], 'blk', perm))  23.6 us
    reduce_sum x14, other arithmetic, lse_parts(): jnp.sum(jnp.exp(scores - jnp.expand_dims(highest, axis)), axis=axis)  9.48 us
    reduce_max x13, other arithmetic, lse_parts(): highest = jnp.max(scores, axis=axis)  7.49 us
    ppermute x15, waiting for transfers between devices, exchange(): moved.append(lax.ppermute(chunks[offset], 'blk', perm))  7.14 us
    reduce_sum x15, other arithmetic, pick_rows(): return jnp.sum(chosen, axis=2, dtype=values.dtype)  4.75 us
    unnamed x14, local copies, waits for them, and re-layouts  3.24 us
    dot_general x2, matrix products, slot_costs(): jnp.einsum('gdi,gdj->gij', slot_real, slot_synth, preferred_element_type=...  1.59 us
  transfers between devices with their start and end apart: 18, of which 5 were waited for; matrix products, arithmetic and copies ran while one was open for 36% of the time, Pallas kernels for 0%

profile of v14, /device:TPU:0, one launch (start us, length us, event | category | flops | bytes accessed | tf_op | source)
XLA Modules:
  0.0 67.1 jit_solution(17500830261018003550)
XLA Ops:
  0.7 5.1 %collective-permute-start.6 = (s32[1024]{0:T(1024)}, s32[1024]{0:T(1024)S(1)}, u32[]{:S(2)}, u32[]{:S(2)}) collective-permute-start(s32[1024]{0:T(1024)} %param.12), channel_id=1, source_target_pairs={{12,0},{8,4},{4,8},{0,12},{13,1},{9,5},{5,9},{1,13},{14,2},{10,6},... | collective-permute-start | bytes 12296 | tf_op jit(solution)/shard_map/ppermute | solution.py:92
  5.8 0.6 collective-permute-start.4
  6.4 0.7 stack_broadcast_in_dim.2
  7.1 0.7 %fusion.37 = (s32[3,1,4,2]{2,3,0,1:T(2,128)S(1)}, s32[3,4,2]{1,2,0:T(2,128)S(1)}) fusion(s32[1,4,2]{1,2,0:T(2,128)S(1)} %stack_broadcast_in_dim.2, s32[1,4,2]{1,2,0:T(2,128)} %bitcast.82, s32[1,4,2]{1,2,0:T(2,128)} %bitcast.83), kind=kLoop, calls=%fused_computation.190 | loop fusion | flops 48 | bytes 288 | tf_op jit(solution)/shard_map/stack | solution.py:138
  7.8 3.8 %collective-permute-start.3 = (bf16[64,1024]{1,0:T(8,128)(2,1)}, bf16[64,1024]{1,0:T(8,128)(2,1)S(1)}, u32[]{:S(2)}, u32[]{:S(2)}) collective-permute-start(bf16[64,1024]{1,0:T(8,128)(2,1)} %param.10), channel_id=1, source_target_pairs={{12,0},{8,4},{4,8},{0,12},{13,1},{9,5},{5,9},{1,13},{14,2},{10,6},... | collective-permute-start | bytes 393224 | tf_op jit(solution)/shard_map/ppermute | solution.py:92
  11.7 0.9 %copy.137 = bf16[8,8,8,128]{3,2,1,0:T(8,128)(2,1)S(1)} copy(bf16[8,8,8,128]{3,1,2,0:T(8,128)(2,1)} %bitcast.68) | data formatting | bytes 262144
  12.6 0.8 %multiply_bitcast_fusion = (f32[1,8,8,128]{3,1,2,0:T(8,128)S(1)}, f32[1,8,8,128]{3,1,2,0:T(8,128)S(1)}) fusion(s32[16,1024]{1,0:T(8,128)} %param.14, s32[]{:T(128)S(6)} %select_n.306, s32[16,1024]{1,0:T(8,128)} %param.13), kind=kLoop, calls=%fused_computation.104 | loop fusion | flops 49152 | bytes 131076
  13.4 0.9 %copy.133 = bf16[8,8,8,128]{3,2,1,0:T(8,128)(2,1)S(1)} copy(bf16[8,8,8,128]{3,1,2,0:T(8,128)(2,1)} %bitcast.69) | data formatting | bytes 262144
  14.5 0.3 select_reduce_fusion.29
  14.8 0.3 slice_reduce_fusion.11
  15.4 1.5 %select_reduce_fusion = bf16[16,64,128]{2,1,0:T(8,128)(2,1)S(1)} fusion(pred[16,8]{1,0:T(8,128)(4,1)S(1)} %iota_compare_fusion.1, bf16[64,8,128]{2,1,0:T(8,128)(2,1)S(1)} %bitcast.62), kind=kLoop, calls=%fused_computation.48 | loop fusion | flops 1966080 | bytes 393344 | tf_op jit(solution)/shard_map/reduce_sum | solution.py:26
  17.7 0.3 slice_reduce_fusion.3
  18.5 0.7 %collective-permute-start.1 = (bf16[64,1024]{1,0:T(8,128)(2,1)S(1)}, bf16[64,1024]{1,0:T(8,128)(2,1)S(1)}, u32[]{:S(2)}, u32[]{:S(2)}) collective-permute-start(bf16[64,1024]{1,0:T(8,128)(2,1)S(1)} %copy-done), channel_id=1, source_target_pairs={{4,0},{0,4},{12,8},{8,12},{5,1},{1,5},{13,9},{9,13},{6,2},{2,6},{1... | collective-permute-start | bytes 393224 | tf_op jit(solution)/shard_map/ppermute | solution.py:92
  19.6 3.7 %collective-permute-done.2 = bf16[64,1024]{1,0:T(8,128)(2,1)S(1)} collective-permute-done((bf16[64,1024]{1,0:T(8,128)(2,1)}, bf16[64,1024]{1,0:T(8,128)(2,1)S(1)}, u32[]{:S(2)}, u32[]{:S(2)}) %collective-permute-start.2) | collective-permute-done | bytes 131104 | tf_op jit(solution)/shard_map/ppermute | solution.py:92
  23.3 2.7 %collective-permute-done.1 = bf16[64,1024]{1,0:T(8,128)(2,1)S(1)} collective-permute-done((bf16[64,1024]{1,0:T(8,128)(2,1)S(1)}, bf16[64,1024]{1,0:T(8,128)(2,1)S(1)}, u32[]{:S(2)}, u32[]{:S(2)}) %collective-permute-start.1) | collective-permute-done | bytes 131104 | tf_op jit(solution)/shard_map/ppermute | solution.py:92
  26.0 0.7 %select_reduce_fusion.12 = (bf16[4,64,128]{2,1,0:T(8,128)(2,1)S(1)}, bf16[4,64,128]{2,1,0:T(8,128)(2,1)S(1)}) fusion(pred[4,8]{1,0:T(4,128)(4,1)S(1)} %iota_compare_fusion.6, bf16[64,8,128]{2,1,0:T(8,128)(2,1)S(1)} %bitcast.63, bf16[64,8,128]{2,1,0:T(8,128)(2,1)S(1)} %bitcast.65, pred[4,8]{1,0:T(4,128)(4,1)S(1)} %iota_compare_fusion.7), kind=kLoop, calls=%fused_computation.68 | loop fusion | flops 983040 | bytes 393280 | tf_op jit(solution)/shard_map/reduce_sum | solution.py:26
  26.7 0.7 %select_reduce_fusion.14 = (bf16[4,64,128]{2,1,0:T(8,128)(2,1)S(1)}, bf16[4,64,128]{2,1,0:T(8,128)(2,1)S(1)}) fusion(pred[4,8]{1,0:T(4,128)(4,1)S(1)} %iota_compare_fusion.8, bf16[64,8,128]{2,1,0:T(8,128)(2,1)S(1)} %bitcast.64, bf16[64,8,128]{2,1,0:T(8,128)(2,1)S(1)} %bitcast.61, pred[4,8]{1,0:T(4,128)(4,1)S(1)} %iota_compare_fusion.9), kind=kLoop, calls=%fused_computation.70 | loop fusion | flops 983040 | bytes 393280 | tf_op jit(solution)/shard_map/reduce_sum | solution.py:26
  27.5 0.8 %fusion.26 = f32[16,128,128]{2,1,0:T(8,128)S(1)} fusion(bf16[16,64,128]{2,1,0:T(8,128)(2,1)S(1)} %select_reduce_fusion, s32[16,128]{1,0:T(8,128)S(1)} %select_reduce_fusion.23, s32[16,128]{1,0:T(8,128)S(1)} %pad_add_fusion, f32[16,128]{1,0:T(8,128)S(1)} %broadcast_multiply_fusion.4, f32[16,128]{1,0:T(8,128)S(1)} %broadcast_multiply_fusion.5, ...), kind=kOutput, calls=%fused_computation.53 | convolution fusion | flops 35520512 | bytes 1605632 | tf_op jit(solution)/shard_map/gdi,gdj->gij/dot_general | solution.py:61
  28.3 0.8 %fusion.27 = f32[16,128,128]{2,1,0:T(8,128)S(1)} fusion(bf16[16,64,128]{2,1,0:T(8,128)(2,1)S(1)} %select_reduce_fusion, s32[16,128]{1,0:T(8,128)S(1)} %pad_add_fusion, s32[16,128]{1,0:T(8,128)S(1)} %select_reduce_fusion.23, f32[16,128]{1,0:T(8,128)S(1)} %broadcast_multiply_fusion.5, f32[16,128]{1,0:T(8,128)S(1)} %broadcast_multiply_fusion.4, ...), kind=kOutput, calls=%fused_computation.54 | convolution fusion | flops 35520512 | bytes 1605632 | tf_op jit(solution)/shard_map/gdi,gdj->gij/dot_general | solution.py:61
  29.4 0.2 exponential_reduce_fusion.2
  30.1 0.2 select_reduce_fusion.11
  30.3 0.6 subtract_reduce_fusion.8
  30.9 0.9 %fusion.7 = f32[4,8,128]{2,1,0:T(8,128)S(1)} fusion(f32[4,8,128]{2,1,0:T(8,128)S(1)} %subtract_reduce_fusion.8, f32[4,128,128]{2,1,0:T(8,128)S(1)} %get-tuple-element.34, f32[4,8,128]{2,1,0:T(8,128)S(1)} %get-tuple-element.47), kind=kLoop, calls=%fused_computation.31 | loop fusion | flops 1568768 | bytes 311296 | tf_op jit(solution)/shard_map/reduce_sum | solution.py:72
  32.0 2.4 %collective-permute-start.9 = (f32[4,9,128]{2,0,1:T(4,128)S(1)}, f32[4,9,128]{2,0,1:T(4,128)S(1)}, u32[]{:S(2)}, u32[]{:S(2)}) collective-permute-start(f32[4,9,128]{2,0,1:T(4,128)S(1)} %pad_maximum_fusion.7), channel_id=1, source_target_pairs={{0,12},{4,8},{8,4},{12,0},{1,13},{5,9},{9,5},{13,1},{2,14},{6,10},... | collective-permute-start | bytes 55304 | tf_op jit(solution)/shard_map/ppermute | solution.py:92
  34.4 0.6 subtract_reduce_fusion.9
  35.0 0.7 %fusion.5 = f32[4,8,128]{2,1,0:T(8,128)S(1)} fusion(f32[4,8,128]{2,1,0:T(8,128)S(1)} %subtract_reduce_fusion.9, f32[4,128,128]{2,1,0:T(8,128)S(1)} %get-tuple-element.35, f32[4,8,128]{2,1,0:T(8,128)S(1)} %get-tuple-element.48), kind=kLoop, calls=%fused_computation.29 | loop fusion | flops 1568768 | bytes 311296 | tf_op jit(solution)/shard_map/reduce_sum | solution.py:72
  36.0 0.6 subtract_reduce_fusion.10
  36.6 0.7 %fusion.3 = f32[4,8,128]{2,1,0:T(8,128)S(1)} fusion(f32[4,8,128]{2,1,0:T(8,128)S(1)} %subtract_reduce_fusion.10, f32[4,128,128]{2,1,0:T(8,128)S(1)} %get-tuple-element.36, f32[4,8,128]{2,1,0:T(8,128)S(1)} %get-tuple-element.49), kind=kLoop, calls=%fused_computation.27 | loop fusion | flops 1568768 | bytes 311296 | tf_op jit(solution)/shard_map/reduce_sum | solution.py:72
  37.5 2.0 %collective-permute-start.7 = (f32[4,9,128]{2,0,1:T(4,128)S(1)}, f32[4,9,128]{2,0,1:T(4,128)S(1)}, u32[]{:S(2)}, u32[]{:S(2)}) collective-permute-start(f32[4,9,128]{2,0,1:T(4,128)S(1)} %pad_maximum_fusion.5), channel_id=1, source_target_pairs={{0,4},{4,0},{8,12},{12,8},{1,5},{5,1},{9,13},{13,9},{2,6},{6,2},{1... | collective-permute-start | bytes 55304 | tf_op jit(solution)/shard_map/ppermute | solution.py:92
  39.6 0.6 subtract_reduce_fusion.11
  40.2 0.7 %fusion.1 = f32[4,8,128]{2,1,0:T(8,128)S(1)} fusion(f32[4,8,128]{2,1,0:T(8,128)S(1)} %subtract_reduce_fusion.11, f32[4,128,128]{2,1,0:T(8,128)S(1)} %get-tuple-element.33, f32[4,8,128]{2,1,0:T(8,128)S(1)} %get-tuple-element.46), kind=kLoop, calls=%fused_computation.25 | loop fusion | flops 1568768 | bytes 311296 | tf_op jit(solution)/shard_map/reduce_sum | solution.py:72
  41.0 0.3 collective-permute-done.7
  41.8 0.2 select_reduce_fusion.9
  42.2 0.1 slice_reduce_fusion.7
  42.6 0.2 select_reduce_fusion.19
  42.9 2.4 %collective-permute-start.12 = (f32[4,8,128]{2,1,0:T(8,128)S(1)}, f32[4,8,128]{2,1,0:T(8,128)S(1)}, u32[]{:S(2)}, u32[]{:S(2)}) collective-permute-start(f32[4,8,128]{2,1,0:T(8,128)S(1)} %get-tuple-element.12), channel_id=1, source_target_pairs={{12,0},{8,4},{4,8},{0,12},{13,1},{9,5},{5,9},{1,13},{14,2},{10,6},... | collective-permute-start | bytes 49160 | tf_op jit(solution)/shard_map/ppermute | solution.py:92
  45.3 1.1 %collective-permute-start.11 = (f32[4,8,128]{2,1,0:T(8,128)S(1)}, f32[4,8,128]{2,1,0:T(8,128)S(1)}, u32[]{:S(2)}, u32[]{:S(2)}) collective-permute-start(f32[4,8,128]{2,1,0:T(8,128)S(1)} %get-tuple-element.11), channel_id=1, source_target_pairs={{8,0},{12,4},{0,8},{4,12},{9,1},{13,5},{1,9},{5,13},{10,2},{14,6},... | collective-permute-start | bytes 49160 | tf_op jit(solution)/shard_map/ppermute | solution.py:92
  46.4 0.9 %collective-permute-start.10 = (f32[4,8,128]{2,1,0:T(8,128)S(1)}, f32[4,8,128]{2,1,0:T(8,128)S(1)}, u32[]{:S(2)}, u32[]{:S(2)}) collective-permute-start(f32[4,8,128]{2,1,0:T(8,128)S(1)} %get-tuple-element.10), channel_id=1, source_target_pairs={{4,0},{0,4},{12,8},{8,12},{5,1},{1,5},{13,9},{9,13},{6,2},{2,6},{1... | collective-permute-start | bytes 49160 | tf_op jit(solution)/shard_map/ppermute | solution.py:92
  47.3 0.6 subtract_reduce_fusion.7
  47.9 0.7 %fusion.9 = f32[4,8,128]{2,1,0:T(8,128)S(1)} fusion(f32[4,8,128]{2,1,0:T(8,128)S(1)} %subtract_reduce_fusion.7, f32[4,128,128]{2,1,0:T(8,128)S(1)} %get-tuple-element.30, f32[4,8,128]{2,1,0:T(8,128)S(1)} %broadcast_multiply_fusion.3), kind=kLoop, calls=%fused_computation.33 | loop fusion | flops 1568768 | bytes 311296 | tf_op jit(solution)/shard_map/reduce_sum | solution.py:72
  48.7 0.6 subtract_reduce_fusion.4
  49.3 0.7 %fusion.15 = f32[4,8,128]{2,1,0:T(8,128)S(1)} fusion(f32[4,8,128]{2,1,0:T(8,128)S(1)} %subtract_reduce_fusion.4, f32[4,128,128]{2,1,0:T(8,128)S(1)} %get-tuple-element.37, f32[4,8,128]{2,1,0:T(8,128)S(1)} %broadcast_multiply_fusion), kind=kLoop, calls=%fused_computation.39 | loop fusion | flops 1568768 | bytes 311296 | tf_op jit(solution)/shard_map/reduce_sum | solution.py:72
  50.1 0.6 subtract_reduce_fusion.5
  50.8 0.7 %fusion.13 = f32[4,8,128]{2,1,0:T(8,128)S(1)} fusion(f32[4,8,128]{2,1,0:T(8,128)S(1)} %subtract_reduce_fusion.5, f32[4,128,128]{2,1,0:T(8,128)S(1)} %get-tuple-element.32, f32[4,8,128]{2,1,0:T(8,128)S(1)} %broadcast_multiply_fusion.1), kind=kLoop, calls=%fused_computation.37 | loop fusion | flops 1568768 | bytes 311296 | tf_op jit(solution)/shard_map/reduce_sum | solution.py:72
  51.5 0.6 subtract_reduce_fusion.6
  52.3 0.7 %fusion.11 = f32[4,8,128]{2,1,0:T(8,128)S(1)} fusion(f32[4,8,128]{2,1,0:T(8,128)S(1)} %subtract_reduce_fusion.6, f32[4,128,128]{2,1,0:T(8,128)S(1)} %get-tuple-element.31, f32[4,8,128]{2,1,0:T(8,128)S(1)} %broadcast_multiply_fusion.2), kind=kLoop, calls=%fused_computation.35 | loop fusion | flops 1568768 | bytes 311296 | tf_op jit(solution)/shard_map/reduce_sum | solution.py:72
  53.1 0.2 select_reduce_fusion.6
  53.7 0.2 select_reduce_fusion.4
  53.9 0.6 subtract_reduce_fusion
  54.6 0.7 %fusion.23 = f32[4,8,128]{2,1,0:T(8,128)S(1)} fusion(f32[4,8,128]{2,1,0:T(8,128)S(1)} %subtract_reduce_fusion, f32[4,8,128]{2,1,0:T(8,128)S(1)} %get-tuple-element.41, f32[4,128,128]{2,1,0:T(8,128)S(1)} %get-tuple-element.34), kind=kLoop, calls=%fused_computation.47 | loop fusion | flops 1568768 | bytes 311296 | tf_op jit(solution)/shard_map/reduce_sum | solution.py:72
  55.4 2.4 %collective-permute-start.16 = (f32[4,8,128]{2,1,0:T(8,128)S(1)}, f32[4,8,128]{2,1,0:T(8,128)S(1)}, u32[]{:S(2)}, u32[]{:S(2)}) collective-permute-start(f32[4,8,128]{2,1,0:T(8,128)S(1)} %add_select_fusion), channel_id=1, source_target_pairs={{0,12},{4,8},{8,4},{12,0},{1,13},{5,9},{9,5},{13,1},{2,14},{6,10},... | collective-permute-start | bytes 49160 | tf_op jit(solution)/shard_map/ppermute | solution.py:92
  57.7 0.6 subtract_reduce_fusion.1
  58.4 0.7 %fusion.21 = f32[4,8,128]{2,1,0:T(8,128)S(1)} fusion(f32[4,8,128]{2,1,0:T(8,128)S(1)} %subtract_reduce_fusion.1, f32[4,8,128]{2,1,0:T(8,128)S(1)} %get-tuple-element.42, f32[4,128,128]{2,1,0:T(8,128)S(1)} %get-tuple-element.35), kind=kLoop, calls=%fused_computation.45 | loop fusion | flops 1568768 | bytes 311296 | tf_op jit(solution)/shard_map/reduce_sum | solution.py:72
  59.2 0.2 collective-permute-start.15
  59.4 0.6 subtract_reduce_fusion.2
  60.1 0.7 %fusion.19 = f32[4,8,128]{2,1,0:T(8,128)S(1)} fusion(f32[4,8,128]{2,1,0:T(8,128)S(1)} %subtract_reduce_fusion.2, f32[4,8,128]{2,1,0:T(8,128)S(1)} %get-tuple-element.43, f32[4,128,128]{2,1,0:T(8,128)S(1)} %get-tuple-element.36), kind=kLoop, calls=%fused_computation.43 | loop fusion | flops 1568768 | bytes 311296 | tf_op jit(solution)/shard_map/reduce_sum | solution.py:72
  60.9 1.8 %collective-permute-start.14 = (f32[4,8,128]{2,1,0:T(8,128)S(1)}, f32[4,8,128]{2,1,0:T(8,128)S(1)}, u32[]{:S(2)}, u32[]{:S(2)}) collective-permute-start(f32[4,8,128]{2,1,0:T(8,128)S(1)} %add_select_fusion.2), channel_id=1, source_target_pairs={{0,4},{4,0},{8,12},{12,8},{1,5},{5,1},{9,13},{13,9},{2,6},{6,2},{1... | collective-permute-start | bytes 49160 | tf_op jit(solution)/shard_map/ppermute | solution.py:92
  62.7 0.6 subtract_reduce_fusion.3
  63.4 0.7 %fusion.17 = f32[4,8,128]{2,1,0:T(8,128)S(1)} fusion(f32[4,8,128]{2,1,0:T(8,128)S(1)} %subtract_reduce_fusion.3, f32[4,8,128]{2,1,0:T(8,128)S(1)} %get-tuple-element.40, f32[4,128,128]{2,1,0:T(8,128)S(1)} %get-tuple-element.33), kind=kLoop, calls=%fused_computation.41 | loop fusion | flops 1568768 | bytes 311296 | tf_op jit(solution)/shard_map/reduce_sum | solution.py:72
  64.2 0.5 collective-permute-done.14
  64.8 0.2 select_reduce_fusion.2
  65.3 0.6 copy.149
  65.9 0.5 collective-permute-done.17
  66.5 0.6 copy.148
  (128 shorter events, 5.7 us)
Async XLA Ops:
  0.6 17.0 %copy-start.2 = (s32[1024]{0:T(1024)S(1)}, s32[1024]{0:T(1024)}, u32[]{:S(2)}) copy-start(s32[1024]{0:T(1024)} %param.12) | copy-start | bytes 12292
  0.6 17.9 %copy-start = (bf16[64,1024]{1,0:T(8,128)(2,1)S(1)}, bf16[64,1024]{1,0:T(8,128)(2,1)}, u32[]{:S(2)}) copy-start(bf16[64,1024]{1,0:T(8,128)(2,1)} %param.10) | copy-start | bytes 393220
  0.7 16.2 %copy-start.1 = (s32[1024]{0:T(1024)S(1)}, s32[1024]{0:T(1024)}, u32[]{:S(2)}) copy-start(s32[1024]{0:T(1024)} %param.11) | copy-start | bytes 12292
  0.7 17.9 %collective-permute-start.6 = (s32[1024]{0:T(1024)}, s32[1024]{0:T(1024)S(1)}, u32[]{:S(2)}, u32[]{:S(2)}) collective-permute-start(s32[1024]{0:T(1024)} %param.12), channel_id=1, source_target_pairs={{12,0},{8,4},{4,8},{0,12},{13,1},{9,5},{5,9},{1,13},{14,2},{10,6},... | collective-permute-start | bytes 12296 | tf_op jit(solution)/shard_map/ppermute | solution.py:92
  5.8 13.5 %collective-permute-start.5 = (s32[1024]{0:T(1024)}, s32[1024]{0:T(1024)S(1)}, u32[]{:S(2)}, u32[]{:S(2)}) collective-permute-start(s32[1024]{0:T(1024)} %param.12), channel_id=1, source_target_pairs={{8,0},{12,4},{0,8},{4,12},{9,1},{13,5},{1,9},{5,13},{10,2},{14,6},... | collective-permute-start | bytes 12296 | tf_op jit(solution)/shard_map/ppermute | solution.py:92
  5.8 13.6 %collective-permute-start.4 = (s32[1024]{0:T(1024)}, s32[1024]{0:T(1024)S(1)}, u32[]{:S(2)}, u32[]{:S(2)}) collective-permute-start(s32[1024]{0:T(1024)} %param.12), channel_id=1, source_target_pairs={{4,0},{0,4},{12,8},{8,12},{5,1},{1,5},{13,9},{9,13},{6,2},{2,6},{1... | collective-permute-start | bytes 12296 | tf_op jit(solution)/shard_map/ppermute | solution.py:92
  7.8 6.6 %collective-permute-start = (s32[3,4,2]{1,2,0:T(2,128)S(1)}, s32[3,4,2]{1,2,0:T(2,128)S(1)}, u32[]{:S(2)}, u32[]{:S(2)}) collective-permute-start(s32[3,4,2]{1,2,0:T(2,128)S(1)} %get-tuple-element.51), channel_id=1, source_target_pairs={{0,1},{1,0},{2,3},{3,2},{4,5},{5,4},{6,7},{7,6},{8,9},{9,8},{10,11... | collective-permute-start | bytes 296 | tf_op jit(solution)/shard_map/ppermute | solution.py:78
  7.8 11.7 %collective-permute-start.3 = (bf16[64,1024]{1,0:T(8,128)(2,1)}, bf16[64,1024]{1,0:T(8,128)(2,1)S(1)}, u32[]{:S(2)}, u32[]{:S(2)}) collective-permute-start(bf16[64,1024]{1,0:T(8,128)(2,1)} %param.10), channel_id=1, source_target_pairs={{12,0},{8,4},{4,8},{0,12},{13,1},{9,5},{5,9},{1,13},{14,2},{10,6},... | collective-permute-start | bytes 393224 | tf_op jit(solution)/shard_map/ppermute | solution.py:92
  14.3 8.9 %collective-permute-start.2 = (bf16[64,1024]{1,0:T(8,128)(2,1)}, bf16[64,1024]{1,0:T(8,128)(2,1)S(1)}, u32[]{:S(2)}, u32[]{:S(2)}) collective-permute-start(bf16[64,1024]{1,0:T(8,128)(2,1)} %param.10), channel_id=1, source_target_pairs={{8,0},{12,4},{0,8},{4,12},{9,1},{13,5},{1,9},{5,13},{10,2},{14,6},... | collective-permute-start | bytes 393224 | tf_op jit(solution)/shard_map/ppermute | solution.py:92
  18.5 7.4 %collective-permute-start.1 = (bf16[64,1024]{1,0:T(8,128)(2,1)S(1)}, bf16[64,1024]{1,0:T(8,128)(2,1)S(1)}, u32[]{:S(2)}, u32[]{:S(2)}) collective-permute-start(bf16[64,1024]{1,0:T(8,128)(2,1)S(1)} %copy-done), channel_id=1, source_target_pairs={{4,0},{0,4},{12,8},{8,12},{5,1},{1,5},{13,9},{9,13},{6,2},{2,6},{1... | collective-permute-start | bytes 393224 | tf_op jit(solution)/shard_map/ppermute | solution.py:92
  32.0 9.0 %collective-permute-start.9 = (f32[4,9,128]{2,0,1:T(4,128)S(1)}, f32[4,9,128]{2,0,1:T(4,128)S(1)}, u32[]{:S(2)}, u32[]{:S(2)}) collective-permute-start(f32[4,9,128]{2,0,1:T(4,128)S(1)} %pad_maximum_fusion.7), channel_id=1, source_target_pairs={{0,12},{4,8},{8,4},{12,0},{1,13},{5,9},{9,5},{13,1},{2,14},{6,10},... | collective-permute-start | bytes 55304 | tf_op jit(solution)/shard_map/ppermute | solution.py:92
  36.0 5.1 %collective-permute-start.8 = (f32[4,9,128]{2,0,1:T(4,128)S(1)}, f32[4,9,128]{2,0,1:T(4,128)S(1)}, u32[]{:S(2)}, u32[]{:S(2)}) collective-permute-start(f32[4,9,128]{2,0,1:T(4,128)S(1)} %pad_maximum_fusion.6), channel_id=1, source_target_pairs={{0,8},{4,12},{8,0},{12,4},{1,9},{5,13},{9,1},{13,5},{2,10},{6,14},... | collective-permute-start | bytes 55304 | tf_op jit(solution)/shard_map/ppermute | solution.py:92
  37.5 3.8 %collective-permute-start.7 = (f32[4,9,128]{2,0,1:T(4,128)S(1)}, f32[4,9,128]{2,0,1:T(4,128)S(1)}, u32[]{:S(2)}, u32[]{:S(2)}) collective-permute-start(f32[4,9,128]{2,0,1:T(4,128)S(1)} %pad_maximum_fusion.5), channel_id=1, source_target_pairs={{0,4},{4,0},{8,12},{12,8},{1,5},{5,1},{9,13},{13,9},{2,6},{6,2},{1... | collective-permute-start | bytes 55304 | tf_op jit(solution)/shard_map/ppermute | solution.py:92
  42.9 5.8 %collective-permute-start.12 = (f32[4,8,128]{2,1,0:T(8,128)S(1)}, f32[4,8,128]{2,1,0:T(8,128)S(1)}, u32[]{:S(2)}, u32[]{:S(2)}) collective-permute-start(f32[4,8,128]{2,1,0:T(8,128)S(1)} %get-tuple-element.12), channel_id=1, source_target_pairs={{12,0},{8,4},{4,8},{0,12},{13,1},{9,5},{5,9},{1,13},{14,2},{10,6},... | collective-permute-start | bytes 49160 | tf_op jit(solution)/shard_map/ppermute | solution.py:92
  45.3 4.8 %collective-permute-start.11 = (f32[4,8,128]{2,1,0:T(8,128)S(1)}, f32[4,8,128]{2,1,0:T(8,128)S(1)}, u32[]{:S(2)}, u32[]{:S(2)}) collective-permute-start(f32[4,8,128]{2,1,0:T(8,128)S(1)} %get-tuple-element.11), channel_id=1, source_target_pairs={{8,0},{12,4},{0,8},{4,12},{9,1},{13,5},{1,9},{5,13},{10,2},{14,6},... | collective-permute-start | bytes 49160 | tf_op jit(solution)/shard_map/ppermute | solution.py:92
  46.4 5.1 %collective-permute-start.10 = (f32[4,8,128]{2,1,0:T(8,128)S(1)}, f32[4,8,128]{2,1,0:T(8,128)S(1)}, u32[]{:S(2)}, u32[]{:S(2)}) collective-permute-start(f32[4,8,128]{2,1,0:T(8,128)S(1)} %get-tuple-element.10), channel_id=1, source_target_pairs={{4,0},{0,4},{12,8},{8,12},{5,1},{1,5},{13,9},{9,13},{6,2},{2,6},{1... | collective-permute-start | bytes 49160 | tf_op jit(solution)/shard_map/ppermute | solution.py:92
  53.6 11.6 %collective-permute-start.13 = (f32[8,8,128]{2,1,0:T(8,128)S(1)}, f32[8,8,128]{2,1,0:T(8,128)S(1)}, u32[]{:S(2)}, u32[]{:S(2)}) collective-permute-start(f32[8,8,128]{2,1,0:T(8,128)S(1)} %bitcast_subtract_fusion.2), channel_id=1, source_target_pairs={{0,1},{1,0},{2,3},{3,2},{4,5},{5,4},{6,7},{7,6},{8,9},{9,8},{10,11... | collective-permute-start | bytes 98312 | tf_op jit(solution)/shard_map/ppermute | solution.py:78
  55.4 8.8 %collective-permute-start.16 = (f32[4,8,128]{2,1,0:T(8,128)S(1)}, f32[4,8,128]{2,1,0:T(8,128)S(1)}, u32[]{:S(2)}, u32[]{:S(2)}) collective-permute-start(f32[4,8,128]{2,1,0:T(8,128)S(1)} %add_select_fusion), channel_id=1, source_target_pairs={{0,12},{4,8},{8,4},{12,0},{1,13},{5,9},{9,5},{13,1},{2,14},{6,10},... | collective-permute-start | bytes 49160 | tf_op jit(solution)/shard_map/ppermute | solution.py:92
  59.2 5.0 %collective-permute-start.15 = (f32[4,8,128]{2,1,0:T(8,128)S(1)}, f32[4,8,128]{2,1,0:T(8,128)S(1)}, u32[]{:S(2)}, u32[]{:S(2)}) collective-permute-start(f32[4,8,128]{2,1,0:T(8,128)S(1)} %add_select_fusion.1), channel_id=1, source_target_pairs={{0,8},{4,12},{8,0},{12,4},{1,9},{5,13},{9,1},{13,5},{2,10},{6,14},... | collective-permute-start | bytes 49160 | tf_op jit(solution)/shard_map/ppermute | solution.py:92
  60.9 3.8 %collective-permute-start.14 = (f32[4,8,128]{2,1,0:T(8,128)S(1)}, f32[4,8,128]{2,1,0:T(8,128)S(1)}, u32[]{:S(2)}, u32[]{:S(2)}) collective-permute-start(f32[4,8,128]{2,1,0:T(8,128)S(1)} %add_select_fusion.2), channel_id=1, source_target_pairs={{0,4},{4,0},{8,12},{12,8},{1,5},{5,1},{9,13},{13,9},{2,6},{6,2},{1... | collective-permute-start | bytes 49160 | tf_op jit(solution)/shard_map/ppermute | solution.py:92
  65.2 1.3 %collective-permute-start.17 = (f32[8,8,128]{2,1,0:T(8,128)S(1)}, f32[8,8,128]{2,1,0:T(8,128)S(1)}, u32[]{:S(2)}, u32[]{:S(2)}) collective-permute-start(f32[8,8,128]{2,1,0:T(8,128)S(1)} %bitcast_subtract_fusion), channel_id=1, source_target_pairs={{0,1},{1,0},{2,3},{3,2},{4,5},{5,4},{6,7},{7,6},{8,9},{9,8},{10,11... | collective-permute-start | bytes 98312 | tf_op jit(solution)/shard_map/ppermute | solution.py:78

commit v15 on v11

--- a/solution.py
+++ b/solution.py
@@ -135,7 +135,17 @@
             peers = jnp.bitwise_xor(my_blk, offsets)
         else:
             peers = (my_blk + offsets) % peer_count
-        everything = send_down([own_synth] * peer_count)
+        half_points = point_count // n_sub
+        own_half = lax.dynamic_slice_in_dim(
+            own_synth.reshape(features + 1, point_count), my_sub * half_points, half_points, 1
+        )
+        arrived = send_down([own_half] * peer_count)[1:]
+        other_half = swap(jnp.stack(arrived))
+        everything = [own_synth]
+        for index, mine in enumerate(arrived):
+            low = jnp.where(my_sub == 0, mine, other_half[index])
+            high = jnp.where(my_sub == 0, other_half[index], mine)
+            everything.append(jnp.concatenate([low, high], axis=1).reshape(features + 1, blocks, BLOCK))
         lists = jnp.stack([pair_block, pair_row, jnp.broadcast_to(pair_count[:, None], pair_block.shape)])
         lists = jnp.stack([lists, swap(lists)], axis=1)
         listed = lax.broadcasted_iota(jnp.int32, lists.shape[1:], 2) < lists[2]

time: 61.2 us -> 64.2 us (1.049)
  other arithmetic: 28.8 us -> 30.4 us
  local copies, waits for them, and re-layouts: 4.99 us -> 6 us
    ppermute x12, waiting for transfers between devices: 3.45 us -> 1.56 us  [exchange(): moved.append(lax.ppermute(chunks[offset], 'blk', perm))]
    ppermute x3 -> x4, waiting for transfers between devices: 0.51 us -> 2.22 us  [swap(): return lax.ppermute(value, 'sub', [(0, 1), (1, 0)])]
    unnamed x8 -> x9, local copies, waits for them, and re-layouts: 2.26 us -> 3.23 us
    concatenate x2, other arithmetic: 0.74 us -> 1.54 us  [shards(): jnp.concatenate([synth_points, synth_cluster.astype(jnp.bfloat16)[None, :...]
    convert_element_type x0 -> x1, other arithmetic: none -> 0.69 us  [shards(): synth_cluster.astype(jnp.bfloat16)[None, :]]
    reduce_max x11 -> x13, other arithmetic: 7.55 us -> 7.49 us  [lse_parts(): highest = jnp.max(scores, axis=axis)]
  transfers between devices with their start and end apart: 15 -> 16, of which waited for: 4 -> 5; matrix products, arithmetic and copies ran while one was open for 40% -> 40% of each run, Pallas kernels for 0% -> 0%
where the time goes in v15:
time: 64.2 us; the launch traced here: 63.8 us
  other arithmetic  30.4 us (47%)
  starting transfers between devices  19.7 us (31%)
  local copies, waits for them, and re-layouts  6 us (9%)
  waiting for transfers between devices  3.78 us (6%)
  matrix products  2.53 us (4%)
  between operations  1.44 us (2%)
    ppermute x12, starting transfers between devices, exchange(): moved.append(lax.ppermute(chunks[offset], 'blk', perm))  19 us
    reduce_sum x14, other arithmetic, lse_parts(): jnp.sum(jnp.exp(scores - jnp.expand_dims(highest, axis)), axis=axis)  9.52 us
    reduce_max x13, other arithmetic, lse_parts(): highest = jnp.max(scores, axis=axis)  7.49 us
    reduce_sum x13, other arithmetic, pick_rows(): return jnp.sum(chosen, axis=2, dtype=values.dtype)  4.56 us
    unnamed x9, local copies, waits for them, and re-layouts  3.23 us
    dot_general x2, matrix products, slot_costs(): jnp.einsum('gdi,gdj->gij', slot_real, slot_synth, preferred_element_type=...  2.53 us
    ppermute x4, waiting for transfers between devices, swap(): return lax.ppermute(value, 'sub', [(0, 1), (1, 0)])  2.22 us
    ppermute x12, waiting for transfers between devices, exchange(): moved.append(lax.ppermute(chunks[offset], 'blk', perm))  1.56 us
  transfers between devices with their start and end apart: 16, of which 5 were waited for; matrix products, arithmetic and copies ran while one was open for 40% of the time, Pallas kernels for 0%

profile of v15, /device:TPU:0, one launch (start us, length us, event | category | flops | bytes accessed | tf_op | source)
XLA Modules:
  0.0 63.8 jit_solution(8799147473820386991)
XLA Ops:
  0.6 0.7 %convert_element_type.75 = bf16[1024]{0:T(1024)(128)(2,1)S(1)} convert(s32[1024]{0:T(1024)} %param.12) | non-fusion elementwise | flops 1024 | bytes 6144 | tf_op jit(solution)/shard_map/convert_element_type | solution.py:124
  1.3 0.8 %fusion.30 = bf16[65,512]{1,0:T(8,128)(2,1)S(1)} fusion(s32[]{:T(128)S(6)} %select_n.300, bf16[64,1024]{1,0:T(8,128)(2,1)} %param.10, bf16[1,1024]{1,0:T(2,128)(2,1)S(1)} %broadcast_in_dim.627), kind=kLoop, calls=%fused_computation.94 | loop fusion | flops 133120 | bytes 199684 | tf_op jit(solution)/shard_map/concatenate | solution.py:123
  2.2 3.0 %collective-permute-start.1 = (bf16[65,512]{1,0:T(8,128)(2,1)S(1)}, bf16[65,512]{1,0:T(8,128)(2,1)S(1)}, u32[]{:S(2)}, u32[]{:S(2)}) collective-permute-start(bf16[65,512]{1,0:T(8,128)(2,1)S(1)} %fusion.30), channel_id=1, source_target_pairs={{4,0},{0,4},{12,8},{8,12},{5,1},{1,5},{13,9},{9,13},{6,2},{2,6},{1... | collective-permute-start | bytes 199688 | tf_op jit(solution)/shard_map/ppermute | solution.py:92
  5.2 2.5 %collective-permute-start.3 = (bf16[65,512]{1,0:T(8,128)(2,1)S(1)}, bf16[65,512]{1,0:T(8,128)(2,1)S(1)}, u32[]{:S(2)}, u32[]{:S(2)}) collective-permute-start(bf16[65,512]{1,0:T(8,128)(2,1)S(1)} %fusion.30), channel_id=1, source_target_pairs={{12,0},{8,4},{4,8},{0,12},{13,1},{9,5},{5,9},{1,13},{14,2},{10,6},... | collective-permute-start | bytes 199688 | tf_op jit(solution)/shard_map/ppermute | solution.py:92
  7.8 0.7 %stack_broadcast_in_dim.2 = s32[1,4,2]{1,2,0:T(2,128)S(1)} broadcast(s32[4]{0:T(128)} %param.17), dimensions={1} | broadcast | bytes 48 | tf_op jit(solution)/shard_map/stack;broadcast_in_dim | solution.py:149
  8.5 0.7 %fusion.40 = (s32[3,1,4,2]{2,3,0,1:T(2,128)S(1)}, s32[3,4,2]{1,2,0:T(2,128)S(1)}) fusion(s32[1,4,2]{1,2,0:T(2,128)S(1)} %stack_broadcast_in_dim.2, s32[1,4,2]{1,2,0:T(2,128)} %bitcast.111, s32[1,4,2]{1,2,0:T(2,128)} %bitcast.112), kind=kLoop, calls=%fused_computation.207 | loop fusion | flops 48 | bytes 288 | tf_op jit(solution)/shard_map/stack | solution.py:150
  9.2 0.7 %convert_bitcast_fusion.3 = bf16[1,1,8,128]{3,2,1,0:T(8,128)(2,1)S(1)} fusion(s32[1024]{0:T(1024)} %param.12), kind=kLoop, calls=%fused_computation.209 | loop fusion | flops 1024 | bytes 6144 | tf_op jit(solution)/shard_map/concatenate | solution.py:123
  9.9 0.9 %copy.134 = bf16[8,8,8,128]{3,2,1,0:T(8,128)(2,1)S(1)} copy(bf16[8,8,8,128]{3,1,2,0:T(8,128)(2,1)} %bitcast.97) | data formatting | bytes 262144
  10.9 0.7 %convert_bitcast_fusion.1 = bf16[8,128]{1,0:T(8,128)(2,1)S(1)} fusion(s32[1024]{0:T(1024)} %param.11), kind=kLoop, calls=%fused_computation.197 | loop fusion | flops 1024 | bytes 6144 | tf_op jit(solution)/shard_map/convert_element_type | solution.py:122
  11.5 0.8 %multiply_bitcast_fusion.1 = f32[1,8,8,128]{3,1,2,0:T(8,128)S(1)} fusion(s32[16,1024]{1,0:T(8,128)} %param.13, s32[]{:T(128)S(6)} %select_n.292), kind=kLoop, calls=%fused_computation.124 | loop fusion | flops 24576 | bytes 65540
  12.3 0.8 %multiply_bitcast_fusion = f32[1,8,8,128]{3,1,2,0:T(8,128)S(1)} fusion(s32[16,1024]{1,0:T(8,128)} %param.14, s32[]{:T(128)S(6)} %select_n.292), kind=kLoop, calls=%fused_computation.122 | loop fusion | flops 24576 | bytes 65540
  13.1 0.9 %copy.138 = bf16[8,8,8,128]{3,2,1,0:T(8,128)(2,1)S(1)} copy(bf16[8,8,8,128]{3,1,2,0:T(8,128)(2,1)} %bitcast.104) | data formatting | bytes 262144
  14.1 0.3 select_reduce_fusion.25
  14.4 0.3 slice_reduce_fusion.11
  15.0 0.3 slice_reduce_fusion.3
  15.8 1.5 %select_reduce_fusion = bf16[16,64,128]{2,1,0:T(8,128)(2,1)S(1)} fusion(pred[16,8]{1,0:T(8,128)(4,1)S(1)} %iota_compare_fusion.1, bf16[64,8,128]{2,1,0:T(8,128)(2,1)S(1)} %bitcast.96), kind=kLoop, calls=%fused_computation.48 | loop fusion | flops 1966080 | bytes 393344 | tf_op jit(solution)/shard_map/reduce_sum | solution.py:26
  17.9 0.4 select_reduce_fusion.4
  18.4 0.6 collective-permute-start.4
  19.1 1.0 %collective-permute-done.4 = bf16[3,65,512]{2,1,0:T(8,128)(2,1)S(1)} collective-permute-done((bf16[3,65,512]{2,1,0:T(8,128)(2,1)S(1)}, bf16[3,65,512]{2,1,0:T(8,128)(2,1)S(1)}, u32[]{:S(2)}, u32[]{:S(2)}) %collective-permute-start.4) | collective-permute-done | bytes 199712 | tf_op jit(solution)/shard_map/ppermute | solution.py:78
  20.4 0.4 select_reduce_fusion.1
  20.8 0.4 select_reduce_fusion.2
  21.2 0.4 select_reduce_fusion.3
  21.7 1.4 %fusion.26 = f32[16,128,128]{2,1,0:T(8,128)S(1)} fusion(bf16[16,64,128]{2,1,0:T(8,128)(2,1)S(1)} %select_reduce_fusion, f32[16,128]{1,0:T(8,128)S(1)} %broadcast_multiply_fusion.4, f32[16,128]{1,0:T(8,128)S(1)} %broadcast_multiply_fusion.5, bf16[16,128]{1,0:T(8,128)(2,1)S(1)} %select_reduce_fusion.23, bf16[16,128]{1,0:T(8,128)(2,1)S(1)} %bitcast.109, ...), kind=kOutput, calls=%fused_computation.53 | convolution fusion | flops 35127296 | bytes 1597440 | tf_op jit(solution)/shard_map/gdi,gdj->gij/dot_general | solution.py:61
  23.1 1.1 %fusion.27 = f32[16,128,128]{2,1,0:T(8,128)S(1)} fusion(bf16[16,64,128]{2,1,0:T(8,128)(2,1)S(1)} %select_reduce_fusion, f32[16,128]{1,0:T(8,128)S(1)} %broadcast_multiply_fusion.5, f32[16,128]{1,0:T(8,128)S(1)} %broadcast_multiply_fusion.4, bf16[16,128]{1,0:T(8,128)(2,1)S(1)} %bitcast.110, bf16[16,128]{1,0:T(8,128)(2,1)S(1)} %select_reduce_fusion.23, ...), kind=kOutput, calls=%fused_computation.54 | convolution fusion | flops 35127296 | bytes 1597440 | tf_op jit(solution)/shard_map/gdi,gdj->gij/dot_general | solution.py:61
  25.2 0.2 select_reduce_fusion.15
  25.5 0.6 subtract_reduce_fusion.8
  26.1 0.7 %fusion.7 = f32[4,8,128]{2,1,0:T(8,128)S(1)} fusion(f32[4,8,128]{2,1,0:T(8,128)S(1)} %subtract_reduce_fusion.8, f32[4,128,128]{2,1,0:T(8,128)S(1)} %get-tuple-element.34, f32[4,8,128]{2,1,0:T(8,128)S(1)} %get-tuple-element.57), kind=kLoop, calls=%fused_computation.31 | loop fusion | flops 1568768 | bytes 311296 | tf_op jit(solution)/shard_map/reduce_sum | solution.py:72
  27.0 3.0 %collective-permute-start.7 = (f32[4,9,128]{2,0,1:T(4,128)S(1)}, f32[4,9,128]{2,0,1:T(4,128)S(1)}, u32[]{:S(2)}, u32[]{:S(2)}) collective-permute-start(f32[4,9,128]{2,0,1:T(4,128)S(1)} %pad_maximum_fusion.11), channel_id=1, source_target_pairs={{0,12},{4,8},{8,4},{12,0},{1,13},{5,9},{9,5},{13,1},{2,14},{6,10},... | collective-permute-start | bytes 55304 | tf_op jit(solution)/shard_map/ppermute | solution.py:92
  30.0 0.6 subtract_reduce_fusion.9
  30.6 0.7 %fusion.5 = f32[4,8,128]{2,1,0:T(8,128)S(1)} fusion(f32[4,8,128]{2,1,0:T(8,128)S(1)} %subtract_reduce_fusion.9, f32[4,128,128]{2,1,0:T(8,128)S(1)} %get-tuple-element.35, f32[4,8,128]{2,1,0:T(8,128)S(1)} %get-tuple-element.58), kind=kLoop, calls=%fused_computation.29 | loop fusion | flops 1568768 | bytes 311296 | tf_op jit(solution)/shard_map/reduce_sum | solution.py:72
  31.5 0.4 collective-permute-start.6
  31.9 0.6 subtract_reduce_fusion.10
  32.5 0.7 %fusion.3 = f32[4,8,128]{2,1,0:T(8,128)S(1)} fusion(f32[4,8,128]{2,1,0:T(8,128)S(1)} %subtract_reduce_fusion.10, f32[4,128,128]{2,1,0:T(8,128)S(1)} %get-tuple-element.36, f32[4,8,128]{2,1,0:T(8,128)S(1)} %get-tuple-element.59), kind=kLoop, calls=%fused_computation.27 | loop fusion | flops 1568768 | bytes 311296 | tf_op jit(solution)/shard_map/reduce_sum | solution.py:72
  33.4 1.2 %collective-permute-start.5 = (f32[4,9,128]{2,0,1:T(4,128)S(1)}, f32[4,9,128]{2,0,1:T(4,128)S(1)}, u32[]{:S(2)}, u32[]{:S(2)}) collective-permute-start(f32[4,9,128]{2,0,1:T(4,128)S(1)} %pad_maximum_fusion.9), channel_id=1, source_target_pairs={{0,4},{4,0},{8,12},{12,8},{1,5},{5,1},{9,13},{13,9},{2,6},{6,2},{1... | collective-permute-start | bytes 55304 | tf_op jit(solution)/shard_map/ppermute | solution.py:92
  34.6 0.6 subtract_reduce_fusion.11
  35.2 0.7 %fusion.1 = f32[4,8,128]{2,1,0:T(8,128)S(1)} fusion(f32[4,8,128]{2,1,0:T(8,128)S(1)} %subtract_reduce_fusion.11, f32[4,128,128]{2,1,0:T(8,128)S(1)} %get-tuple-element.33, f32[4,8,128]{2,1,0:T(8,128)S(1)} %get-tuple-element.56), kind=kLoop, calls=%fused_computation.25 | loop fusion | flops 1568768 | bytes 311296 | tf_op jit(solution)/shard_map/reduce_sum | solution.py:72
  36.0 0.2 collective-permute-done.6
  36.3 0.9 %collective-permute-done.5 = f32[4,9,128]{2,0,1:T(4,128)S(1)} collective-permute-done((f32[4,9,128]{2,0,1:T(4,128)S(1)}, f32[4,9,128]{2,0,1:T(4,128)S(1)}, u32[]{:S(2)}, u32[]{:S(2)}) %collective-permute-start.5) | collective-permute-done | bytes 18464 | tf_op jit(solution)/shard_map/ppermute | solution.py:92
  37.7 0.2 select_reduce_fusion.13
  38.5 0.2 select_reduce_fusion.19
  38.7 2.5 %collective-permute-start.10 = (f32[4,8,128]{2,1,0:T(8,128)S(1)}, f32[4,8,128]{2,1,0:T(8,128)S(1)}, u32[]{:S(2)}, u32[]{:S(2)}) collective-permute-start(f32[4,8,128]{2,1,0:T(8,128)S(1)} %get-tuple-element.12), channel_id=1, source_target_pairs={{12,0},{8,4},{4,8},{0,12},{13,1},{9,5},{5,9},{1,13},{14,2},{10,6},... | collective-permute-start | bytes 49160 | tf_op jit(solution)/shard_map/ppermute | solution.py:92
  41.5 1.7 %collective-permute-start.8 = (f32[4,8,128]{2,1,0:T(8,128)S(1)}, f32[4,8,128]{2,1,0:T(8,128)S(1)}, u32[]{:S(2)}, u32[]{:S(2)}) collective-permute-start(f32[4,8,128]{2,1,0:T(8,128)S(1)} %get-tuple-element.10), channel_id=1, source_target_pairs={{4,0},{0,4},{12,8},{8,12},{5,1},{1,5},{13,9},{9,13},{6,2},{2,6},{1... | collective-permute-start | bytes 49160 | tf_op jit(solution)/shard_map/ppermute | solution.py:92
  43.2 0.6 subtract_reduce_fusion.7
  43.8 0.7 %fusion.9 = f32[4,8,128]{2,1,0:T(8,128)S(1)} fusion(f32[4,8,128]{2,1,0:T(8,128)S(1)} %subtract_reduce_fusion.7, f32[4,128,128]{2,1,0:T(8,128)S(1)} %get-tuple-element.30, f32[4,8,128]{2,1,0:T(8,128)S(1)} %broadcast_multiply_fusion.3), kind=kLoop, calls=%fused_computation.33 | loop fusion | flops 1568768 | bytes 311296 | tf_op jit(solution)/shard_map/reduce_sum | solution.py:72
  44.6 0.6 subtract_reduce_fusion.4
  45.2 0.7 %fusion.15 = f32[4,8,128]{2,1,0:T(8,128)S(1)} fusion(f32[4,8,128]{2,1,0:T(8,128)S(1)} %subtract_reduce_fusion.4, f32[4,128,128]{2,1,0:T(8,128)S(1)} %get-tuple-element.37, f32[4,8,128]{2,1,0:T(8,128)S(1)} %broadcast_multiply_fusion), kind=kLoop, calls=%fused_computation.39 | loop fusion | flops 1568768 | bytes 311296 | tf_op jit(solution)/shard_map/reduce_sum | solution.py:72
  46.0 0.6 subtract_reduce_fusion.5
  46.6 0.7 %fusion.13 = f32[4,8,128]{2,1,0:T(8,128)S(1)} fusion(f32[4,8,128]{2,1,0:T(8,128)S(1)} %subtract_reduce_fusion.5, f32[4,128,128]{2,1,0:T(8,128)S(1)} %get-tuple-element.32, f32[4,8,128]{2,1,0:T(8,128)S(1)} %broadcast_multiply_fusion.1), kind=kLoop, calls=%fused_computation.37 | loop fusion | flops 1568768 | bytes 311296 | tf_op jit(solution)/shard_map/reduce_sum | solution.py:72
  47.4 0.6 subtract_reduce_fusion.6
  48.1 0.7 %fusion.11 = f32[4,8,128]{2,1,0:T(8,128)S(1)} fusion(f32[4,8,128]{2,1,0:T(8,128)S(1)} %subtract_reduce_fusion.6, f32[4,128,128]{2,1,0:T(8,128)S(1)} %get-tuple-element.31, f32[4,8,128]{2,1,0:T(8,128)S(1)} %broadcast_multiply_fusion.2), kind=kLoop, calls=%fused_computation.35 | loop fusion | flops 1568768 | bytes 311296 | tf_op jit(solution)/shard_map/reduce_sum | solution.py:72
  49.8 0.6 subtract_reduce_fusion
  50.4 1.0 %fusion.23 = f32[4,8,128]{2,1,0:T(8,128)S(1)} fusion(f32[4,8,128]{2,1,0:T(8,128)S(1)} %subtract_reduce_fusion, f32[4,8,128]{2,1,0:T(8,128)S(1)} %get-tuple-element.51, f32[4,128,128]{2,1,0:T(8,128)S(1)} %get-tuple-element.34), kind=kLoop, calls=%fused_computation.47 | loop fusion | flops 1568768 | bytes 311296 | tf_op jit(solution)/shard_map/reduce_sum | solution.py:72
  51.5 2.5 %collective-permute-start.14 = (f32[4,8,128]{2,1,0:T(8,128)S(1)}, f32[4,8,128]{2,1,0:T(8,128)S(1)}, u32[]{:S(2)}, u32[]{:S(2)}) collective-permute-start(f32[4,8,128]{2,1,0:T(8,128)S(1)} %add_select_fusion), channel_id=1, source_target_pairs={{0,12},{4,8},{8,4},{12,0},{1,13},{5,9},{9,5},{13,1},{2,14},{6,10},... | collective-permute-start | bytes 49160 | tf_op jit(solution)/shard_map/ppermute | solution.py:92
  54.0 0.6 subtract_reduce_fusion.1
  54.6 0.7 %fusion.21 = f32[4,8,128]{2,1,0:T(8,128)S(1)} fusion(f32[4,8,128]{2,1,0:T(8,128)S(1)} %subtract_reduce_fusion.1, f32[4,8,128]{2,1,0:T(8,128)S(1)} %get-tuple-element.52, f32[4,128,128]{2,1,0:T(8,128)S(1)} %get-tuple-element.35), kind=kLoop, calls=%fused_computation.45 | loop fusion | flops 1568768 | bytes 311296 | tf_op jit(solution)/shard_map/reduce_sum | solution.py:72
  55.5 0.6 subtract_reduce_fusion.2
  56.1 0.7 %fusion.19 = f32[4,8,128]{2,1,0:T(8,128)S(1)} fusion(f32[4,8,128]{2,1,0:T(8,128)S(1)} %subtract_reduce_fusion.2, f32[4,8,128]{2,1,0:T(8,128)S(1)} %get-tuple-element.53, f32[4,128,128]{2,1,0:T(8,128)S(1)} %get-tuple-element.36), kind=kLoop, calls=%fused_computation.43 | loop fusion | flops 1568768 | bytes 311296 | tf_op jit(solution)/shard_map/reduce_sum | solution.py:72
  56.9 1.9 %collective-permute-start.12 = (f32[4,8,128]{2,1,0:T(8,128)S(1)}, f32[4,8,128]{2,1,0:T(8,128)S(1)}, u32[]{:S(2)}, u32[]{:S(2)}) collective-permute-start(f32[4,8,128]{2,1,0:T(8,128)S(1)} %add_select_fusion.2), channel_id=1, source_target_pairs={{0,4},{4,0},{8,12},{12,8},{1,5},{5,1},{9,13},{13,9},{2,6},{6,2},{1... | collective-permute-start | bytes 49160 | tf_op jit(solution)/shard_map/ppermute | solution.py:92
  58.8 0.6 subtract_reduce_fusion.3
  59.5 0.7 %fusion.17 = f32[4,8,128]{2,1,0:T(8,128)S(1)} fusion(f32[4,8,128]{2,1,0:T(8,128)S(1)} %subtract_reduce_fusion.3, f32[4,8,128]{2,1,0:T(8,128)S(1)} %get-tuple-element.50, f32[4,128,128]{2,1,0:T(8,128)S(1)} %get-tuple-element.33), kind=kLoop, calls=%fused_computation.41 | loop fusion | flops 1568768 | bytes 311296 | tf_op jit(solution)/shard_map/reduce_sum | solution.py:72
  60.3 0.4 collective-permute-done.12
  61.3 1.2 %collective-permute-done.15 = f32[8,8,128]{2,1,0:T(8,128)S(1)} collective-permute-done((f32[8,8,128]{2,1,0:T(8,128)S(1)}, f32[8,8,128]{2,1,0:T(8,128)S(1)}, u32[]{:S(2)}, u32[]{:S(2)}) %collective-permute-start.15) | collective-permute-done | bytes 32800 | tf_op jit(solution)/shard_map/ppermute | solution.py:78
  62.5 0.6 %copy.151 = f32[2,8,8,128]{3,1,2,0:T(8,128)} copy(f32[2,8,8,128]{3,2,1,0:T(8,128)S(1)} %bitcast.102) | data formatting | bytes 131072
  63.1 0.6 %copy.150 = f32[2,8,8,128]{3,1,2,0:T(8,128)} copy(f32[2,8,8,128]{3,2,1,0:T(8,128)S(1)} %bitcast.103) | data formatting | bytes 131072
  (132 shorter events, 6.8 us)
Async XLA Ops:
  2.2 16.2 %collective-permute-start.1 = (bf16[65,512]{1,0:T(8,128)(2,1)S(1)}, bf16[65,512]{1,0:T(8,128)(2,1)S(1)}, u32[]{:S(2)}, u32[]{:S(2)}) collective-permute-start(bf16[65,512]{1,0:T(8,128)(2,1)S(1)} %fusion.30), channel_id=1, source_target_pairs={{4,0},{0,4},{12,8},{8,12},{5,1},{1,5},{13,9},{9,13},{6,2},{2,6},{1... | collective-permute-start | bytes 199688 | tf_op jit(solution)/shard_map/ppermute | solution.py:92
  5.2 13.2 %collective-permute-start.3 = (bf16[65,512]{1,0:T(8,128)(2,1)S(1)}, bf16[65,512]{1,0:T(8,128)(2,1)S(1)}, u32[]{:S(2)}, u32[]{:S(2)}) collective-permute-start(bf16[65,512]{1,0:T(8,128)(2,1)S(1)} %fusion.30), channel_id=1, source_target_pairs={{12,0},{8,4},{4,8},{0,12},{13,1},{9,5},{5,9},{1,13},{14,2},{10,6},... | collective-permute-start | bytes 199688 | tf_op jit(solution)/shard_map/ppermute | solution.py:92
  7.7 10.7 %collective-permute-start.2 = (bf16[65,512]{1,0:T(8,128)(2,1)S(1)}, bf16[65,512]{1,0:T(8,128)(2,1)S(1)}, u32[]{:S(2)}, u32[]{:S(2)}) collective-permute-start(bf16[65,512]{1,0:T(8,128)(2,1)S(1)} %fusion.30), channel_id=1, source_target_pairs={{8,0},{12,4},{0,8},{4,12},{9,1},{13,5},{1,9},{5,13},{10,2},{14,6},... | collective-permute-start | bytes 199688 | tf_op jit(solution)/shard_map/ppermute | solution.py:92
  9.2 4.9 %collective-permute-start = (s32[3,4,2]{1,2,0:T(2,128)S(1)}, s32[3,4,2]{1,2,0:T(2,128)S(1)}, u32[]{:S(2)}, u32[]{:S(2)}) collective-permute-start(s32[3,4,2]{1,2,0:T(2,128)S(1)} %get-tuple-element.61), channel_id=1, source_target_pairs={{0,1},{1,0},{2,3},{3,2},{4,5},{5,4},{6,7},{7,6},{8,9},{9,8},{10,11... | collective-permute-start | bytes 296 | tf_op jit(solution)/shard_map/ppermute | solution.py:78
  18.4 1.7 %collective-permute-start.4 = (bf16[3,65,512]{2,1,0:T(8,128)(2,1)S(1)}, bf16[3,65,512]{2,1,0:T(8,128)(2,1)S(1)}, u32[]{:S(2)}, u32[]{:S(2)}) collective-permute-start(bf16[3,65,512]{2,1,0:T(8,128)(2,1)S(1)} %pad_maximum_fusion.1), channel_id=1, source_target_pairs={{0,1},{1,0},{2,3},{3,2},{4,5},{5,4},{6,7},{7,6},{8,9},{9,8},{10,11... | collective-permute-start | bytes 599048 | tf_op jit(solution)/shard_map/ppermute | solution.py:78
  27.0 9.0 %collective-permute-start.7 = (f32[4,9,128]{2,0,1:T(4,128)S(1)}, f32[4,9,128]{2,0,1:T(4,128)S(1)}, u32[]{:S(2)}, u32[]{:S(2)}) collective-permute-start(f32[4,9,128]{2,0,1:T(4,128)S(1)} %pad_maximum_fusion.11), channel_id=1, source_target_pairs={{0,12},{4,8},{8,4},{12,0},{1,13},{5,9},{9,5},{13,1},{2,14},{6,10},... | collective-permute-start | bytes 55304 | tf_op jit(solution)/shard_map/ppermute | solution.py:92
  31.5 4.8 %collective-permute-start.6 = (f32[4,9,128]{2,0,1:T(4,128)S(1)}, f32[4,9,128]{2,0,1:T(4,128)S(1)}, u32[]{:S(2)}, u32[]{:S(2)}) collective-permute-start(f32[4,9,128]{2,0,1:T(4,128)S(1)} %pad_maximum_fusion.10), channel_id=1, source_target_pairs={{0,8},{4,12},{8,0},{12,4},{1,9},{5,13},{9,1},{13,5},{2,10},{6,14},... | collective-permute-start | bytes 55304 | tf_op jit(solution)/shard_map/ppermute | solution.py:92
  33.4 3.8 %collective-permute-start.5 = (f32[4,9,128]{2,0,1:T(4,128)S(1)}, f32[4,9,128]{2,0,1:T(4,128)S(1)}, u32[]{:S(2)}, u32[]{:S(2)}) collective-permute-start(f32[4,9,128]{2,0,1:T(4,128)S(1)} %pad_maximum_fusion.9), channel_id=1, source_target_pairs={{0,4},{4,0},{8,12},{12,8},{1,5},{5,1},{9,13},{13,9},{2,6},{6,2},{1... | collective-permute-start | bytes 55304 | tf_op jit(solution)/shard_map/ppermute | solution.py:92
  38.7 5.8 %collective-permute-start.10 = (f32[4,8,128]{2,1,0:T(8,128)S(1)}, f32[4,8,128]{2,1,0:T(8,128)S(1)}, u32[]{:S(2)}, u32[]{:S(2)}) collective-permute-start(f32[4,8,128]{2,1,0:T(8,128)S(1)} %get-tuple-element.12), channel_id=1, source_target_pairs={{12,0},{8,4},{4,8},{0,12},{13,1},{9,5},{5,9},{1,13},{14,2},{10,6},... | collective-permute-start | bytes 49160 | tf_op jit(solution)/shard_map/ppermute | solution.py:92
  41.3 4.7 %collective-permute-start.9 = (f32[4,8,128]{2,1,0:T(8,128)S(1)}, f32[4,8,128]{2,1,0:T(8,128)S(1)}, u32[]{:S(2)}, u32[]{:S(2)}) collective-permute-start(f32[4,8,128]{2,1,0:T(8,128)S(1)} %get-tuple-element.11), channel_id=1, source_target_pairs={{8,0},{12,4},{0,8},{4,12},{9,1},{13,5},{1,9},{5,13},{10,2},{14,6},... | collective-permute-start | bytes 49160 | tf_op jit(solution)/shard_map/ppermute | solution.py:92
  41.5 5.9 %collective-permute-start.8 = (f32[4,8,128]{2,1,0:T(8,128)S(1)}, f32[4,8,128]{2,1,0:T(8,128)S(1)}, u32[]{:S(2)}, u32[]{:S(2)}) collective-permute-start(f32[4,8,128]{2,1,0:T(8,128)S(1)} %get-tuple-element.10), channel_id=1, source_target_pairs={{4,0},{0,4},{12,8},{8,12},{5,1},{1,5},{13,9},{9,13},{6,2},{2,6},{1... | collective-permute-start | bytes 49160 | tf_op jit(solution)/shard_map/ppermute | solution.py:92
  49.7 11.6 %collective-permute-start.11 = (f32[8,8,128]{2,1,0:T(8,128)S(1)}, f32[8,8,128]{2,1,0:T(8,128)S(1)}, u32[]{:S(2)}, u32[]{:S(2)}) collective-permute-start(f32[8,8,128]{2,1,0:T(8,128)S(1)} %bitcast_subtract_fusion.2), channel_id=1, source_target_pairs={{0,1},{1,0},{2,3},{3,2},{4,5},{5,4},{6,7},{7,6},{8,9},{9,8},{10,11... | collective-permute-start | bytes 98312 | tf_op jit(solution)/shard_map/ppermute | solution.py:78
  51.5 8.8 %collective-permute-start.14 = (f32[4,8,128]{2,1,0:T(8,128)S(1)}, f32[4,8,128]{2,1,0:T(8,128)S(1)}, u32[]{:S(2)}, u32[]{:S(2)}) collective-permute-start(f32[4,8,128]{2,1,0:T(8,128)S(1)} %add_select_fusion), channel_id=1, source_target_pairs={{0,12},{4,8},{8,4},{12,0},{1,13},{5,9},{9,5},{13,1},{2,14},{6,10},... | collective-permute-start | bytes 49160 | tf_op jit(solution)/shard_map/ppermute | solution.py:92
  55.4 4.9 %collective-permute-start.13 = (f32[4,8,128]{2,1,0:T(8,128)S(1)}, f32[4,8,128]{2,1,0:T(8,128)S(1)}, u32[]{:S(2)}, u32[]{:S(2)}) collective-permute-start(f32[4,8,128]{2,1,0:T(8,128)S(1)} %add_select_fusion.1), channel_id=1, source_target_pairs={{0,8},{4,12},{8,0},{12,4},{1,9},{5,13},{9,1},{13,5},{2,10},{6,14},... | collective-permute-start | bytes 49160 | tf_op jit(solution)/shard_map/ppermute | solution.py:92
  56.9 3.8 %collective-permute-start.12 = (f32[4,8,128]{2,1,0:T(8,128)S(1)}, f32[4,8,128]{2,1,0:T(8,128)S(1)}, u32[]{:S(2)}, u32[]{:S(2)}) collective-permute-start(f32[4,8,128]{2,1,0:T(8,128)S(1)} %add_select_fusion.2), channel_id=1, source_target_pairs={{0,4},{4,0},{8,12},{12,8},{1,5},{5,1},{9,13},{13,9},{2,6},{6,2},{1... | collective-permute-start | bytes 49160 | tf_op jit(solution)/shard_map/ppermute | solution.py:92
  61.2 1.3 %collective-permute-start.15 = (f32[8,8,128]{2,1,0:T(8,128)S(1)}, f32[8,8,128]{2,1,0:T(8,128)S(1)}, u32[]{:S(2)}, u32[]{:S(2)}) collective-permute-start(f32[8,8,128]{2,1,0:T(8,128)S(1)} %bitcast_subtract_fusion), channel_id=1, source_target_pairs={{0,1},{1,0},{2,3},{3,2},{4,5},{5,4},{6,7},{7,6},{8,9},{9,8},{10,11... | collective-permute-start | bytes 98312 | tf_op jit(solution)/shard_map/ppermute | solution.py:78

commit v16 on v11

--- a/solution.py
+++ b/solution.py
@@ -159,21 +159,14 @@
         real_pot = jnp.zeros((half, blocks, BLOCK), jnp.float32)
         for sweep_index in range(ITERS):
             if sweep_index == 0:
-                panel = jnp.zeros((slot_count, 1, BLOCK), jnp.float32)
+                panels = [jnp.zeros((wide, 1, BLOCK), jnp.float32)] * peer_count
             else:
-                panel = jnp.concatenate(
-                    send_down(
-                        [
-                            pick_rows(synth_pot, requested[offset * wide : (offset + 1) * wide], blocks)
-                            for offset in range(peer_count)
-                        ]
-                    ),
-                    axis=0,
-                )
+                arrived = send_down([synth_pot] * peer_count)
+                panels = [pick_rows(arrived[offset], wanted[offset], blocks) for offset in range(peer_count)]
             highest, mass_sum = [], []
             for offset in range(peer_count):
                 piece = slice(offset * wide, (offset + 1) * wide)
-                scores = (panel[piece] / SMOOTH)[:, :, :, None] - cost_rows[piece, None]
+                scores = (panels[offset] / SMOOTH)[:, :, :, None] - cost_rows[piece, None]
                 parts = lse_parts(scores, 2)
                 highest.append(parts[0])
                 mass_sum.append(parts[1])

time: 61.2 us -> 62.3 us (1.018)
  waiting for transfers between devices: 3.96 us -> 5.35 us
    ppermute x12, waiting for transfers between devices: 3.45 us -> 4.84 us  [exchange(): moved.append(lax.ppermute(chunks[offset], 'blk', perm))]
    reduce_sum x13 -> x16, other arithmetic: 4.56 us -> 4.79 us  [pick_rows(): return jnp.sum(chosen, axis=2, dtype=values.dtype)]
    reduce_max x11 -> x13, other arithmetic: 7.55 us -> 7.5 us  [lse_parts(): highest = jnp.max(scores, axis=axis)]
    reduce_sum x14 -> x12, other arithmetic: 9.49 us -> 9.5 us  [lse_parts(): jnp.sum(jnp.exp(scores - jnp.expand_dims(highest, axis)), axis=axis)]
  transfers between devices with their start and end apart: 15 -> 15, of which waited for: 4 -> 7; matrix products, arithmetic and copies ran while one was open for 40% -> 35% of each run, Pallas kernels for 0% -> 0%
where the time goes in v16:
time: 62.3 us; the launch traced here: 62 us
  other arithmetic  28.7 us (46%)
  starting transfers between devices  19.2 us (31%)
  waiting for transfers between devices  5.35 us (9%)
  local copies, waits for them, and re-layouts  4.84 us (8%)
  matrix products  2.53 us (4%)
  between operations  1.36 us (2%)
    ppermute x12, starting transfers between devices, exchange(): moved.append(lax.ppermute(chunks[offset], 'blk', perm))  19.1 us
    reduce_sum x12, other arithmetic, lse_parts(): jnp.sum(jnp.exp(scores - jnp.expand_dims(highest, axis)), axis=axis)  9.5 us
    reduce_max x13, other arithmetic, lse_parts(): highest = jnp.max(scores, axis=axis)  7.5 us
    ppermute x12, waiting for transfers between devices, exchange(): moved.append(lax.ppermute(chunks[offset], 'blk', perm))  4.84 us
    reduce_sum x16, other arithmetic, pick_rows(): return jnp.sum(chosen, axis=2, dtype=values.dtype)  4.79 us
    dot_general x2, matrix products, slot_costs(): jnp.einsum('gdi,gdj->gij', slot_real, slot_synth, preferred_element_type=...  2.53 us
    unnamed x8, local copies, waits for them, and re-layouts  2.26 us
    unnamed x2, other arithmetic  1.55 us
  transfers between devices with their start and end apart: 15, of which 7 were waited for; matrix products, arithmetic and copies ran while one was open for 35% of the time, Pallas kernels for 0%

profile of v16, /device:TPU:0, one launch (start us, length us, event | category | flops | bytes accessed | tf_op | source)
XLA Modules:
  0.0 62.0 jit_solution(1514800762520845889)
XLA Ops:
  0.6 0.7 %convert_bitcast_fusion.3 = (bf16[1,1,8,128]{3,2,1,0:T(8,128)(2,1)S(1)}, bf16[1,8,128]{2,1,0:T(8,128)(2,1)S(1)}) fusion(s32[1024]{0:T(1024)} %param.12), kind=kLoop, calls=%fused_computation.182 | loop fusion | flops 1024 | bytes 8192 | tf_op jit(solution)/shard_map/concatenate | solution.py:123
  1.4 0.9 %copy.135 = bf16[8,8,8,128]{3,2,1,0:T(8,128)(2,1)S(1)} copy(bf16[8,8,8,128]{3,1,2,0:T(8,128)(2,1)} %bitcast.69) | data formatting | bytes 262144
  2.3 5.1 %collective-permute-start.3 = (bf16[65,8,128]{2,1,0:T(8,128)(2,1)S(1)}, bf16[65,8,128]{2,1,0:T(8,128)(2,1)S(1)}, u32[]{:S(2)}, u32[]{:S(2)}) collective-permute-start(bf16[65,8,128]{2,1,0:T(8,128)(2,1)S(1)} %pad_maximum_fusion.1), channel_id=1, source_target_pairs={{12,0},{8,4},{4,8},{0,12},{13,1},{9,5},{5,9},{1,13},{14,2},{10,6},... | collective-permute-start | bytes 399368 | tf_op jit(solution)/shard_map/ppermute | solution.py:92
  7.4 0.6 %collective-permute-start.1 = (bf16[65,8,128]{2,1,0:T(8,128)(2,1)S(1)}, bf16[65,8,128]{2,1,0:T(8,128)(2,1)S(1)}, u32[]{:S(2)}, u32[]{:S(2)}) collective-permute-start(bf16[65,8,128]{2,1,0:T(8,128)(2,1)S(1)} %pad_maximum_fusion.1), channel_id=1, source_target_pairs={{4,0},{0,4},{12,8},{8,12},{5,1},{1,5},{13,9},{9,13},{6,2},{2,6},{1... | collective-permute-start | bytes 399368 | tf_op jit(solution)/shard_map/ppermute | solution.py:92
  8.1 0.7 %stack_broadcast_in_dim.2 = s32[1,4,2]{1,2,0:T(2,128)S(1)} broadcast(s32[4]{0:T(128)} %param.17), dimensions={1} | broadcast | bytes 48 | tf_op jit(solution)/shard_map/stack;broadcast_in_dim | solution.py:139
  8.7 0.7 %fusion.39 = (s32[3,1,4,2]{2,3,0,1:T(2,128)S(1)}, s32[3,4,2]{1,2,0:T(2,128)S(1)}) fusion(s32[1,4,2]{1,2,0:T(2,128)S(1)} %stack_broadcast_in_dim.2, s32[1,4,2]{1,2,0:T(2,128)} %bitcast.77, s32[1,4,2]{1,2,0:T(2,128)} %bitcast.78), kind=kLoop, calls=%fused_computation.186 | loop fusion | flops 48 | bytes 288 | tf_op jit(solution)/shard_map/stack | solution.py:140
  9.5 0.7 %convert_bitcast_fusion.1 = bf16[8,128]{1,0:T(8,128)(2,1)S(1)} fusion(s32[1024]{0:T(1024)} %param.11), kind=kLoop, calls=%fused_computation.175 | loop fusion | flops 1024 | bytes 6144 | tf_op jit(solution)/shard_map/convert_element_type | solution.py:122
  10.2 0.8 %multiply_bitcast_fusion.1 = f32[1,8,8,128]{3,1,2,0:T(8,128)S(1)} fusion(s32[16,1024]{1,0:T(8,128)} %param.13, s32[]{:T(128)S(6)} %select_n.261), kind=kLoop, calls=%fused_computation.109 | loop fusion | flops 24576 | bytes 65540
  11.0 0.8 %multiply_bitcast_fusion = f32[1,8,8,128]{3,1,2,0:T(8,128)S(1)} fusion(s32[16,1024]{1,0:T(8,128)} %param.14, s32[]{:T(128)S(6)} %select_n.261), kind=kLoop, calls=%fused_computation.108 | loop fusion | flops 24576 | bytes 65540
  11.9 0.3 select_reduce_fusion.25
  12.2 0.3 slice_reduce_fusion.7
  12.7 0.3 slice_reduce_fusion.3
  13.7 1.5 %select_reduce_fusion = bf16[16,64,128]{2,1,0:T(8,128)(2,1)S(1)} fusion(pred[16,8]{1,0:T(8,128)(4,1)S(1)} %iota_compare_fusion.1, bf16[64,8,128]{2,1,0:T(8,128)(2,1)S(1)} %bitcast.66), kind=kLoop, calls=%fused_computation.48 | loop fusion | flops 1966080 | bytes 393344 | tf_op jit(solution)/shard_map/reduce_sum | solution.py:26
  15.8 0.4 select_reduce_fusion.4
  16.2 0.4 select_reduce_fusion.1
  16.6 2.1 %collective-permute-done.2 = bf16[65,8,128]{2,1,0:T(8,128)(2,1)S(1)} collective-permute-done((bf16[65,8,128]{2,1,0:T(8,128)(2,1)S(1)}, bf16[65,8,128]{2,1,0:T(8,128)(2,1)S(1)}, u32[]{:S(2)}, u32[]{:S(2)}) %collective-permute-start.2) | collective-permute-done | bytes 133152 | tf_op jit(solution)/shard_map/ppermute | solution.py:92
  18.7 0.4 select_reduce_fusion.2
  19.1 0.4 select_reduce_fusion.3
  19.6 1.4 %fusion.26 = f32[16,128,128]{2,1,0:T(8,128)S(1)} fusion(bf16[16,64,128]{2,1,0:T(8,128)(2,1)S(1)} %select_reduce_fusion, f32[16,128]{1,0:T(8,128)S(1)} %broadcast_multiply_fusion.4, f32[16,128]{1,0:T(8,128)S(1)} %broadcast_multiply_fusion.5, bf16[16,128]{1,0:T(8,128)(2,1)S(1)} %select_reduce_fusion.23, bf16[16,128]{1,0:T(8,128)(2,1)S(1)} %bitcast.75, ...), kind=kOutput, calls=%fused_computation.53 | convolution fusion | flops 35127296 | bytes 1597440 | tf_op jit(solution)/shard_map/gdi,gdj->gij/dot_general | solution.py:61
  21.0 1.1 %fusion.27 = f32[16,128,128]{2,1,0:T(8,128)S(1)} fusion(bf16[16,64,128]{2,1,0:T(8,128)(2,1)S(1)} %select_reduce_fusion, f32[16,128]{1,0:T(8,128)S(1)} %broadcast_multiply_fusion.5, f32[16,128]{1,0:T(8,128)S(1)} %broadcast_multiply_fusion.4, bf16[16,128]{1,0:T(8,128)(2,1)S(1)} %bitcast.76, bf16[16,128]{1,0:T(8,128)(2,1)S(1)} %select_reduce_fusion.23, ...), kind=kOutput, calls=%fused_computation.54 | convolution fusion | flops 35127296 | bytes 1597440 | tf_op jit(solution)/shard_map/gdi,gdj->gij/dot_general | solution.py:61
  22.4 0.2 exponential_reduce_fusion.2
  23.1 0.2 select_reduce_fusion.15
  23.4 0.6 %subtract_reduce_fusion.8 = f32[4,8,128]{2,1,0:T(8,128)S(1)} fusion(f32[4,128,128]{2,1,0:T(8,128)S(1)} %get-tuple-element.26, f32[4,8,128]{2,1,0:T(8,128)S(1)} %get-tuple-element.39), kind=kLoop, calls=%fused_computation.17 | loop fusion | flops 1044480 | bytes 294912 | tf_op jit(solution)/shard_map/reduce_max | solution.py:71
  24.0 0.7 %fusion.7 = f32[4,8,128]{2,1,0:T(8,128)S(1)} fusion(f32[4,8,128]{2,1,0:T(8,128)S(1)} %subtract_reduce_fusion.8, f32[4,128,128]{2,1,0:T(8,128)S(1)} %get-tuple-element.26, f32[4,8,128]{2,1,0:T(8,128)S(1)} %get-tuple-element.39), kind=kLoop, calls=%fused_computation.31 | loop fusion | flops 1568768 | bytes 311296 | tf_op jit(solution)/shard_map/reduce_sum | solution.py:72
  24.9 2.5 %collective-permute-start.6 = (f32[4,9,128]{2,0,1:T(4,128)S(1)}, f32[4,9,128]{2,0,1:T(4,128)S(1)}, u32[]{:S(2)}, u32[]{:S(2)}) collective-permute-start(f32[4,9,128]{2,0,1:T(4,128)S(1)} %pad_maximum_fusion.8), channel_id=1, source_target_pairs={{0,12},{4,8},{8,4},{12,0},{1,13},{5,9},{9,5},{13,1},{2,14},{6,10},... | collective-permute-start | bytes 55304 | tf_op jit(solution)/shard_map/ppermute | solution.py:92
  27.4 0.6 subtract_reduce_fusion.9
  28.1 0.7 %fusion.5 = f32[4,8,128]{2,1,0:T(8,128)S(1)} fusion(f32[4,8,128]{2,1,0:T(8,128)S(1)} %subtract_reduce_fusion.9, f32[4,128,128]{2,1,0:T(8,128)S(1)} %get-tuple-element.27, f32[4,8,128]{2,1,0:T(8,128)S(1)} %get-tuple-element.40), kind=kLoop, calls=%fused_computation.29 | loop fusion | flops 1568768 | bytes 311296 | tf_op jit(solution)/shard_map/reduce_sum | solution.py:72
  29.0 0.6 %subtract_reduce_fusion.10 = f32[4,8,128]{2,1,0:T(8,128)S(1)} fusion(f32[4,128,128]{2,1,0:T(8,128)S(1)} %get-tuple-element.28, f32[4,8,128]{2,1,0:T(8,128)S(1)} %get-tuple-element.41), kind=kLoop, calls=%fused_computation.21 | loop fusion | flops 1044480 | bytes 294912 | tf_op jit(solution)/shard_map/reduce_max | solution.py:71
  29.6 0.7 %fusion.3 = f32[4,8,128]{2,1,0:T(8,128)S(1)} fusion(f32[4,8,128]{2,1,0:T(8,128)S(1)} %subtract_reduce_fusion.10, f32[4,128,128]{2,1,0:T(8,128)S(1)} %get-tuple-element.28, f32[4,8,128]{2,1,0:T(8,128)S(1)} %get-tuple-element.41), kind=kLoop, calls=%fused_computation.27 | loop fusion | flops 1568768 | bytes 311296 | tf_op jit(solution)/shard_map/reduce_sum | solution.py:72
  30.6 1.9 %collective-permute-start.4 = (f32[4,9,128]{2,0,1:T(4,128)S(1)}, f32[4,9,128]{2,0,1:T(4,128)S(1)}, u32[]{:S(2)}, u32[]{:S(2)}) collective-permute-start(f32[4,9,128]{2,0,1:T(4,128)S(1)} %pad_maximum_fusion.6), channel_id=1, source_target_pairs={{0,4},{4,0},{8,12},{12,8},{1,5},{5,1},{9,13},{13,9},{2,6},{6,2},{1... | collective-permute-start | bytes 55304 | tf_op jit(solution)/shard_map/ppermute | solution.py:92
  32.5 0.6 subtract_reduce_fusion.11
  33.1 0.7 %fusion.1 = f32[4,8,128]{2,1,0:T(8,128)S(1)} fusion(f32[4,8,128]{2,1,0:T(8,128)S(1)} %subtract_reduce_fusion.11, f32[4,128,128]{2,1,0:T(8,128)S(1)} %get-tuple-element.25, f32[4,8,128]{2,1,0:T(8,128)S(1)} %get-tuple-element.38), kind=kLoop, calls=%fused_computation.25 | loop fusion | flops 1568768 | bytes 311296 | tf_op jit(solution)/shard_map/reduce_sum | solution.py:72
  33.9 0.4 collective-permute-done.4
  34.8 0.2 select_reduce_fusion.13
  35.2 2.4 %collective-permute-start.9 = (f32[8,8,128]{2,1,0:T(8,128)S(1)}, f32[8,8,128]{2,1,0:T(8,128)S(1)}, u32[]{:S(2)}, u32[]{:S(2)}) collective-permute-start(f32[8,8,128]{2,1,0:T(8,128)S(1)} %bitcast_subtract_fusion.1), channel_id=1, source_target_pairs={{12,0},{8,4},{4,8},{0,12},{13,1},{9,5},{5,9},{1,13},{14,2},{10,6},... | collective-permute-start | bytes 98312 | tf_op jit(solution)/shard_map/ppermute | solution.py:92
  37.6 1.0 %collective-permute-start.8 = (f32[8,8,128]{2,1,0:T(8,128)S(1)}, f32[8,8,128]{2,1,0:T(8,128)S(1)}, u32[]{:S(2)}, u32[]{:S(2)}) collective-permute-start(f32[8,8,128]{2,1,0:T(8,128)S(1)} %bitcast_subtract_fusion.1), channel_id=1, source_target_pairs={{8,0},{12,4},{0,8},{4,12},{9,1},{13,5},{1,9},{5,13},{10,2},{14,6},... | collective-permute-start | bytes 98312 | tf_op jit(solution)/shard_map/ppermute | solution.py:92
  38.6 1.0 %collective-permute-start.7 = (f32[8,8,128]{2,1,0:T(8,128)S(1)}, f32[8,8,128]{2,1,0:T(8,128)S(1)}, u32[]{:S(2)}, u32[]{:S(2)}) collective-permute-start(f32[8,8,128]{2,1,0:T(8,128)S(1)} %bitcast_subtract_fusion.1), channel_id=1, source_target_pairs={{4,0},{0,4},{12,8},{8,12},{5,1},{1,5},{13,9},{9,13},{6,2},{2,6},{1... | collective-permute-start | bytes 98312 | tf_op jit(solution)/shard_map/ppermute | solution.py:92
  39.8 0.6 %subtract_reduce_fusion.7 = f32[4,8,128]{2,1,0:T(8,128)S(1)} fusion(f32[4,128,128]{2,1,0:T(8,128)S(1)} %get-tuple-element.22, f32[4,8,128]{2,1,0:T(8,128)S(1)} %broadcast_multiply_fusion.3), kind=kLoop, calls=%fused_computation.15 | loop fusion | flops 1044480 | bytes 294912 | tf_op jit(solution)/shard_map/reduce_max | solution.py:71
  40.4 0.9 %collective-permute-done.9 = f32[8,8,128]{2,1,0:T(8,128)S(1)} collective-permute-done((f32[8,8,128]{2,1,0:T(8,128)S(1)}, f32[8,8,128]{2,1,0:T(8,128)S(1)}, u32[]{:S(2)}, u32[]{:S(2)}) %collective-permute-start.9) | collective-permute-done | bytes 32800 | tf_op jit(solution)/shard_map/ppermute | solution.py:92
  41.4 1.0 %collective-permute-done.8 = f32[8,8,128]{2,1,0:T(8,128)S(1)} collective-permute-done((f32[8,8,128]{2,1,0:T(8,128)S(1)}, f32[8,8,128]{2,1,0:T(8,128)S(1)}, u32[]{:S(2)}, u32[]{:S(2)}) %collective-permute-start.8) | collective-permute-done | bytes 32800 | tf_op jit(solution)/shard_map/ppermute | solution.py:92
  42.6 0.2 collective-permute-done.7
  42.9 0.6 %subtract_reduce_fusion.4 = f32[4,8,128]{2,1,0:T(8,128)S(1)} fusion(f32[4,128,128]{2,1,0:T(8,128)S(1)} %get-tuple-element.29, f32[4,8,128]{2,1,0:T(8,128)S(1)} %broadcast_multiply_fusion), kind=kLoop, calls=%fused_computation.9 | loop fusion | flops 1044480 | bytes 294912 | tf_op jit(solution)/shard_map/reduce_max | solution.py:71
  43.5 0.6 %subtract_reduce_fusion.5 = f32[4,8,128]{2,1,0:T(8,128)S(1)} fusion(f32[4,128,128]{2,1,0:T(8,128)S(1)} %get-tuple-element.24, f32[4,8,128]{2,1,0:T(8,128)S(1)} %broadcast_multiply_fusion.1), kind=kLoop, calls=%fused_computation.11 | loop fusion | flops 1044480 | bytes 294912 | tf_op jit(solution)/shard_map/reduce_max | solution.py:71
  44.2 0.6 %subtract_reduce_fusion.6 = f32[4,8,128]{2,1,0:T(8,128)S(1)} fusion(f32[4,128,128]{2,1,0:T(8,128)S(1)} %get-tuple-element.23, f32[4,8,128]{2,1,0:T(8,128)S(1)} %broadcast_multiply_fusion.2), kind=kLoop, calls=%fused_computation.13 | loop fusion | flops 1044480 | bytes 294912 | tf_op jit(solution)/shard_map/reduce_max | solution.py:71
  44.8 1.5 %fusion.13 = (f32[4,8,128]{2,1,0:T(8,128)S(1)}, f32[4,8,128]{2,1,0:T(8,128)S(1)}) fusion(f32[4,8,128]{2,1,0:T(8,128)S(1)} %subtract_reduce_fusion.5, f32[4,128,128]{2,1,0:T(8,128)S(1)} %get-tuple-element.24, f32[4,8,128]{2,1,0:T(8,128)S(1)} %broadcast_multiply_fusion.1, f32[4,8,128]{2,1,0:T(8,128)S(1)} %subtract_reduce_fusion.4, ...), kind=kLoop, calls=%fused_computation.37 | loop fusion | flops 3137536 | bytes 622592 | tf_op jit(solution)/shard_map/reduce_sum | solution.py:72
  46.4 1.5 %fusion.9 = (f32[4,8,128]{2,1,0:T(8,128)S(1)}, f32[4,8,128]{2,1,0:T(8,128)S(1)}) fusion(f32[4,8,128]{2,1,0:T(8,128)S(1)} %subtract_reduce_fusion.7, f32[4,128,128]{2,1,0:T(8,128)S(1)} %get-tuple-element.22, f32[4,8,128]{2,1,0:T(8,128)S(1)} %broadcast_multiply_fusion.3, f32[4,8,128]{2,1,0:T(8,128)S(1)} %subtract_reduce_fusion.6, ...), kind=kLoop, calls=%fused_computation.33 | loop fusion | flops 3137536 | bytes 622592 | tf_op jit(solution)/shard_map/reduce_sum | solution.py:72
  48.0 0.2 select_reduce_fusion.10
  48.5 0.2 select_reduce_fusion.8
  48.8 0.6 %subtract_reduce_fusion = f32[4,8,128]{2,1,0:T(8,128)S(1)} fusion(f32[4,8,128]{2,1,0:T(8,128)S(1)} %get-tuple-element.33, f32[4,128,128]{2,1,0:T(8,128)S(1)} %get-tuple-element.26), kind=kLoop, calls=%fused_computation.1 | loop fusion | flops 1044480 | bytes 294912 | tf_op jit(solution)/shard_map/reduce_max | solution.py:71
  49.4 0.7 %fusion.23 = f32[4,8,128]{2,1,0:T(8,128)S(1)} fusion(f32[4,8,128]{2,1,0:T(8,128)S(1)} %subtract_reduce_fusion, f32[4,8,128]{2,1,0:T(8,128)S(1)} %get-tuple-element.33, f32[4,128,128]{2,1,0:T(8,128)S(1)} %get-tuple-element.26), kind=kLoop, calls=%fused_computation.47 | loop fusion | flops 1568768 | bytes 311296 | tf_op jit(solution)/shard_map/reduce_sum | solution.py:72
  50.2 2.2 %collective-permute-start.13 = (f32[4,8,128]{2,1,0:T(8,128)S(1)}, f32[4,8,128]{2,1,0:T(8,128)S(1)}, u32[]{:S(2)}, u32[]{:S(2)}) collective-permute-start(f32[4,8,128]{2,1,0:T(8,128)S(1)} %add_select_fusion), channel_id=1, source_target_pairs={{0,12},{4,8},{8,4},{12,0},{1,13},{5,9},{9,5},{13,1},{2,14},{6,10},... | collective-permute-start | bytes 49160 | tf_op jit(solution)/shard_map/ppermute | solution.py:92
  52.5 0.6 %subtract_reduce_fusion.1 = f32[4,8,128]{2,1,0:T(8,128)S(1)} fusion(f32[4,8,128]{2,1,0:T(8,128)S(1)} %get-tuple-element.34, f32[4,128,128]{2,1,0:T(8,128)S(1)} %get-tuple-element.27), kind=kLoop, calls=%fused_computation.3 | loop fusion | flops 1044480 | bytes 294912 | tf_op jit(solution)/shard_map/reduce_max | solution.py:71
  53.1 1.0 %fusion.21 = f32[4,8,128]{2,1,0:T(8,128)S(1)} fusion(f32[4,8,128]{2,1,0:T(8,128)S(1)} %subtract_reduce_fusion.1, f32[4,8,128]{2,1,0:T(8,128)S(1)} %get-tuple-element.34, f32[4,128,128]{2,1,0:T(8,128)S(1)} %get-tuple-element.27), kind=kLoop, calls=%fused_computation.45 | loop fusion | flops 1568768 | bytes 311296 | tf_op jit(solution)/shard_map/reduce_sum | solution.py:72
  54.2 0.2 collective-permute-start.12
  54.3 0.6 %subtract_reduce_fusion.2 = f32[4,8,128]{2,1,0:T(8,128)S(1)} fusion(f32[4,8,128]{2,1,0:T(8,128)S(1)} %get-tuple-element.35, f32[4,128,128]{2,1,0:T(8,128)S(1)} %get-tuple-element.28), kind=kLoop, calls=%fused_computation.5 | loop fusion | flops 1044480 | bytes 294912 | tf_op jit(solution)/shard_map/reduce_max | solution.py:71
  55.0 0.7 %fusion.19 = f32[4,8,128]{2,1,0:T(8,128)S(1)} fusion(f32[4,8,128]{2,1,0:T(8,128)S(1)} %subtract_reduce_fusion.2, f32[4,8,128]{2,1,0:T(8,128)S(1)} %get-tuple-element.35, f32[4,128,128]{2,1,0:T(8,128)S(1)} %get-tuple-element.28), kind=kLoop, calls=%fused_computation.43 | loop fusion | flops 1568768 | bytes 311296 | tf_op jit(solution)/shard_map/reduce_sum | solution.py:72
  55.8 2.0 %collective-permute-start.11 = (f32[4,8,128]{2,1,0:T(8,128)S(1)}, f32[4,8,128]{2,1,0:T(8,128)S(1)}, u32[]{:S(2)}, u32[]{:S(2)}) collective-permute-start(f32[4,8,128]{2,1,0:T(8,128)S(1)} %add_select_fusion.2), channel_id=1, source_target_pairs={{0,4},{4,0},{8,12},{12,8},{1,5},{5,1},{9,13},{13,9},{2,6},{6,2},{1... | collective-permute-start | bytes 49160 | tf_op jit(solution)/shard_map/ppermute | solution.py:92
  57.8 0.6 %subtract_reduce_fusion.3 = f32[4,8,128]{2,1,0:T(8,128)S(1)} fusion(f32[4,8,128]{2,1,0:T(8,128)S(1)} %get-tuple-element.32, f32[4,128,128]{2,1,0:T(8,128)S(1)} %get-tuple-element.25), kind=kLoop, calls=%fused_computation.7 | loop fusion | flops 1044480 | bytes 294912 | tf_op jit(solution)/shard_map/reduce_max | solution.py:71
  58.4 0.7 %fusion.17 = f32[4,8,128]{2,1,0:T(8,128)S(1)} fusion(f32[4,8,128]{2,1,0:T(8,128)S(1)} %subtract_reduce_fusion.3, f32[4,8,128]{2,1,0:T(8,128)S(1)} %get-tuple-element.32, f32[4,128,128]{2,1,0:T(8,128)S(1)} %get-tuple-element.25), kind=kLoop, calls=%fused_computation.41 | loop fusion | flops 1568768 | bytes 311296 | tf_op jit(solution)/shard_map/reduce_sum | solution.py:72
  59.3 0.3 collective-permute-done.11
  59.7 0.2 select_reduce_fusion.6
  60.2 0.6 %copy.149 = f32[2,8,8,128]{3,1,2,0:T(8,128)} copy(f32[2,8,8,128]{3,2,1,0:T(8,128)S(1)} %bitcast.67) | data formatting | bytes 131072
  60.8 0.5 collective-permute-done.14
  61.4 0.6 %copy.148 = f32[2,8,8,128]{3,1,2,0:T(8,128)} copy(f32[2,8,8,128]{3,2,1,0:T(8,128)S(1)} %bitcast.68) | data formatting | bytes 131072
  (115 shorter events, 5.4 us)
Async XLA Ops:
  0.6 11.1 %copy-start = (bf16[64,1024]{1,0:T(8,128)(2,1)S(1)}, bf16[64,1024]{1,0:T(8,128)(2,1)}, u32[]{:S(2)}) copy-start(bf16[64,1024]{1,0:T(8,128)(2,1)} %param.9) | copy-start | bytes 393220
  2.3 13.9 %collective-permute-start.3 = (bf16[65,8,128]{2,1,0:T(8,128)(2,1)S(1)}, bf16[65,8,128]{2,1,0:T(8,128)(2,1)S(1)}, u32[]{:S(2)}, u32[]{:S(2)}) collective-permute-start(bf16[65,8,128]{2,1,0:T(8,128)(2,1)S(1)} %pad_maximum_fusion.1), channel_id=1, source_target_pairs={{12,0},{8,4},{4,8},{0,12},{13,1},{9,5},{5,9},{1,13},{14,2},{10,6},... | collective-permute-start | bytes 399368 | tf_op jit(solution)/shard_map/ppermute | solution.py:92
  7.4 11.2 %collective-permute-start.2 = (bf16[65,8,128]{2,1,0:T(8,128)(2,1)S(1)}, bf16[65,8,128]{2,1,0:T(8,128)(2,1)S(1)}, u32[]{:S(2)}, u32[]{:S(2)}) collective-permute-start(bf16[65,8,128]{2,1,0:T(8,128)(2,1)S(1)} %pad_maximum_fusion.1), channel_id=1, source_target_pairs={{8,0},{12,4},{0,8},{4,12},{9,1},{13,5},{1,9},{5,13},{10,2},{14,6},... | collective-permute-start | bytes 399368 | tf_op jit(solution)/shard_map/ppermute | solution.py:92
  7.4 11.6 %collective-permute-start.1 = (bf16[65,8,128]{2,1,0:T(8,128)(2,1)S(1)}, bf16[65,8,128]{2,1,0:T(8,128)(2,1)S(1)}, u32[]{:S(2)}, u32[]{:S(2)}) collective-permute-start(bf16[65,8,128]{2,1,0:T(8,128)(2,1)S(1)} %pad_maximum_fusion.1), channel_id=1, source_target_pairs={{4,0},{0,4},{12,8},{8,12},{5,1},{1,5},{13,9},{9,13},{6,2},{2,6},{1... | collective-permute-start | bytes 399368 | tf_op jit(solution)/shard_map/ppermute | solution.py:92
  9.4 2.4 %collective-permute-start = (s32[3,4,2]{1,2,0:T(2,128)S(1)}, s32[3,4,2]{1,2,0:T(2,128)S(1)}, u32[]{:S(2)}, u32[]{:S(2)}) collective-permute-start(s32[3,4,2]{1,2,0:T(2,128)S(1)} %get-tuple-element.45), channel_id=1, source_target_pairs={{0,1},{1,0},{2,3},{3,2},{4,5},{5,4},{6,7},{7,6},{8,9},{9,8},{10,11... | collective-permute-start | bytes 296 | tf_op jit(solution)/shard_map/ppermute | solution.py:78
  24.9 9.0 %collective-permute-start.6 = (f32[4,9,128]{2,0,1:T(4,128)S(1)}, f32[4,9,128]{2,0,1:T(4,128)S(1)}, u32[]{:S(2)}, u32[]{:S(2)}) collective-permute-start(f32[4,9,128]{2,0,1:T(4,128)S(1)} %pad_maximum_fusion.8), channel_id=1, source_target_pairs={{0,12},{4,8},{8,4},{12,0},{1,13},{5,9},{9,5},{13,1},{2,14},{6,10},... | collective-permute-start | bytes 55304 | tf_op jit(solution)/shard_map/ppermute | solution.py:92
  29.0 5.0 %collective-permute-start.5 = (f32[4,9,128]{2,0,1:T(4,128)S(1)}, f32[4,9,128]{2,0,1:T(4,128)S(1)}, u32[]{:S(2)}, u32[]{:S(2)}) collective-permute-start(f32[4,9,128]{2,0,1:T(4,128)S(1)} %pad_maximum_fusion.7), channel_id=1, source_target_pairs={{0,8},{4,12},{8,0},{12,4},{1,9},{5,13},{9,1},{13,5},{2,10},{6,14},... | collective-permute-start | bytes 55304 | tf_op jit(solution)/shard_map/ppermute | solution.py:92
  30.6 3.8 %collective-permute-start.4 = (f32[4,9,128]{2,0,1:T(4,128)S(1)}, f32[4,9,128]{2,0,1:T(4,128)S(1)}, u32[]{:S(2)}, u32[]{:S(2)}) collective-permute-start(f32[4,9,128]{2,0,1:T(4,128)S(1)} %pad_maximum_fusion.6), channel_id=1, source_target_pairs={{0,4},{4,0},{8,12},{12,8},{1,5},{5,1},{9,13},{13,9},{2,6},{6,2},{1... | collective-permute-start | bytes 55304 | tf_op jit(solution)/shard_map/ppermute | solution.py:92
  35.2 6.1 %collective-permute-start.9 = (f32[8,8,128]{2,1,0:T(8,128)S(1)}, f32[8,8,128]{2,1,0:T(8,128)S(1)}, u32[]{:S(2)}, u32[]{:S(2)}) collective-permute-start(f32[8,8,128]{2,1,0:T(8,128)S(1)} %bitcast_subtract_fusion.1), channel_id=1, source_target_pairs={{12,0},{8,4},{4,8},{0,12},{13,1},{9,5},{5,9},{1,13},{14,2},{10,6},... | collective-permute-start | bytes 98312 | tf_op jit(solution)/shard_map/ppermute | solution.py:92
  37.6 4.8 %collective-permute-start.8 = (f32[8,8,128]{2,1,0:T(8,128)S(1)}, f32[8,8,128]{2,1,0:T(8,128)S(1)}, u32[]{:S(2)}, u32[]{:S(2)}) collective-permute-start(f32[8,8,128]{2,1,0:T(8,128)S(1)} %bitcast_subtract_fusion.1), channel_id=1, source_target_pairs={{8,0},{12,4},{0,8},{4,12},{9,1},{13,5},{1,9},{5,13},{10,2},{14,6},... | collective-permute-start | bytes 98312 | tf_op jit(solution)/shard_map/ppermute | solution.py:92
  38.6 4.2 %collective-permute-start.7 = (f32[8,8,128]{2,1,0:T(8,128)S(1)}, f32[8,8,128]{2,1,0:T(8,128)S(1)}, u32[]{:S(2)}, u32[]{:S(2)}) collective-permute-start(f32[8,8,128]{2,1,0:T(8,128)S(1)} %bitcast_subtract_fusion.1), channel_id=1, source_target_pairs={{4,0},{0,4},{12,8},{8,12},{5,1},{1,5},{13,9},{9,13},{6,2},{2,6},{1... | collective-permute-start | bytes 98312 | tf_op jit(solution)/shard_map/ppermute | solution.py:92
  48.5 11.7 %collective-permute-start.10 = (f32[8,8,128]{2,1,0:T(8,128)S(1)}, f32[8,8,128]{2,1,0:T(8,128)S(1)}, u32[]{:S(2)}, u32[]{:S(2)}) collective-permute-start(f32[8,8,128]{2,1,0:T(8,128)S(1)} %bitcast_subtract_fusion.2), channel_id=1, source_target_pairs={{0,1},{1,0},{2,3},{3,2},{4,5},{5,4},{6,7},{7,6},{8,9},{9,8},{10,11... | collective-permute-start | bytes 98312 | tf_op jit(solution)/shard_map/ppermute | solution.py:78
  50.2 9.0 %collective-permute-start.13 = (f32[4,8,128]{2,1,0:T(8,128)S(1)}, f32[4,8,128]{2,1,0:T(8,128)S(1)}, u32[]{:S(2)}, u32[]{:S(2)}) collective-permute-start(f32[4,8,128]{2,1,0:T(8,128)S(1)} %add_select_fusion), channel_id=1, source_target_pairs={{0,12},{4,8},{8,4},{12,0},{1,13},{5,9},{9,5},{13,1},{2,14},{6,10},... | collective-permute-start | bytes 49160 | tf_op jit(solution)/shard_map/ppermute | solution.py:92
  54.2 5.1 %collective-permute-start.12 = (f32[4,8,128]{2,1,0:T(8,128)S(1)}, f32[4,8,128]{2,1,0:T(8,128)S(1)}, u32[]{:S(2)}, u32[]{:S(2)}) collective-permute-start(f32[4,8,128]{2,1,0:T(8,128)S(1)} %add_select_fusion.1), channel_id=1, source_target_pairs={{0,8},{4,12},{8,0},{12,4},{1,9},{5,13},{9,1},{13,5},{2,10},{6,14},... | collective-permute-start | bytes 49160 | tf_op jit(solution)/shard_map/ppermute | solution.py:92
  55.8 3.8 %collective-permute-start.11 = (f32[4,8,128]{2,1,0:T(8,128)S(1)}, f32[4,8,128]{2,1,0:T(8,128)S(1)}, u32[]{:S(2)}, u32[]{:S(2)}) collective-permute-start(f32[4,8,128]{2,1,0:T(8,128)S(1)} %add_select_fusion.2), channel_id=1, source_target_pairs={{0,4},{4,0},{8,12},{12,8},{1,5},{5,1},{9,13},{13,9},{2,6},{6,2},{1... | collective-permute-start | bytes 49160 | tf_op jit(solution)/shard_map/ppermute | solution.py:92
  60.1 1.3 %collective-permute-start.14 = (f32[8,8,128]{2,1,0:T(8,128)S(1)}, f32[8,8,128]{2,1,0:T(8,128)S(1)}, u32[]{:S(2)}, u32[]{:S(2)}) collective-permute-start(f32[8,8,128]{2,1,0:T(8,128)S(1)} %bitcast_subtract_fusion), channel_id=1, source_target_pairs={{0,1},{1,0},{2,3},{3,2},{4,5},{5,4},{6,7},{7,6},{8,9},{9,8},{10,11... | collective-permute-start | bytes 98312 | tf_op jit(solution)/shard_map/ppermute | solution.py:78

commit v17 on v11

--- a/solution.py
+++ b/solution.py
@@ -170,15 +170,18 @@
                     ),
                     axis=0,
                 )
-            highest, mass_sum = [], []
-            for offset in range(peer_count):
-                piece = slice(offset * wide, (offset + 1) * wide)
-                scores = (panel[piece] / SMOOTH)[:, :, :, None] - cost_rows[piece, None]
-                parts = lse_parts(scores, 2)
-                highest.append(parts[0])
-                mass_sum.append(parts[1])
-            highest = jnp.concatenate(highest, axis=0)
-            mass_sum = jnp.concatenate(mass_sum, axis=0)
+            if sweep_index == 0:
+                highest, mass_sum = lse_parts(0.0 - cost_cols[:, None], 3)
+            else:
+                highest, mass_sum = [], []
+                for offset in range(peer_count):
+                    piece = slice(offset * wide, (offset + 1) * wide)
+                    scores = (panel[piece] / SMOOTH)[:, :, :, None] - cost_rows[piece, None]
+                    parts = lse_parts(scores, 2)
+                    highest.append(parts[0])
+                    mass_sum.append(parts[1])
+                highest = jnp.concatenate(highest, axis=0)
+                mass_sum = jnp.concatenate(mass_sum, axis=0)
             highest = jnp.where(usable, highest, SENTINEL)
             mass_sum = jnp.where(usable, mass_sum, 0.0)
             block_top, summed = fold_blocks(highest, mass_sum, rows_used, blocks)

time: 61.2 us -> 66.9 us (1.093)
  waiting for transfers between devices: 3.96 us -> 9.38 us
  local copies, waits for them, and re-layouts: 4.99 us -> 6.11 us
  other arithmetic: 28.8 us -> 27.9 us
    ppermute x12, waiting for transfers between devices: 3.45 us -> 8.86 us  [exchange(): moved.append(lax.ppermute(chunks[offset], 'blk', perm))]
    unnamed x2 -> x1, other arithmetic: 1.55 us -> 0.8 us
    reduce_sum x14 -> x13, other arithmetic: 9.49 us -> 9.39 us  [lse_parts(): jnp.sum(jnp.exp(scores - jnp.expand_dims(highest, axis)), axis=axis)]
    reduce_max x11 -> x12, other arithmetic: 7.55 us -> 7.48 us  [lse_parts(): highest = jnp.max(scores, axis=axis)]
  transfers between devices with their start and end apart: 15 -> 15, of which waited for: 4 -> 8; matrix products, arithmetic and copies ran while one was open for 40% -> 35% of each run, Pallas kernels for 0% -> 0%
where the time goes in v17:
time: 66.9 us; the launch traced here: 66.7 us
  other arithmetic  27.9 us (42%)
  starting transfers between devices  19.3 us (29%)
  waiting for transfers between devices  9.38 us (14%)
  local copies, waits for them, and re-layouts  6.11 us (9%)
  matrix products  2.55 us (4%)
  between operations  1.41 us (2%)
    ppermute x12, starting transfers between devices, exchange(): moved.append(lax.ppermute(chunks[offset], 'blk', perm))  19.2 us
    reduce_sum x13, other arithmetic, lse_parts(): jnp.sum(jnp.exp(scores - jnp.expand_dims(highest, axis)), axis=axis)  9.39 us
    ppermute x12, waiting for transfers between devices, exchange(): moved.append(lax.ppermute(chunks[offset], 'blk', perm))  8.86 us
    reduce_max x12, other arithmetic, lse_parts(): highest = jnp.max(scores, axis=axis)  7.48 us
    reduce_sum x13, other arithmetic, pick_rows(): return jnp.sum(chosen, axis=2, dtype=values.dtype)  4.56 us
    dot_general x2, matrix products, slot_costs(): jnp.einsum('gdi,gdj->gij', slot_real, slot_synth, preferred_element_type=...  2.55 us
    unnamed x8, local copies, waits for them, and re-layouts  2.26 us
  transfers between devices with their start and end apart: 15, of which 8 were waited for; matrix products, arithmetic and copies ran while one was open for 35% of the time, Pallas kernels for 0%

profile of v17, /device:TPU:0, one launch (start us, length us, event | category | flops | bytes accessed | tf_op | source)
XLA Modules:
  0.0 66.7 jit_solution(9262787606694283526)
XLA Ops:
  0.6 0.7 %convert_bitcast_fusion.3 = (bf16[1,1,8,128]{3,2,1,0:T(8,128)(2,1)S(1)}, bf16[1,8,128]{2,1,0:T(8,128)(2,1)S(1)}) fusion(s32[1024]{0:T(1024)} %param.12), kind=kLoop, calls=%fused_computation.182 | loop fusion | flops 1024 | bytes 8192 | tf_op jit(solution)/shard_map/concatenate | solution.py:123
  1.4 0.9 %copy.190 = bf16[8,8,8,128]{3,2,1,0:T(8,128)(2,1)S(1)} copy(bf16[8,8,8,128]{3,1,2,0:T(8,128)(2,1)} %bitcast.69) | data formatting | bytes 262144
  2.3 5.1 %collective-permute-start.3 = (bf16[65,8,128]{2,1,0:T(8,128)(2,1)S(1)}, bf16[65,8,128]{2,1,0:T(8,128)(2,1)S(1)}, u32[]{:S(2)}, u32[]{:S(2)}) collective-permute-start(bf16[65,8,128]{2,1,0:T(8,128)(2,1)S(1)} %pad_maximum_fusion.1), channel_id=1, source_target_pairs={{12,0},{8,4},{4,8},{0,12},{13,1},{9,5},{5,9},{1,13},{14,2},{10,6},... | collective-permute-start | bytes 399368 | tf_op jit(solution)/shard_map/ppermute | solution.py:92
  7.4 0.6 collective-permute-start.1
  8.1 0.7 stack_broadcast_in_dim.2
  8.7 0.7 %fusion.38 = (s32[3,1,4,2]{2,3,0,1:T(2,128)S(1)}, s32[3,4,2]{1,2,0:T(2,128)S(1)}) fusion(s32[1,4,2]{1,2,0:T(2,128)S(1)} %stack_broadcast_in_dim.2, s32[1,4,2]{1,2,0:T(2,128)} %bitcast.77, s32[1,4,2]{1,2,0:T(2,128)} %bitcast.78), kind=kLoop, calls=%fused_computation.187 | loop fusion | flops 48 | bytes 288 | tf_op jit(solution)/shard_map/stack | solution.py:140
  9.5 0.7 %convert_bitcast_fusion.1 = bf16[8,128]{1,0:T(8,128)(2,1)S(1)} fusion(s32[1024]{0:T(1024)} %param.11), kind=kLoop, calls=%fused_computation.175 | loop fusion | flops 1024 | bytes 6144 | tf_op jit(solution)/shard_map/convert_element_type | solution.py:122
  10.2 0.8 %multiply_bitcast_fusion = (f32[1,8,8,128]{3,1,2,0:T(8,128)S(1)}, f32[1,8,8,128]{3,1,2,0:T(8,128)S(1)}) fusion(s32[16,1024]{1,0:T(8,128)} %param.14, s32[]{:T(128)S(6)} %select_n.261, s32[16,1024]{1,0:T(8,128)} %param.13), kind=kLoop, calls=%fused_computation.101 | loop fusion | flops 49152 | bytes 131076
  11.1 0.3 select_reduce_fusion.25
  11.5 0.3 slice_reduce_fusion.3
  11.8 0.3 slice_reduce_fusion.11
  13.5 1.4 %select_reduce_fusion = bf16[16,64,128]{2,1,0:T(8,128)(2,1)S(1)} fusion(pred[16,8]{1,0:T(8,128)(4,1)S(1)} %iota_compare_fusion.1, bf16[64,8,128]{2,1,0:T(8,128)(2,1)S(1)} %bitcast.66), kind=kLoop, calls=%fused_computation.48 | loop fusion | flops 1966080 | bytes 393344 | tf_op jit(solution)/shard_map/reduce_sum | solution.py:26
  15.1 0.4 select_reduce_fusion.4
  15.5 0.4 select_reduce_fusion.1
  15.9 2.8 %collective-permute-done.2 = bf16[65,8,128]{2,1,0:T(8,128)(2,1)S(1)} collective-permute-done((bf16[65,8,128]{2,1,0:T(8,128)(2,1)S(1)}, bf16[65,8,128]{2,1,0:T(8,128)(2,1)S(1)}, u32[]{:S(2)}, u32[]{:S(2)}) %collective-permute-start.2) | collective-permute-done | bytes 133152 | tf_op jit(solution)/shard_map/ppermute | solution.py:92
  18.7 0.4 select_reduce_fusion.2
  19.1 0.4 select_reduce_fusion.3
  19.6 1.3 %fusion.27 = f32[16,128,128]{1,2,0:T(8,128)S(1)} fusion(bf16[16,64,128]{2,1,0:T(8,128)(2,1)S(1)} %select_reduce_fusion, f32[16,128]{1,0:T(8,128)S(1)} %broadcast_multiply_fusion.5, f32[16,128]{1,0:T(8,128)S(1)} %broadcast_multiply_fusion.4, bf16[16,128]{1,0:T(8,128)(2,1)S(1)} %select_reduce_fusion.23, bf16[16,128]{1,0:T(8,128)(2,1)S(1)} %bitcast.75, ...), kind=kOutput, calls=%fused_computation.54 | convolution fusion | flops 35127296 | bytes 1597440 | tf_op jit(solution)/shard_map/gdi,gdj->gij/dot_general | solution.py:61
  21.0 1.2 %subtract_reduce_fusion.12 = (f32[16,128]{1,0:T(8,128)S(1)}, f32[16,128,128]{1,2,0:T(8,128)S(1)}) fusion(bf16[16,128]{1,0:T(8,128)(2,1)S(1)} %bitcast.76, bf16[16,128]{1,0:T(8,128)(2,1)S(1)} %select_reduce_fusion.23, bf16[16,64,128]{2,1,0:T(8,128)(2,1)S(1)} %select_reduce_fusion, bf16[16,65,128]{2,1,0:T(8,128)(2,1)S(1)} %pad_maximum_fusion, ...), kind=kOutput, calls=%fused_computation.56 | convolution fusion | flops 35649536 | bytes 1605632 | tf_op jit(solution)/shard_map/gdi,gdj->gij/dot_general | solution.py:61
  23.2 0.2 select_reduce_fusion.15
  23.5 0.6 subtract_reduce_fusion.11
  24.1 0.8 %fusion.1 = f32[4,8,128]{2,1,0:T(8,128)S(1)} fusion(f32[4,8,128]{2,1,0:T(8,128)S(1)} %subtract_reduce_fusion.11, f32[4,128,128]{2,1,0:T(8,128)S(1)} %copy.171, f32[4,8,128]{2,1,0:T(8,128)S(1)} %get-tuple-element.39), kind=kLoop, calls=%fused_computation.25 | loop fusion | flops 1568768 | bytes 311296 | tf_op jit(solution)/shard_map/reduce_sum | solution.py:72
  25.0 0.6 subtract_reduce_fusion.8
  25.6 0.7 %fusion.7 = f32[4,8,128]{2,1,0:T(8,128)S(1)} fusion(f32[4,8,128]{2,1,0:T(8,128)S(1)} %subtract_reduce_fusion.8, f32[4,128,128]{2,1,0:T(8,128)S(1)} %copy.177, f32[4,8,128]{2,1,0:T(8,128)S(1)} %get-tuple-element.40), kind=kLoop, calls=%fused_computation.31 | loop fusion | flops 1568768 | bytes 311296 | tf_op jit(solution)/shard_map/reduce_sum | solution.py:72
  26.5 2.5 %collective-permute-start.6 = (f32[4,9,128]{2,0,1:T(4,128)S(1)}, f32[4,9,128]{2,0,1:T(4,128)S(1)}, u32[]{:S(2)}, u32[]{:S(2)}) collective-permute-start(f32[4,9,128]{2,0,1:T(4,128)S(1)} %pad_maximum_fusion.8), channel_id=1, source_target_pairs={{0,12},{4,8},{8,4},{12,0},{1,13},{5,9},{9,5},{13,1},{2,14},{6,10},... | collective-permute-start | bytes 55304 | tf_op jit(solution)/shard_map/ppermute | solution.py:92
  29.2 0.6 subtract_reduce_fusion.9
  29.8 0.7 %fusion.5 = f32[4,8,128]{2,1,0:T(8,128)S(1)} fusion(f32[4,8,128]{2,1,0:T(8,128)S(1)} %subtract_reduce_fusion.9, f32[4,128,128]{2,1,0:T(8,128)S(1)} %copy.175, f32[4,8,128]{2,1,0:T(8,128)S(1)} %get-tuple-element.41), kind=kLoop, calls=%fused_computation.29 | loop fusion | flops 1568768 | bytes 311296 | tf_op jit(solution)/shard_map/reduce_sum | solution.py:72
  30.9 0.6 subtract_reduce_fusion.10
  31.5 0.7 %fusion.3 = f32[4,8,128]{2,1,0:T(8,128)S(1)} fusion(f32[4,8,128]{2,1,0:T(8,128)S(1)} %subtract_reduce_fusion.10, f32[4,128,128]{2,1,0:T(8,128)S(1)} %copy.173, f32[4,8,128]{2,1,0:T(8,128)S(1)} %get-tuple-element.42), kind=kLoop, calls=%fused_computation.27 | loop fusion | flops 1568768 | bytes 311296 | tf_op jit(solution)/shard_map/reduce_sum | solution.py:72
  32.4 1.9 %collective-permute-start.4 = (f32[4,9,128]{2,0,1:T(4,128)S(1)}, f32[4,9,128]{2,0,1:T(4,128)S(1)}, u32[]{:S(2)}, u32[]{:S(2)}) collective-permute-start(f32[4,9,128]{2,0,1:T(4,128)S(1)} %pad_maximum_fusion.6), channel_id=1, source_target_pairs={{0,4},{4,0},{8,12},{12,8},{1,5},{5,1},{9,13},{13,9},{2,6},{6,2},{1... | collective-permute-start | bytes 55304 | tf_op jit(solution)/shard_map/ppermute | solution.py:92
  35.0 0.4 collective-permute-done.5
  35.4 0.8 %collective-permute-done.4 = f32[4,9,128]{2,0,1:T(4,128)S(1)} collective-permute-done((f32[4,9,128]{2,0,1:T(4,128)S(1)}, f32[4,9,128]{2,0,1:T(4,128)S(1)}, u32[]{:S(2)}, u32[]{:S(2)}) %collective-permute-start.4) | collective-permute-done | bytes 18464 | tf_op jit(solution)/shard_map/ppermute | solution.py:92
  37.1 0.2 select_reduce_fusion.13
  37.5 0.2 select_reduce_fusion.19
  37.8 2.0 %collective-permute-start.7 = (f32[4,8,128]{2,1,0:T(8,128)S(1)}, f32[4,8,128]{2,1,0:T(8,128)S(1)}, u32[]{:S(2)}, u32[]{:S(2)}) collective-permute-start(f32[4,8,128]{2,1,0:T(8,128)S(1)} %get-tuple-element.3), channel_id=1, source_target_pairs={{4,0},{0,4},{12,8},{8,12},{5,1},{1,5},{13,9},{9,13},{6,2},{2,6},{1... | collective-permute-start | bytes 49160 | tf_op jit(solution)/shard_map/ppermute | solution.py:92
  39.7 0.6 subtract_reduce_fusion.7
  40.3 0.7 %fusion.9 = f32[4,8,128]{2,1,0:T(8,128)S(1)} fusion(f32[4,8,128]{2,1,0:T(8,128)S(1)} %subtract_reduce_fusion.7, f32[4,128,128]{2,1,0:T(8,128)S(1)} %copy.181, f32[4,8,128]{2,1,0:T(8,128)S(1)} %broadcast_multiply_fusion.3), kind=kLoop, calls=%fused_computation.33 | loop fusion | flops 1568768 | bytes 311296 | tf_op jit(solution)/shard_map/reduce_sum | solution.py:72
  41.1 1.1 %collective-permute-start.8 = (f32[4,8,128]{2,1,0:T(8,128)S(1)}, f32[4,8,128]{2,1,0:T(8,128)S(1)}, u32[]{:S(2)}, u32[]{:S(2)}) collective-permute-start(f32[4,8,128]{2,1,0:T(8,128)S(1)} %get-tuple-element.4), channel_id=1, source_target_pairs={{8,0},{12,4},{0,8},{4,12},{9,1},{13,5},{1,9},{5,13},{10,2},{14,6},... | collective-permute-start | bytes 49160 | tf_op jit(solution)/shard_map/ppermute | solution.py:92
  42.2 1.5 %collective-permute-start.9 = (f32[4,8,128]{2,1,0:T(8,128)S(1)}, f32[4,8,128]{2,1,0:T(8,128)S(1)}, u32[]{:S(2)}, u32[]{:S(2)}) collective-permute-start(f32[4,8,128]{2,1,0:T(8,128)S(1)} %get-tuple-element.5), channel_id=1, source_target_pairs={{12,0},{8,4},{4,8},{0,12},{13,1},{9,5},{5,9},{1,13},{14,2},{10,6},... | collective-permute-start | bytes 49160 | tf_op jit(solution)/shard_map/ppermute | solution.py:92
  43.7 0.6 subtract_reduce_fusion.6
  44.4 0.7 %fusion.11 = f32[4,8,128]{2,1,0:T(8,128)S(1)} fusion(f32[4,8,128]{2,1,0:T(8,128)S(1)} %subtract_reduce_fusion.6, f32[4,128,128]{2,1,0:T(8,128)S(1)} %copy.182, f32[4,8,128]{2,1,0:T(8,128)S(1)} %broadcast_multiply_fusion.2), kind=kLoop, calls=%fused_computation.35 | loop fusion | flops 1568768 | bytes 311296 | tf_op jit(solution)/shard_map/reduce_sum | solution.py:72
  45.1 0.7 %collective-permute-done.8 = f32[4,8,128]{2,1,0:T(8,128)S(1)} collective-permute-done((f32[4,8,128]{2,1,0:T(8,128)S(1)}, f32[4,8,128]{2,1,0:T(8,128)S(1)}, u32[]{:S(2)}, u32[]{:S(2)}) %collective-permute-start.8) | collective-permute-done | bytes 16416 | tf_op jit(solution)/shard_map/ppermute | solution.py:92
  45.8 0.6 subtract_reduce_fusion.5
  46.4 0.7 %fusion.13 = f32[4,8,128]{2,1,0:T(8,128)S(1)} fusion(f32[4,8,128]{2,1,0:T(8,128)S(1)} %subtract_reduce_fusion.5, f32[4,128,128]{2,1,0:T(8,128)S(1)} %copy.183, f32[4,8,128]{2,1,0:T(8,128)S(1)} %broadcast_multiply_fusion.1), kind=kLoop, calls=%fused_computation.37 | loop fusion | flops 1568768 | bytes 311296 | tf_op jit(solution)/shard_map/reduce_sum | solution.py:72
  47.2 0.5 collective-permute-done.9
  47.7 0.6 subtract_reduce_fusion.4
  48.4 1.0 %fusion.15 = f32[4,8,128]{2,1,0:T(8,128)S(1)} fusion(f32[4,8,128]{2,1,0:T(8,128)S(1)} %subtract_reduce_fusion.4, f32[4,128,128]{2,1,0:T(8,128)S(1)} %copy.184, f32[4,8,128]{2,1,0:T(8,128)S(1)} %broadcast_multiply_fusion), kind=kLoop, calls=%fused_computation.39 | loop fusion | flops 1568768 | bytes 311296 | tf_op jit(solution)/shard_map/reduce_sum | solution.py:72
  49.6 0.2 select_reduce_fusion.10
  50.4 0.6 subtract_reduce_fusion.3
  51.0 0.7 %fusion.17 = f32[4,8,128]{2,1,0:T(8,128)S(1)} fusion(f32[4,8,128]{2,1,0:T(8,128)S(1)} %subtract_reduce_fusion.3, f32[4,8,128]{2,1,0:T(8,128)S(1)} %get-tuple-element.33, f32[4,128,128]{2,1,0:T(8,128)S(1)} %copy.171), kind=kLoop, calls=%fused_computation.41 | loop fusion | flops 1568768 | bytes 311296 | tf_op jit(solution)/shard_map/reduce_sum | solution.py:72
  51.7 0.6 subtract_reduce_fusion
  52.4 0.7 %fusion.23 = f32[4,8,128]{2,1,0:T(8,128)S(1)} fusion(f32[4,8,128]{2,1,0:T(8,128)S(1)} %subtract_reduce_fusion, f32[4,8,128]{2,1,0:T(8,128)S(1)} %get-tuple-element.34, f32[4,128,128]{2,1,0:T(8,128)S(1)} %copy.177), kind=kLoop, calls=%fused_computation.47 | loop fusion | flops 1568768 | bytes 311296 | tf_op jit(solution)/shard_map/reduce_sum | solution.py:72
  53.2 0.6 subtract_reduce_fusion.1
  53.8 0.7 %fusion.21 = f32[4,8,128]{2,1,0:T(8,128)S(1)} fusion(f32[4,8,128]{2,1,0:T(8,128)S(1)} %subtract_reduce_fusion.1, f32[4,8,128]{2,1,0:T(8,128)S(1)} %get-tuple-element.35, f32[4,128,128]{2,1,0:T(8,128)S(1)} %copy.175), kind=kLoop, calls=%fused_computation.45 | loop fusion | flops 1568768 | bytes 311296 | tf_op jit(solution)/shard_map/reduce_sum | solution.py:72
  54.7 0.6 subtract_reduce_fusion.2
  55.3 0.7 %fusion.19 = f32[4,8,128]{2,1,0:T(8,128)S(1)} fusion(f32[4,8,128]{2,1,0:T(8,128)S(1)} %subtract_reduce_fusion.2, f32[4,8,128]{2,1,0:T(8,128)S(1)} %get-tuple-element.36, f32[4,128,128]{2,1,0:T(8,128)S(1)} %copy.173), kind=kLoop, calls=%fused_computation.43 | loop fusion | flops 1568768 | bytes 311296 | tf_op jit(solution)/shard_map/reduce_sum | solution.py:72
  56.1 0.2 collective-permute-start.11
  56.4 2.3 %collective-permute-start.12 = (f32[4,8,128]{2,1,0:T(8,128)S(1)}, f32[4,8,128]{2,1,0:T(8,128)S(1)}, u32[]{:S(2)}, u32[]{:S(2)}) collective-permute-start(f32[4,8,128]{2,1,0:T(8,128)S(1)} %add_select_fusion.1), channel_id=1, source_target_pairs={{0,8},{4,12},{8,0},{12,4},{1,9},{5,13},{9,1},{13,5},{2,10},{6,14},... | collective-permute-start | bytes 49160 | tf_op jit(solution)/shard_map/ppermute | solution.py:92
  58.7 1.9 %collective-permute-start.13 = (f32[4,8,128]{2,1,0:T(8,128)S(1)}, f32[4,8,128]{2,1,0:T(8,128)S(1)}, u32[]{:S(2)}, u32[]{:S(2)}) collective-permute-start(f32[4,8,128]{2,1,0:T(8,128)S(1)} %add_select_fusion), channel_id=1, source_target_pairs={{0,12},{4,8},{8,4},{12,0},{1,13},{5,9},{9,5},{13,1},{2,14},{6,10},... | collective-permute-start | bytes 49160 | tf_op jit(solution)/shard_map/ppermute | solution.py:92
  60.6 0.4 collective-permute-done.12
  61.0 3.2 %collective-permute-done.13 = f32[4,8,128]{2,1,0:T(8,128)S(1)} collective-permute-done((f32[4,8,128]{2,1,0:T(8,128)S(1)}, f32[4,8,128]{2,1,0:T(8,128)S(1)}, u32[]{:S(2)}, u32[]{:S(2)}) %collective-permute-start.13) | collective-permute-done | bytes 16416 | tf_op jit(solution)/shard_map/ppermute | solution.py:92
  64.8 0.6 copy.204
  65.5 0.5 collective-permute-done.14
  66.0 0.6 copy.203
  (126 shorter events, 7.0 us)
Async XLA Ops:
  0.6 10.4 %copy-start = (bf16[64,1024]{1,0:T(8,128)(2,1)S(1)}, bf16[64,1024]{1,0:T(8,128)(2,1)}, u32[]{:S(2)}) copy-start(bf16[64,1024]{1,0:T(8,128)(2,1)} %param.9) | copy-start | bytes 393220
  2.3 13.2 %collective-permute-start.3 = (bf16[65,8,128]{2,1,0:T(8,128)(2,1)S(1)}, bf16[65,8,128]{2,1,0:T(8,128)(2,1)S(1)}, u32[]{:S(2)}, u32[]{:S(2)}) collective-permute-start(bf16[65,8,128]{2,1,0:T(8,128)(2,1)S(1)} %pad_maximum_fusion.1), channel_id=1, source_target_pairs={{12,0},{8,4},{4,8},{0,12},{13,1},{9,5},{5,9},{1,13},{14,2},{10,6},... | collective-permute-start | bytes 399368 | tf_op jit(solution)/shard_map/ppermute | solution.py:92
  7.4 11.2 %collective-permute-start.2 = (bf16[65,8,128]{2,1,0:T(8,128)(2,1)S(1)}, bf16[65,8,128]{2,1,0:T(8,128)(2,1)S(1)}, u32[]{:S(2)}, u32[]{:S(2)}) collective-permute-start(bf16[65,8,128]{2,1,0:T(8,128)(2,1)S(1)} %pad_maximum_fusion.1), channel_id=1, source_target_pairs={{8,0},{12,4},{0,8},{4,12},{9,1},{13,5},{1,9},{5,13},{10,2},{14,6},... | collective-permute-start | bytes 399368 | tf_op jit(solution)/shard_map/ppermute | solution.py:92
  7.4 11.6 %collective-permute-start.1 = (bf16[65,8,128]{2,1,0:T(8,128)(2,1)S(1)}, bf16[65,8,128]{2,1,0:T(8,128)(2,1)S(1)}, u32[]{:S(2)}, u32[]{:S(2)}) collective-permute-start(bf16[65,8,128]{2,1,0:T(8,128)(2,1)S(1)} %pad_maximum_fusion.1), channel_id=1, source_target_pairs={{4,0},{0,4},{12,8},{8,12},{5,1},{1,5},{13,9},{9,13},{6,2},{2,6},{1... | collective-permute-start | bytes 399368 | tf_op jit(solution)/shard_map/ppermute | solution.py:92
  9.4 1.6 %collective-permute-start = (s32[3,4,2]{1,2,0:T(2,128)S(1)}, s32[3,4,2]{1,2,0:T(2,128)S(1)}, u32[]{:S(2)}, u32[]{:S(2)}) collective-permute-start(s32[3,4,2]{1,2,0:T(2,128)S(1)} %get-tuple-element.46), channel_id=1, source_target_pairs={{0,1},{1,0},{2,3},{3,2},{4,5},{5,4},{6,7},{7,6},{8,9},{9,8},{10,11... | collective-permute-start | bytes 296 | tf_op jit(solution)/shard_map/ppermute | solution.py:78
  26.5 8.4 %collective-permute-start.6 = (f32[4,9,128]{2,0,1:T(4,128)S(1)}, f32[4,9,128]{2,0,1:T(4,128)S(1)}, u32[]{:S(2)}, u32[]{:S(2)}) collective-permute-start(f32[4,9,128]{2,0,1:T(4,128)S(1)} %pad_maximum_fusion.8), channel_id=1, source_target_pairs={{0,12},{4,8},{8,4},{12,0},{1,13},{5,9},{9,5},{13,1},{2,14},{6,10},... | collective-permute-start | bytes 55304 | tf_op jit(solution)/shard_map/ppermute | solution.py:92
  30.7 4.7 %collective-permute-start.5 = (f32[4,9,128]{2,0,1:T(4,128)S(1)}, f32[4,9,128]{2,0,1:T(4,128)S(1)}, u32[]{:S(2)}, u32[]{:S(2)}) collective-permute-start(f32[4,9,128]{2,0,1:T(4,128)S(1)} %pad_maximum_fusion.7), channel_id=1, source_target_pairs={{0,8},{4,12},{8,0},{12,4},{1,9},{5,13},{9,1},{13,5},{2,10},{6,14},... | collective-permute-start | bytes 55304 | tf_op jit(solution)/shard_map/ppermute | solution.py:92
  32.4 3.8 %collective-permute-start.4 = (f32[4,9,128]{2,0,1:T(4,128)S(1)}, f32[4,9,128]{2,0,1:T(4,128)S(1)}, u32[]{:S(2)}, u32[]{:S(2)}) collective-permute-start(f32[4,9,128]{2,0,1:T(4,128)S(1)} %pad_maximum_fusion.6), channel_id=1, source_target_pairs={{0,4},{4,0},{8,12},{12,8},{1,5},{5,1},{9,13},{13,9},{2,6},{6,2},{1... | collective-permute-start | bytes 55304 | tf_op jit(solution)/shard_map/ppermute | solution.py:92
  37.8 6.0 %collective-permute-start.7 = (f32[4,8,128]{2,1,0:T(8,128)S(1)}, f32[4,8,128]{2,1,0:T(8,128)S(1)}, u32[]{:S(2)}, u32[]{:S(2)}) collective-permute-start(f32[4,8,128]{2,1,0:T(8,128)S(1)} %get-tuple-element.3), channel_id=1, source_target_pairs={{4,0},{0,4},{12,8},{8,12},{5,1},{1,5},{13,9},{9,13},{6,2},{2,6},{1... | collective-permute-start | bytes 49160 | tf_op jit(solution)/shard_map/ppermute | solution.py:92
  41.1 4.7 %collective-permute-start.8 = (f32[4,8,128]{2,1,0:T(8,128)S(1)}, f32[4,8,128]{2,1,0:T(8,128)S(1)}, u32[]{:S(2)}, u32[]{:S(2)}) collective-permute-start(f32[4,8,128]{2,1,0:T(8,128)S(1)} %get-tuple-element.4), channel_id=1, source_target_pairs={{8,0},{12,4},{0,8},{4,12},{9,1},{13,5},{1,9},{5,13},{10,2},{14,6},... | collective-permute-start | bytes 49160 | tf_op jit(solution)/shard_map/ppermute | solution.py:92
  42.2 5.5 %collective-permute-start.9 = (f32[4,8,128]{2,1,0:T(8,128)S(1)}, f32[4,8,128]{2,1,0:T(8,128)S(1)}, u32[]{:S(2)}, u32[]{:S(2)}) collective-permute-start(f32[4,8,128]{2,1,0:T(8,128)S(1)} %get-tuple-element.5), channel_id=1, source_target_pairs={{12,0},{8,4},{4,8},{0,12},{13,1},{9,5},{5,9},{1,13},{14,2},{10,6},... | collective-permute-start | bytes 49160 | tf_op jit(solution)/shard_map/ppermute | solution.py:92
  50.0 14.8 %collective-permute-start.10 = (f32[8,8,128]{2,1,0:T(8,128)S(1)}, f32[8,8,128]{2,1,0:T(8,128)S(1)}, u32[]{:S(2)}, u32[]{:S(2)}) collective-permute-start(f32[8,8,128]{2,1,0:T(8,128)S(1)} %bitcast_subtract_fusion.2), channel_id=1, source_target_pairs={{0,1},{1,0},{2,3},{3,2},{4,5},{5,4},{6,7},{7,6},{8,9},{9,8},{10,11... | collective-permute-start | bytes 98312 | tf_op jit(solution)/shard_map/ppermute | solution.py:78
  56.1 4.5 %collective-permute-start.11 = (f32[4,8,128]{2,1,0:T(8,128)S(1)}, f32[4,8,128]{2,1,0:T(8,128)S(1)}, u32[]{:S(2)}, u32[]{:S(2)}) collective-permute-start(f32[4,8,128]{2,1,0:T(8,128)S(1)} %add_select_fusion.2), channel_id=1, source_target_pairs={{0,4},{4,0},{8,12},{12,8},{1,5},{5,1},{9,13},{13,9},{2,6},{6,2},{1... | collective-permute-start | bytes 49160 | tf_op jit(solution)/shard_map/ppermute | solution.py:92
  56.4 4.7 %collective-permute-start.12 = (f32[4,8,128]{2,1,0:T(8,128)S(1)}, f32[4,8,128]{2,1,0:T(8,128)S(1)}, u32[]{:S(2)}, u32[]{:S(2)}) collective-permute-start(f32[4,8,128]{2,1,0:T(8,128)S(1)} %add_select_fusion.1), channel_id=1, source_target_pairs={{0,8},{4,12},{8,0},{12,4},{1,9},{5,13},{9,1},{13,5},{2,10},{6,14},... | collective-permute-start | bytes 49160 | tf_op jit(solution)/shard_map/ppermute | solution.py:92
  58.7 5.5 %collective-permute-start.13 = (f32[4,8,128]{2,1,0:T(8,128)S(1)}, f32[4,8,128]{2,1,0:T(8,128)S(1)}, u32[]{:S(2)}, u32[]{:S(2)}) collective-permute-start(f32[4,8,128]{2,1,0:T(8,128)S(1)} %add_select_fusion), channel_id=1, source_target_pairs={{0,12},{4,8},{8,4},{12,0},{1,13},{5,9},{9,5},{13,1},{2,14},{6,10},... | collective-permute-start | bytes 49160 | tf_op jit(solution)/shard_map/ppermute | solution.py:92
  64.7 1.3 %collective-permute-start.14 = (f32[8,8,128]{2,1,0:T(8,128)S(1)}, f32[8,8,128]{2,1,0:T(8,128)S(1)}, u32[]{:S(2)}, u32[]{:S(2)}) collective-permute-start(f32[8,8,128]{2,1,0:T(8,128)S(1)} %bitcast_subtract_fusion), channel_id=1, source_target_pairs={{0,1},{1,0},{2,3},{3,2},{4,5},{5,4},{6,7},{7,6},{8,9},{9,8},{10,11... | collective-permute-start | bytes 98312 | tf_op jit(solution)/shard_map/ppermute | solution.py:78

commit v18 on v11

--- a/solution.py
+++ b/solution.py
@@ -192,15 +192,19 @@
                 highest, mass_sum = lse_parts(scores, 2)
                 lse = jnp.where(usable[piece], highest + jnp.log(mass_sum), SENTINEL)
                 if sweep_index == 0:
-                    block_ids = jnp.broadcast_to(
-                        wanted[offset].reshape(wide, 1, 1).astype(jnp.float32), (wide, 1, BLOCK)
+                    block_ids = jnp.concatenate(
+                        [wanted[offset].astype(jnp.float32)[None, :], jnp.zeros((1, BLOCK - wide), jnp.float32)],
+                        axis=1,
                     )
-                    lse = jnp.concatenate([lse, block_ids], axis=1)
+                    lse = jnp.concatenate([lse.reshape(wide * half, BLOCK), block_ids], axis=0)
                 chunks[offset] = lse
-            back = jnp.concatenate(send_up(chunks), axis=0)
+            moved = send_up(chunks)
             if sweep_index == 0:
-                requested = back[:, half, 0].astype(jnp.int32)
-                back = back[:, :half]
+                requested = jnp.concatenate(
+                    [chunk[wide * half, :wide].astype(jnp.int32) for chunk in moved], axis=0
+                )
+                moved = [chunk[: wide * half].reshape(wide, half, BLOCK) for chunk in moved]
+            back = jnp.concatenate(moved, axis=0)
             block_top, summed = fold_lse(back, requested, blocks)
             synth_pot = finish(log_synth, block_top, summed)
 

time: 61.2 us -> 60.3 us (0.985)
  waiting for transfers between devices: 3.96 us -> 2.5 us
    ppermute x12, waiting for transfers between devices: 3.45 us -> 1.99 us  [exchange(): moved.append(lax.ppermute(chunks[offset], 'blk', perm))]
    reduce_max x11 -> x12, other arithmetic: 7.55 us -> 7.52 us  [lse_parts(): highest = jnp.max(scores, axis=axis)]
    unnamed x8 -> x7, local copies, waits for them, and re-layouts: 2.26 us -> 2.24 us
  transfers between devices with their start and end apart: 15 -> 15, of which waited for: 4 -> 4; matrix products, arithmetic and copies ran while one was open for 40% -> 42% of each run, Pallas kernels for 0% -> 0%
where the time goes in v18:
time: 60.3 us; the launch traced here: 59.9 us
  other arithmetic  28.8 us (48%)
  starting transfers between devices  19.4 us (32%)
  local copies, waits for them, and re-layouts  5.31 us (9%)
  matrix products  2.53 us (4%)
  waiting for transfers between devices  2.5 us (4%)
  between operations  1.38 us (2%)
    ppermute x12, starting transfers between devices, exchange(): moved.append(lax.ppermute(chunks[offset], 'blk', perm))  19.2 us
    reduce_sum x14, other arithmetic, lse_parts(): jnp.sum(jnp.exp(scores - jnp.expand_dims(highest, axis)), axis=axis)  9.51 us
    reduce_max x12, other arithmetic, lse_parts(): highest = jnp.max(scores, axis=axis)  7.52 us
    reduce_sum x13, other arithmetic, pick_rows(): return jnp.sum(chosen, axis=2, dtype=values.dtype)  4.57 us
    dot_general x2, matrix products, slot_costs(): jnp.einsum('gdi,gdj->gij', slot_real, slot_synth, preferred_element_type=...  2.53 us
    unnamed x7, local copies, waits for them, and re-layouts  2.24 us
    ppermute x12, waiting for transfers between devices, exchange(): moved.append(lax.ppermute(chunks[offset], 'blk', perm))  1.99 us
    unnamed x2, other arithmetic  1.55 us
  transfers between devices with their start and end apart: 15, of which 4 were waited for; matrix products, arithmetic and copies ran while one was open for 42% of the time, Pallas kernels for 0%

profile of v18, /device:TPU:0, one launch (start us, length us, event | category | flops | bytes accessed | tf_op | source)
XLA Modules:
  0.0 59.9 jit_solution(3383441867355578609)
XLA Ops:
  0.6 0.7 %convert_bitcast_fusion.3 = (bf16[1,1,8,128]{3,2,1,0:T(8,128)(2,1)S(1)}, bf16[1,8,128]{2,1,0:T(8,128)(2,1)S(1)}) fusion(s32[1024]{0:T(1024)} %param.12), kind=kLoop, calls=%fused_computation.191 | loop fusion | flops 1024 | bytes 8192 | tf_op jit(solution)/shard_map/concatenate | solution.py:123
  1.4 0.9 %copy.32 = bf16[8,8,8,128]{3,2,1,0:T(8,128)(2,1)S(1)} copy(bf16[8,8,8,128]{3,1,2,0:T(8,128)(2,1)} %bitcast.85) | data formatting | bytes 262144
  2.3 5.1 %collective-permute-start.3 = (bf16[65,8,128]{2,1,0:T(8,128)(2,1)S(1)}, bf16[65,8,128]{2,1,0:T(8,128)(2,1)S(1)}, u32[]{:S(2)}, u32[]{:S(2)}) collective-permute-start(bf16[65,8,128]{2,1,0:T(8,128)(2,1)S(1)} %pad_maximum_fusion.1), channel_id=1, source_target_pairs={{12,0},{8,4},{4,8},{0,12},{13,1},{9,5},{5,9},{1,13},{14,2},{10,6},... | collective-permute-start | bytes 399368 | tf_op jit(solution)/shard_map/ppermute | solution.py:92
  7.4 0.6 %collective-permute-start.1 = (bf16[65,8,128]{2,1,0:T(8,128)(2,1)S(1)}, bf16[65,8,128]{2,1,0:T(8,128)(2,1)S(1)}, u32[]{:S(2)}, u32[]{:S(2)}) collective-permute-start(bf16[65,8,128]{2,1,0:T(8,128)(2,1)S(1)} %pad_maximum_fusion.1), channel_id=1, source_target_pairs={{4,0},{0,4},{12,8},{8,12},{5,1},{1,5},{13,9},{9,13},{6,2},{2,6},{1... | collective-permute-start | bytes 399368 | tf_op jit(solution)/shard_map/ppermute | solution.py:92
  8.1 0.7 %stack_broadcast_in_dim.2 = s32[1,4,2]{1,2,0:T(2,128)S(1)} broadcast(s32[4]{0:T(128)} %param.17), dimensions={1} | broadcast | bytes 48 | tf_op jit(solution)/shard_map/stack;broadcast_in_dim | solution.py:139
  8.7 0.7 %fusion.41 = (s32[3,1,4,2]{2,3,0,1:T(2,128)S(1)}, s32[3,4,2]{1,2,0:T(2,128)S(1)}) fusion(s32[1,4,2]{1,2,0:T(2,128)S(1)} %stack_broadcast_in_dim.2, s32[1,4,2]{1,2,0:T(2,128)} %bitcast.93, s32[1,4,2]{1,2,0:T(2,128)} %bitcast.94), kind=kLoop, calls=%fused_computation.202 | loop fusion | flops 48 | bytes 288 | tf_op jit(solution)/shard_map/stack | solution.py:140
  9.5 0.7 %convert_bitcast_fusion.1 = bf16[8,128]{1,0:T(8,128)(2,1)S(1)} fusion(s32[1024]{0:T(1024)} %param.11), kind=kLoop, calls=%fused_computation.180 | loop fusion | flops 1024 | bytes 6144 | tf_op jit(solution)/shard_map/convert_element_type | solution.py:122
  10.2 0.8 %multiply_bitcast_fusion.1 = f32[1,8,8,128]{3,1,2,0:T(8,128)S(1)} fusion(s32[16,1024]{1,0:T(8,128)} %param.13, s32[]{:T(128)S(6)} %select_n.271), kind=kLoop, calls=%fused_computation.109 | loop fusion | flops 24576 | bytes 65540
  11.0 0.8 %multiply_bitcast_fusion = f32[1,8,8,128]{3,1,2,0:T(8,128)S(1)} fusion(s32[16,1024]{1,0:T(8,128)} %param.14, s32[]{:T(128)S(6)} %select_n.271), kind=kLoop, calls=%fused_computation.108 | loop fusion | flops 24576 | bytes 65540
  11.9 0.3 select_reduce_fusion.25
  12.2 0.3 slice_reduce_fusion.4
  12.4 0.2 convert_reduce_fusion.2
  12.6 0.1 copy.28
  12.7 0.3 slice_reduce_fusion
  13.4 1.5 %select_reduce_fusion = bf16[16,64,128]{2,1,0:T(8,128)(2,1)S(1)} fusion(pred[16,8]{1,0:T(8,128)(4,1)S(1)} %iota_compare_fusion.2, bf16[64,8,128]{2,1,0:T(8,128)(2,1)S(1)} %bitcast.82), kind=kLoop, calls=%fused_computation.48 | loop fusion | flops 1966080 | bytes 393344 | tf_op jit(solution)/shard_map/reduce_sum | solution.py:26
  16.8 0.4 select_reduce_fusion.4
  17.2 0.4 select_reduce_fusion.1
  17.6 1.1 %collective-permute-done.2 = bf16[65,8,128]{2,1,0:T(8,128)(2,1)S(1)} collective-permute-done((bf16[65,8,128]{2,1,0:T(8,128)(2,1)S(1)}, bf16[65,8,128]{2,1,0:T(8,128)(2,1)S(1)}, u32[]{:S(2)}, u32[]{:S(2)}) %collective-permute-start.2) | collective-permute-done | bytes 133152 | tf_op jit(solution)/shard_map/ppermute | solution.py:92
  18.7 0.4 select_reduce_fusion.2
  19.1 0.4 select_reduce_fusion.3
  19.6 1.4 %fusion.26 = f32[16,128,128]{2,1,0:T(8,128)S(1)} fusion(bf16[16,64,128]{2,1,0:T(8,128)(2,1)S(1)} %select_reduce_fusion, f32[16,128]{1,0:T(8,128)S(1)} %broadcast_multiply_fusion.4, f32[16,128]{1,0:T(8,128)S(1)} %broadcast_multiply_fusion.5, bf16[16,128]{1,0:T(8,128)(2,1)S(1)} %select_reduce_fusion.23, bf16[16,128]{1,0:T(8,128)(2,1)S(1)} %bitcast.91, ...), kind=kOutput, calls=%fused_computation.53 | convolution fusion | flops 35127296 | bytes 1597440 | tf_op jit(solution)/shard_map/gdi,gdj->gij/dot_general | solution.py:61
  21.0 1.1 %fusion.27 = f32[16,128,128]{2,1,0:T(8,128)S(1)} fusion(bf16[16,64,128]{2,1,0:T(8,128)(2,1)S(1)} %select_reduce_fusion, f32[16,128]{1,0:T(8,128)S(1)} %broadcast_multiply_fusion.5, f32[16,128]{1,0:T(8,128)S(1)} %broadcast_multiply_fusion.4, bf16[16,128]{1,0:T(8,128)(2,1)S(1)} %bitcast.92, bf16[16,128]{1,0:T(8,128)(2,1)S(1)} %select_reduce_fusion.23, ...), kind=kOutput, calls=%fused_computation.54 | convolution fusion | flops 35127296 | bytes 1597440 | tf_op jit(solution)/shard_map/gdi,gdj->gij/dot_general | solution.py:61
  22.4 0.2 exponential_reduce_fusion.2
  23.1 0.2 select_reduce_fusion.15
  23.4 1.3 %subtract_reduce_fusion.9 = (f32[4,8,128]{2,1,0:T(8,128)S(1)}, f32[4,8,128]{2,1,0:T(8,128)S(1)}) fusion(f32[4,128,128]{2,1,0:T(8,128)S(1)} %get-tuple-element.33, f32[4,8,128]{2,1,0:T(8,128)S(1)} %get-tuple-element.46, f32[4,128,128]{2,1,0:T(8,128)S(1)} %get-tuple-element.34, f32[4,8,128]{2,1,0:T(8,128)S(1)} %get-tuple-element.47), kind=kLoop, calls=%fused_computation.19 | loop fusion | flops 2088960 | bytes 589824 | tf_op jit(solution)/shard_map/reduce_max | solution.py:71
  24.7 0.7 %fusion.5 = f32[4,8,128]{2,1,0:T(8,128)S(1)} fusion(f32[4,8,128]{2,1,0:T(8,128)S(1)} %get-tuple-element.53, f32[4,128,128]{2,1,0:T(8,128)S(1)} %get-tuple-element.33, f32[4,8,128]{2,1,0:T(8,128)S(1)} %get-tuple-element.46), kind=kLoop, calls=%fused_computation.29 | loop fusion | flops 1568768 | bytes 311296 | tf_op jit(solution)/shard_map/reduce_sum | solution.py:72
  25.5 2.7 %collective-permute-start.6 = (f32[33,128]{1,0:T(8,128)S(1)}, f32[33,128]{1,0:T(8,128)S(1)}, u32[]{:S(2)}, u32[]{:S(2)}) collective-permute-start(f32[33,128]{1,0:T(8,128)S(1)} %select_maximum_fusion), channel_id=1, source_target_pairs={{0,12},{4,8},{8,4},{12,0},{1,13},{5,9},{9,5},{13,1},{2,14},{6,10},... | collective-permute-start | bytes 50696 | tf_op jit(solution)/shard_map/ppermute | solution.py:92
  28.2 0.7 %fusion.3 = f32[4,8,128]{2,1,0:T(8,128)S(1)} fusion(f32[4,8,128]{2,1,0:T(8,128)S(1)} %get-tuple-element.54, f32[4,128,128]{2,1,0:T(8,128)S(1)} %get-tuple-element.34, f32[4,8,128]{2,1,0:T(8,128)S(1)} %get-tuple-element.47), kind=kLoop, calls=%fused_computation.27 | loop fusion | flops 1568768 | bytes 311296 | tf_op jit(solution)/shard_map/reduce_sum | solution.py:72
  29.1 0.6 %subtract_reduce_fusion.11 = f32[4,8,128]{2,1,0:T(8,128)S(1)} fusion(f32[4,128,128]{2,1,0:T(8,128)S(1)} %get-tuple-element.35, f32[4,8,128]{2,1,0:T(8,128)S(1)} %get-tuple-element.48), kind=kLoop, calls=%fused_computation.23 | loop fusion | flops 1044480 | bytes 294912 | tf_op jit(solution)/shard_map/reduce_max | solution.py:71
  29.8 0.7 %fusion.1 = f32[4,8,128]{2,1,0:T(8,128)S(1)} fusion(f32[4,8,128]{2,1,0:T(8,128)S(1)} %subtract_reduce_fusion.11, f32[4,128,128]{2,1,0:T(8,128)S(1)} %get-tuple-element.35, f32[4,8,128]{2,1,0:T(8,128)S(1)} %get-tuple-element.48), kind=kLoop, calls=%fused_computation.25 | loop fusion | flops 1568768 | bytes 311296 | tf_op jit(solution)/shard_map/reduce_sum | solution.py:72
  30.6 1.8 %collective-permute-start.4 = (f32[33,128]{1,0:T(8,128)S(1)}, f32[33,128]{1,0:T(8,128)S(1)}, u32[]{:S(2)}, u32[]{:S(2)}) collective-permute-start(f32[33,128]{1,0:T(8,128)S(1)} %select_maximum_fusion.2), channel_id=1, source_target_pairs={{0,4},{4,0},{8,12},{12,8},{1,5},{5,1},{9,13},{13,9},{2,6},{6,2},{1... | collective-permute-start | bytes 50696 | tf_op jit(solution)/shard_map/ppermute | solution.py:92
  32.4 0.6 %subtract_reduce_fusion.8 = f32[4,8,128]{2,1,0:T(8,128)S(1)} fusion(f32[4,128,128]{2,1,0:T(8,128)S(1)} %get-tuple-element.32, f32[4,8,128]{2,1,0:T(8,128)S(1)} %get-tuple-element.45), kind=kLoop, calls=%fused_computation.17 | loop fusion | flops 1044480 | bytes 294912 | tf_op jit(solution)/shard_map/reduce_max | solution.py:71
  33.0 0.7 %fusion.7 = f32[4,8,128]{2,1,0:T(8,128)S(1)} fusion(f32[4,8,128]{2,1,0:T(8,128)S(1)} %subtract_reduce_fusion.8, f32[4,128,128]{2,1,0:T(8,128)S(1)} %get-tuple-element.32, f32[4,8,128]{2,1,0:T(8,128)S(1)} %get-tuple-element.45), kind=kLoop, calls=%fused_computation.31 | loop fusion | flops 1568768 | bytes 311296 | tf_op jit(solution)/shard_map/reduce_sum | solution.py:72
  33.8 0.6 %collective-permute-done.4 = f32[33,128]{1,0:T(8,128)S(1)} collective-permute-done((f32[33,128]{1,0:T(8,128)S(1)}, f32[33,128]{1,0:T(8,128)S(1)}, u32[]{:S(2)}, u32[]{:S(2)}) %collective-permute-start.4) | collective-permute-done | bytes 16928 | tf_op jit(solution)/shard_map/ppermute | solution.py:92
  35.0 0.2 select_reduce_fusion.13
  35.4 0.2 select_reduce_fusion.19
  35.6 2.4 %collective-permute-start.9 = (f32[4,8,128]{2,1,0:T(8,128)S(1)}, f32[4,8,128]{2,1,0:T(8,128)S(1)}, u32[]{:S(2)}, u32[]{:S(2)}) collective-permute-start(f32[4,8,128]{2,1,0:T(8,128)S(1)} %get-tuple-element.12), channel_id=1, source_target_pairs={{12,0},{8,4},{4,8},{0,12},{13,1},{9,5},{5,9},{1,13},{14,2},{10,6},... | collective-permute-start | bytes 49160 | tf_op jit(solution)/shard_map/ppermute | solution.py:92
  38.1 0.8 %collective-permute-start.8 = (f32[4,8,128]{2,1,0:T(8,128)S(1)}, f32[4,8,128]{2,1,0:T(8,128)S(1)}, u32[]{:S(2)}, u32[]{:S(2)}) collective-permute-start(f32[4,8,128]{2,1,0:T(8,128)S(1)} %get-tuple-element.11), channel_id=1, source_target_pairs={{8,0},{12,4},{0,8},{4,12},{9,1},{13,5},{1,9},{5,13},{10,2},{14,6},... | collective-permute-start | bytes 49160 | tf_op jit(solution)/shard_map/ppermute | solution.py:92
  38.9 1.2 %collective-permute-start.7 = (f32[4,8,128]{2,1,0:T(8,128)S(1)}, f32[4,8,128]{2,1,0:T(8,128)S(1)}, u32[]{:S(2)}, u32[]{:S(2)}) collective-permute-start(f32[4,8,128]{2,1,0:T(8,128)S(1)} %get-tuple-element.10), channel_id=1, source_target_pairs={{4,0},{0,4},{12,8},{8,12},{5,1},{1,5},{13,9},{9,13},{6,2},{2,6},{1... | collective-permute-start | bytes 49160 | tf_op jit(solution)/shard_map/ppermute | solution.py:92
  40.1 0.6 %subtract_reduce_fusion.7 = f32[4,8,128]{2,1,0:T(8,128)S(1)} fusion(f32[4,128,128]{2,1,0:T(8,128)S(1)} %get-tuple-element.29, f32[4,8,128]{2,1,0:T(8,128)S(1)} %broadcast_multiply_fusion.3), kind=kLoop, calls=%fused_computation.15 | loop fusion | flops 1044480 | bytes 294912 | tf_op jit(solution)/shard_map/reduce_max | solution.py:71
  40.7 0.7 %fusion.9 = f32[4,8,128]{2,1,0:T(8,128)S(1)} fusion(f32[4,8,128]{2,1,0:T(8,128)S(1)} %subtract_reduce_fusion.7, f32[4,128,128]{2,1,0:T(8,128)S(1)} %get-tuple-element.29, f32[4,8,128]{2,1,0:T(8,128)S(1)} %broadcast_multiply_fusion.3), kind=kLoop, calls=%fused_computation.33 | loop fusion | flops 1568768 | bytes 311296 | tf_op jit(solution)/shard_map/reduce_sum | solution.py:72
  41.5 0.6 %subtract_reduce_fusion.4 = f32[4,8,128]{2,1,0:T(8,128)S(1)} fusion(f32[4,128,128]{2,1,0:T(8,128)S(1)} %get-tuple-element.36, f32[4,8,128]{2,1,0:T(8,128)S(1)} %broadcast_multiply_fusion), kind=kLoop, calls=%fused_computation.9 | loop fusion | flops 1044480 | bytes 294912 | tf_op jit(solution)/shard_map/reduce_max | solution.py:71
  42.1 0.7 %fusion.15 = f32[4,8,128]{2,1,0:T(8,128)S(1)} fusion(f32[4,8,128]{2,1,0:T(8,128)S(1)} %subtract_reduce_fusion.4, f32[4,128,128]{2,1,0:T(8,128)S(1)} %get-tuple-element.36, f32[4,8,128]{2,1,0:T(8,128)S(1)} %broadcast_multiply_fusion), kind=kLoop, calls=%fused_computation.39 | loop fusion | flops 1568768 | bytes 311296 | tf_op jit(solution)/shard_map/reduce_sum | solution.py:72
  42.9 0.6 %subtract_reduce_fusion.5 = f32[4,8,128]{2,1,0:T(8,128)S(1)} fusion(f32[4,128,128]{2,1,0:T(8,128)S(1)} %get-tuple-element.31, f32[4,8,128]{2,1,0:T(8,128)S(1)} %broadcast_multiply_fusion.1), kind=kLoop, calls=%fused_computation.11 | loop fusion | flops 1044480 | bytes 294912 | tf_op jit(solution)/shard_map/reduce_max | solution.py:71
  43.5 0.7 %fusion.13 = f32[4,8,128]{2,1,0:T(8,128)S(1)} fusion(f32[4,8,128]{2,1,0:T(8,128)S(1)} %subtract_reduce_fusion.5, f32[4,128,128]{2,1,0:T(8,128)S(1)} %get-tuple-element.31, f32[4,8,128]{2,1,0:T(8,128)S(1)} %broadcast_multiply_fusion.1), kind=kLoop, calls=%fused_computation.37 | loop fusion | flops 1568768 | bytes 311296 | tf_op jit(solution)/shard_map/reduce_sum | solution.py:72
  44.3 0.6 %subtract_reduce_fusion.6 = f32[4,8,128]{2,1,0:T(8,128)S(1)} fusion(f32[4,128,128]{2,1,0:T(8,128)S(1)} %get-tuple-element.30, f32[4,8,128]{2,1,0:T(8,128)S(1)} %broadcast_multiply_fusion.2), kind=kLoop, calls=%fused_computation.13 | loop fusion | flops 1044480 | bytes 294912 | tf_op jit(solution)/shard_map/reduce_max | solution.py:71
  45.0 0.7 %fusion.11 = f32[4,8,128]{2,1,0:T(8,128)S(1)} fusion(f32[4,8,128]{2,1,0:T(8,128)S(1)} %subtract_reduce_fusion.6, f32[4,128,128]{2,1,0:T(8,128)S(1)} %get-tuple-element.30, f32[4,8,128]{2,1,0:T(8,128)S(1)} %broadcast_multiply_fusion.2), kind=kLoop, calls=%fused_computation.35 | loop fusion | flops 1568768 | bytes 311296 | tf_op jit(solution)/shard_map/reduce_sum | solution.py:72
  45.9 0.2 select_reduce_fusion.10
  46.5 0.2 select_reduce_fusion.8
  46.7 0.6 %subtract_reduce_fusion = f32[4,8,128]{2,1,0:T(8,128)S(1)} fusion(f32[4,8,128]{2,1,0:T(8,128)S(1)} %get-tuple-element.40, f32[4,128,128]{2,1,0:T(8,128)S(1)} %get-tuple-element.33), kind=kLoop, calls=%fused_computation.1 | loop fusion | flops 1044480 | bytes 294912 | tf_op jit(solution)/shard_map/reduce_max | solution.py:71
  47.3 0.7 %fusion.23 = f32[4,8,128]{2,1,0:T(8,128)S(1)} fusion(f32[4,8,128]{2,1,0:T(8,128)S(1)} %subtract_reduce_fusion, f32[4,8,128]{2,1,0:T(8,128)S(1)} %get-tuple-element.40, f32[4,128,128]{2,1,0:T(8,128)S(1)} %get-tuple-element.33), kind=kLoop, calls=%fused_computation.47 | loop fusion | flops 1568768 | bytes 311296 | tf_op jit(solution)/shard_map/reduce_sum | solution.py:72
  48.2 2.4 %collective-permute-start.13 = (f32[4,8,128]{2,1,0:T(8,128)S(1)}, f32[4,8,128]{2,1,0:T(8,128)S(1)}, u32[]{:S(2)}, u32[]{:S(2)}) collective-permute-start(f32[4,8,128]{2,1,0:T(8,128)S(1)} %add_select_fusion), channel_id=1, source_target_pairs={{0,12},{4,8},{8,4},{12,0},{1,13},{5,9},{9,5},{13,1},{2,14},{6,10},... | collective-permute-start | bytes 49160 | tf_op jit(solution)/shard_map/ppermute | solution.py:92
  50.5 0.6 %subtract_reduce_fusion.1 = f32[4,8,128]{2,1,0:T(8,128)S(1)} fusion(f32[4,8,128]{2,1,0:T(8,128)S(1)} %get-tuple-element.41, f32[4,128,128]{2,1,0:T(8,128)S(1)} %get-tuple-element.34), kind=kLoop, calls=%fused_computation.3 | loop fusion | flops 1044480 | bytes 294912 | tf_op jit(solution)/shard_map/reduce_max | solution.py:71
  51.2 1.0 %fusion.21 = f32[4,8,128]{2,1,0:T(8,128)S(1)} fusion(f32[4,8,128]{2,1,0:T(8,128)S(1)} %subtract_reduce_fusion.1, f32[4,8,128]{2,1,0:T(8,128)S(1)} %get-tuple-element.41, f32[4,128,128]{2,1,0:T(8,128)S(1)} %get-tuple-element.34), kind=kLoop, calls=%fused_computation.45 | loop fusion | flops 1568768 | bytes 311296 | tf_op jit(solution)/shard_map/reduce_sum | solution.py:72
  52.2 0.6 %subtract_reduce_fusion.2 = f32[4,8,128]{2,1,0:T(8,128)S(1)} fusion(f32[4,8,128]{2,1,0:T(8,128)S(1)} %get-tuple-element.42, f32[4,128,128]{2,1,0:T(8,128)S(1)} %get-tuple-element.35), kind=kLoop, calls=%fused_computation.5 | loop fusion | flops 1044480 | bytes 294912 | tf_op jit(solution)/shard_map/reduce_max | solution.py:71
  52.9 0.7 %fusion.19 = f32[4,8,128]{2,1,0:T(8,128)S(1)} fusion(f32[4,8,128]{2,1,0:T(8,128)S(1)} %subtract_reduce_fusion.2, f32[4,8,128]{2,1,0:T(8,128)S(1)} %get-tuple-element.42, f32[4,128,128]{2,1,0:T(8,128)S(1)} %get-tuple-element.35), kind=kLoop, calls=%fused_computation.43 | loop fusion | flops 1568768 | bytes 311296 | tf_op jit(solution)/shard_map/reduce_sum | solution.py:72
  53.7 2.0 %collective-permute-start.11 = (f32[4,8,128]{2,1,0:T(8,128)S(1)}, f32[4,8,128]{2,1,0:T(8,128)S(1)}, u32[]{:S(2)}, u32[]{:S(2)}) collective-permute-start(f32[4,8,128]{2,1,0:T(8,128)S(1)} %add_select_fusion.2), channel_id=1, source_target_pairs={{0,4},{4,0},{8,12},{12,8},{1,5},{5,1},{9,13},{13,9},{2,6},{6,2},{1... | collective-permute-start | bytes 49160 | tf_op jit(solution)/shard_map/ppermute | solution.py:92
  55.7 0.6 %subtract_reduce_fusion.3 = f32[4,8,128]{2,1,0:T(8,128)S(1)} fusion(f32[4,8,128]{2,1,0:T(8,128)S(1)} %get-tuple-element.39, f32[4,128,128]{2,1,0:T(8,128)S(1)} %get-tuple-element.32), kind=kLoop, calls=%fused_computation.7 | loop fusion | flops 1044480 | bytes 294912 | tf_op jit(solution)/shard_map/reduce_max | solution.py:71
  56.4 0.7 %fusion.17 = f32[4,8,128]{2,1,0:T(8,128)S(1)} fusion(f32[4,8,128]{2,1,0:T(8,128)S(1)} %subtract_reduce_fusion.3, f32[4,8,128]{2,1,0:T(8,128)S(1)} %get-tuple-element.39, f32[4,128,128]{2,1,0:T(8,128)S(1)} %get-tuple-element.32), kind=kLoop, calls=%fused_computation.41 | loop fusion | flops 1568768 | bytes 311296 | tf_op jit(solution)/shard_map/reduce_sum | solution.py:72
  57.2 0.3 collective-permute-done.11
  57.6 0.2 select_reduce_fusion.6
  58.1 0.6 %copy.45 = f32[2,8,8,128]{3,1,2,0:T(8,128)} copy(f32[2,8,8,128]{3,2,1,0:T(8,128)S(1)} %bitcast.83) | data formatting | bytes 131072
  58.7 0.5 collective-permute-done.14
  59.3 0.6 %copy.44 = f32[2,8,8,128]{3,1,2,0:T(8,128)} copy(f32[2,8,8,128]{3,2,1,0:T(8,128)S(1)} %bitcast.84) | data formatting | bytes 131072
  (120 shorter events, 5.6 us)
Async XLA Ops:
  0.6 11.1 %copy-start = (bf16[64,1024]{1,0:T(8,128)(2,1)S(1)}, bf16[64,1024]{1,0:T(8,128)(2,1)}, u32[]{:S(2)}) copy-start(bf16[64,1024]{1,0:T(8,128)(2,1)} %param.9) | copy-start | bytes 393220
  2.3 14.9 %collective-permute-start.3 = (bf16[65,8,128]{2,1,0:T(8,128)(2,1)S(1)}, bf16[65,8,128]{2,1,0:T(8,128)(2,1)S(1)}, u32[]{:S(2)}, u32[]{:S(2)}) collective-permute-start(bf16[65,8,128]{2,1,0:T(8,128)(2,1)S(1)} %pad_maximum_fusion.1), channel_id=1, source_target_pairs={{12,0},{8,4},{4,8},{0,12},{13,1},{9,5},{5,9},{1,13},{14,2},{10,6},... | collective-permute-start | bytes 399368 | tf_op jit(solution)/shard_map/ppermute | solution.py:92
  7.4 11.2 %collective-permute-start.2 = (bf16[65,8,128]{2,1,0:T(8,128)(2,1)S(1)}, bf16[65,8,128]{2,1,0:T(8,128)(2,1)S(1)}, u32[]{:S(2)}, u32[]{:S(2)}) collective-permute-start(bf16[65,8,128]{2,1,0:T(8,128)(2,1)S(1)} %pad_maximum_fusion.1), channel_id=1, source_target_pairs={{8,0},{12,4},{0,8},{4,12},{9,1},{13,5},{1,9},{5,13},{10,2},{14,6},... | collective-permute-start | bytes 399368 | tf_op jit(solution)/shard_map/ppermute | solution.py:92
  7.4 11.6 %collective-permute-start.1 = (bf16[65,8,128]{2,1,0:T(8,128)(2,1)S(1)}, bf16[65,8,128]{2,1,0:T(8,128)(2,1)S(1)}, u32[]{:S(2)}, u32[]{:S(2)}) collective-permute-start(bf16[65,8,128]{2,1,0:T(8,128)(2,1)S(1)} %pad_maximum_fusion.1), channel_id=1, source_target_pairs={{4,0},{0,4},{12,8},{8,12},{5,1},{1,5},{13,9},{9,13},{6,2},{2,6},{1... | collective-permute-start | bytes 399368 | tf_op jit(solution)/shard_map/ppermute | solution.py:92
  9.4 2.4 %collective-permute-start = (s32[3,4,2]{1,2,0:T(2,128)S(1)}, s32[3,4,2]{1,2,0:T(2,128)S(1)}, u32[]{:S(2)}, u32[]{:S(2)}) collective-permute-start(s32[3,4,2]{1,2,0:T(2,128)S(1)} %get-tuple-element.52), channel_id=1, source_target_pairs={{0,1},{1,0},{2,3},{3,2},{4,5},{5,4},{6,7},{7,6},{8,9},{9,8},{10,11... | collective-permute-start | bytes 296 | tf_op jit(solution)/shard_map/ppermute | solution.py:78
  25.5 9.1 %collective-permute-start.6 = (f32[33,128]{1,0:T(8,128)S(1)}, f32[33,128]{1,0:T(8,128)S(1)}, u32[]{:S(2)}, u32[]{:S(2)}) collective-permute-start(f32[33,128]{1,0:T(8,128)S(1)} %select_maximum_fusion), channel_id=1, source_target_pairs={{0,12},{4,8},{8,4},{12,0},{1,13},{5,9},{9,5},{13,1},{2,14},{6,10},... | collective-permute-start | bytes 50696 | tf_op jit(solution)/shard_map/ppermute | solution.py:92
  29.1 5.5 %collective-permute-start.5 = (f32[33,128]{1,0:T(8,128)S(1)}, f32[33,128]{1,0:T(8,128)S(1)}, u32[]{:S(2)}, u32[]{:S(2)}) collective-permute-start(f32[33,128]{1,0:T(8,128)S(1)} %select_maximum_fusion.1), channel_id=1, source_target_pairs={{0,8},{4,12},{8,0},{12,4},{1,9},{5,13},{9,1},{13,5},{2,10},{6,14},... | collective-permute-start | bytes 50696 | tf_op jit(solution)/shard_map/ppermute | solution.py:92
  30.6 3.8 %collective-permute-start.4 = (f32[33,128]{1,0:T(8,128)S(1)}, f32[33,128]{1,0:T(8,128)S(1)}, u32[]{:S(2)}, u32[]{:S(2)}) collective-permute-start(f32[33,128]{1,0:T(8,128)S(1)} %select_maximum_fusion.2), channel_id=1, source_target_pairs={{0,4},{4,0},{8,12},{12,8},{1,5},{5,1},{9,13},{13,9},{2,6},{6,2},{1... | collective-permute-start | bytes 50696 | tf_op jit(solution)/shard_map/ppermute | solution.py:92
  35.6 5.8 %collective-permute-start.9 = (f32[4,8,128]{2,1,0:T(8,128)S(1)}, f32[4,8,128]{2,1,0:T(8,128)S(1)}, u32[]{:S(2)}, u32[]{:S(2)}) collective-permute-start(f32[4,8,128]{2,1,0:T(8,128)S(1)} %get-tuple-element.12), channel_id=1, source_target_pairs={{12,0},{8,4},{4,8},{0,12},{13,1},{9,5},{5,9},{1,13},{14,2},{10,6},... | collective-permute-start | bytes 49160 | tf_op jit(solution)/shard_map/ppermute | solution.py:92
  38.1 4.8 %collective-permute-start.8 = (f32[4,8,128]{2,1,0:T(8,128)S(1)}, f32[4,8,128]{2,1,0:T(8,128)S(1)}, u32[]{:S(2)}, u32[]{:S(2)}) collective-permute-start(f32[4,8,128]{2,1,0:T(8,128)S(1)} %get-tuple-element.11), channel_id=1, source_target_pairs={{8,0},{12,4},{0,8},{4,12},{9,1},{13,5},{1,9},{5,13},{10,2},{14,6},... | collective-permute-start | bytes 49160 | tf_op jit(solution)/shard_map/ppermute | solution.py:92
  38.9 5.4 %collective-permute-start.7 = (f32[4,8,128]{2,1,0:T(8,128)S(1)}, f32[4,8,128]{2,1,0:T(8,128)S(1)}, u32[]{:S(2)}, u32[]{:S(2)}) collective-permute-start(f32[4,8,128]{2,1,0:T(8,128)S(1)} %get-tuple-element.10), channel_id=1, source_target_pairs={{4,0},{0,4},{12,8},{8,12},{5,1},{1,5},{13,9},{9,13},{6,2},{2,6},{1... | collective-permute-start | bytes 49160 | tf_op jit(solution)/shard_map/ppermute | solution.py:92
  46.4 11.7 %collective-permute-start.10 = (f32[8,8,128]{2,1,0:T(8,128)S(1)}, f32[8,8,128]{2,1,0:T(8,128)S(1)}, u32[]{:S(2)}, u32[]{:S(2)}) collective-permute-start(f32[8,8,128]{2,1,0:T(8,128)S(1)} %bitcast_subtract_fusion.2), channel_id=1, source_target_pairs={{0,1},{1,0},{2,3},{3,2},{4,5},{5,4},{6,7},{7,6},{8,9},{9,8},{10,11... | collective-permute-start | bytes 98312 | tf_op jit(solution)/shard_map/ppermute | solution.py:78
  48.2 9.0 %collective-permute-start.13 = (f32[4,8,128]{2,1,0:T(8,128)S(1)}, f32[4,8,128]{2,1,0:T(8,128)S(1)}, u32[]{:S(2)}, u32[]{:S(2)}) collective-permute-start(f32[4,8,128]{2,1,0:T(8,128)S(1)} %add_select_fusion), channel_id=1, source_target_pairs={{0,12},{4,8},{8,4},{12,0},{1,13},{5,9},{9,5},{13,1},{2,14},{6,10},... | collective-permute-start | bytes 49160 | tf_op jit(solution)/shard_map/ppermute | solution.py:92
  52.2 5.0 %collective-permute-start.12 = (f32[4,8,128]{2,1,0:T(8,128)S(1)}, f32[4,8,128]{2,1,0:T(8,128)S(1)}, u32[]{:S(2)}, u32[]{:S(2)}) collective-permute-start(f32[4,8,128]{2,1,0:T(8,128)S(1)} %add_select_fusion.1), channel_id=1, source_target_pairs={{0,8},{4,12},{8,0},{12,4},{1,9},{5,13},{9,1},{13,5},{2,10},{6,14},... | collective-permute-start | bytes 49160 | tf_op jit(solution)/shard_map/ppermute | solution.py:92
  53.7 3.8 %collective-permute-start.11 = (f32[4,8,128]{2,1,0:T(8,128)S(1)}, f32[4,8,128]{2,1,0:T(8,128)S(1)}, u32[]{:S(2)}, u32[]{:S(2)}) collective-permute-start(f32[4,8,128]{2,1,0:T(8,128)S(1)} %add_select_fusion.2), channel_id=1, source_target_pairs={{0,4},{4,0},{8,12},{12,8},{1,5},{5,1},{9,13},{13,9},{2,6},{6,2},{1... | collective-permute-start | bytes 49160 | tf_op jit(solution)/shard_map/ppermute | solution.py:92
  58.0 1.3 %collective-permute-start.14 = (f32[8,8,128]{2,1,0:T(8,128)S(1)}, f32[8,8,128]{2,1,0:T(8,128)S(1)}, u32[]{:S(2)}, u32[]{:S(2)}) collective-permute-start(f32[8,8,128]{2,1,0:T(8,128)S(1)} %bitcast_subtract_fusion), channel_id=1, source_target_pairs={{0,1},{1,0},{2,3},{3,2},{4,5},{5,4},{6,7},{7,6},{8,9},{9,8},{10,11... | collective-permute-start | bytes 98312 | tf_op jit(solution)/shard_map/ppermute | solution.py:78

commit v19 on v18

--- a/solution.py
+++ b/solution.py
@@ -120,9 +120,7 @@
         my_sub = lax.axis_index("sub")
         own_real = real_points.reshape(features, blocks, BLOCK)
         real_tags = real_cluster.reshape(1, blocks, BLOCK).astype(jnp.bfloat16)
-        own_synth = jnp.concatenate(
-            [synth_points, synth_cluster.astype(jnp.bfloat16)[None, :]], axis=0
-        ).reshape(features + 1, blocks, BLOCK)
+        own_synth = jnp.concatenate([synth_points, synth_cluster.astype(jnp.bfloat16)[None, :]], axis=0)
         log_real = jnp.log(
             lax.dynamic_slice_in_dim(real_weight, my_sub * half, half, 0).astype(jnp.float32) + 0.5
         ).reshape(half, blocks, BLOCK)
@@ -146,7 +144,11 @@
         rows_used = rows_used.reshape(slot_count)
         usable = usable.reshape(slot_count)[:, None, None] > 0
         far = jnp.concatenate(
-            [pick_rows(everything[offset], wanted[offset], blocks) for offset in range(peer_count)], axis=0
+            [
+                pick_rows(everything[offset].reshape(features + 1, blocks, BLOCK), wanted[offset], blocks)
+                for offset in range(peer_count)
+            ],
+            axis=0,
         )
         far_y = far[:, :features]
         far_tags = far[:, features]

time: 60.3 us -> 62.2 us (1.032)
  local copies, waits for them, and re-layouts: 5.31 us -> 6.38 us
    unnamed x7 -> x11, local copies, waits for them, and re-layouts: 2.24 us -> 3.26 us
    convert_element_type x0 -> x1, other arithmetic: none -> 0.69 us  [shards(): synth_cluster.astype(jnp.bfloat16)[None, :]]
    reduce_sum x13 -> x11, other arithmetic: 4.57 us -> 4.43 us  [pick_rows(): return jnp.sum(chosen, axis=2, dtype=values.dtype)]
    reduce_max x12 -> x13, other arithmetic: 7.52 us -> 7.49 us  [lse_parts(): highest = jnp.max(scores, axis=axis)]
  transfers between devices with their start and end apart: 15 -> 15, of which waited for: 4 -> 4; matrix products, arithmetic and copies ran while one was open for 42% -> 43% of each run, Pallas kernels for 0% -> 0%
where the time goes in v19:
time: 62.2 us; the launch traced here: 61.8 us
  other arithmetic  29.3 us (47%)
  starting transfers between devices  19.4 us (31%)
  local copies, waits for them, and re-layouts  6.38 us (10%)
  waiting for transfers between devices  2.75 us (4%)
  matrix products  2.53 us (4%)
  between operations  1.43 us (2%)
    ppermute x12, starting transfers between devices, exchange(): moved.append(lax.ppermute(chunks[offset], 'blk', perm))  19.2 us
    reduce_sum x14, other arithmetic, lse_parts(): jnp.sum(jnp.exp(scores - jnp.expand_dims(highest, axis)), axis=axis)  9.52 us
    reduce_max x13, other arithmetic, lse_parts(): highest = jnp.max(scores, axis=axis)  7.49 us
    reduce_sum x11, other arithmetic, pick_rows(): return jnp.sum(chosen, axis=2, dtype=values.dtype)  4.43 us
    unnamed x11, local copies, waits for them, and re-layouts  3.26 us
    dot_general x2, matrix products, slot_costs(): jnp.einsum('gdi,gdj->gij', slot_real, slot_synth, preferred_element_type=...  2.53 us
    ppermute x12, waiting for transfers between devices, exchange(): moved.append(lax.ppermute(chunks[offset], 'blk', perm))  2.23 us
    unnamed x2, other arithmetic  1.55 us
  transfers between devices with their start and end apart: 15, of which 4 were waited for; matrix products, arithmetic and copies ran while one was open for 43% of the time, Pallas kernels for 0%

profile of v19, /device:TPU:0, one launch (start us, length us, event | category | flops | bytes accessed | tf_op | source)
XLA Modules:
  0.0 61.8 jit_solution(16913032760931787202)
XLA Ops:
  0.6 1.0 %constant_dynamic-update-slice_fusion.1 = bf16[65,1024]{1,0:T(8,128)(2,1)S(1)} fusion(bf16[64,1024]{1,0:T(8,128)(2,1)} %param.10), kind=kLoop, calls=%fused_computation.154 | loop fusion | bytes 262144
  1.6 0.7 %convert_element_type.119 = bf16[1024]{0:T(1024)(128)(2,1)S(1)} convert(s32[1024]{0:T(1024)} %param.12) | non-fusion elementwise | flops 1024 | bytes 6144 | tf_op jit(solution)/shard_map/convert_element_type | solution.py:123
  2.3 5.1 %collective-permute-start.3 = (bf16[65,1024]{1,0:T(8,128)(2,1)S(1)}, bf16[65,1024]{1,0:T(8,128)(2,1)S(1)}, u32[]{:S(2)}, u32[]{:S(2)}) collective-permute-start(bf16[65,1024]{1,0:T(8,128)(2,1)S(1)} %constant_dynamic-update-slice_fusion), channel_id=1, source_target_pairs={{12,0},{8,4},{4,8},{0,12},{13,1},{9,5},{5,9},{1,13},{14,2},{10,6},... | collective-permute-start | bytes 399368 | tf_op jit(solution)/shard_map/ppermute | solution.py:92
  7.4 0.6 %collective-permute-start.1 = (bf16[65,1024]{1,0:T(8,128)(2,1)S(1)}, bf16[65,1024]{1,0:T(8,128)(2,1)S(1)}, u32[]{:S(2)}, u32[]{:S(2)}) collective-permute-start(bf16[65,1024]{1,0:T(8,128)(2,1)S(1)} %constant_dynamic-update-slice_fusion), channel_id=1, source_target_pairs={{4,0},{0,4},{12,8},{8,12},{5,1},{1,5},{13,9},{9,13},{6,2},{2,6},{1... | collective-permute-start | bytes 399368 | tf_op jit(solution)/shard_map/ppermute | solution.py:92
  8.1 0.7 %stack_broadcast_in_dim.2 = s32[1,4,2]{1,2,0:T(2,128)S(1)} broadcast(s32[4]{0:T(128)} %param.17), dimensions={1} | broadcast | bytes 48 | tf_op jit(solution)/shard_map/stack;broadcast_in_dim | solution.py:137
  8.7 0.7 %fusion.41 = (s32[3,1,4,2]{2,3,0,1:T(2,128)S(1)}, s32[3,4,2]{1,2,0:T(2,128)S(1)}) fusion(s32[1,4,2]{1,2,0:T(2,128)S(1)} %stack_broadcast_in_dim.2, s32[1,4,2]{1,2,0:T(2,128)} %bitcast.103, s32[1,4,2]{1,2,0:T(2,128)} %bitcast.104), kind=kLoop, calls=%fused_computation.201 | loop fusion | flops 48 | bytes 288 | tf_op jit(solution)/shard_map/stack | solution.py:138
  9.4 0.7 %convert_bitcast_fusion.2 = bf16[1,1,8,128]{3,2,1,0:T(8,128)(2,1)S(1)} fusion(s32[1024]{0:T(1024)} %param.12), kind=kLoop, calls=%fused_computation.203 | loop fusion | flops 1024 | bytes 6144 | tf_op jit(solution)/shard_map/concatenate | solution.py:123
  10.2 0.9 %copy.32 = bf16[8,8,8,128]{3,2,1,0:T(8,128)(2,1)S(1)} copy(bf16[8,8,8,128]{3,1,2,0:T(8,128)(2,1)} %bitcast.89) | data formatting | bytes 262144
  11.1 0.7 %convert_bitcast_fusion.1 = bf16[8,128]{1,0:T(8,128)(2,1)S(1)} fusion(s32[1024]{0:T(1024)} %param.11), kind=kLoop, calls=%fused_computation.181 | loop fusion | flops 1024 | bytes 6144 | tf_op jit(solution)/shard_map/convert_element_type | solution.py:122
  11.8 0.8 %multiply_bitcast_fusion.1 = f32[1,8,8,128]{3,1,2,0:T(8,128)S(1)} fusion(s32[16,1024]{1,0:T(8,128)} %param.13, s32[]{:T(128)S(6)} %select_n.271), kind=kLoop, calls=%fused_computation.108 | loop fusion | flops 24576 | bytes 65540
  12.6 0.8 %multiply_bitcast_fusion = f32[1,8,8,128]{3,1,2,0:T(8,128)S(1)} fusion(s32[16,1024]{1,0:T(8,128)} %param.14, s32[]{:T(128)S(6)} %select_n.271), kind=kLoop, calls=%fused_computation.107 | loop fusion | flops 24576 | bytes 65540
  13.5 0.3 select_reduce_fusion.25
  13.8 0.3 slice_reduce_fusion.4
  14.4 1.5 %select_reduce_fusion = bf16[16,64,128]{2,1,0:T(8,128)(2,1)S(1)} fusion(pred[16,8]{1,0:T(8,128)(4,1)S(1)} %iota_compare_fusion.2, bf16[64,8,128]{2,1,0:T(8,128)(2,1)S(1)} %bitcast.88), kind=kLoop, calls=%fused_computation.48 | loop fusion | flops 1966080 | bytes 393344 | tf_op jit(solution)/shard_map/reduce_sum | solution.py:26
  16.5 0.3 slice_reduce_fusion
  16.8 0.2 convert_reduce_fusion.2
  18.4 1.4 %collective-permute-done.2 = bf16[65,1024]{1,0:T(8,128)(2,1)S(1)} collective-permute-done((bf16[65,1024]{1,0:T(8,128)(2,1)S(1)}, bf16[65,1024]{1,0:T(8,128)(2,1)S(1)}, u32[]{:S(2)}, u32[]{:S(2)}) %collective-permute-start.2) | collective-permute-done | bytes 133152 | tf_op jit(solution)/shard_map/ppermute | solution.py:92
  20.0 0.7 %select_reduce_fusion.1 = (bf16[4,65,128]{2,1,0:T(8,128)(2,1)S(1)}, bf16[4,65,128]{2,1,0:T(8,128)(2,1)S(1)}) fusion(pred[4,8]{1,0:T(4,128)(4,1)S(1)} %iota_compare_fusion.6, bf16[65,8,128]{2,1,0:T(8,128)(2,1)S(1)} %slice.201, bf16[65,8,128]{2,1,0:T(8,128)(2,1)S(1)} %slice.200, pred[4,8]{1,0:T(4,128)(4,1)S(1)} %iota_compare_fusion.7), kind=kLoop, calls=%fused_computation.55 | loop fusion | flops 998400 | bytes 399424 | tf_op jit(solution)/shard_map/reduce_sum | solution.py:26
  20.7 0.7 %select_reduce_fusion.3 = (bf16[4,65,128]{2,1,0:T(8,128)(2,1)S(1)}, bf16[4,65,128]{2,1,0:T(8,128)(2,1)S(1)}) fusion(pred[4,8]{1,0:T(4,128)(4,1)S(1)} %iota_compare_fusion.8, bf16[65,8,128]{2,1,0:T(8,128)(2,1)S(1)} %slice.199, bf16[65,8,128]{2,1,0:T(8,128)(2,1)S(1)} %maximum_bitcast_fusion, pred[4,8]{1,0:T(4,128)(4,1)S(1)} %iota_compare_fusion.9), kind=kLoop, calls=%fused_computation.57 | loop fusion | flops 998400 | bytes 399424 | tf_op jit(solution)/shard_map/reduce_sum | solution.py:26
  21.6 1.4 %fusion.26 = f32[16,128,128]{2,1,0:T(8,128)S(1)} fusion(bf16[16,64,128]{2,1,0:T(8,128)(2,1)S(1)} %select_reduce_fusion, f32[16,128]{1,0:T(8,128)S(1)} %broadcast_multiply_fusion.4, f32[16,128]{1,0:T(8,128)S(1)} %broadcast_multiply_fusion.5, bf16[16,128]{1,0:T(8,128)(2,1)S(1)} %select_reduce_fusion.23, bf16[16,128]{1,0:T(8,128)(2,1)S(1)} %bitcast.101, ...), kind=kOutput, calls=%fused_computation.53 | convolution fusion | flops 35127296 | bytes 1597440 | tf_op jit(solution)/shard_map/gdi,gdj->gij/dot_general | solution.py:61
  23.0 1.1 %fusion.27 = f32[16,128,128]{2,1,0:T(8,128)S(1)} fusion(bf16[16,64,128]{2,1,0:T(8,128)(2,1)S(1)} %select_reduce_fusion, f32[16,128]{1,0:T(8,128)S(1)} %broadcast_multiply_fusion.5, f32[16,128]{1,0:T(8,128)S(1)} %broadcast_multiply_fusion.4, bf16[16,128]{1,0:T(8,128)(2,1)S(1)} %bitcast.102, bf16[16,128]{1,0:T(8,128)(2,1)S(1)} %select_reduce_fusion.23, ...), kind=kOutput, calls=%fused_computation.54 | convolution fusion | flops 35127296 | bytes 1597440 | tf_op jit(solution)/shard_map/gdi,gdj->gij/dot_general | solution.py:61
  24.4 0.2 exponential_reduce_fusion.2
  25.1 0.2 select_reduce_fusion.15
  25.4 0.6 %subtract_reduce_fusion.9 = f32[4,8,128]{2,1,0:T(8,128)S(1)} fusion(f32[4,128,128]{2,1,0:T(8,128)S(1)} %get-tuple-element.33, f32[4,8,128]{2,1,0:T(8,128)S(1)} %get-tuple-element.46), kind=kLoop, calls=%fused_computation.19 | loop fusion | flops 1044480 | bytes 294912 | tf_op jit(solution)/shard_map/reduce_max | solution.py:71
  26.0 0.7 %fusion.5 = f32[4,8,128]{2,1,0:T(8,128)S(1)} fusion(f32[4,8,128]{2,1,0:T(8,128)S(1)} %subtract_reduce_fusion.9, f32[4,128,128]{2,1,0:T(8,128)S(1)} %get-tuple-element.33, f32[4,8,128]{2,1,0:T(8,128)S(1)} %get-tuple-element.46), kind=kLoop, calls=%fused_computation.29 | loop fusion | flops 1568768 | bytes 311296 | tf_op jit(solution)/shard_map/reduce_sum | solution.py:72
  26.8 2.6 %collective-permute-start.6 = (f32[33,128]{1,0:T(8,128)S(1)}, f32[33,128]{1,0:T(8,128)S(1)}, u32[]{:S(2)}, u32[]{:S(2)}) collective-permute-start(f32[33,128]{1,0:T(8,128)S(1)} %select_maximum_fusion), channel_id=1, source_target_pairs={{0,12},{4,8},{8,4},{12,0},{1,13},{5,9},{9,5},{13,1},{2,14},{6,10},... | collective-permute-start | bytes 50696 | tf_op jit(solution)/shard_map/ppermute | solution.py:92
  29.4 0.6 %subtract_reduce_fusion.10 = f32[4,8,128]{2,1,0:T(8,128)S(1)} fusion(f32[4,128,128]{2,1,0:T(8,128)S(1)} %get-tuple-element.34, f32[4,8,128]{2,1,0:T(8,128)S(1)} %get-tuple-element.47), kind=kLoop, calls=%fused_computation.21 | loop fusion | flops 1044480 | bytes 294912 | tf_op jit(solution)/shard_map/reduce_max | solution.py:71
  30.0 0.7 %fusion.3 = f32[4,8,128]{2,1,0:T(8,128)S(1)} fusion(f32[4,8,128]{2,1,0:T(8,128)S(1)} %subtract_reduce_fusion.10, f32[4,128,128]{2,1,0:T(8,128)S(1)} %get-tuple-element.34, f32[4,8,128]{2,1,0:T(8,128)S(1)} %get-tuple-element.47), kind=kLoop, calls=%fused_computation.27 | loop fusion | flops 1568768 | bytes 311296 | tf_op jit(solution)/shard_map/reduce_sum | solution.py:72
  31.0 0.6 %subtract_reduce_fusion.11 = f32[4,8,128]{2,1,0:T(8,128)S(1)} fusion(f32[4,128,128]{2,1,0:T(8,128)S(1)} %get-tuple-element.35, f32[4,8,128]{2,1,0:T(8,128)S(1)} %get-tuple-element.48), kind=kLoop, calls=%fused_computation.23 | loop fusion | flops 1044480 | bytes 294912 | tf_op jit(solution)/shard_map/reduce_max | solution.py:71
  31.6 0.7 %fusion.1 = f32[4,8,128]{2,1,0:T(8,128)S(1)} fusion(f32[4,8,128]{2,1,0:T(8,128)S(1)} %subtract_reduce_fusion.11, f32[4,128,128]{2,1,0:T(8,128)S(1)} %get-tuple-element.35, f32[4,8,128]{2,1,0:T(8,128)S(1)} %get-tuple-element.48), kind=kLoop, calls=%fused_computation.25 | loop fusion | flops 1568768 | bytes 311296 | tf_op jit(solution)/shard_map/reduce_sum | solution.py:72
  32.4 1.9 %collective-permute-start.4 = (f32[33,128]{1,0:T(8,128)S(1)}, f32[33,128]{1,0:T(8,128)S(1)}, u32[]{:S(2)}, u32[]{:S(2)}) collective-permute-start(f32[33,128]{1,0:T(8,128)S(1)} %select_maximum_fusion.2), channel_id=1, source_target_pairs={{0,4},{4,0},{8,12},{12,8},{1,5},{5,1},{9,13},{13,9},{2,6},{6,2},{1... | collective-permute-start | bytes 50696 | tf_op jit(solution)/shard_map/ppermute | solution.py:92
  34.3 0.6 %subtract_reduce_fusion.8 = f32[4,8,128]{2,1,0:T(8,128)S(1)} fusion(f32[4,128,128]{2,1,0:T(8,128)S(1)} %get-tuple-element.32, f32[4,8,128]{2,1,0:T(8,128)S(1)} %get-tuple-element.45), kind=kLoop, calls=%fused_computation.17 | loop fusion | flops 1044480 | bytes 294912 | tf_op jit(solution)/shard_map/reduce_max | solution.py:71
  35.0 0.7 %fusion.7 = f32[4,8,128]{2,1,0:T(8,128)S(1)} fusion(f32[4,8,128]{2,1,0:T(8,128)S(1)} %subtract_reduce_fusion.8, f32[4,128,128]{2,1,0:T(8,128)S(1)} %get-tuple-element.32, f32[4,8,128]{2,1,0:T(8,128)S(1)} %get-tuple-element.45), kind=kLoop, calls=%fused_computation.31 | loop fusion | flops 1568768 | bytes 311296 | tf_op jit(solution)/shard_map/reduce_sum | solution.py:72
  35.8 0.5 collective-permute-done.4
  36.8 0.2 select_reduce_fusion.13
  37.2 0.2 select_reduce_fusion.19
  37.5 2.4 %collective-permute-start.9 = (f32[4,8,128]{2,1,0:T(8,128)S(1)}, f32[4,8,128]{2,1,0:T(8,128)S(1)}, u32[]{:S(2)}, u32[]{:S(2)}) collective-permute-start(f32[4,8,128]{2,1,0:T(8,128)S(1)} %get-tuple-element.12), channel_id=1, source_target_pairs={{12,0},{8,4},{4,8},{0,12},{13,1},{9,5},{5,9},{1,13},{14,2},{10,6},... | collective-permute-start | bytes 49160 | tf_op jit(solution)/shard_map/ppermute | solution.py:92
  39.9 1.0 %collective-permute-start.8 = (f32[4,8,128]{2,1,0:T(8,128)S(1)}, f32[4,8,128]{2,1,0:T(8,128)S(1)}, u32[]{:S(2)}, u32[]{:S(2)}) collective-permute-start(f32[4,8,128]{2,1,0:T(8,128)S(1)} %get-tuple-element.11), channel_id=1, source_target_pairs={{8,0},{12,4},{0,8},{4,12},{9,1},{13,5},{1,9},{5,13},{10,2},{14,6},... | collective-permute-start | bytes 49160 | tf_op jit(solution)/shard_map/ppermute | solution.py:92
  40.8 1.1 %collective-permute-start.7 = (f32[4,8,128]{2,1,0:T(8,128)S(1)}, f32[4,8,128]{2,1,0:T(8,128)S(1)}, u32[]{:S(2)}, u32[]{:S(2)}) collective-permute-start(f32[4,8,128]{2,1,0:T(8,128)S(1)} %get-tuple-element.10), channel_id=1, source_target_pairs={{4,0},{0,4},{12,8},{8,12},{5,1},{1,5},{13,9},{9,13},{6,2},{2,6},{1... | collective-permute-start | bytes 49160 | tf_op jit(solution)/shard_map/ppermute | solution.py:92
  41.9 0.6 %subtract_reduce_fusion.7 = f32[4,8,128]{2,1,0:T(8,128)S(1)} fusion(f32[4,128,128]{2,1,0:T(8,128)S(1)} %get-tuple-element.29, f32[4,8,128]{2,1,0:T(8,128)S(1)} %broadcast_multiply_fusion.3), kind=kLoop, calls=%fused_computation.15 | loop fusion | flops 1044480 | bytes 294912 | tf_op jit(solution)/shard_map/reduce_max | solution.py:71
  42.5 0.7 %fusion.9 = f32[4,8,128]{2,1,0:T(8,128)S(1)} fusion(f32[4,8,128]{2,1,0:T(8,128)S(1)} %subtract_reduce_fusion.7, f32[4,128,128]{2,1,0:T(8,128)S(1)} %get-tuple-element.29, f32[4,8,128]{2,1,0:T(8,128)S(1)} %broadcast_multiply_fusion.3), kind=kLoop, calls=%fused_computation.33 | loop fusion | flops 1568768 | bytes 311296 | tf_op jit(solution)/shard_map/reduce_sum | solution.py:72
  43.3 0.6 %subtract_reduce_fusion.4 = f32[4,8,128]{2,1,0:T(8,128)S(1)} fusion(f32[4,128,128]{2,1,0:T(8,128)S(1)} %get-tuple-element.36, f32[4,8,128]{2,1,0:T(8,128)S(1)} %broadcast_multiply_fusion), kind=kLoop, calls=%fused_computation.9 | loop fusion | flops 1044480 | bytes 294912 | tf_op jit(solution)/shard_map/reduce_max | solution.py:71
  44.0 0.7 %fusion.15 = f32[4,8,128]{2,1,0:T(8,128)S(1)} fusion(f32[4,8,128]{2,1,0:T(8,128)S(1)} %subtract_reduce_fusion.4, f32[4,128,128]{2,1,0:T(8,128)S(1)} %get-tuple-element.36, f32[4,8,128]{2,1,0:T(8,128)S(1)} %broadcast_multiply_fusion), kind=kLoop, calls=%fused_computation.39 | loop fusion | flops 1568768 | bytes 311296 | tf_op jit(solution)/shard_map/reduce_sum | solution.py:72
  44.7 0.6 %subtract_reduce_fusion.5 = f32[4,8,128]{2,1,0:T(8,128)S(1)} fusion(f32[4,128,128]{2,1,0:T(8,128)S(1)} %get-tuple-element.31, f32[4,8,128]{2,1,0:T(8,128)S(1)} %broadcast_multiply_fusion.1), kind=kLoop, calls=%fused_computation.11 | loop fusion | flops 1044480 | bytes 294912 | tf_op jit(solution)/shard_map/reduce_max | solution.py:71
  45.4 0.7 %fusion.13 = f32[4,8,128]{2,1,0:T(8,128)S(1)} fusion(f32[4,8,128]{2,1,0:T(8,128)S(1)} %subtract_reduce_fusion.5, f32[4,128,128]{2,1,0:T(8,128)S(1)} %get-tuple-element.31, f32[4,8,128]{2,1,0:T(8,128)S(1)} %broadcast_multiply_fusion.1), kind=kLoop, calls=%fused_computation.37 | loop fusion | flops 1568768 | bytes 311296 | tf_op jit(solution)/shard_map/reduce_sum | solution.py:72
  46.1 0.6 %subtract_reduce_fusion.6 = f32[4,8,128]{2,1,0:T(8,128)S(1)} fusion(f32[4,128,128]{2,1,0:T(8,128)S(1)} %get-tuple-element.30, f32[4,8,128]{2,1,0:T(8,128)S(1)} %broadcast_multiply_fusion.2), kind=kLoop, calls=%fused_computation.13 | loop fusion | flops 1044480 | bytes 294912 | tf_op jit(solution)/shard_map/reduce_max | solution.py:71
  46.9 0.7 %fusion.11 = f32[4,8,128]{2,1,0:T(8,128)S(1)} fusion(f32[4,8,128]{2,1,0:T(8,128)S(1)} %subtract_reduce_fusion.6, f32[4,128,128]{2,1,0:T(8,128)S(1)} %get-tuple-element.30, f32[4,8,128]{2,1,0:T(8,128)S(1)} %broadcast_multiply_fusion.2), kind=kLoop, calls=%fused_computation.35 | loop fusion | flops 1568768 | bytes 311296 | tf_op jit(solution)/shard_map/reduce_sum | solution.py:72
  47.7 0.2 select_reduce_fusion.10
  48.3 0.2 select_reduce_fusion.8
  48.5 0.6 %subtract_reduce_fusion = f32[4,8,128]{2,1,0:T(8,128)S(1)} fusion(f32[4,8,128]{2,1,0:T(8,128)S(1)} %get-tuple-element.40, f32[4,128,128]{2,1,0:T(8,128)S(1)} %get-tuple-element.33), kind=kLoop, calls=%fused_computation.1 | loop fusion | flops 1044480 | bytes 294912 | tf_op jit(solution)/shard_map/reduce_max | solution.py:71
  49.2 1.0 %fusion.23 = f32[4,8,128]{2,1,0:T(8,128)S(1)} fusion(f32[4,8,128]{2,1,0:T(8,128)S(1)} %subtract_reduce_fusion, f32[4,8,128]{2,1,0:T(8,128)S(1)} %get-tuple-element.40, f32[4,128,128]{2,1,0:T(8,128)S(1)} %get-tuple-element.33), kind=kLoop, calls=%fused_computation.47 | loop fusion | flops 1568768 | bytes 311296 | tf_op jit(solution)/shard_map/reduce_sum | solution.py:72
  50.2 2.4 %collective-permute-start.13 = (f32[4,8,128]{2,1,0:T(8,128)S(1)}, f32[4,8,128]{2,1,0:T(8,128)S(1)}, u32[]{:S(2)}, u32[]{:S(2)}) collective-permute-start(f32[4,8,128]{2,1,0:T(8,128)S(1)} %add_select_fusion), channel_id=1, source_target_pairs={{0,12},{4,8},{8,4},{12,0},{1,13},{5,9},{9,5},{13,1},{2,14},{6,10},... | collective-permute-start | bytes 49160 | tf_op jit(solution)/shard_map/ppermute | solution.py:92
  52.6 0.6 %subtract_reduce_fusion.1 = f32[4,8,128]{2,1,0:T(8,128)S(1)} fusion(f32[4,8,128]{2,1,0:T(8,128)S(1)} %get-tuple-element.41, f32[4,128,128]{2,1,0:T(8,128)S(1)} %get-tuple-element.34), kind=kLoop, calls=%fused_computation.3 | loop fusion | flops 1044480 | bytes 294912 | tf_op jit(solution)/shard_map/reduce_max | solution.py:71
  53.2 0.7 %fusion.21 = f32[4,8,128]{2,1,0:T(8,128)S(1)} fusion(f32[4,8,128]{2,1,0:T(8,128)S(1)} %subtract_reduce_fusion.1, f32[4,8,128]{2,1,0:T(8,128)S(1)} %get-tuple-element.41, f32[4,128,128]{2,1,0:T(8,128)S(1)} %get-tuple-element.34), kind=kLoop, calls=%fused_computation.45 | loop fusion | flops 1568768 | bytes 311296 | tf_op jit(solution)/shard_map/reduce_sum | solution.py:72
  54.1 0.6 %subtract_reduce_fusion.2 = f32[4,8,128]{2,1,0:T(8,128)S(1)} fusion(f32[4,8,128]{2,1,0:T(8,128)S(1)} %get-tuple-element.42, f32[4,128,128]{2,1,0:T(8,128)S(1)} %get-tuple-element.35), kind=kLoop, calls=%fused_computation.5 | loop fusion | flops 1044480 | bytes 294912 | tf_op jit(solution)/shard_map/reduce_max | solution.py:71
  54.7 0.7 %fusion.19 = f32[4,8,128]{2,1,0:T(8,128)S(1)} fusion(f32[4,8,128]{2,1,0:T(8,128)S(1)} %subtract_reduce_fusion.2, f32[4,8,128]{2,1,0:T(8,128)S(1)} %get-tuple-element.42, f32[4,128,128]{2,1,0:T(8,128)S(1)} %get-tuple-element.35), kind=kLoop, calls=%fused_computation.43 | loop fusion | flops 1568768 | bytes 311296 | tf_op jit(solution)/shard_map/reduce_sum | solution.py:72
  55.6 2.0 %collective-permute-start.11 = (f32[4,8,128]{2,1,0:T(8,128)S(1)}, f32[4,8,128]{2,1,0:T(8,128)S(1)}, u32[]{:S(2)}, u32[]{:S(2)}) collective-permute-start(f32[4,8,128]{2,1,0:T(8,128)S(1)} %add_select_fusion.2), channel_id=1, source_target_pairs={{0,4},{4,0},{8,12},{12,8},{1,5},{5,1},{9,13},{13,9},{2,6},{6,2},{1... | collective-permute-start | bytes 49160 | tf_op jit(solution)/shard_map/ppermute | solution.py:92
  57.5 0.6 %subtract_reduce_fusion.3 = f32[4,8,128]{2,1,0:T(8,128)S(1)} fusion(f32[4,8,128]{2,1,0:T(8,128)S(1)} %get-tuple-element.39, f32[4,128,128]{2,1,0:T(8,128)S(1)} %get-tuple-element.32), kind=kLoop, calls=%fused_computation.7 | loop fusion | flops 1044480 | bytes 294912 | tf_op jit(solution)/shard_map/reduce_max | solution.py:71
  58.2 0.7 %fusion.17 = f32[4,8,128]{2,1,0:T(8,128)S(1)} fusion(f32[4,8,128]{2,1,0:T(8,128)S(1)} %subtract_reduce_fusion.3, f32[4,8,128]{2,1,0:T(8,128)S(1)} %get-tuple-element.39, f32[4,128,128]{2,1,0:T(8,128)S(1)} %get-tuple-element.32), kind=kLoop, calls=%fused_computation.41 | loop fusion | flops 1568768 | bytes 311296 | tf_op jit(solution)/shard_map/reduce_sum | solution.py:72
  59.0 0.3 collective-permute-done.11
  59.4 0.2 select_reduce_fusion.6
  60.0 0.6 %copy.47 = f32[2,8,8,128]{3,1,2,0:T(8,128)} copy(f32[2,8,8,128]{3,2,1,0:T(8,128)S(1)} %bitcast.91) | data formatting | bytes 131072
  60.6 0.5 collective-permute-done.14
  61.1 0.6 %copy.46 = f32[2,8,8,128]{3,1,2,0:T(8,128)} copy(f32[2,8,8,128]{3,2,1,0:T(8,128)S(1)} %bitcast.92) | data formatting | bytes 131072
  (127 shorter events, 5.9 us)
Async XLA Ops:
  0.6 12.8 %copy-start = (bf16[64,1024]{1,0:T(8,128)(2,1)S(1)}, bf16[64,1024]{1,0:T(8,128)(2,1)}, u32[]{:S(2)}) copy-start(bf16[64,1024]{1,0:T(8,128)(2,1)} %param.9) | copy-start | bytes 393220
  2.3 16.1 %collective-permute-start.3 = (bf16[65,1024]{1,0:T(8,128)(2,1)S(1)}, bf16[65,1024]{1,0:T(8,128)(2,1)S(1)}, u32[]{:S(2)}, u32[]{:S(2)}) collective-permute-start(bf16[65,1024]{1,0:T(8,128)(2,1)S(1)} %constant_dynamic-update-slice_fusion), channel_id=1, source_target_pairs={{12,0},{8,4},{4,8},{0,12},{13,1},{9,5},{5,9},{1,13},{14,2},{10,6},... | collective-permute-start | bytes 399368 | tf_op jit(solution)/shard_map/ppermute | solution.py:92
  7.4 12.5 %collective-permute-start.2 = (bf16[65,1024]{1,0:T(8,128)(2,1)S(1)}, bf16[65,1024]{1,0:T(8,128)(2,1)S(1)}, u32[]{:S(2)}, u32[]{:S(2)}) collective-permute-start(bf16[65,1024]{1,0:T(8,128)(2,1)S(1)} %constant_dynamic-update-slice_fusion), channel_id=1, source_target_pairs={{8,0},{12,4},{0,8},{4,12},{9,1},{13,5},{1,9},{5,13},{10,2},{14,6},... | collective-permute-start | bytes 399368 | tf_op jit(solution)/shard_map/ppermute | solution.py:92
  7.4 12.5 %collective-permute-start.1 = (bf16[65,1024]{1,0:T(8,128)(2,1)S(1)}, bf16[65,1024]{1,0:T(8,128)(2,1)S(1)}, u32[]{:S(2)}, u32[]{:S(2)}) collective-permute-start(bf16[65,1024]{1,0:T(8,128)(2,1)S(1)} %constant_dynamic-update-slice_fusion), channel_id=1, source_target_pairs={{4,0},{0,4},{12,8},{8,12},{5,1},{1,5},{13,9},{9,13},{6,2},{2,6},{1... | collective-permute-start | bytes 399368 | tf_op jit(solution)/shard_map/ppermute | solution.py:92
  9.4 4.0 %collective-permute-start = (s32[3,4,2]{1,2,0:T(2,128)S(1)}, s32[3,4,2]{1,2,0:T(2,128)S(1)}, u32[]{:S(2)}, u32[]{:S(2)}) collective-permute-start(s32[3,4,2]{1,2,0:T(2,128)S(1)} %get-tuple-element.50), channel_id=1, source_target_pairs={{0,1},{1,0},{2,3},{3,2},{4,5},{5,4},{6,7},{7,6},{8,9},{9,8},{10,11... | collective-permute-start | bytes 296 | tf_op jit(solution)/shard_map/ppermute | solution.py:78
  26.8 9.6 %collective-permute-start.6 = (f32[33,128]{1,0:T(8,128)S(1)}, f32[33,128]{1,0:T(8,128)S(1)}, u32[]{:S(2)}, u32[]{:S(2)}) collective-permute-start(f32[33,128]{1,0:T(8,128)S(1)} %select_maximum_fusion), channel_id=1, source_target_pairs={{0,12},{4,8},{8,4},{12,0},{1,13},{5,9},{9,5},{13,1},{2,14},{6,10},... | collective-permute-start | bytes 50696 | tf_op jit(solution)/shard_map/ppermute | solution.py:92
  30.9 5.5 %collective-permute-start.5 = (f32[33,128]{1,0:T(8,128)S(1)}, f32[33,128]{1,0:T(8,128)S(1)}, u32[]{:S(2)}, u32[]{:S(2)}) collective-permute-start(f32[33,128]{1,0:T(8,128)S(1)} %select_maximum_fusion.1), channel_id=1, source_target_pairs={{0,8},{4,12},{8,0},{12,4},{1,9},{5,13},{9,1},{13,5},{2,10},{6,14},... | collective-permute-start | bytes 50696 | tf_op jit(solution)/shard_map/ppermute | solution.py:92
  32.4 3.8 %collective-permute-start.4 = (f32[33,128]{1,0:T(8,128)S(1)}, f32[33,128]{1,0:T(8,128)S(1)}, u32[]{:S(2)}, u32[]{:S(2)}) collective-permute-start(f32[33,128]{1,0:T(8,128)S(1)} %select_maximum_fusion.2), channel_id=1, source_target_pairs={{0,4},{4,0},{8,12},{12,8},{1,5},{5,1},{9,13},{13,9},{2,6},{6,2},{1... | collective-permute-start | bytes 50696 | tf_op jit(solution)/shard_map/ppermute | solution.py:92
  37.5 5.8 %collective-permute-start.9 = (f32[4,8,128]{2,1,0:T(8,128)S(1)}, f32[4,8,128]{2,1,0:T(8,128)S(1)}, u32[]{:S(2)}, u32[]{:S(2)}) collective-permute-start(f32[4,8,128]{2,1,0:T(8,128)S(1)} %get-tuple-element.12), channel_id=1, source_target_pairs={{12,0},{8,4},{4,8},{0,12},{13,1},{9,5},{5,9},{1,13},{14,2},{10,6},... | collective-permute-start | bytes 49160 | tf_op jit(solution)/shard_map/ppermute | solution.py:92
  39.9 4.8 %collective-permute-start.8 = (f32[4,8,128]{2,1,0:T(8,128)S(1)}, f32[4,8,128]{2,1,0:T(8,128)S(1)}, u32[]{:S(2)}, u32[]{:S(2)}) collective-permute-start(f32[4,8,128]{2,1,0:T(8,128)S(1)} %get-tuple-element.11), channel_id=1, source_target_pairs={{8,0},{12,4},{0,8},{4,12},{9,1},{13,5},{1,9},{5,13},{10,2},{14,6},... | collective-permute-start | bytes 49160 | tf_op jit(solution)/shard_map/ppermute | solution.py:92
  40.8 5.3 %collective-permute-start.7 = (f32[4,8,128]{2,1,0:T(8,128)S(1)}, f32[4,8,128]{2,1,0:T(8,128)S(1)}, u32[]{:S(2)}, u32[]{:S(2)}) collective-permute-start(f32[4,8,128]{2,1,0:T(8,128)S(1)} %get-tuple-element.10), channel_id=1, source_target_pairs={{4,0},{0,4},{12,8},{8,12},{5,1},{1,5},{13,9},{9,13},{6,2},{2,6},{1... | collective-permute-start | bytes 49160 | tf_op jit(solution)/shard_map/ppermute | solution.py:92
  48.2 11.7 %collective-permute-start.10 = (f32[8,8,128]{2,1,0:T(8,128)S(1)}, f32[8,8,128]{2,1,0:T(8,128)S(1)}, u32[]{:S(2)}, u32[]{:S(2)}) collective-permute-start(f32[8,8,128]{2,1,0:T(8,128)S(1)} %bitcast_subtract_fusion.2), channel_id=1, source_target_pairs={{0,1},{1,0},{2,3},{3,2},{4,5},{5,4},{6,7},{7,6},{8,9},{9,8},{10,11... | collective-permute-start | bytes 98312 | tf_op jit(solution)/shard_map/ppermute | solution.py:78
  50.2 8.8 %collective-permute-start.13 = (f32[4,8,128]{2,1,0:T(8,128)S(1)}, f32[4,8,128]{2,1,0:T(8,128)S(1)}, u32[]{:S(2)}, u32[]{:S(2)}) collective-permute-start(f32[4,8,128]{2,1,0:T(8,128)S(1)} %add_select_fusion), channel_id=1, source_target_pairs={{0,12},{4,8},{8,4},{12,0},{1,13},{5,9},{9,5},{13,1},{2,14},{6,10},... | collective-permute-start | bytes 49160 | tf_op jit(solution)/shard_map/ppermute | solution.py:92
  54.0 5.0 %collective-permute-start.12 = (f32[4,8,128]{2,1,0:T(8,128)S(1)}, f32[4,8,128]{2,1,0:T(8,128)S(1)}, u32[]{:S(2)}, u32[]{:S(2)}) collective-permute-start(f32[4,8,128]{2,1,0:T(8,128)S(1)} %add_select_fusion.1), channel_id=1, source_target_pairs={{0,8},{4,12},{8,0},{12,4},{1,9},{5,13},{9,1},{13,5},{2,10},{6,14},... | collective-permute-start | bytes 49160 | tf_op jit(solution)/shard_map/ppermute | solution.py:92
  55.6 3.8 %collective-permute-start.11 = (f32[4,8,128]{2,1,0:T(8,128)S(1)}, f32[4,8,128]{2,1,0:T(8,128)S(1)}, u32[]{:S(2)}, u32[]{:S(2)}) collective-permute-start(f32[4,8,128]{2,1,0:T(8,128)S(1)} %add_select_fusion.2), channel_id=1, source_target_pairs={{0,4},{4,0},{8,12},{12,8},{1,5},{5,1},{9,13},{13,9},{2,6},{6,2},{1... | collective-permute-start | bytes 49160 | tf_op jit(solution)/shard_map/ppermute | solution.py:92
  59.8 1.3 %collective-permute-start.14 = (f32[8,8,128]{2,1,0:T(8,128)S(1)}, f32[8,8,128]{2,1,0:T(8,128)S(1)}, u32[]{:S(2)}, u32[]{:S(2)}) collective-permute-start(f32[8,8,128]{2,1,0:T(8,128)S(1)} %bitcast_subtract_fusion), channel_id=1, source_target_pairs={{0,1},{1,0},{2,3},{3,2},{4,5},{5,4},{6,7},{7,6},{8,9},{9,8},{10,11... | collective-permute-start | bytes 98312 | tf_op jit(solution)/shard_map/ppermute | solution.py:78
